TPU v7x, 128 devices: a whole 4x4x4 slice. The times are simulated.
128 devices in a mesh: grp: 4 (over y), dev: 32 (over z, x, core).
Axes of the slice: x: 4, y: 4, z: 4, core: 2. Of those that a mesh axis runs over, the one named last changes fastest.
Arguments:
- basis: float32 [8, 256, 16, 512], P(None, ('grp', 'dev')), may hold values from -6 to 6
- diagonal: float32 [256, 512], P(('grp', 'dev')), may hold values from 0.5 to 8
- near_blocks: bfloat16 [2048, 512, 512], P(('grp', 'dev')), may hold values from -0.03125 to 0.03125
- far_u: bfloat16 [14336, 32, 512], P(('grp', 'dev')), may hold values from -0.25 to 0.25
- far_v: bfloat16 [14336, 32, 512], P(('grp', 'dev')), may hold values from -0.125 to 0.125
- block_row: int32 [16384], P(('grp', 'dev')), may hold values from 0 to 1
- block_dest: int32 [16384, 1], P(('grp', 'dev')), may hold values from 0 to 127; in each aligned block of 128 rows (0 to 127, 128 to 255, ...) at most 2 rows name the same one
- block_col: int32 [16384], P(('grp', 'dev')), may hold values from 0 to 1
Outputs:
- next_vector: float32 [256, 16, 512], P(('grp', 'dev'))
- hess_column: float32 [9, 16], replicated
Inputs may be any that keep to these rules, and one draw needn't show every extreme that they name: `block_dest`: among the 128 blocks of one device at most 2 name the same owning device, and this most is reached on some device.
All inputs are finite; a program needn't handle non-finite values.
Results may differ from a plain program's by a relative error of at most 0.0017.
Values sent between devices are 32-bit elements; how exact they have to be, the bound alone decides.
No kernel may reach another device: no remote copies, remote signals or barrier semaphores. Data moves between devices by JAX's collectives and lax.ppermute only.
A program may use at most 128 MiB of HBM per device.

v0:
```python
import jax
import jax.numpy as jnp
from jax import lax
from jax.sharding import PartitionSpec as P


def on_device(basis, diagonal, near_blocks, far_u, far_v, block_row, block_dest, block_col):
    highest = lax.Precision.HIGHEST
    basis_count = basis.shape[0]
    clusters = basis.shape[1]
    sources = basis.shape[2]
    cluster_size = basis.shape[3]
    near_count = near_blocks.shape[0]
    devices = lax.axis_size(("grp", "dev"))
    vector = basis[basis_count - 1]
    vec_low = vector.astype(jnp.bfloat16)
    picked = vec_low[block_row]
    near_part = jnp.einsum(
        "snc,scd->snd", picked[:near_count], near_blocks, preferred_element_type=jnp.float32
    )
    coeff = jnp.einsum(
        "snc,skc->snk", picked[near_count:], far_u, preferred_element_type=jnp.float32
    ).astype(jnp.bfloat16)
    far_part = jnp.einsum("snk,skc->snc", coeff, far_v, preferred_element_type=jnp.float32)
    parts = jnp.concatenate([near_part, far_part], axis=0)
    target_dev = block_dest[:, 0]
    target = target_dev * clusters + block_col
    slab = jnp.zeros((devices * clusters, sources, cluster_size), jnp.float32).at[target].add(parts)
    summed = lax.psum_scatter(slab, ("grp", "dev"), scatter_dimension=0, tiled=True)
    image = diagonal[:, None, :] * vector + summed
    panels = clusters * cluster_size * devices
    local_first = jnp.einsum("knjc,njc->kj", basis, image, precision=highest)
    first = lax.psum(local_first, ("grp", "dev")) / panels
    once = image - jnp.einsum("kj,knjc->njc", first, basis, precision=highest)
    local_second = jnp.einsum("knjc,njc->kj", basis, once, precision=highest)
    second = lax.psum(local_second, ("grp", "dev")) / panels
    twice = once - jnp.einsum("kj,knjc->njc", second, basis, precision=highest)
    square = lax.psum(jnp.sum(twice * twice, axis=(0, 2)), ("grp", "dev")) / panels
    beta = jnp.sqrt(square + 1e-06)
    next_vector = twice / beta[None, :, None]
    hess_column = jnp.concatenate([first + second, beta[None, :]], axis=0)
    return (next_vector, hess_column)


def solution(mesh):
    in_specs = (
        P(None, ("grp", "dev"), None, None),
        P(("grp", "dev"), None),
        P(("grp", "dev"), None, None),
        P(("grp", "dev"), None, None),
        P(("grp", "dev"), None, None),
        P(("grp", "dev")),
        P(("grp", "dev"), None),
        P(("grp", "dev")),
    )
    out_specs = (P(("grp", "dev"), None, None), P())
    return jax.shard_map(
        on_device, mesh=mesh, in_specs=in_specs, out_specs=out_specs, check_vma=False
    )
```

profile of v0, /device:TPU:0, one launch (start us, length us, event | category | flops | bytes accessed | tf_op | source)
XLA Modules:
  0.0 907.1 jit_solution(5115005452646583750)
XLA Ops:
  7.2 0.0 reduce-scatter.2.cloned.1.call-start
  7.2 0.7 compare_select_fusion
  7.9 0.8 bitcast_convert_fusion
  8.7 0.7 gather_fusion
  9.4 0.0 copy-start.3
  9.4 3.2 convolution_convert_fusion
  12.7 1.2 copy-done.3
  13.9 0.0 copy-start.4
  13.9 0.0 copy-start.5
  13.9 0.0 copy-start.1
  13.9 1.2 fusion.14
  15.1 0.0 copy-done.4
  15.1 0.0 copy-done.5
  15.1 0.8 copy-done.1
  16.0 0.6 fusion.13
  16.6 2.8 pad_maximum_fusion
  19.4 4.3 broadcast_in_dim.14
  23.7 20.2 %scatter_fusion = f32[256,16,512]{2,1,0:T(8,128)} fusion(f32[256,16,512]{2,1,0:T(8,128)} %broadcast_in_dim.14, s32[128]{0:T(128)S(1)} %compare_select_fusion.1, f32[128,16,512]{2,1,0:T(8,128)} %pad_maximum_fusion), kind=kCustom, calls=%fused_computation.1 | custom fusion | flops 1048576 | bytes 12583424 | tf_op jit(solution)/shard_map/scatter-add | solution.py:28
  43.9 0.0 copy-start
  43.9 0.0 copy-start.2
  43.9 0.0 reduce-scatter.2.cloned.1.call-update
  43.9 660.2 %reduce-scatter.2.cloned.1.call-done = f32[2,16,512]{2,1,0:T(8,128)} async-done(((f32[256,16,512]{2,1,0:T(8,128)}), f32[2,16,512]{2,1,0:T(8,128)}) %reduce-scatter.2.cloned.1.call-update) | async-done | bytes 65552 | tf_op jit(solution)/shard_map/reduce_scatter | solution.py:29
  704.1 0.0 copy-done
  704.1 0.0 copy-done.2
  704.1 0.9 fusion.8
  704.9 1.5 fusion.6
  706.4 0.1 copy.12
  706.5 62.5 %psum.21 = f32[8,16]{1,0:T(8,128)S(1)} all-reduce(f32[8,16]{1,0:T(8,128)S(1)} %bitcast.53), channel_id=1, replica_groups=mesh['grp'=4,'dev'=32] {'grp','dev'}, use_global_device_ids=true, to_apply=%region_2.0 | all-reduce | flops 128 | bytes 1024 | tf_op jit(solution)/shard_map/psum | solution.py:33
  768.9 0.1 copy.13
  769.0 0.8 fusion.4
  769.9 1.5 fusion.2
  771.3 0.1 copy.16
  771.4 61.9 %psum.22 = f32[8,16]{1,0:T(8,128)S(1)} all-reduce(f32[8,16]{1,0:T(8,128)S(1)} %bitcast.54), channel_id=1, replica_groups=mesh['grp'=4,'dev'=32] {'grp','dev'}, use_global_device_ids=true, to_apply=%region_3.0 | all-reduce | flops 128 | bytes 1024 | tf_op jit(solution)/shard_map/psum | solution.py:36
  833.3 0.1 copy.17
  833.4 0.8 fusion
  834.2 0.1 multiply_reduce_fusion
  834.4 64.5 %psum.23 = f32[16]{0:T(128)S(1)} all-reduce(f32[16]{0:T(128)S(1)} %multiply_reduce_fusion), channel_id=1, replica_groups=mesh['grp'=4,'dev'=32] {'grp','dev'}, use_global_device_ids=true, to_apply=%region_5.0 | all-reduce | flops 16 | bytes 128 | tf_op jit(solution)/shard_map/psum | solution.py:38
  898.9 0.7 broadcast_divide_fusion
  899.6 0.6 pad_maximum_fusion.1
  (6 shorter events, 0.0 us)
Async XLA Ops:
  7.2 696.9 %reduce-scatter.2.cloned.1.call-start = ((), (), s32[]{:S(2)}) async-start(), calls=%async_computation.1 | async-start | bytes 8454144 | tf_op jit(solution)/shard_map/reduce_scatter | solution.py:29
  9.4 4.5 copy-start.3
  13.9 1.2 copy-start.4
  13.9 1.2 copy-start.5
  13.9 2.1 copy-start.1
  43.9 660.2 %copy-start = (f32[8,2,16,512]{3,2,1,0:T(8,128)S(1)}, f32[8,2,16,512]{3,2,1,0:T(8,128)}, u32[]{:S(2)}) copy-start(f32[8,2,16,512]{3,2,1,0:T(8,128)} %param.8) | copy-start | bytes 1572868
  43.9 660.2 %copy-start.2 = (f32[2,512]{1,0:T(2,128)S(1)}, f32[2,512]{1,0:T(2,128)}, u32[]{:S(2)}) copy-start(f32[2,512]{1,0:T(2,128)} %param.9) | copy-start | bytes 12292
Sparse Core Ops, SparseCore 0:
  44.0 660.0 reduce-scatter.1
where the time goes:
time: 908 us; the launch traced here: 907 us
  waiting for transfers between devices  660 us (73%)
  blocking collectives  189 us (21%)
  other arithmetic  26 us (3%)
  between operations  14.1 us (2%)
  matrix products  9.58 us (1%)
    reduce_scatter x1, waiting for transfers between devices, on_device(): lax.psum_scatter(slab, ('grp', 'dev'), scatter_dimension=0, tiled=True)  660 us
    psum x1, blocking collectives, on_device(): lax.psum(jnp.sum(twice * twice, axis=(0, 2)), ('grp', 'dev')) / panels  64.5 us
    psum x1, blocking collectives, on_device(): first = lax.psum(local_first, ('grp', 'dev')) / panels  62.5 us
    psum x1, blocking collectives, on_device(): second = lax.psum(local_second, ('grp', 'dev')) / panels  61.9 us
    scatter-add x1, other arithmetic, on_device(): jnp.zeros((devices * clusters, sources, cluster_size), jnp.float32)  20.2 us
  transfers between devices with their start and end apart: 1, of which 1 were waited for; matrix products, arithmetic and copies ran while one was open for 0% of the time, Pallas kernels for 0%

commit v1 on v0

v1 whole, which is shorter than its diff:
```python
import jax
import jax.numpy as jnp
from jax import lax
from jax.sharding import PartitionSpec as P

AXES = ("grp", "dev")
SIZES = {"y": 4, "z": 4, "x": 4, "c": 2}
STRIDE = {"y": 32, "z": 8, "x": 2, "c": 1}


def coord(g, axis):
    return (g // STRIDE[axis]) % SIZES[axis]


def moved(axis, k):
    n, s = SIZES[axis], STRIDE[axis]
    pairs = []
    for g in range(128):
        c = (g // s) % n
        pairs.append((g, g + (((c + k) % n) - c) * s))
    return pairs


def flipped(bit):
    return [(g, g ^ (1 << bit)) for g in range(128)]


def all_sum(v):
    for bit in range(7):
        v = v + lax.ppermute(v, AXES, flipped(bit))
    return v


def reduce_to_owner(slab):
    rest = slab.shape[1:]
    slab = slab.reshape((2, -1) + rest[-2:])
    d = slab[0] + lax.ppermute(slab[1], AXES, moved("c", 1))
    for axis in ("x", "z", "y"):
        d = d.reshape((4, -1) + rest[-2:])
        acc = d[0]
        for k in (1, 2, 3):
            acc = acc + lax.ppermute(d[k], AXES, moved(axis, k))
        d = acc
    return d


def on_device(basis, diagonal, near_blocks, far_u, far_v, block_row, block_dest, block_col):
    highest = lax.Precision.HIGHEST
    basis_count = basis.shape[0]
    clusters = basis.shape[1]
    sources = basis.shape[2]
    cluster_size = basis.shape[3]
    near_count = near_blocks.shape[0]
    devices = lax.axis_size(AXES)
    me = lax.axis_index(AXES)
    vector = basis[basis_count - 1]
    vec_low = vector.astype(jnp.bfloat16)
    picked = vec_low[block_row]
    near_part = jnp.einsum(
        "snc,scd->snd", picked[:near_count], near_blocks, preferred_element_type=jnp.float32
    )
    coeff = jnp.einsum(
        "snc,skc->snk", picked[near_count:], far_u, preferred_element_type=jnp.float32
    ).astype(jnp.bfloat16)
    far_part = jnp.einsum("snk,skc->snc", coeff, far_v, preferred_element_type=jnp.float32)
    parts = jnp.concatenate([near_part, far_part], axis=0)
    dest = block_dest[:, 0]
    rel = {a: (coord(dest, a) - coord(me, a)) % SIZES[a] for a in SIZES}
    slot = (((rel["c"] * 4 + rel["x"]) * 4 + rel["z"]) * 4 + rel["y"]) * clusters + block_col
    slab = jnp.zeros((devices * clusters, sources, cluster_size), jnp.float32).at[slot].add(parts)
    summed = reduce_to_owner(slab.reshape(2, 4, 4, 4, clusters, sources, cluster_size))
    image = diagonal[:, None, :] * vector + summed
    panels = clusters * cluster_size * devices
    local_first = jnp.einsum("knjc,njc->kj", basis, image, precision=highest)
    local_gram = jnp.einsum("knjc,mnjc->kmj", basis, basis, precision=highest)
    both = all_sum(jnp.concatenate([local_first, local_gram.reshape(-1, sources)], axis=0))
    first = both[:basis_count] / panels
    gram = both[basis_count:].reshape(basis_count, basis_count, sources) / panels
    second = first - jnp.einsum("kmj,mj->kj", gram, first, precision=highest)
    total = first + second
    twice = image - jnp.einsum("kj,knjc->njc", total, basis, precision=highest)
    square = all_sum(jnp.sum(twice * twice, axis=(0, 2))) / panels
    beta = jnp.sqrt(square + 1e-06)
    next_vector = twice / beta[None, :, None]
    hess_column = jnp.concatenate([total, beta[None, :]], axis=0)
    return (next_vector, hess_column)


def solution(mesh):
    in_specs = (
        P(None, AXES, None, None),
        P(AXES, None),
        P(AXES, None, None),
        P(AXES, None, None),
        P(AXES, None, None),
        P(AXES),
        P(AXES, None),
        P(AXES),
    )
    out_specs = (P(AXES, None, None), P())
    return jax.shard_map(
        on_device, mesh=mesh, in_specs=in_specs, out_specs=out_specs, check_vma=False
    )
```

time: 908 us -> 189 us (0.21)
  waiting for transfers between devices: 660 us -> 99.7 us
  blocking collectives: 189 us -> 0 us
  starting transfers between devices: 0.04 us -> 38.3 us
  between operations: 14.1 us -> 0.89 us
    reduce_scatter x1 -> x0, waiting for transfers between devices: 660 us -> none  [on_device(): lax.psum_scatter(slab, ('grp', 'dev'), scatter_dimension=0, tiled=True)]
    psum x3 -> x0, blocking collectives: 189 us -> none  [the longest x1 64.5 us: on_device(): lax.psum(jnp.sum(twice * twice, axis=(0, 2)), ('grp', 'dev')) / panels]
    ppermute x0 -> x24, waiting for transfers between devices: none -> 99.7 us  [the longest x9 55.7 us: reduce_to_owner(): acc = acc + lax.ppermute(d[k], AXES, moved(axis, k))]
    ppermute x0 -> x24, starting transfers between devices: none -> 38.3 us  [the longest x14 19.9 us: all_sum(): v = v + lax.ppermute(v, AXES, flipped(bit))]
  transfers between devices with their start and end apart: 1 -> 24, of which waited for: 1 -> 21; matrix products, arithmetic and copies ran while one was open for 0% -> 1% of each run, Pallas kernels for 0% -> 0%
where the time goes in v1:
time: 189 us; the launch traced here: 188 us
  waiting for transfers between devices  99.7 us (53%)
  starting transfers between devices  38.3 us (20%)
  other arithmetic  27.7 us (15%)
  local copies, waits for them, and re-layouts  10.8 us (6%)
  matrix products  10.7 us (6%)
    ppermute x9, waiting for transfers between devices, reduce_to_owner(): acc = acc + lax.ppermute(d[k], AXES, moved(axis, k))  55.7 us
    ppermute x14, waiting for transfers between devices, all_sum(): v = v + lax.ppermute(v, AXES, flipped(bit))  36.9 us
    scatter-add x1, other arithmetic, on_device(): jnp.zeros((devices * clusters, sources, cluster_size), jnp.float32).at[slot]  20.4 us
    ppermute x14, starting transfers between devices, all_sum(): v = v + lax.ppermute(v, AXES, flipped(bit))  19.9 us
    ppermute x9, starting transfers between devices, reduce_to_owner(): acc = acc + lax.ppermute(d[k], AXES, moved(axis, k))  18.3 us
    ppermute x1, waiting for transfers between devices, reduce_to_owner(): d = slab[0] + lax.ppermute(slab[1], AXES, moved('c', 1))  7.15 us
    broadcast_in_dim x1, local copies, waits for them, and re-layouts, on_device(): jnp.zeros((devices * clusters, sources, cluster_size), jnp.float32).at[slot]  4.32 us
  transfers between devices with their start and end apart: 24, of which 21 were waited for; matrix products, arithmetic and copies ran while one was open for 1% of the time, Pallas kernels for 0%

profile of v1, /device:TPU:0, one launch (start us, length us, event | category | flops | bytes accessed | tf_op | source)
XLA Modules:
  0.0 188.0 jit_solution(1793263570878272300)
XLA Ops:
  2.9 3.2 %convolution_convert_fusion = bf16[112,16,32]{2,1,0:T(8,128)(2,1)S(1)} fusion(bf16[128,16,512]{2,1,0:T(8,128)(2,1)S(1)} %gather_fusion, bf16[112,32,512]{2,1,0:T(8,128)(2,1)} %param.11), kind=kOutput, calls=%fused_computation.4 | convolution fusion | flops 58777600 | bytes 5881856 | tf_op jit(solution)/shard_map/snc,skc->snk/dot_general | solution.py:62
  6.2 1.2 copy-done.5
  7.4 1.2 fusion.38
  8.6 2.7 %fusion.37 = f32[112,16,512]{2,1,0:T(8,128)S(1)} fusion(bf16[112,16,32]{2,1,0:T(8,128)(2,1)S(1)} %convolution_convert_fusion, bf16[112,32,512]{2,1,0:T(8,128)(2,1)} %param.12), kind=kOutput, calls=%fused_computation.94 | convolution fusion | flops 58720256 | bytes 7454720 | tf_op jit(solution)/shard_map/snk,skc->snc/dot_general | solution.py:65
  11.3 2.8 %pad_maximum_fusion = f32[128,16,512]{2,1,0:T(8,128)} fusion(f32[112,16,512]{2,1,0:T(8,128)S(1)} %fusion.37, f32[16,16,512]{2,1,0:T(8,128)S(1)} %fusion.38), kind=kLoop, calls=%fused_computation.3 | loop fusion | flops 1048576 | bytes 8388608 | tf_op jit(solution)/shard_map/concatenate | solution.py:66
  14.2 4.3 %broadcast_in_dim.14 = f32[256,16,512]{2,1,0:T(8,128)} broadcast(f32[]{:T(128)} %constant.155.clone.1), dimensions={} | broadcast | bytes 8388612 | tf_op jit(solution)/shard_map/broadcast_in_dim | solution.py:70
  18.5 20.4 %scatter_fusion = f32[256,16,512]{2,1,0:T(8,128)} fusion(f32[256,16,512]{2,1,0:T(8,128)} %broadcast_in_dim.14, s32[128]{0:T(128)S(1)} %compare_select_fusion.1, f32[128,16,512]{2,1,0:T(8,128)} %pad_maximum_fusion), kind=kCustom, calls=%fused_computation.1 | custom fusion | flops 1048576 | bytes 12583424 | tf_op jit(solution)/shard_map/scatter-add | solution.py:70
  38.9 2.8 %slice.93 = f32[128,16,512]{2,1,0:T(8,128)S(1)} slice(f32[256,16,512]{2,1,0:T(8,128)} %scatter_fusion), slice={[128:256], [0:16], [0:512]} | slice | bytes 8388608 | tf_op jit(solution)/shard_map/slice | solution.py:37
  41.8 7.1 %collective-permute-done = f32[128,16,512]{2,1,0:T(8,128)S(1)} collective-permute-done((f32[128,16,512]{2,1,0:T(8,128)S(1)}, f32[128,16,512]{2,1,0:T(8,128)S(1)}, u32[]{:S(2)}, u32[]{:S(2)}) %collective-permute-start) | collective-permute-done | bytes 4194336 | tf_op jit(solution)/shard_map/ppermute | solution.py:37
  49.0 1.5 slice_add_fusion
  51.0 1.6 collective-permute-start.1
  52.6 2.7 %collective-permute-start.2 = (f32[32,16,512]{2,1,0:T(8,128)S(1)}, f32[32,16,512]{2,1,0:T(8,128)S(1)}, u32[]{:S(2)}, u32[]{:S(2)}) collective-permute-start(f32[32,16,512]{2,1,0:T(8,128)S(1)} %get-tuple-element.6), channel_id=1, source_target_pairs={{0,4},{1,5},{2,6},{3,7},{4,0},{5,1},{6,2},{7,3},{8,12},{9,13},{10,... | collective-permute-start | bytes 3145736 | tf_op jit(solution)/shard_map/ppermute | solution.py:42
  55.3 1.5 collective-permute-start.3
  56.8 20.7 %collective-permute-done.1 = f32[32,16,512]{2,1,0:T(8,128)S(1)} collective-permute-done((f32[32,16,512]{2,1,0:T(8,128)S(1)}, f32[32,16,512]{2,1,0:T(8,128)S(1)}, u32[]{:S(2)}, u32[]{:S(2)}) %collective-permute-start.1) | collective-permute-done | bytes 1048608 | tf_op jit(solution)/shard_map/ppermute | solution.py:42
  77.5 23.4 %collective-permute-done.2 = f32[32,16,512]{2,1,0:T(8,128)S(1)} collective-permute-done((f32[32,16,512]{2,1,0:T(8,128)S(1)}, f32[32,16,512]{2,1,0:T(8,128)S(1)}, u32[]{:S(2)}, u32[]{:S(2)}) %collective-permute-start.2) | collective-permute-done | bytes 1048608 | tf_op jit(solution)/shard_map/ppermute | solution.py:42
  101.6 2.1 %collective-permute-start.4 = (f32[8,16,512]{2,1,0:T(8,128)S(1)}, f32[8,16,512]{2,1,0:T(8,128)S(1)}, u32[]{:S(2)}, u32[]{:S(2)}) collective-permute-start(f32[8,16,512]{2,1,0:T(8,128)S(1)} %get-tuple-element.7), channel_id=1, source_target_pairs={{0,8},{1,9},{2,10},{3,11},{4,12},{5,13},{6,14},{7,15},{8,16},{9,17... | collective-permute-start | bytes 786440 | tf_op jit(solution)/shard_map/ppermute | solution.py:42
  103.7 3.6 %collective-permute-start.5 = (f32[8,16,512]{2,1,0:T(8,128)S(1)}, f32[8,16,512]{2,1,0:T(8,128)S(1)}, u32[]{:S(2)}, u32[]{:S(2)}) collective-permute-start(f32[8,16,512]{2,1,0:T(8,128)S(1)} %get-tuple-element.9), channel_id=1, source_target_pairs={{0,16},{1,17},{2,18},{3,19},{4,20},{5,21},{6,22},{7,23},{8,24},{9,... | collective-permute-start | bytes 786440 | tf_op jit(solution)/shard_map/ppermute | solution.py:42
  108.2 3.9 %collective-permute-done.4 = f32[8,16,512]{2,1,0:T(8,128)S(1)} collective-permute-done((f32[8,16,512]{2,1,0:T(8,128)S(1)}, f32[8,16,512]{2,1,0:T(8,128)S(1)}, u32[]{:S(2)}, u32[]{:S(2)}) %collective-permute-start.4) | collective-permute-done | bytes 262176 | tf_op jit(solution)/shard_map/ppermute | solution.py:42
  112.1 6.3 %collective-permute-done.5 = f32[8,16,512]{2,1,0:T(8,128)S(1)} collective-permute-done((f32[8,16,512]{2,1,0:T(8,128)S(1)}, f32[8,16,512]{2,1,0:T(8,128)S(1)}, u32[]{:S(2)}, u32[]{:S(2)}) %collective-permute-start.5) | collective-permute-done | bytes 262176 | tf_op jit(solution)/shard_map/ppermute | solution.py:42
  118.5 1.6 collective-permute-start.7
  120.1 2.9 %collective-permute-start.8 = (f32[2,16,512]{2,1,0:T(8,128)S(1)}, f32[2,16,512]{2,1,0:T(8,128)S(1)}, u32[]{:S(2)}, u32[]{:S(2)}) collective-permute-start(f32[2,16,512]{2,1,0:T(8,128)S(1)} %get-tuple-element.12), channel_id=1, source_target_pairs={{0,64},{1,65},{2,66},{3,67},{4,68},{5,69},{6,70},{7,71},{8,72},{9,... | collective-permute-start | bytes 196616 | tf_op jit(solution)/shard_map/ppermute | solution.py:42
  123.0 1.4 collective-permute-start.9
  124.4 1.3 convolution_bitcast_fusion
  125.9 1.3 collective-permute-done.9
  127.3 1.5 fusion.4
  128.9 1.2 collective-permute-done.10
  130.1 1.4 collective-permute-start.11
  131.5 2.6 %collective-permute-done.11 = f32[72,16]{1,0:T(8,128)S(1)} collective-permute-done((f32[72,16]{1,0:T(8,128)S(1)}, f32[72,16]{1,0:T(8,128)S(1)}, u32[]{:S(2)}, u32[]{:S(2)}) %collective-permute-start.11) | collective-permute-done | bytes 4640 | tf_op jit(solution)/shard_map/ppermute | solution.py:30
  134.1 2.5 %collective-permute-start.12 = (f32[72,16]{1,0:T(8,128)S(1)}, f32[72,16]{1,0:T(8,128)S(1)}, u32[]{:S(2)}, u32[]{:S(2)}) collective-permute-start(f32[72,16]{1,0:T(8,128)S(1)} %add.194), channel_id=1, source_target_pairs={{0,4},{1,5},{2,6},{3,7},{4,0},{5,1},{6,2},{7,3},{8,12},{9,13},{10,... | collective-permute-start | bytes 13832 | tf_op jit(solution)/shard_map/ppermute | solution.py:30
  136.6 3.0 %collective-permute-done.12 = f32[72,16]{1,0:T(8,128)S(1)} collective-permute-done((f32[72,16]{1,0:T(8,128)S(1)}, f32[72,16]{1,0:T(8,128)S(1)}, u32[]{:S(2)}, u32[]{:S(2)}) %collective-permute-start.12) | collective-permute-done | bytes 4640 | tf_op jit(solution)/shard_map/ppermute | solution.py:30
  139.6 1.2 collective-permute-start.13
  140.8 2.7 %collective-permute-done.13 = f32[72,16]{1,0:T(8,128)S(1)} collective-permute-done((f32[72,16]{1,0:T(8,128)S(1)}, f32[72,16]{1,0:T(8,128)S(1)}, u32[]{:S(2)}, u32[]{:S(2)}) %collective-permute-start.13) | collective-permute-done | bytes 4640 | tf_op jit(solution)/shard_map/ppermute | solution.py:30
  143.6 2.3 %collective-permute-start.14 = (f32[72,16]{1,0:T(8,128)S(1)}, f32[72,16]{1,0:T(8,128)S(1)}, u32[]{:S(2)}, u32[]{:S(2)}) collective-permute-start(f32[72,16]{1,0:T(8,128)S(1)} %add.196), channel_id=1, source_target_pairs={{0,16},{1,17},{2,18},{3,19},{4,20},{5,21},{6,22},{7,23},{8,24},{9,... | collective-permute-start | bytes 13832 | tf_op jit(solution)/shard_map/ppermute | solution.py:30
  145.9 3.1 %collective-permute-done.14 = f32[72,16]{1,0:T(8,128)S(1)} collective-permute-done((f32[72,16]{1,0:T(8,128)S(1)}, f32[72,16]{1,0:T(8,128)S(1)}, u32[]{:S(2)}, u32[]{:S(2)}) %collective-permute-start.14) | collective-permute-done | bytes 4640 | tf_op jit(solution)/shard_map/ppermute | solution.py:30
  149.4 3.6 %collective-permute-done.15 = f32[72,16]{1,0:T(8,128)S(1)} collective-permute-done((f32[72,16]{1,0:T(8,128)S(1)}, f32[72,16]{1,0:T(8,128)S(1)}, u32[]{:S(2)}, u32[]{:S(2)}) %collective-permute-start.15) | collective-permute-done | bytes 4640 | tf_op jit(solution)/shard_map/ppermute | solution.py:30
  153.0 2.1 %collective-permute-start.16 = (f32[72,16]{1,0:T(8,128)S(1)}, f32[72,16]{1,0:T(8,128)S(1)}, u32[]{:S(2)}, u32[]{:S(2)}) collective-permute-start(f32[72,16]{1,0:T(8,128)S(1)} %add.198), channel_id=1, source_target_pairs={{0,64},{1,65},{2,66},{3,67},{4,68},{5,69},{6,70},{7,71},{8,72},{9,... | collective-permute-start | bytes 13832 | tf_op jit(solution)/shard_map/ppermute | solution.py:30
  155.1 3.4 %collective-permute-done.16 = f32[72,16]{1,0:T(8,128)S(1)} collective-permute-done((f32[72,16]{1,0:T(8,128)S(1)}, f32[72,16]{1,0:T(8,128)S(1)}, u32[]{:S(2)}, u32[]{:S(2)}) %collective-permute-start.16) | collective-permute-done | bytes 4640 | tf_op jit(solution)/shard_map/ppermute | solution.py:30
  160.8 1.3 collective-permute-start.18
  162.1 2.2 %collective-permute-done.18 = f32[16]{0:T(128)S(1)} collective-permute-done((f32[16]{0:T(128)S(1)}, f32[16]{0:T(128)S(1)}, u32[]{:S(2)}, u32[]{:S(2)}) %collective-permute-start.18) | collective-permute-done | bytes 96 | tf_op jit(solution)/shard_map/ppermute | solution.py:30
  164.3 2.5 %collective-permute-start.19 = (f32[16]{0:T(128)S(1)}, f32[16]{0:T(128)S(1)}, u32[]{:S(2)}, u32[]{:S(2)}) collective-permute-start(f32[16]{0:T(128)S(1)} %add.202), channel_id=1, source_target_pairs={{0,4},{1,5},{2,6},{3,7},{4,0},{5,1},{6,2},{7,3},{8,12},{9,13},{10,... | collective-permute-start | bytes 200 | tf_op jit(solution)/shard_map/ppermute | solution.py:30
  166.8 2.6 %collective-permute-done.19 = f32[16]{0:T(128)S(1)} collective-permute-done((f32[16]{0:T(128)S(1)}, f32[16]{0:T(128)S(1)}, u32[]{:S(2)}, u32[]{:S(2)}) %collective-permute-start.19) | collective-permute-done | bytes 96 | tf_op jit(solution)/shard_map/ppermute | solution.py:30
  169.4 1.2 collective-permute-start.20
  170.6 2.3 %collective-permute-done.20 = f32[16]{0:T(128)S(1)} collective-permute-done((f32[16]{0:T(128)S(1)}, f32[16]{0:T(128)S(1)}, u32[]{:S(2)}, u32[]{:S(2)}) %collective-permute-start.20) | collective-permute-done | bytes 96 | tf_op jit(solution)/shard_map/ppermute | solution.py:30
  173.0 2.3 %collective-permute-start.21 = (f32[16]{0:T(128)S(1)}, f32[16]{0:T(128)S(1)}, u32[]{:S(2)}, u32[]{:S(2)}) collective-permute-start(f32[16]{0:T(128)S(1)} %add.204), channel_id=1, source_target_pairs={{0,16},{1,17},{2,18},{3,19},{4,20},{5,21},{6,22},{7,23},{8,24},{9,... | collective-permute-start | bytes 200 | tf_op jit(solution)/shard_map/ppermute | solution.py:30
  175.3 2.8 %collective-permute-done.21 = f32[16]{0:T(128)S(1)} collective-permute-done((f32[16]{0:T(128)S(1)}, f32[16]{0:T(128)S(1)}, u32[]{:S(2)}, u32[]{:S(2)}) %collective-permute-start.21) | collective-permute-done | bytes 96 | tf_op jit(solution)/shard_map/ppermute | solution.py:30
  178.5 3.2 %collective-permute-done.22 = f32[16]{0:T(128)S(1)} collective-permute-done((f32[16]{0:T(128)S(1)}, f32[16]{0:T(128)S(1)}, u32[]{:S(2)}, u32[]{:S(2)}) %collective-permute-start.22) | collective-permute-done | bytes 96 | tf_op jit(solution)/shard_map/ppermute | solution.py:30
  181.6 2.1 %collective-permute-start.23 = (f32[16]{0:T(128)S(1)}, f32[16]{0:T(128)S(1)}, u32[]{:S(2)}, u32[]{:S(2)}) collective-permute-start(f32[16]{0:T(128)S(1)} %add.206), channel_id=1, source_target_pairs={{0,64},{1,65},{2,66},{3,67},{4,68},{5,69},{6,70},{7,71},{8,72},{9,... | collective-permute-start | bytes 200 | tf_op jit(solution)/shard_map/ppermute | solution.py:30
  183.7 3.0 %collective-permute-done.23 = f32[16]{0:T(128)S(1)} collective-permute-done((f32[16]{0:T(128)S(1)}, f32[16]{0:T(128)S(1)}, u32[]{:S(2)}, u32[]{:S(2)}) %collective-permute-start.23) | collective-permute-done | bytes 96 | tf_op jit(solution)/shard_map/ppermute | solution.py:30
  (58 shorter events, 9.4 us)
Async XLA Ops:
  2.9 4.5 %copy-start.5 = (bf16[16,512,512]{2,1,0:T(8,128)(2,1)S(1)}, bf16[16,512,512]{2,1,0:T(8,128)(2,1)}, u32[]{:S(2)}) copy-start(bf16[16,512,512]{2,1,0:T(8,128)(2,1)} %param.10) | copy-start | bytes 25165828
  11.3 2.9 %copy-start.3 = (s32[128]{0:T(128)S(1)}, s32[128]{0:T(128)}, u32[]{:S(2)}) copy-start(s32[128]{0:T(128)} %param.15) | copy-start | bytes 1540
  11.3 2.9 %copy-start.4 = (s32[128,1]{0,1:T(1,128)S(1)}, s32[128,1]{0,1:T(1,128)}, u32[]{:S(2)}) copy-start(s32[128,1]{0,1:T(1,128)} %param.14) | copy-start | bytes 1540
  38.9 10.1 %copy-start = (f32[256,16,512]{2,1,0:T(8,128)S(1)}, f32[256,16,512]{2,1,0:T(8,128)}, u32[]{:S(2)}) copy-start(f32[256,16,512]{2,1,0:T(8,128)} %scatter_fusion) | copy-start | bytes 25165828
  41.7 7.2 %collective-permute-start = (f32[128,16,512]{2,1,0:T(8,128)S(1)}, f32[128,16,512]{2,1,0:T(8,128)S(1)}, u32[]{:S(2)}, u32[]{:S(2)}) collective-permute-start(f32[128,16,512]{2,1,0:T(8,128)S(1)} %slice.93), channel_id=1, source_target_pairs={{0,1},{1,0},{2,3},{3,2},{4,5},{5,4},{6,7},{7,6},{8,9},{9,8},{10,11... | collective-permute-start | bytes 12582920 | tf_op jit(solution)/shard_map/ppermute | solution.py:37
  51.0 26.5 %collective-permute-start.1 = (f32[32,16,512]{2,1,0:T(8,128)S(1)}, f32[32,16,512]{2,1,0:T(8,128)S(1)}, u32[]{:S(2)}, u32[]{:S(2)}) collective-permute-start(f32[32,16,512]{2,1,0:T(8,128)S(1)} %get-tuple-element.4), channel_id=1, source_target_pairs={{0,2},{1,3},{2,4},{3,5},{4,6},{5,7},{6,0},{7,1},{8,10},{9,11},{10,... | collective-permute-start | bytes 3145736 | tf_op jit(solution)/shard_map/ppermute | solution.py:42
  52.6 48.3 %collective-permute-start.2 = (f32[32,16,512]{2,1,0:T(8,128)S(1)}, f32[32,16,512]{2,1,0:T(8,128)S(1)}, u32[]{:S(2)}, u32[]{:S(2)}) collective-permute-start(f32[32,16,512]{2,1,0:T(8,128)S(1)} %get-tuple-element.6), channel_id=1, source_target_pairs={{0,4},{1,5},{2,6},{3,7},{4,0},{5,1},{6,2},{7,3},{8,12},{9,13},{10,... | collective-permute-start | bytes 3145736 | tf_op jit(solution)/shard_map/ppermute | solution.py:42
  55.3 69.1 %copy-start.1 = (f32[8,2,16,512]{3,2,1,0:T(8,128)S(1)}, f32[8,2,16,512]{3,2,1,0:T(8,128)}, u32[]{:S(2)}) copy-start(f32[8,2,16,512]{3,2,1,0:T(8,128)} %param.8) | copy-start | bytes 1572868
  55.3 71.9 %copy-start.2 = (f32[2,512]{1,0:T(2,128)S(1)}, f32[2,512]{1,0:T(2,128)}, u32[]{:S(2)}) copy-start(f32[2,512]{1,0:T(2,128)} %param.9) | copy-start | bytes 12292
  55.3 45.6 %collective-permute-start.3 = (f32[32,16,512]{2,1,0:T(8,128)S(1)}, f32[32,16,512]{2,1,0:T(8,128)S(1)}, u32[]{:S(2)}, u32[]{:S(2)}) collective-permute-start(f32[32,16,512]{2,1,0:T(8,128)S(1)} %get-tuple-element.5), channel_id=1, source_target_pairs={{0,6},{1,7},{2,0},{3,1},{4,2},{5,3},{6,4},{7,5},{8,14},{9,15},{10,... | collective-permute-start | bytes 3145736 | tf_op jit(solution)/shard_map/ppermute | solution.py:42
  101.6 10.5 %collective-permute-start.4 = (f32[8,16,512]{2,1,0:T(8,128)S(1)}, f32[8,16,512]{2,1,0:T(8,128)S(1)}, u32[]{:S(2)}, u32[]{:S(2)}) collective-permute-start(f32[8,16,512]{2,1,0:T(8,128)S(1)} %get-tuple-element.7), channel_id=1, source_target_pairs={{0,8},{1,9},{2,10},{3,11},{4,12},{5,13},{6,14},{7,15},{8,16},{9,17... | collective-permute-start | bytes 786440 | tf_op jit(solution)/shard_map/ppermute | solution.py:42
  103.7 14.7 %collective-permute-start.5 = (f32[8,16,512]{2,1,0:T(8,128)S(1)}, f32[8,16,512]{2,1,0:T(8,128)S(1)}, u32[]{:S(2)}, u32[]{:S(2)}) collective-permute-start(f32[8,16,512]{2,1,0:T(8,128)S(1)} %get-tuple-element.9), channel_id=1, source_target_pairs={{0,16},{1,17},{2,18},{3,19},{4,20},{5,21},{6,22},{7,23},{8,24},{9,... | collective-permute-start | bytes 786440 | tf_op jit(solution)/shard_map/ppermute | solution.py:42
  107.3 11.1 %collective-permute-start.6 = (f32[8,16,512]{2,1,0:T(8,128)S(1)}, f32[8,16,512]{2,1,0:T(8,128)S(1)}, u32[]{:S(2)}, u32[]{:S(2)}) collective-permute-start(f32[8,16,512]{2,1,0:T(8,128)S(1)} %get-tuple-element.8), channel_id=1, source_target_pairs={{0,24},{1,25},{2,26},{3,27},{4,28},{5,29},{6,30},{7,31},{8,0},{9,1... | collective-permute-start | bytes 786440 | tf_op jit(solution)/shard_map/ppermute | solution.py:42
  118.5 7.3 %collective-permute-start.7 = (f32[2,16,512]{2,1,0:T(8,128)S(1)}, f32[2,16,512]{2,1,0:T(8,128)S(1)}, u32[]{:S(2)}, u32[]{:S(2)}) collective-permute-start(f32[2,16,512]{2,1,0:T(8,128)S(1)} %get-tuple-element.10), channel_id=1, source_target_pairs={{0,32},{1,33},{2,34},{3,35},{4,36},{5,37},{6,38},{7,39},{8,40},{9,... | collective-permute-start | bytes 196616 | tf_op jit(solution)/shard_map/ppermute | solution.py:42
  120.1 5.8 %collective-permute-start.8 = (f32[2,16,512]{2,1,0:T(8,128)S(1)}, f32[2,16,512]{2,1,0:T(8,128)S(1)}, u32[]{:S(2)}, u32[]{:S(2)}) collective-permute-start(f32[2,16,512]{2,1,0:T(8,128)S(1)} %get-tuple-element.12), channel_id=1, source_target_pairs={{0,64},{1,65},{2,66},{3,67},{4,68},{5,69},{6,70},{7,71},{8,72},{9,... | collective-permute-start | bytes 196616 | tf_op jit(solution)/shard_map/ppermute | solution.py:42
  123.0 4.3 %collective-permute-start.9 = (f32[2,16,512]{2,1,0:T(8,128)S(1)}, f32[2,16,512]{2,1,0:T(8,128)S(1)}, u32[]{:S(2)}, u32[]{:S(2)}) collective-permute-start(f32[2,16,512]{2,1,0:T(8,128)S(1)} %get-tuple-element.11), channel_id=1, source_target_pairs={{0,96},{1,97},{2,98},{3,99},{4,100},{5,101},{6,102},{7,103},{8,104... | collective-permute-start | bytes 196616 | tf_op jit(solution)/shard_map/ppermute | solution.py:42
  128.8 1.2 collective-permute-start.10
  130.1 4.0 %collective-permute-start.11 = (f32[72,16]{1,0:T(8,128)S(1)}, f32[72,16]{1,0:T(8,128)S(1)}, u32[]{:S(2)}, u32[]{:S(2)}) collective-permute-start(f32[72,16]{1,0:T(8,128)S(1)} %fusion.33), channel_id=1, source_target_pairs={{0,2},{1,3},{2,0},{3,1},{4,6},{5,7},{6,4},{7,5},{8,10},{9,11},{10,... | collective-permute-start | bytes 13832 | tf_op jit(solution)/shard_map/ppermute | solution.py:30
  134.1 5.5 %collective-permute-start.12 = (f32[72,16]{1,0:T(8,128)S(1)}, f32[72,16]{1,0:T(8,128)S(1)}, u32[]{:S(2)}, u32[]{:S(2)}) collective-permute-start(f32[72,16]{1,0:T(8,128)S(1)} %add.194), channel_id=1, source_target_pairs={{0,4},{1,5},{2,6},{3,7},{4,0},{5,1},{6,2},{7,3},{8,12},{9,13},{10,... | collective-permute-start | bytes 13832 | tf_op jit(solution)/shard_map/ppermute | solution.py:30
  139.6 4.0 %collective-permute-start.13 = (f32[72,16]{1,0:T(8,128)S(1)}, f32[72,16]{1,0:T(8,128)S(1)}, u32[]{:S(2)}, u32[]{:S(2)}) collective-permute-start(f32[72,16]{1,0:T(8,128)S(1)} %add.195), channel_id=1, source_target_pairs={{0,8},{1,9},{2,10},{3,11},{4,12},{5,13},{6,14},{7,15},{8,0},{9,1},... | collective-permute-start | bytes 13832 | tf_op jit(solution)/shard_map/ppermute | solution.py:30
  143.6 5.5 %collective-permute-start.14 = (f32[72,16]{1,0:T(8,128)S(1)}, f32[72,16]{1,0:T(8,128)S(1)}, u32[]{:S(2)}, u32[]{:S(2)}) collective-permute-start(f32[72,16]{1,0:T(8,128)S(1)} %add.196), channel_id=1, source_target_pairs={{0,16},{1,17},{2,18},{3,19},{4,20},{5,21},{6,22},{7,23},{8,24},{9,... | collective-permute-start | bytes 13832 | tf_op jit(solution)/shard_map/ppermute | solution.py:30
  149.0 4.0 %collective-permute-start.15 = (f32[72,16]{1,0:T(8,128)S(1)}, f32[72,16]{1,0:T(8,128)S(1)}, u32[]{:S(2)}, u32[]{:S(2)}) collective-permute-start(f32[72,16]{1,0:T(8,128)S(1)} %add.197), channel_id=1, source_target_pairs={{0,32},{1,33},{2,34},{3,35},{4,36},{5,37},{6,38},{7,39},{8,40},{9,... | collective-permute-start | bytes 13832 | tf_op jit(solution)/shard_map/ppermute | solution.py:30
  153.0 5.5 %collective-permute-start.16 = (f32[72,16]{1,0:T(8,128)S(1)}, f32[72,16]{1,0:T(8,128)S(1)}, u32[]{:S(2)}, u32[]{:S(2)}) collective-permute-start(f32[72,16]{1,0:T(8,128)S(1)} %add.198), channel_id=1, source_target_pairs={{0,64},{1,65},{2,66},{3,67},{4,68},{5,69},{6,70},{7,71},{8,72},{9,... | collective-permute-start | bytes 13832 | tf_op jit(solution)/shard_map/ppermute | solution.py:30
  159.5 1.2 collective-permute-start.17
  160.8 3.6 %collective-permute-start.18 = (f32[16]{0:T(128)S(1)}, f32[16]{0:T(128)S(1)}, u32[]{:S(2)}, u32[]{:S(2)}) collective-permute-start(f32[16]{0:T(128)S(1)} %add.201), channel_id=1, source_target_pairs={{0,2},{1,3},{2,0},{3,1},{4,6},{5,7},{6,4},{7,5},{8,10},{9,11},{10,... | collective-permute-start | bytes 200 | tf_op jit(solution)/shard_map/ppermute | solution.py:30
  164.3 5.1 %collective-permute-start.19 = (f32[16]{0:T(128)S(1)}, f32[16]{0:T(128)S(1)}, u32[]{:S(2)}, u32[]{:S(2)}) collective-permute-start(f32[16]{0:T(128)S(1)} %add.202), channel_id=1, source_target_pairs={{0,4},{1,5},{2,6},{3,7},{4,0},{5,1},{6,2},{7,3},{8,12},{9,13},{10,... | collective-permute-start | bytes 200 | tf_op jit(solution)/shard_map/ppermute | solution.py:30
  169.4 3.6 %collective-permute-start.20 = (f32[16]{0:T(128)S(1)}, f32[16]{0:T(128)S(1)}, u32[]{:S(2)}, u32[]{:S(2)}) collective-permute-start(f32[16]{0:T(128)S(1)} %add.203), channel_id=1, source_target_pairs={{0,8},{1,9},{2,10},{3,11},{4,12},{5,13},{6,14},{7,15},{8,0},{9,1},... | collective-permute-start | bytes 200 | tf_op jit(solution)/shard_map/ppermute | solution.py:30
  173.0 5.1 %collective-permute-start.21 = (f32[16]{0:T(128)S(1)}, f32[16]{0:T(128)S(1)}, u32[]{:S(2)}, u32[]{:S(2)}) collective-permute-start(f32[16]{0:T(128)S(1)} %add.204), channel_id=1, source_target_pairs={{0,16},{1,17},{2,18},{3,19},{4,20},{5,21},{6,22},{7,23},{8,24},{9,... | collective-permute-start | bytes 200 | tf_op jit(solution)/shard_map/ppermute | solution.py:30
  178.1 3.6 %collective-permute-start.22 = (f32[16]{0:T(128)S(1)}, f32[16]{0:T(128)S(1)}, u32[]{:S(2)}, u32[]{:S(2)}) collective-permute-start(f32[16]{0:T(128)S(1)} %add.205), channel_id=1, source_target_pairs={{0,32},{1,33},{2,34},{3,35},{4,36},{5,37},{6,38},{7,39},{8,40},{9,... | collective-permute-start | bytes 200 | tf_op jit(solution)/shard_map/ppermute | solution.py:30
  181.6 5.1 %collective-permute-start.23 = (f32[16]{0:T(128)S(1)}, f32[16]{0:T(128)S(1)}, u32[]{:S(2)}, u32[]{:S(2)}) collective-permute-start(f32[16]{0:T(128)S(1)} %add.206), channel_id=1, source_target_pairs={{0,64},{1,65},{2,66},{3,67},{4,68},{5,69},{6,70},{7,71},{8,72},{9,... | collective-permute-start | bytes 200 | tf_op jit(solution)/shard_map/ppermute | solution.py:30

commit v2 on v1

--- a/solution.py
+++ b/solution.py
@@ -31,17 +31,23 @@
     return v
 
 
-def reduce_to_owner(slab):
-    rest = slab.shape[1:]
-    slab = slab.reshape((2, -1) + rest[-2:])
-    d = slab[0] + lax.ppermute(slab[1], AXES, moved("c", 1))
-    for axis in ("x", "z", "y"):
-        d = d.reshape((4, -1) + rest[-2:])
-        acc = d[0]
-        for k in (1, 2, 3):
-            acc = acc + lax.ppermute(d[k], AXES, moved(axis, k))
-        d = acc
-    return d
+def spread(pieces, axis):
+    acc = pieces[0]
+    for k in (1, 2, 3):
+        acc = acc + lax.ppermute(pieces[k], AXES, moved(axis, k))
+    return acc
+
+
+def reduce_to_owner(keep, send):
+    tail = keep.shape[1:]
+    d = keep + lax.ppermute(send, AXES, moved("c", 1))
+    first_half = d[:64].reshape((4, 16) + tail)
+    second_half = d[64:].reshape((4, 16) + tail)
+    a = spread(first_half, "x").reshape((4, 4) + tail)
+    b = spread(second_half, "z").reshape((4, 4) + tail)
+    a = spread(a, "z")
+    b = spread(b, "x")
+    return spread(jnp.stack([a, b], axis=1), "y")
 
 
 def on_device(basis, diagonal, near_blocks, far_u, far_v, block_row, block_dest, block_col):
@@ -63,12 +69,25 @@
         "snc,skc->snk", picked[near_count:], far_u, preferred_element_type=jnp.float32
     ).astype(jnp.bfloat16)
     far_part = jnp.einsum("snk,skc->snc", coeff, far_v, preferred_element_type=jnp.float32)
-    parts = jnp.concatenate([near_part, far_part], axis=0)
     dest = block_dest[:, 0]
     rel = {a: (coord(dest, a) - coord(me, a)) % SIZES[a] for a in SIZES}
-    slot = (((rel["c"] * 4 + rel["x"]) * 4 + rel["z"]) * 4 + rel["y"]) * clusters + block_col
-    slab = jnp.zeros((devices * clusters, sources, cluster_size), jnp.float32).at[slot].add(parts)
-    summed = reduce_to_owner(slab.reshape(2, 4, 4, 4, clusters, sources, cluster_size))
+    inner = jnp.where(
+        block_col == 0,
+        (rel["x"] * 4 + rel["z"]) * 4 + rel["y"],
+        64 + (rel["z"] * 4 + rel["x"]) * 4 + rel["y"],
+    )
+    slot = rel["c"] * 128 + inner
+    rows = jnp.arange(128, dtype=slot.dtype)[:, None]
+    flat_near = near_part.reshape(near_count, -1)
+    flat_far = far_part.reshape(far_part.shape[0], -1)
+
+    def gathered(offset):
+        hits = (slot[None, :] == rows + offset).astype(jnp.float32)
+        out = jnp.dot(hits[:, :near_count], flat_near, precision=highest)
+        out = out + jnp.dot(hits[:, near_count:], flat_far, precision=highest)
+        return out.reshape(128, sources, cluster_size)
+
+    summed = reduce_to_owner(gathered(0), gathered(128))
     image = diagonal[:, None, :] * vector + summed
     panels = clusters * cluster_size * devices
     local_first = jnp.einsum("knjc,njc->kj", basis, image, precision=highest)

time: 189 us -> 170 us (0.90)
  other arithmetic: 27.7 us -> 4.55 us
  waiting for transfers between devices: 99.7 us -> 81.1 us
  starting transfers between devices: 38.3 us -> 49.6 us
  matrix products: 10.7 us -> 18.7 us
  local copies, waits for them, and re-layouts: 10.8 us -> 14.6 us
    scatter-add x1 -> x0, other arithmetic: 20.4 us -> none  [on_device(): jnp.zeros((devices * clusters, sources, cluster_size), jnp.float32).at[slot]]
    ppermute x10 -> x16, waiting for transfers between devices: 62.8 us -> 47.6 us  [the longest x15 47.6 us: spread(): acc = acc + lax.ppermute(pieces[k], AXES, moved(axis, k))]
    unnamed x12 -> x18, local copies, waits for them, and re-layouts: 1.26 us -> 12.6 us
    dot_general x0 -> x4, matrix products: none -> 8.68 us  [the longest x2 5.11 us: gathered(): out = out + jnp.dot(hits[:, near_count:], flat_far, precision=highest)]
    ppermute x10 -> x16, starting transfers between devices: 18.4 us -> 26.1 us  [the longest x15 26 us: spread(): acc = acc + lax.ppermute(pieces[k], AXES, moved(axis, k))]
    broadcast_in_dim x1 -> x0, local copies, waits for them, and re-layouts: 4.32 us -> none  [on_device(): jnp.zeros((devices * clusters, sources, cluster_size), jnp.float32).at[slot]]
    ppermute x14, starting transfers between devices: 19.9 us -> 23.5 us  [all_sum(): v = v + lax.ppermute(v, AXES, flipped(bit))]
    dot_general x1, matrix products: 1.19 us -> 4.73 us  [on_device(): jnp.einsum('snc,scd->snd', picked[:near_count], near_blocks, preferred_el...]
  transfers between devices with their start and end apart: 24 -> 30, of which waited for: 21 -> 23; matrix products, arithmetic and copies ran while one was open for 1% -> 6% of each run, Pallas kernels for 0% -> 0%
where the time goes in v2:
time: 170 us
  waiting for transfers between devices  81.1 us (48%)
  starting transfers between devices  49.6 us (29%)
  matrix products  18.7 us (11%)
  local copies, waits for them, and re-layouts  14.6 us (9%)
  other arithmetic  4.55 us (3%)
    ppermute x15, waiting for transfers between devices, spread(): acc = acc + lax.ppermute(pieces[k], AXES, moved(axis, k))  47.6 us
    ppermute x14, waiting for transfers between devices, all_sum(): v = v + lax.ppermute(v, AXES, flipped(bit))  33.6 us
    ppermute x15, starting transfers between devices, spread(): acc = acc + lax.ppermute(pieces[k], AXES, moved(axis, k))  26 us
    ppermute x14, starting transfers between devices, all_sum(): v = v + lax.ppermute(v, AXES, flipped(bit))  23.5 us
    unnamed x18, local copies, waits for them, and re-layouts  12.6 us
    dot_general x2, matrix products, gathered(): out = out + jnp.dot(hits[:, near_count:], flat_far, precision=highest)  5.11 us
    dot_general x1, matrix products, on_device(): jnp.einsum('snc,scd->snd', picked[:near_count], near_blocks, preferred_el...  4.73 us
    dot_general x2, matrix products, gathered(): out = jnp.dot(hits[:, :near_count], flat_near, precision=highest)  3.57 us
  transfers between devices with their start and end apart: 30, of which 23 were waited for; matrix products, arithmetic and copies ran while one was open for 6% of the time, Pallas kernels for 0%

profile of v2, /device:TPU:0, one launch (start us, length us, event | category | flops | bytes accessed | tf_op | source)
XLA Modules:
  0.0 169.5 jit_solution(11932574877840159009)
XLA Ops:
  2.9 4.7 %fusion.56 = f32[16,16,512]{2,1,0:T(8,128)S(1)} fusion(bf16[128,16,512]{2,1,0:T(8,128)(2,1)S(1)} %gather_fusion, bf16[16,512,512]{2,1,0:T(8,128)(2,1)} %param.10), kind=kOutput, calls=%fused_computation.124 | convolution fusion | flops 134217728 | bytes 11010048 | tf_op jit(solution)/shard_map/snc,scd->snd/dot_general | solution.py:65
  10.7 4.5 %copy.48 = f32[14,8,16,512]{3,1,2,0:T(8,128)} copy(f32[14,8,16,512]{3,2,1,0:T(8,128)S(1)} %bitcast.101) | data formatting | bytes 7340032
  15.3 1.8 %fusion.28 = f32[128,8192]{1,0:T(8,128)S(1)} fusion(f32[16,8192]{1,0:T(8,128)S(1)} %bitcast.102, pred[128,128]{1,0:T(32,128)(4,1)S(1)} %get-tuple-element.21), kind=kOutput, calls=%fused_computation.50 | convolution fusion | flops 201326592 | bytes 4734976 | tf_op jit(solution)/shard_map/dot_general | solution.py:86
  17.2 2.5 %convolution_add_fusion = f32[128,8192]{1,0:T(8,128)S(1)} fusion(f32[128,8192]{1,0:T(8,128)S(1)} %fusion.28, f32[112,8192]{1,0:T(8,128)S(1)} %bitcast.97, pred[128,128]{1,0:T(32,128)(4,1)S(1)} %get-tuple-element.21), kind=kOutput, calls=%fused_computation.1 | convolution fusion | flops 1410334720 | bytes 12075008 | tf_op jit(solution)/shard_map/dot_general | solution.py:87
  19.7 3.4 %copy.50 = f32[16,8,16,512]{3,2,1,0:T(8,128)S(1)} copy(f32[16,8,16,512]{3,1,2,0:T(8,128)S(1)} %bitcast.100) | data formatting | bytes 8388608
  23.2 1.8 %fusion.31 = f32[128,8192]{1,0:T(8,128)S(1)} fusion(f32[16,8192]{1,0:T(8,128)S(1)} %bitcast.103, pred[128,128]{1,0:T(32,128)(4,1)S(1)} %get-tuple-element.20), kind=kOutput, calls=%fused_computation.53 | convolution fusion | flops 201326592 | bytes 4734976 | tf_op jit(solution)/shard_map/dot_general | solution.py:86
  25.0 2.6 %convolution_add_fusion.1 = f32[128,8192]{1,0:T(8,128)S(1)} fusion(f32[128,8192]{1,0:T(8,128)S(1)} %fusion.31, f32[112,8192]{1,0:T(8,128)S(1)} %bitcast.98, pred[128,128]{1,0:T(32,128)(4,1)S(1)} %get-tuple-element.20), kind=kOutput, calls=%fused_computation.2 | convolution fusion | flops 1410334720 | bytes 12075008 | tf_op jit(solution)/shard_map/dot_general | solution.py:87
  27.7 3.3 %copy.49 = f32[16,8,16,512]{3,2,1,0:T(8,128)S(1)} copy(f32[16,8,16,512]{3,1,2,0:T(8,128)S(1)} %bitcast.99) | data formatting | bytes 8388608
  30.9 1.5 bitcast_add_fusion
  32.5 1.7 collective-permute-start.1
  34.2 2.7 %collective-permute-start.2 = (f32[16,16,512]{2,1,0:T(8,128)S(1)}, f32[16,16,512]{2,1,0:T(8,128)S(1)}, u32[]{:S(2)}, u32[]{:S(2)}) collective-permute-start(f32[16,16,512]{2,1,0:T(8,128)S(1)} %get-tuple-element.10), channel_id=1, source_target_pairs={{0,4},{1,5},{2,6},{3,7},{4,0},{5,1},{6,2},{7,3},{8,12},{9,13},{10,... | collective-permute-start | bytes 1572872 | tf_op jit(solution)/shard_map/ppermute | solution.py:37
  36.9 1.4 collective-permute-start.3
  38.4 9.8 %collective-permute-done.1 = f32[16,16,512]{2,1,0:T(8,128)S(1)} collective-permute-done((f32[16,16,512]{2,1,0:T(8,128)S(1)}, f32[16,16,512]{2,1,0:T(8,128)S(1)}, u32[]{:S(2)}, u32[]{:S(2)}) %collective-permute-start.1) | collective-permute-done | bytes 524320 | tf_op jit(solution)/shard_map/ppermute | solution.py:37
  48.1 12.3 %collective-permute-done.2 = f32[16,16,512]{2,1,0:T(8,128)S(1)} collective-permute-done((f32[16,16,512]{2,1,0:T(8,128)S(1)}, f32[16,16,512]{2,1,0:T(8,128)S(1)}, u32[]{:S(2)}, u32[]{:S(2)}) %collective-permute-start.2) | collective-permute-done | bytes 524320 | tf_op jit(solution)/shard_map/ppermute | solution.py:37
  60.9 2.0 %collective-permute-start.7 = (f32[16,16,512]{2,1,0:T(8,128)S(1)}, f32[16,16,512]{2,1,0:T(8,128)S(1)}, u32[]{:S(2)}, u32[]{:S(2)}) collective-permute-start(f32[16,16,512]{2,1,0:T(8,128)S(1)} %get-tuple-element.7), channel_id=1, source_target_pairs={{0,8},{1,9},{2,10},{3,11},{4,12},{5,13},{6,14},{7,15},{8,16},{9,17... | collective-permute-start | bytes 1572872 | tf_op jit(solution)/shard_map/ppermute | solution.py:37
  62.9 3.6 %collective-permute-start.8 = (f32[16,16,512]{2,1,0:T(8,128)S(1)}, f32[16,16,512]{2,1,0:T(8,128)S(1)}, u32[]{:S(2)}, u32[]{:S(2)}) collective-permute-start(f32[16,16,512]{2,1,0:T(8,128)S(1)} %get-tuple-element.6), channel_id=1, source_target_pairs={{0,16},{1,17},{2,18},{3,19},{4,20},{5,21},{6,22},{7,23},{8,24},{9,... | collective-permute-start | bytes 1572872 | tf_op jit(solution)/shard_map/ppermute | solution.py:37
  69.1 9.9 %collective-permute-done.7 = f32[16,16,512]{2,1,0:T(8,128)S(1)} collective-permute-done((f32[16,16,512]{2,1,0:T(8,128)S(1)}, f32[16,16,512]{2,1,0:T(8,128)S(1)}, u32[]{:S(2)}, u32[]{:S(2)}) %collective-permute-start.7) | collective-permute-done | bytes 524320 | tf_op jit(solution)/shard_map/ppermute | solution.py:37
  79.8 10.7 %collective-permute-done.8 = f32[16,16,512]{2,1,0:T(8,128)S(1)} collective-permute-done((f32[16,16,512]{2,1,0:T(8,128)S(1)}, f32[16,16,512]{2,1,0:T(8,128)S(1)}, u32[]{:S(2)}, u32[]{:S(2)}) %collective-permute-start.8) | collective-permute-done | bytes 524320 | tf_op jit(solution)/shard_map/ppermute | solution.py:37
  90.8 1.4 collective-permute-start.10
  92.2 2.4 %collective-permute-start.11 = (f32[4,16,512]{2,1,0:T(8,128)S(1)}, f32[4,16,512]{2,1,0:T(8,128)S(1)}, u32[]{:S(2)}, u32[]{:S(2)}) collective-permute-start(f32[4,16,512]{2,1,0:T(8,128)S(1)} %get-tuple-element.16), channel_id=1, source_target_pairs={{0,4},{1,5},{2,6},{3,7},{4,0},{5,1},{6,2},{7,3},{8,12},{9,13},{10,... | collective-permute-start | bytes 393224 | tf_op jit(solution)/shard_map/ppermute | solution.py:37
  94.6 1.6 collective-permute-start.12
  96.2 1.4 collective-permute-done.10
  97.6 1.4 collective-permute-done.11
  99.6 1.6 collective-permute-start.13
  101.3 2.9 %collective-permute-start.14 = (f32[2,16,512]{2,1,0:T(8,128)S(1)}, f32[2,16,512]{2,1,0:T(8,128)S(1)}, u32[]{:S(2)}, u32[]{:S(2)}) collective-permute-start(f32[2,16,512]{2,1,0:T(8,128)S(1)} %get-tuple-element.19), channel_id=1, source_target_pairs={{0,64},{1,65},{2,66},{3,67},{4,68},{5,69},{6,70},{7,71},{8,72},{9,... | collective-permute-start | bytes 196616 | tf_op jit(solution)/shard_map/ppermute | solution.py:37
  108.5 1.5 fusion.6
  111.3 1.9 %collective-permute-start.17 = (f32[72,16]{1,0:T(8,128)S(1)}, f32[72,16]{1,0:T(8,128)S(1)}, u32[]{:S(2)}, u32[]{:S(2)}) collective-permute-start(f32[72,16]{1,0:T(8,128)S(1)} %fusion.51), channel_id=1, source_target_pairs={{0,2},{1,3},{2,0},{3,1},{4,6},{5,7},{6,4},{7,5},{8,10},{9,11},{10,... | collective-permute-start | bytes 13832 | tf_op jit(solution)/shard_map/ppermute | solution.py:30
  113.1 2.2 %collective-permute-done.17 = f32[72,16]{1,0:T(8,128)S(1)} collective-permute-done((f32[72,16]{1,0:T(8,128)S(1)}, f32[72,16]{1,0:T(8,128)S(1)}, u32[]{:S(2)}, u32[]{:S(2)}) %collective-permute-start.17) | collective-permute-done | bytes 4640 | tf_op jit(solution)/shard_map/ppermute | solution.py:30
  115.3 2.5 %collective-permute-start.18 = (f32[72,16]{1,0:T(8,128)S(1)}, f32[72,16]{1,0:T(8,128)S(1)}, u32[]{:S(2)}, u32[]{:S(2)}) collective-permute-start(f32[72,16]{1,0:T(8,128)S(1)} %add.239), channel_id=1, source_target_pairs={{0,4},{1,5},{2,6},{3,7},{4,0},{5,1},{6,2},{7,3},{8,12},{9,13},{10,... | collective-permute-start | bytes 13832 | tf_op jit(solution)/shard_map/ppermute | solution.py:30
  117.7 3.0 %collective-permute-done.18 = f32[72,16]{1,0:T(8,128)S(1)} collective-permute-done((f32[72,16]{1,0:T(8,128)S(1)}, f32[72,16]{1,0:T(8,128)S(1)}, u32[]{:S(2)}, u32[]{:S(2)}) %collective-permute-start.18) | collective-permute-done | bytes 4640 | tf_op jit(solution)/shard_map/ppermute | solution.py:30
  120.8 2.3 %collective-permute-start.19 = (f32[72,16]{1,0:T(8,128)S(1)}, f32[72,16]{1,0:T(8,128)S(1)}, u32[]{:S(2)}, u32[]{:S(2)}) collective-permute-start(f32[72,16]{1,0:T(8,128)S(1)} %add.240), channel_id=1, source_target_pairs={{0,8},{1,9},{2,10},{3,11},{4,12},{5,13},{6,14},{7,15},{8,0},{9,1},... | collective-permute-start | bytes 13832 | tf_op jit(solution)/shard_map/ppermute | solution.py:30
  123.1 1.9 %collective-permute-done.19 = f32[72,16]{1,0:T(8,128)S(1)} collective-permute-done((f32[72,16]{1,0:T(8,128)S(1)}, f32[72,16]{1,0:T(8,128)S(1)}, u32[]{:S(2)}, u32[]{:S(2)}) %collective-permute-start.19) | collective-permute-done | bytes 4640 | tf_op jit(solution)/shard_map/ppermute | solution.py:30
  125.1 2.6 %collective-permute-start.20 = (f32[72,16]{1,0:T(8,128)S(1)}, f32[72,16]{1,0:T(8,128)S(1)}, u32[]{:S(2)}, u32[]{:S(2)}) collective-permute-start(f32[72,16]{1,0:T(8,128)S(1)} %add.241), channel_id=1, source_target_pairs={{0,16},{1,17},{2,18},{3,19},{4,20},{5,21},{6,22},{7,23},{8,24},{9,... | collective-permute-start | bytes 13832 | tf_op jit(solution)/shard_map/ppermute | solution.py:30
  127.7 2.8 %collective-permute-done.20 = f32[72,16]{1,0:T(8,128)S(1)} collective-permute-done((f32[72,16]{1,0:T(8,128)S(1)}, f32[72,16]{1,0:T(8,128)S(1)}, u32[]{:S(2)}, u32[]{:S(2)}) %collective-permute-start.20) | collective-permute-done | bytes 4640 | tf_op jit(solution)/shard_map/ppermute | solution.py:30
  130.9 3.6 %collective-permute-done.21 = f32[72,16]{1,0:T(8,128)S(1)} collective-permute-done((f32[72,16]{1,0:T(8,128)S(1)}, f32[72,16]{1,0:T(8,128)S(1)}, u32[]{:S(2)}, u32[]{:S(2)}) %collective-permute-start.21) | collective-permute-done | bytes 4640 | tf_op jit(solution)/shard_map/ppermute | solution.py:30
  134.5 2.0 %collective-permute-start.22 = (f32[72,16]{1,0:T(8,128)S(1)}, f32[72,16]{1,0:T(8,128)S(1)}, u32[]{:S(2)}, u32[]{:S(2)}) collective-permute-start(f32[72,16]{1,0:T(8,128)S(1)} %add.243), channel_id=1, source_target_pairs={{0,64},{1,65},{2,66},{3,67},{4,68},{5,69},{6,70},{7,71},{8,72},{9,... | collective-permute-start | bytes 13832 | tf_op jit(solution)/shard_map/ppermute | solution.py:30
  136.5 3.5 %collective-permute-done.22 = f32[72,16]{1,0:T(8,128)S(1)} collective-permute-done((f32[72,16]{1,0:T(8,128)S(1)}, f32[72,16]{1,0:T(8,128)S(1)}, u32[]{:S(2)}, u32[]{:S(2)}) %collective-permute-start.22) | collective-permute-done | bytes 4640 | tf_op jit(solution)/shard_map/ppermute | solution.py:30
  142.3 1.7 %collective-permute-start.24 = (f32[16]{0:T(128)S(1)}, f32[16]{0:T(128)S(1)}, u32[]{:S(2)}, u32[]{:S(2)}) collective-permute-start(f32[16]{0:T(128)S(1)} %add.246), channel_id=1, source_target_pairs={{0,2},{1,3},{2,0},{3,1},{4,6},{5,7},{6,4},{7,5},{8,10},{9,11},{10,... | collective-permute-start | bytes 200 | tf_op jit(solution)/shard_map/ppermute | solution.py:30
  144.0 1.8 %collective-permute-done.24 = f32[16]{0:T(128)S(1)} collective-permute-done((f32[16]{0:T(128)S(1)}, f32[16]{0:T(128)S(1)}, u32[]{:S(2)}, u32[]{:S(2)}) %collective-permute-start.24) | collective-permute-done | bytes 96 | tf_op jit(solution)/shard_map/ppermute | solution.py:30
  145.8 2.7 %collective-permute-start.25 = (f32[16]{0:T(128)S(1)}, f32[16]{0:T(128)S(1)}, u32[]{:S(2)}, u32[]{:S(2)}) collective-permute-start(f32[16]{0:T(128)S(1)} %add.247), channel_id=1, source_target_pairs={{0,4},{1,5},{2,6},{3,7},{4,0},{5,1},{6,2},{7,3},{8,12},{9,13},{10,... | collective-permute-start | bytes 200 | tf_op jit(solution)/shard_map/ppermute | solution.py:30
  148.6 2.3 %collective-permute-done.25 = f32[16]{0:T(128)S(1)} collective-permute-done((f32[16]{0:T(128)S(1)}, f32[16]{0:T(128)S(1)}, u32[]{:S(2)}, u32[]{:S(2)}) %collective-permute-start.25) | collective-permute-done | bytes 96 | tf_op jit(solution)/shard_map/ppermute | solution.py:30
  150.9 2.0 %collective-permute-start.26 = (f32[16]{0:T(128)S(1)}, f32[16]{0:T(128)S(1)}, u32[]{:S(2)}, u32[]{:S(2)}) collective-permute-start(f32[16]{0:T(128)S(1)} %add.248), channel_id=1, source_target_pairs={{0,8},{1,9},{2,10},{3,11},{4,12},{5,13},{6,14},{7,15},{8,0},{9,1},... | collective-permute-start | bytes 200 | tf_op jit(solution)/shard_map/ppermute | solution.py:30
  152.9 1.5 collective-permute-done.26
  154.5 2.6 %collective-permute-start.27 = (f32[16]{0:T(128)S(1)}, f32[16]{0:T(128)S(1)}, u32[]{:S(2)}, u32[]{:S(2)}) collective-permute-start(f32[16]{0:T(128)S(1)} %add.249), channel_id=1, source_target_pairs={{0,16},{1,17},{2,18},{3,19},{4,20},{5,21},{6,22},{7,23},{8,24},{9,... | collective-permute-start | bytes 200 | tf_op jit(solution)/shard_map/ppermute | solution.py:30
  157.1 2.5 %collective-permute-done.27 = f32[16]{0:T(128)S(1)} collective-permute-done((f32[16]{0:T(128)S(1)}, f32[16]{0:T(128)S(1)}, u32[]{:S(2)}, u32[]{:S(2)}) %collective-permute-start.27) | collective-permute-done | bytes 96 | tf_op jit(solution)/shard_map/ppermute | solution.py:30
  160.2 3.0 %collective-permute-done.28 = f32[16]{0:T(128)S(1)} collective-permute-done((f32[16]{0:T(128)S(1)}, f32[16]{0:T(128)S(1)}, u32[]{:S(2)}, u32[]{:S(2)}) %collective-permute-start.28) | collective-permute-done | bytes 96 | tf_op jit(solution)/shard_map/ppermute | solution.py:30
  163.1 2.0 %collective-permute-start.29 = (f32[16]{0:T(128)S(1)}, f32[16]{0:T(128)S(1)}, u32[]{:S(2)}, u32[]{:S(2)}) collective-permute-start(f32[16]{0:T(128)S(1)} %add.251), channel_id=1, source_target_pairs={{0,64},{1,65},{2,66},{3,67},{4,68},{5,69},{6,70},{7,71},{8,72},{9,... | collective-permute-start | bytes 200 | tf_op jit(solution)/shard_map/ppermute | solution.py:30
  165.1 3.1 %collective-permute-done.29 = f32[16]{0:T(128)S(1)} collective-permute-done((f32[16]{0:T(128)S(1)}, f32[16]{0:T(128)S(1)}, u32[]{:S(2)}, u32[]{:S(2)}) %collective-permute-start.29) | collective-permute-done | bytes 96 | tf_op jit(solution)/shard_map/ppermute | solution.py:30
  (80 shorter events, 20.6 us)
Async XLA Ops:
  2.9 5.1 %copy-start.3 = (bf16[112,32,512]{2,1,0:T(8,128)(2,1)S(1)}, bf16[112,32,512]{2,1,0:T(8,128)(2,1)}, u32[]{:S(2)}) copy-start(bf16[112,32,512]{2,1,0:T(8,128)(2,1)} %param.11) | copy-start | bytes 11010052
  8.0 2.0 %copy-start.2 = (bf16[112,32,512]{2,1,0:T(8,128)(2,1)S(1)}, bf16[112,32,512]{2,1,0:T(8,128)(2,1)}, u32[]{:S(2)}) copy-start(bf16[112,32,512]{2,1,0:T(8,128)(2,1)} %param.12) | copy-start | bytes 11010052
  10.6 4.5 %copy-start.5 = (s32[128]{0:T(128)S(1)}, s32[128]{0:T(128)}, u32[]{:S(2)}) copy-start(s32[128]{0:T(128)} %param.15) | copy-start | bytes 1540
  10.6 4.5 %copy-start.6 = (s32[128,1]{0,1:T(1,128)S(1)}, s32[128,1]{0,1:T(1,128)}, u32[]{:S(2)}) copy-start(s32[128,1]{0,1:T(1,128)} %param.14) | copy-start | bytes 1540
  15.2 2.0 %copy-start = (f32[14,8,16,512]{3,1,2,0:T(8,128)S(1)}, f32[14,8,16,512]{3,1,2,0:T(8,128)}, u32[]{:S(2)}) copy-start(f32[14,8,16,512]{3,1,2,0:T(8,128)} %copy.48) | copy-start | bytes 11010052
  23.2 7.8 %collective-permute-start = (f32[128,16,512]{2,1,0:T(8,128)S(1)}, f32[128,16,512]{2,1,0:T(8,128)S(1)}, u32[]{:S(2)}, u32[]{:S(2)}) collective-permute-start(f32[128,16,512]{2,1,0:T(8,128)S(1)} %bitcast.104), channel_id=1, source_target_pairs={{0,1},{1,0},{2,3},{3,2},{4,5},{5,4},{6,7},{7,6},{8,9},{9,8},{10,11... | collective-permute-start | bytes 12582920 | tf_op jit(solution)/shard_map/ppermute | solution.py:43
  32.5 15.6 %collective-permute-start.1 = (f32[16,16,512]{2,1,0:T(8,128)S(1)}, f32[16,16,512]{2,1,0:T(8,128)S(1)}, u32[]{:S(2)}, u32[]{:S(2)}) collective-permute-start(f32[16,16,512]{2,1,0:T(8,128)S(1)} %get-tuple-element.8), channel_id=1, source_target_pairs={{0,2},{1,3},{2,4},{3,5},{4,6},{5,7},{6,0},{7,1},{8,10},{9,11},{10,... | collective-permute-start | bytes 1572872 | tf_op jit(solution)/shard_map/ppermute | solution.py:37
  34.2 26.3 %collective-permute-start.2 = (f32[16,16,512]{2,1,0:T(8,128)S(1)}, f32[16,16,512]{2,1,0:T(8,128)S(1)}, u32[]{:S(2)}, u32[]{:S(2)}) collective-permute-start(f32[16,16,512]{2,1,0:T(8,128)S(1)} %get-tuple-element.10), channel_id=1, source_target_pairs={{0,4},{1,5},{2,6},{3,7},{4,0},{5,1},{6,2},{7,3},{8,12},{9,13},{10,... | collective-permute-start | bytes 1572872 | tf_op jit(solution)/shard_map/ppermute | solution.py:37
  36.9 23.5 %collective-permute-start.3 = (f32[16,16,512]{2,1,0:T(8,128)S(1)}, f32[16,16,512]{2,1,0:T(8,128)S(1)}, u32[]{:S(2)}, u32[]{:S(2)}) collective-permute-start(f32[16,16,512]{2,1,0:T(8,128)S(1)} %get-tuple-element.9), channel_id=1, source_target_pairs={{0,6},{1,7},{2,0},{3,1},{4,2},{5,3},{6,4},{7,5},{8,14},{9,15},{10,... | collective-permute-start | bytes 1572872 | tf_op jit(solution)/shard_map/ppermute | solution.py:37
  60.9 44.6 %copy-start.1 = (f32[8,2,16,512]{3,2,1,0:T(8,128)S(1)}, f32[8,2,16,512]{3,2,1,0:T(8,128)}, u32[]{:S(2)}) copy-start(f32[8,2,16,512]{3,2,1,0:T(8,128)} %param.8) | copy-start | bytes 1572868
  60.9 47.5 %copy-start.4 = (f32[2,512]{1,0:T(2,128)S(1)}, f32[2,512]{1,0:T(2,128)}, u32[]{:S(2)}) copy-start(f32[2,512]{1,0:T(2,128)} %param.9) | copy-start | bytes 12292
  60.9 18.1 %collective-permute-start.7 = (f32[16,16,512]{2,1,0:T(8,128)S(1)}, f32[16,16,512]{2,1,0:T(8,128)S(1)}, u32[]{:S(2)}, u32[]{:S(2)}) collective-permute-start(f32[16,16,512]{2,1,0:T(8,128)S(1)} %get-tuple-element.7), channel_id=1, source_target_pairs={{0,8},{1,9},{2,10},{3,11},{4,12},{5,13},{6,14},{7,15},{8,16},{9,17... | collective-permute-start | bytes 1572872 | tf_op jit(solution)/shard_map/ppermute | solution.py:37
  62.9 27.6 %collective-permute-start.8 = (f32[16,16,512]{2,1,0:T(8,128)S(1)}, f32[16,16,512]{2,1,0:T(8,128)S(1)}, u32[]{:S(2)}, u32[]{:S(2)}) collective-permute-start(f32[16,16,512]{2,1,0:T(8,128)S(1)} %get-tuple-element.6), channel_id=1, source_target_pairs={{0,16},{1,17},{2,18},{3,19},{4,20},{5,21},{6,22},{7,23},{8,24},{9,... | collective-permute-start | bytes 1572872 | tf_op jit(solution)/shard_map/ppermute | solution.py:37
  66.5 24.1 %collective-permute-start.9 = (f32[16,16,512]{2,1,0:T(8,128)S(1)}, f32[16,16,512]{2,1,0:T(8,128)S(1)}, u32[]{:S(2)}, u32[]{:S(2)}) collective-permute-start(f32[16,16,512]{2,1,0:T(8,128)S(1)} %get-tuple-element.5), channel_id=1, source_target_pairs={{0,24},{1,25},{2,26},{3,27},{4,28},{5,29},{6,30},{7,31},{8,0},{9,1... | collective-permute-start | bytes 1572872 | tf_op jit(solution)/shard_map/ppermute | solution.py:37
  67.5 27.1 %collective-permute-start.4 = (f32[4,16,512]{2,1,0:T(8,128)S(1)}, f32[4,16,512]{2,1,0:T(8,128)S(1)}, u32[]{:S(2)}, u32[]{:S(2)}) collective-permute-start(f32[4,16,512]{2,1,0:T(8,128)S(1)} %get-tuple-element.11), channel_id=1, source_target_pairs={{0,8},{1,9},{2,10},{3,11},{4,12},{5,13},{6,14},{7,15},{8,16},{9,17... | collective-permute-start | bytes 393224 | tf_op jit(solution)/shard_map/ppermute | solution.py:37
  68.6 27.6 %collective-permute-start.5 = (f32[4,16,512]{2,1,0:T(8,128)S(1)}, f32[4,16,512]{2,1,0:T(8,128)S(1)}, u32[]{:S(2)}, u32[]{:S(2)}) collective-permute-start(f32[4,16,512]{2,1,0:T(8,128)S(1)} %get-tuple-element.13), channel_id=1, source_target_pairs={{0,16},{1,17},{2,18},{3,19},{4,20},{5,21},{6,22},{7,23},{8,24},{9,... | collective-permute-start | bytes 393224 | tf_op jit(solution)/shard_map/ppermute | solution.py:37
  79.0 17.2 %collective-permute-start.6 = (f32[4,16,512]{2,1,0:T(8,128)S(1)}, f32[4,16,512]{2,1,0:T(8,128)S(1)}, u32[]{:S(2)}, u32[]{:S(2)}) collective-permute-start(f32[4,16,512]{2,1,0:T(8,128)S(1)} %get-tuple-element.12), channel_id=1, source_target_pairs={{0,24},{1,25},{2,26},{3,27},{4,28},{5,29},{6,30},{7,31},{8,0},{9,1... | collective-permute-start | bytes 393224 | tf_op jit(solution)/shard_map/ppermute | solution.py:37
  90.8 6.8 %collective-permute-start.10 = (f32[4,16,512]{2,1,0:T(8,128)S(1)}, f32[4,16,512]{2,1,0:T(8,128)S(1)}, u32[]{:S(2)}, u32[]{:S(2)}) collective-permute-start(f32[4,16,512]{2,1,0:T(8,128)S(1)} %get-tuple-element.14), channel_id=1, source_target_pairs={{0,2},{1,3},{2,4},{3,5},{4,6},{5,7},{6,0},{7,1},{8,10},{9,11},{10,... | collective-permute-start | bytes 393224 | tf_op jit(solution)/shard_map/ppermute | solution.py:37
  92.2 6.8 %collective-permute-start.11 = (f32[4,16,512]{2,1,0:T(8,128)S(1)}, f32[4,16,512]{2,1,0:T(8,128)S(1)}, u32[]{:S(2)}, u32[]{:S(2)}) collective-permute-start(f32[4,16,512]{2,1,0:T(8,128)S(1)} %get-tuple-element.16), channel_id=1, source_target_pairs={{0,4},{1,5},{2,6},{3,7},{4,0},{5,1},{6,2},{7,3},{8,12},{9,13},{10,... | collective-permute-start | bytes 393224 | tf_op jit(solution)/shard_map/ppermute | solution.py:37
  94.6 5.0 %collective-permute-start.12 = (f32[4,16,512]{2,1,0:T(8,128)S(1)}, f32[4,16,512]{2,1,0:T(8,128)S(1)}, u32[]{:S(2)}, u32[]{:S(2)}) collective-permute-start(f32[4,16,512]{2,1,0:T(8,128)S(1)} %get-tuple-element.15), channel_id=1, source_target_pairs={{0,6},{1,7},{2,0},{3,1},{4,2},{5,3},{6,4},{7,5},{8,14},{9,15},{10,... | collective-permute-start | bytes 393224 | tf_op jit(solution)/shard_map/ppermute | solution.py:37
  99.6 7.3 %collective-permute-start.13 = (f32[2,16,512]{2,1,0:T(8,128)S(1)}, f32[2,16,512]{2,1,0:T(8,128)S(1)}, u32[]{:S(2)}, u32[]{:S(2)}) collective-permute-start(f32[2,16,512]{2,1,0:T(8,128)S(1)} %get-tuple-element.17), channel_id=1, source_target_pairs={{0,32},{1,33},{2,34},{3,35},{4,36},{5,37},{6,38},{7,39},{8,40},{9,... | collective-permute-start | bytes 196616 | tf_op jit(solution)/shard_map/ppermute | solution.py:37
  101.3 5.8 %collective-permute-start.14 = (f32[2,16,512]{2,1,0:T(8,128)S(1)}, f32[2,16,512]{2,1,0:T(8,128)S(1)}, u32[]{:S(2)}, u32[]{:S(2)}) collective-permute-start(f32[2,16,512]{2,1,0:T(8,128)S(1)} %get-tuple-element.19), channel_id=1, source_target_pairs={{0,64},{1,65},{2,66},{3,67},{4,68},{5,69},{6,70},{7,71},{8,72},{9,... | collective-permute-start | bytes 196616 | tf_op jit(solution)/shard_map/ppermute | solution.py:37
  104.2 4.3 %collective-permute-start.15 = (f32[2,16,512]{2,1,0:T(8,128)S(1)}, f32[2,16,512]{2,1,0:T(8,128)S(1)}, u32[]{:S(2)}, u32[]{:S(2)}) collective-permute-start(f32[2,16,512]{2,1,0:T(8,128)S(1)} %get-tuple-element.18), channel_id=1, source_target_pairs={{0,96},{1,97},{2,98},{3,99},{4,100},{5,101},{6,102},{7,103},{8,104... | collective-permute-start | bytes 196616 | tf_op jit(solution)/shard_map/ppermute | solution.py:37
  110.0 1.2 collective-permute-start.16
  111.3 4.0 %collective-permute-start.17 = (f32[72,16]{1,0:T(8,128)S(1)}, f32[72,16]{1,0:T(8,128)S(1)}, u32[]{:S(2)}, u32[]{:S(2)}) collective-permute-start(f32[72,16]{1,0:T(8,128)S(1)} %fusion.51), channel_id=1, source_target_pairs={{0,2},{1,3},{2,0},{3,1},{4,6},{5,7},{6,4},{7,5},{8,10},{9,11},{10,... | collective-permute-start | bytes 13832 | tf_op jit(solution)/shard_map/ppermute | solution.py:30
  115.3 5.5 %collective-permute-start.18 = (f32[72,16]{1,0:T(8,128)S(1)}, f32[72,16]{1,0:T(8,128)S(1)}, u32[]{:S(2)}, u32[]{:S(2)}) collective-permute-start(f32[72,16]{1,0:T(8,128)S(1)} %add.239), channel_id=1, source_target_pairs={{0,4},{1,5},{2,6},{3,7},{4,0},{5,1},{6,2},{7,3},{8,12},{9,13},{10,... | collective-permute-start | bytes 13832 | tf_op jit(solution)/shard_map/ppermute | solution.py:30
  120.8 4.3 %collective-permute-start.19 = (f32[72,16]{1,0:T(8,128)S(1)}, f32[72,16]{1,0:T(8,128)S(1)}, u32[]{:S(2)}, u32[]{:S(2)}) collective-permute-start(f32[72,16]{1,0:T(8,128)S(1)} %add.240), channel_id=1, source_target_pairs={{0,8},{1,9},{2,10},{3,11},{4,12},{5,13},{6,14},{7,15},{8,0},{9,1},... | collective-permute-start | bytes 13832 | tf_op jit(solution)/shard_map/ppermute | solution.py:30
  125.1 5.5 %collective-permute-start.20 = (f32[72,16]{1,0:T(8,128)S(1)}, f32[72,16]{1,0:T(8,128)S(1)}, u32[]{:S(2)}, u32[]{:S(2)}) collective-permute-start(f32[72,16]{1,0:T(8,128)S(1)} %add.241), channel_id=1, source_target_pairs={{0,16},{1,17},{2,18},{3,19},{4,20},{5,21},{6,22},{7,23},{8,24},{9,... | collective-permute-start | bytes 13832 | tf_op jit(solution)/shard_map/ppermute | solution.py:30
  130.5 4.0 %collective-permute-start.21 = (f32[72,16]{1,0:T(8,128)S(1)}, f32[72,16]{1,0:T(8,128)S(1)}, u32[]{:S(2)}, u32[]{:S(2)}) collective-permute-start(f32[72,16]{1,0:T(8,128)S(1)} %add.242), channel_id=1, source_target_pairs={{0,32},{1,33},{2,34},{3,35},{4,36},{5,37},{6,38},{7,39},{8,40},{9,... | collective-permute-start | bytes 13832 | tf_op jit(solution)/shard_map/ppermute | solution.py:30
  134.5 5.5 %collective-permute-start.22 = (f32[72,16]{1,0:T(8,128)S(1)}, f32[72,16]{1,0:T(8,128)S(1)}, u32[]{:S(2)}, u32[]{:S(2)}) collective-permute-start(f32[72,16]{1,0:T(8,128)S(1)} %add.243), channel_id=1, source_target_pairs={{0,64},{1,65},{2,66},{3,67},{4,68},{5,69},{6,70},{7,71},{8,72},{9,... | collective-permute-start | bytes 13832 | tf_op jit(solution)/shard_map/ppermute | solution.py:30
  141.0 1.2 collective-permute-start.23
  142.3 3.6 %collective-permute-start.24 = (f32[16]{0:T(128)S(1)}, f32[16]{0:T(128)S(1)}, u32[]{:S(2)}, u32[]{:S(2)}) collective-permute-start(f32[16]{0:T(128)S(1)} %add.246), channel_id=1, source_target_pairs={{0,2},{1,3},{2,0},{3,1},{4,6},{5,7},{6,4},{7,5},{8,10},{9,11},{10,... | collective-permute-start | bytes 200 | tf_op jit(solution)/shard_map/ppermute | solution.py:30
  145.8 5.1 %collective-permute-start.25 = (f32[16]{0:T(128)S(1)}, f32[16]{0:T(128)S(1)}, u32[]{:S(2)}, u32[]{:S(2)}) collective-permute-start(f32[16]{0:T(128)S(1)} %add.247), channel_id=1, source_target_pairs={{0,4},{1,5},{2,6},{3,7},{4,0},{5,1},{6,2},{7,3},{8,12},{9,13},{10,... | collective-permute-start | bytes 200 | tf_op jit(solution)/shard_map/ppermute | solution.py:30
  150.9 3.6 %collective-permute-start.26 = (f32[16]{0:T(128)S(1)}, f32[16]{0:T(128)S(1)}, u32[]{:S(2)}, u32[]{:S(2)}) collective-permute-start(f32[16]{0:T(128)S(1)} %add.248), channel_id=1, source_target_pairs={{0,8},{1,9},{2,10},{3,11},{4,12},{5,13},{6,14},{7,15},{8,0},{9,1},... | collective-permute-start | bytes 200 | tf_op jit(solution)/shard_map/ppermute | solution.py:30
  154.5 5.1 %collective-permute-start.27 = (f32[16]{0:T(128)S(1)}, f32[16]{0:T(128)S(1)}, u32[]{:S(2)}, u32[]{:S(2)}) collective-permute-start(f32[16]{0:T(128)S(1)} %add.249), channel_id=1, source_target_pairs={{0,16},{1,17},{2,18},{3,19},{4,20},{5,21},{6,22},{7,23},{8,24},{9,... | collective-permute-start | bytes 200 | tf_op jit(solution)/shard_map/ppermute | solution.py:30
  159.6 3.6 %collective-permute-start.28 = (f32[16]{0:T(128)S(1)}, f32[16]{0:T(128)S(1)}, u32[]{:S(2)}, u32[]{:S(2)}) collective-permute-start(f32[16]{0:T(128)S(1)} %add.250), channel_id=1, source_target_pairs={{0,32},{1,33},{2,34},{3,35},{4,36},{5,37},{6,38},{7,39},{8,40},{9,... | collective-permute-start | bytes 200 | tf_op jit(solution)/shard_map/ppermute | solution.py:30
  163.1 5.1 %collective-permute-start.29 = (f32[16]{0:T(128)S(1)}, f32[16]{0:T(128)S(1)}, u32[]{:S(2)}, u32[]{:S(2)}) collective-permute-start(f32[16]{0:T(128)S(1)} %add.251), channel_id=1, source_target_pairs={{0,64},{1,65},{2,66},{3,67},{4,68},{5,69},{6,70},{7,71},{8,72},{9,... | collective-permute-start | bytes 200 | tf_op jit(solution)/shard_map/ppermute | solution.py:30

commit v3 on v1

--- a/solution.py
+++ b/solution.py
@@ -12,10 +12,11 @@
     return (g // STRIDE[axis]) % SIZES[axis]
 
 
-def moved(axis, k):
-    n, s = SIZES[axis], STRIDE[axis]
+def moved(axis, k, other=None):
     pairs = []
     for g in range(128):
+        a = other if (other is not None and g % 2 == 1) else axis
+        n, s = SIZES[a], STRIDE[a]
         c = (g // s) % n
         pairs.append((g, g + (((c + k) % n) - c) * s))
     return pairs
@@ -31,17 +32,18 @@
     return v
 
 
-def reduce_to_owner(slab):
-    rest = slab.shape[1:]
-    slab = slab.reshape((2, -1) + rest[-2:])
-    d = slab[0] + lax.ppermute(slab[1], AXES, moved("c", 1))
-    for axis in ("x", "z", "y"):
-        d = d.reshape((4, -1) + rest[-2:])
-        acc = d[0]
-        for k in (1, 2, 3):
-            acc = acc + lax.ppermute(d[k], AXES, moved(axis, k))
-        d = acc
-    return d
+def spread(pieces, axis, other=None):
+    acc = pieces[0]
+    for k in (1, 2, 3):
+        acc = acc + lax.ppermute(pieces[k], AXES, moved(axis, k, other))
+    return acc
+
+
+def reduce_to_owner(keep, send):
+    d = keep + lax.ppermute(send, AXES, moved("c", 1))
+    d = spread(d, "x", "z")
+    d = spread(d, "z", "x")
+    return spread(d, "y")
 
 
 def on_device(basis, diagonal, near_blocks, far_u, far_v, block_row, block_dest, block_col):
@@ -63,12 +65,24 @@
         "snc,skc->snk", picked[near_count:], far_u, preferred_element_type=jnp.float32
     ).astype(jnp.bfloat16)
     far_part = jnp.einsum("snk,skc->snc", coeff, far_v, preferred_element_type=jnp.float32)
-    parts = jnp.concatenate([near_part, far_part], axis=0)
     dest = block_dest[:, 0]
     rel = {a: (coord(dest, a) - coord(me, a)) % SIZES[a] for a in SIZES}
-    slot = (((rel["c"] * 4 + rel["x"]) * 4 + rel["z"]) * 4 + rel["y"]) * clusters + block_col
-    slab = jnp.zeros((devices * clusters, sources, cluster_size), jnp.float32).at[slot].add(parts)
-    summed = reduce_to_owner(slab.reshape(2, 4, 4, 4, clusters, sources, cluster_size))
+    to_core = coord(dest, "c")
+    order = jnp.where(to_core == 0, rel["x"] * 4 + rel["z"], rel["z"] * 4 + rel["x"])
+    slot = ((rel["c"] * 16 + order) * 4 + rel["y"]) * clusters + block_col
+    blocks = slot.shape[0]
+    numbers = jnp.arange(blocks, dtype=jnp.int32)
+    spots = devices * clusters
+    lowest = jnp.full((spots,), blocks, jnp.int32).at[slot].min(numbers)
+    highest_block = jnp.full((spots,), -1, jnp.int32).at[slot].max(numbers)
+    second_block = jnp.where(highest_block > lowest, highest_block, blocks)
+    table = jnp.concatenate(
+        [near_part, far_part, jnp.zeros((1, sources, cluster_size), jnp.float32)], axis=0
+    )
+    slab = table[lowest] + table[second_block]
+    shape = (2, 4, 4, 4, clusters, sources, cluster_size)
+    slab = slab.reshape(shape)
+    summed = reduce_to_owner(slab[0], slab[1])
     image = diagonal[:, None, :] * vector + summed
     panels = clusters * cluster_size * devices
     local_first = jnp.einsum("knjc,njc->kj", basis, image, precision=highest)

time: 189 us -> 167 us (0.88)
  waiting for transfers between devices: 99.7 us -> 71.2 us
  local copies, waits for them, and re-layouts: 10.8 us -> 21.3 us
  other arithmetic: 27.7 us -> 21.2 us
  starting transfers between devices: 38.3 us -> 41.3 us
    ppermute x10, waiting for transfers between devices: 62.8 us -> 37.3 us  [the longest x9 30.2 us: spread(): acc = acc + lax.ppermute(pieces[k], AXES, moved(axis, k, other))]
    scatter-add x1 -> x0, other arithmetic: 20.4 us -> none  [on_device(): jnp.zeros((devices * clusters, sources, cluster_size), jnp.float32).at[slot]]
    gather x0 -> x2, local copies, waits for them, and re-layouts: none -> 13 us  [on_device(): slab = table[lowest] + table[second_block]]
    add x3 -> x4, other arithmetic: 2.13 us -> 13.8 us  [the longest x1 12.1 us: on_device(): slab = table[lowest] + table[second_block]]
    broadcast_in_dim x1 -> x0, local copies, waits for them, and re-layouts: 4.32 us -> none  [on_device(): jnp.zeros((devices * clusters, sources, cluster_size), jnp.float32).at[slot]]
    ppermute x14, starting transfers between devices: 19.9 us -> 22.9 us  [all_sum(): v = v + lax.ppermute(v, AXES, flipped(bit))]
    ppermute x14, waiting for transfers between devices: 36.9 us -> 33.8 us  [all_sum(): v = v + lax.ppermute(v, AXES, flipped(bit))]
    another operation x0 -> x2, other arithmetic: none -> 2.86 us  [the longest x1 1.43 us: on_device(): highest_block = jnp.full((spots,), -1, jnp.int32).at[slot].max(numbers)]
where the time goes in v3:
time: 167 us
  waiting for transfers between devices  71.2 us (43%)
  starting transfers between devices  41.3 us (25%)
  local copies, waits for them, and re-layouts  21.3 us (13%)
  other arithmetic  21.2 us (13%)
  matrix products  10.7 us (6%)
    ppermute x14, waiting for transfers between devices, all_sum(): v = v + lax.ppermute(v, AXES, flipped(bit))  33.8 us
    ppermute x9, waiting for transfers between devices, spread(): acc = acc + lax.ppermute(pieces[k], AXES, moved(axis, k, other))  30.2 us
    ppermute x14, starting transfers between devices, all_sum(): v = v + lax.ppermute(v, AXES, flipped(bit))  22.9 us
    ppermute x9, starting transfers between devices, spread(): acc = acc + lax.ppermute(pieces[k], AXES, moved(axis, k, other))  18.3 us
    gather x2, local copies, waits for them, and re-layouts, on_device(): slab = table[lowest] + table[second_block]  13 us
    add x1, other arithmetic, on_device(): slab = table[lowest] + table[second_block]  12.1 us
    ppermute x1, waiting for transfers between devices, reduce_to_owner(): d = keep + lax.ppermute(send, AXES, moved('c', 1))  7.15 us
    slice x1, local copies, waits for them, and re-layouts, on_device(): summed = reduce_to_owner(slab[0], slab[1])  4.53 us
  transfers between devices with their start and end apart: 24, of which 21 were waited for; matrix products, arithmetic and copies ran while one was open for 1% of the time, Pallas kernels for 0%

profile of v3, /device:TPU:0, one launch (start us, length us, event | category | flops | bytes accessed | tf_op | source)
XLA Modules:
  0.0 166.5 jit_solution(6735132040019925661)
XLA Ops:
  2.9 3.2 %convolution_convert_fusion = bf16[112,16,32]{2,1,0:T(8,128)(2,1)S(1)} fusion(bf16[128,16,512]{2,1,0:T(8,128)(2,1)S(1)} %gather_fusion, bf16[112,32,512]{2,1,0:T(8,128)(2,1)} %param.11), kind=kOutput, calls=%fused_computation.6 | convolution fusion | flops 58777600 | bytes 5881856 | tf_op jit(solution)/shard_map/snc,skc->snk/dot_general | solution.py:64
  6.2 1.2 copy-done.4
  8.7 1.4 scatter_custom_fusion.1
  10.1 1.4 scatter_custom_fusion
  11.6 2.7 %fusion.40 = f32[112,16,512]{2,1,0:T(8,128)S(1)} fusion(bf16[112,16,32]{2,1,0:T(8,128)(2,1)S(1)} %convolution_convert_fusion, bf16[112,32,512]{2,1,0:T(8,128)(2,1)} %param.12), kind=kOutput, calls=%fused_computation.114 | convolution fusion | flops 58720256 | bytes 7454720 | tf_op jit(solution)/shard_map/snk,skc->snc/dot_general | solution.py:67
  14.2 2.3 %maximum_maximum_fusion = f32[129,16,512]{2,1,0:T(8,128)} fusion(f32[112,16,512]{2,1,0:T(8,128)S(1)} %fusion.40, f32[16,16,512]{2,1,0:T(8,128)S(1)} %fusion.41, f32[129]{0:T(256)S(1)} %pad.6.clone), kind=kLoop, calls=%fused_computation.5 | loop fusion | flops 2113536 | bytes 8421892 | tf_op jit(solution)/shard_map/concatenate | solution.py:79
  16.5 6.5 %gather_fusion.2 = f32[256,16,512]{2,1,0:T(8,128)} fusion(f32[129,16,512]{2,1,0:T(8,128)} %maximum_maximum_fusion, s32[1024]{0:T(1024)S(1)} %get-tuple-element.17), kind=kCustom, calls=%fused_computation.2 | custom fusion | bytes 16778240 | tf_op jit(solution)/shard_map/gather | solution.py:82
  23.1 6.5 %gather_fusion.1 = f32[256,16,512]{2,1,0:T(8,128)} fusion(f32[129,16,512]{2,1,0:T(8,128)} %maximum_maximum_fusion, s32[1024]{0:T(1024)S(1)} %get-tuple-element.18), kind=kCustom, calls=%fused_computation.1 | custom fusion | bytes 16778240 | tf_op jit(solution)/shard_map/gather | solution.py:82
  29.6 12.1 %add.194 = f32[256,16,512]{2,1,0:T(8,128)} add(f32[256,16,512]{2,1,0:T(8,128)} %gather_fusion.1, f32[256,16,512]{2,1,0:T(8,128)} %gather_fusion.2) | non-fusion elementwise | flops 2097152 | bytes 25165824 | tf_op jit(solution)/shard_map/add | solution.py:82
  41.7 4.5 %fusion.39 = (f32[128,16,512]{2,1,0:T(8,128)S(1)}, f32[128,16,512]{2,1,0:T(8,128)S(1)}) fusion(f32[256,16,512]{2,1,0:T(8,128)} %add.194), kind=kLoop, calls=%fused_computation.113 | loop fusion | bytes 16777216 | tf_op jit(solution)/shard_map/slice | solution.py:85
  46.3 7.1 %collective-permute-done = f32[4,4,4,2,16,512]{5,4,3,2,1,0:T(8,128)S(1)} collective-permute-done((f32[4,4,4,2,16,512]{5,4,3,2,1,0:T(8,128)S(1)}, f32[4,4,4,2,16,512]{5,4,3,2,1,0:T(8,128)S(1)}, u32[]{:S(2)}, u32[]{:S(2)}) %collective-permute-start) | collective-permute-done | bytes 4194336 | tf_op jit(solution)/shard_map/ppermute | solution.py:43
  55.0 1.7 %collective-permute-start.1 = (f32[4,4,2,16,512]{4,3,2,1,0:T(8,128)S(1)}, f32[4,4,2,16,512]{4,3,2,1,0:T(8,128)S(1)}, u32[]{:S(2)}, u32[]{:S(2)}) collective-permute-start(f32[4,4,2,16,512]{4,3,2,1,0:T(8,128)S(1)} %get-tuple-element.6), channel_id=1, source_target_pairs={{0,2},{1,9},{2,4},{3,11},{4,6},{5,13},{6,0},{7,15},{8,10},{9,17},{... | collective-permute-start | bytes 3145736 | tf_op jit(solution)/shard_map/ppermute | solution.py:38
  56.7 2.7 %collective-permute-start.2 = (f32[4,4,2,16,512]{4,3,2,1,0:T(8,128)S(1)}, f32[4,4,2,16,512]{4,3,2,1,0:T(8,128)S(1)}, u32[]{:S(2)}, u32[]{:S(2)}) collective-permute-start(f32[4,4,2,16,512]{4,3,2,1,0:T(8,128)S(1)} %get-tuple-element.8), channel_id=1, source_target_pairs={{0,4},{1,17},{2,6},{3,19},{4,0},{5,21},{6,2},{7,23},{8,12},{9,25},... | collective-permute-start | bytes 3145736 | tf_op jit(solution)/shard_map/ppermute | solution.py:38
  59.4 1.4 collective-permute-start.3
  60.9 10.2 %collective-permute-done.1 = f32[4,4,2,16,512]{4,3,2,1,0:T(8,128)S(1)} collective-permute-done((f32[4,4,2,16,512]{4,3,2,1,0:T(8,128)S(1)}, f32[4,4,2,16,512]{4,3,2,1,0:T(8,128)S(1)}, u32[]{:S(2)}, u32[]{:S(2)}) %collective-permute-start.1) | collective-permute-done | bytes 1048608 | tf_op jit(solution)/shard_map/ppermute | solution.py:38
  71.1 12.3 %collective-permute-done.2 = f32[4,4,2,16,512]{4,3,2,1,0:T(8,128)S(1)} collective-permute-done((f32[4,4,2,16,512]{4,3,2,1,0:T(8,128)S(1)}, f32[4,4,2,16,512]{4,3,2,1,0:T(8,128)S(1)}, u32[]{:S(2)}, u32[]{:S(2)}) %collective-permute-start.2) | collective-permute-done | bytes 1048608 | tf_op jit(solution)/shard_map/ppermute | solution.py:38
  84.1 2.0 %collective-permute-start.4 = (f32[4,2,16,512]{3,2,1,0:T(8,128)S(1)}, f32[4,2,16,512]{3,2,1,0:T(8,128)S(1)}, u32[]{:S(2)}, u32[]{:S(2)}) collective-permute-start(f32[4,2,16,512]{3,2,1,0:T(8,128)S(1)} %get-tuple-element.9), channel_id=1, source_target_pairs={{0,8},{1,3},{2,10},{3,5},{4,12},{5,7},{6,14},{7,1},{8,16},{9,11},{... | collective-permute-start | bytes 786440 | tf_op jit(solution)/shard_map/ppermute | solution.py:38
  86.1 3.6 %collective-permute-start.5 = (f32[4,2,16,512]{3,2,1,0:T(8,128)S(1)}, f32[4,2,16,512]{3,2,1,0:T(8,128)S(1)}, u32[]{:S(2)}, u32[]{:S(2)}) collective-permute-start(f32[4,2,16,512]{3,2,1,0:T(8,128)S(1)} %get-tuple-element.11), channel_id=1, source_target_pairs={{0,16},{1,5},{2,18},{3,7},{4,20},{5,1},{6,22},{7,3},{8,24},{9,13},... | collective-permute-start | bytes 786440 | tf_op jit(solution)/shard_map/ppermute | solution.py:38
  90.7 1.9 %collective-permute-done.4 = f32[4,2,16,512]{3,2,1,0:T(8,128)S(1)} collective-permute-done((f32[4,2,16,512]{3,2,1,0:T(8,128)S(1)}, f32[4,2,16,512]{3,2,1,0:T(8,128)S(1)}, u32[]{:S(2)}, u32[]{:S(2)}) %collective-permute-start.4) | collective-permute-done | bytes 262176 | tf_op jit(solution)/shard_map/ppermute | solution.py:38
  92.6 4.3 %collective-permute-done.5 = f32[4,2,16,512]{3,2,1,0:T(8,128)S(1)} collective-permute-done((f32[4,2,16,512]{3,2,1,0:T(8,128)S(1)}, f32[4,2,16,512]{3,2,1,0:T(8,128)S(1)}, u32[]{:S(2)}, u32[]{:S(2)}) %collective-permute-start.5) | collective-permute-done | bytes 262176 | tf_op jit(solution)/shard_map/ppermute | solution.py:38
  96.9 1.6 collective-permute-start.7
  98.6 2.9 %collective-permute-start.8 = (f32[2,16,512]{2,1,0:T(8,128)S(1)}, f32[2,16,512]{2,1,0:T(8,128)S(1)}, u32[]{:S(2)}, u32[]{:S(2)}) collective-permute-start(f32[2,16,512]{2,1,0:T(8,128)S(1)} %get-tuple-element.14), channel_id=1, source_target_pairs={{0,64},{1,65},{2,66},{3,67},{4,68},{5,69},{6,70},{7,71},{8,72},{9,... | collective-permute-start | bytes 196616 | tf_op jit(solution)/shard_map/ppermute | solution.py:38
  101.5 1.3 collective-permute-start.9
  102.8 1.3 convolution_bitcast_fusion
  104.4 1.3 collective-permute-done.9
  105.8 1.5 fusion.5
  108.6 2.0 %collective-permute-start.11 = (f32[72,16]{1,0:T(8,128)S(1)}, f32[72,16]{1,0:T(8,128)S(1)}, u32[]{:S(2)}, u32[]{:S(2)}) collective-permute-start(f32[72,16]{1,0:T(8,128)S(1)} %fusion.38), channel_id=1, source_target_pairs={{0,2},{1,3},{2,0},{3,1},{4,6},{5,7},{6,4},{7,5},{8,10},{9,11},{10,... | collective-permute-start | bytes 13832 | tf_op jit(solution)/shard_map/ppermute | solution.py:31
  110.6 2.1 %collective-permute-done.11 = f32[72,16]{1,0:T(8,128)S(1)} collective-permute-done((f32[72,16]{1,0:T(8,128)S(1)}, f32[72,16]{1,0:T(8,128)S(1)}, u32[]{:S(2)}, u32[]{:S(2)}) %collective-permute-start.11) | collective-permute-done | bytes 4640 | tf_op jit(solution)/shard_map/ppermute | solution.py:31
  112.6 2.9 %collective-permute-start.12 = (f32[72,16]{1,0:T(8,128)S(1)}, f32[72,16]{1,0:T(8,128)S(1)}, u32[]{:S(2)}, u32[]{:S(2)}) collective-permute-start(f32[72,16]{1,0:T(8,128)S(1)} %add.207), channel_id=1, source_target_pairs={{0,4},{1,5},{2,6},{3,7},{4,0},{5,1},{6,2},{7,3},{8,12},{9,13},{10,... | collective-permute-start | bytes 13832 | tf_op jit(solution)/shard_map/ppermute | solution.py:31
  115.6 2.5 %collective-permute-done.12 = f32[72,16]{1,0:T(8,128)S(1)} collective-permute-done((f32[72,16]{1,0:T(8,128)S(1)}, f32[72,16]{1,0:T(8,128)S(1)}, u32[]{:S(2)}, u32[]{:S(2)}) %collective-permute-start.12) | collective-permute-done | bytes 4640 | tf_op jit(solution)/shard_map/ppermute | solution.py:31
  118.1 1.5 collective-permute-start.13
  119.6 2.4 %collective-permute-done.13 = f32[72,16]{1,0:T(8,128)S(1)} collective-permute-done((f32[72,16]{1,0:T(8,128)S(1)}, f32[72,16]{1,0:T(8,128)S(1)}, u32[]{:S(2)}, u32[]{:S(2)}) %collective-permute-start.13) | collective-permute-done | bytes 4640 | tf_op jit(solution)/shard_map/ppermute | solution.py:31
  122.1 2.5 %collective-permute-start.14 = (f32[72,16]{1,0:T(8,128)S(1)}, f32[72,16]{1,0:T(8,128)S(1)}, u32[]{:S(2)}, u32[]{:S(2)}) collective-permute-start(f32[72,16]{1,0:T(8,128)S(1)} %add.209), channel_id=1, source_target_pairs={{0,16},{1,17},{2,18},{3,19},{4,20},{5,21},{6,22},{7,23},{8,24},{9,... | collective-permute-start | bytes 13832 | tf_op jit(solution)/shard_map/ppermute | solution.py:31
  124.6 2.9 %collective-permute-done.14 = f32[72,16]{1,0:T(8,128)S(1)} collective-permute-done((f32[72,16]{1,0:T(8,128)S(1)}, f32[72,16]{1,0:T(8,128)S(1)}, u32[]{:S(2)}, u32[]{:S(2)}) %collective-permute-start.14) | collective-permute-done | bytes 4640 | tf_op jit(solution)/shard_map/ppermute | solution.py:31
  127.9 3.6 %collective-permute-done.15 = f32[72,16]{1,0:T(8,128)S(1)} collective-permute-done((f32[72,16]{1,0:T(8,128)S(1)}, f32[72,16]{1,0:T(8,128)S(1)}, u32[]{:S(2)}, u32[]{:S(2)}) %collective-permute-start.15) | collective-permute-done | bytes 4640 | tf_op jit(solution)/shard_map/ppermute | solution.py:31
  131.5 2.0 %collective-permute-start.16 = (f32[72,16]{1,0:T(8,128)S(1)}, f32[72,16]{1,0:T(8,128)S(1)}, u32[]{:S(2)}, u32[]{:S(2)}) collective-permute-start(f32[72,16]{1,0:T(8,128)S(1)} %add.211), channel_id=1, source_target_pairs={{0,64},{1,65},{2,66},{3,67},{4,68},{5,69},{6,70},{7,71},{8,72},{9,... | collective-permute-start | bytes 13832 | tf_op jit(solution)/shard_map/ppermute | solution.py:31
  133.5 3.5 %collective-permute-done.16 = f32[72,16]{1,0:T(8,128)S(1)} collective-permute-done((f32[72,16]{1,0:T(8,128)S(1)}, f32[72,16]{1,0:T(8,128)S(1)}, u32[]{:S(2)}, u32[]{:S(2)}) %collective-permute-start.16) | collective-permute-done | bytes 4640 | tf_op jit(solution)/shard_map/ppermute | solution.py:31
  139.3 1.9 %collective-permute-start.18 = (f32[16]{0:T(128)S(1)}, f32[16]{0:T(128)S(1)}, u32[]{:S(2)}, u32[]{:S(2)}) collective-permute-start(f32[16]{0:T(128)S(1)} %add.214), channel_id=1, source_target_pairs={{0,2},{1,3},{2,0},{3,1},{4,6},{5,7},{6,4},{7,5},{8,10},{9,11},{10,... | collective-permute-start | bytes 200 | tf_op jit(solution)/shard_map/ppermute | solution.py:31
  141.2 1.7 %collective-permute-done.18 = f32[16]{0:T(128)S(1)} collective-permute-done((f32[16]{0:T(128)S(1)}, f32[16]{0:T(128)S(1)}, u32[]{:S(2)}, u32[]{:S(2)}) %collective-permute-start.18) | collective-permute-done | bytes 96 | tf_op jit(solution)/shard_map/ppermute | solution.py:31
  142.8 2.9 %collective-permute-start.19 = (f32[16]{0:T(128)S(1)}, f32[16]{0:T(128)S(1)}, u32[]{:S(2)}, u32[]{:S(2)}) collective-permute-start(f32[16]{0:T(128)S(1)} %add.215), channel_id=1, source_target_pairs={{0,4},{1,5},{2,6},{3,7},{4,0},{5,1},{6,2},{7,3},{8,12},{9,13},{10,... | collective-permute-start | bytes 200 | tf_op jit(solution)/shard_map/ppermute | solution.py:31
  145.8 2.1 %collective-permute-done.19 = f32[16]{0:T(128)S(1)} collective-permute-done((f32[16]{0:T(128)S(1)}, f32[16]{0:T(128)S(1)}, u32[]{:S(2)}, u32[]{:S(2)}) %collective-permute-start.19) | collective-permute-done | bytes 96 | tf_op jit(solution)/shard_map/ppermute | solution.py:31
  147.9 1.5 collective-permute-start.20
  149.4 2.1 %collective-permute-done.20 = f32[16]{0:T(128)S(1)} collective-permute-done((f32[16]{0:T(128)S(1)}, f32[16]{0:T(128)S(1)}, u32[]{:S(2)}, u32[]{:S(2)}) %collective-permute-start.20) | collective-permute-done | bytes 96 | tf_op jit(solution)/shard_map/ppermute | solution.py:31
  151.5 2.5 %collective-permute-start.21 = (f32[16]{0:T(128)S(1)}, f32[16]{0:T(128)S(1)}, u32[]{:S(2)}, u32[]{:S(2)}) collective-permute-start(f32[16]{0:T(128)S(1)} %add.217), channel_id=1, source_target_pairs={{0,16},{1,17},{2,18},{3,19},{4,20},{5,21},{6,22},{7,23},{8,24},{9,... | collective-permute-start | bytes 200 | tf_op jit(solution)/shard_map/ppermute | solution.py:31
  154.0 2.6 %collective-permute-done.21 = f32[16]{0:T(128)S(1)} collective-permute-done((f32[16]{0:T(128)S(1)}, f32[16]{0:T(128)S(1)}, u32[]{:S(2)}, u32[]{:S(2)}) %collective-permute-start.21) | collective-permute-done | bytes 96 | tf_op jit(solution)/shard_map/ppermute | solution.py:31
  157.2 2.9 %collective-permute-done.22 = f32[16]{0:T(128)S(1)} collective-permute-done((f32[16]{0:T(128)S(1)}, f32[16]{0:T(128)S(1)}, u32[]{:S(2)}, u32[]{:S(2)}) %collective-permute-start.22) | collective-permute-done | bytes 96 | tf_op jit(solution)/shard_map/ppermute | solution.py:31
  160.1 2.0 %collective-permute-start.23 = (f32[16]{0:T(128)S(1)}, f32[16]{0:T(128)S(1)}, u32[]{:S(2)}, u32[]{:S(2)}) collective-permute-start(f32[16]{0:T(128)S(1)} %add.219), channel_id=1, source_target_pairs={{0,64},{1,65},{2,66},{3,67},{4,68},{5,69},{6,70},{7,71},{8,72},{9,... | collective-permute-start | bytes 200 | tf_op jit(solution)/shard_map/ppermute | solution.py:31
  162.1 3.1 %collective-permute-done.23 = f32[16]{0:T(128)S(1)} collective-permute-done((f32[16]{0:T(128)S(1)}, f32[16]{0:T(128)S(1)}, u32[]{:S(2)}, u32[]{:S(2)}) %collective-permute-start.23) | collective-permute-done | bytes 96 | tf_op jit(solution)/shard_map/ppermute | solution.py:31
  (64 shorter events, 13.1 us)
Async XLA Ops:
  2.9 4.5 %copy-start.4 = (bf16[16,512,512]{2,1,0:T(8,128)(2,1)S(1)}, bf16[16,512,512]{2,1,0:T(8,128)(2,1)}, u32[]{:S(2)}) copy-start(bf16[16,512,512]{2,1,0:T(8,128)(2,1)} %param.10) | copy-start | bytes 25165828
  7.4 1.2 copy-start.2
  7.4 1.2 copy-start.3
  46.2 7.2 %collective-permute-start = (f32[4,4,4,2,16,512]{5,4,3,2,1,0:T(8,128)S(1)}, f32[4,4,4,2,16,512]{5,4,3,2,1,0:T(8,128)S(1)}, u32[]{:S(2)}, u32[]{:S(2)}) collective-permute-start(f32[4,4,4,2,16,512]{5,4,3,2,1,0:T(8,128)S(1)} %bitcast.112), channel_id=1, source_target_pairs={{0,1},{1,0},{2,3},{3,2},{4,5},{5,4},{6,7},{7,6},{8,9},{9,8},{10,11... | collective-permute-start | bytes 12582920 | tf_op jit(solution)/shard_map/ppermute | solution.py:43
  55.0 16.1 %collective-permute-start.1 = (f32[4,4,2,16,512]{4,3,2,1,0:T(8,128)S(1)}, f32[4,4,2,16,512]{4,3,2,1,0:T(8,128)S(1)}, u32[]{:S(2)}, u32[]{:S(2)}) collective-permute-start(f32[4,4,2,16,512]{4,3,2,1,0:T(8,128)S(1)} %get-tuple-element.6), channel_id=1, source_target_pairs={{0,2},{1,9},{2,4},{3,11},{4,6},{5,13},{6,0},{7,15},{8,10},{9,17},{... | collective-permute-start | bytes 3145736 | tf_op jit(solution)/shard_map/ppermute | solution.py:38
  56.7 26.7 %collective-permute-start.2 = (f32[4,4,2,16,512]{4,3,2,1,0:T(8,128)S(1)}, f32[4,4,2,16,512]{4,3,2,1,0:T(8,128)S(1)}, u32[]{:S(2)}, u32[]{:S(2)}) collective-permute-start(f32[4,4,2,16,512]{4,3,2,1,0:T(8,128)S(1)} %get-tuple-element.8), channel_id=1, source_target_pairs={{0,4},{1,17},{2,6},{3,19},{4,0},{5,21},{6,2},{7,23},{8,12},{9,25},... | collective-permute-start | bytes 3145736 | tf_op jit(solution)/shard_map/ppermute | solution.py:38
  59.4 43.4 %copy-start = (f32[8,2,16,512]{3,2,1,0:T(8,128)S(1)}, f32[8,2,16,512]{3,2,1,0:T(8,128)}, u32[]{:S(2)}) copy-start(f32[8,2,16,512]{3,2,1,0:T(8,128)} %param.8) | copy-start | bytes 1572868
  59.4 46.3 %copy-start.1 = (f32[2,512]{1,0:T(2,128)S(1)}, f32[2,512]{1,0:T(2,128)}, u32[]{:S(2)}) copy-start(f32[2,512]{1,0:T(2,128)} %param.9) | copy-start | bytes 12292
  59.4 24.0 %collective-permute-start.3 = (f32[4,4,2,16,512]{4,3,2,1,0:T(8,128)S(1)}, f32[4,4,2,16,512]{4,3,2,1,0:T(8,128)S(1)}, u32[]{:S(2)}, u32[]{:S(2)}) collective-permute-start(f32[4,4,2,16,512]{4,3,2,1,0:T(8,128)S(1)} %get-tuple-element.7), channel_id=1, source_target_pairs={{0,6},{1,25},{2,0},{3,27},{4,2},{5,29},{6,4},{7,31},{8,14},{9,1},{... | collective-permute-start | bytes 3145736 | tf_op jit(solution)/shard_map/ppermute | solution.py:38
  84.1 8.5 %collective-permute-start.4 = (f32[4,2,16,512]{3,2,1,0:T(8,128)S(1)}, f32[4,2,16,512]{3,2,1,0:T(8,128)S(1)}, u32[]{:S(2)}, u32[]{:S(2)}) collective-permute-start(f32[4,2,16,512]{3,2,1,0:T(8,128)S(1)} %get-tuple-element.9), channel_id=1, source_target_pairs={{0,8},{1,3},{2,10},{3,5},{4,12},{5,7},{6,14},{7,1},{8,16},{9,11},{... | collective-permute-start | bytes 786440 | tf_op jit(solution)/shard_map/ppermute | solution.py:38
  86.1 10.7 %collective-permute-start.5 = (f32[4,2,16,512]{3,2,1,0:T(8,128)S(1)}, f32[4,2,16,512]{3,2,1,0:T(8,128)S(1)}, u32[]{:S(2)}, u32[]{:S(2)}) collective-permute-start(f32[4,2,16,512]{3,2,1,0:T(8,128)S(1)} %get-tuple-element.11), channel_id=1, source_target_pairs={{0,16},{1,5},{2,18},{3,7},{4,20},{5,1},{6,22},{7,3},{8,24},{9,13},... | collective-permute-start | bytes 786440 | tf_op jit(solution)/shard_map/ppermute | solution.py:38
  89.7 7.2 %collective-permute-start.6 = (f32[4,2,16,512]{3,2,1,0:T(8,128)S(1)}, f32[4,2,16,512]{3,2,1,0:T(8,128)S(1)}, u32[]{:S(2)}, u32[]{:S(2)}) collective-permute-start(f32[4,2,16,512]{3,2,1,0:T(8,128)S(1)} %get-tuple-element.10), channel_id=1, source_target_pairs={{0,24},{1,7},{2,26},{3,1},{4,28},{5,3},{6,30},{7,5},{8,0},{9,15},{... | collective-permute-start | bytes 786440 | tf_op jit(solution)/shard_map/ppermute | solution.py:38
  96.9 7.3 %collective-permute-start.7 = (f32[2,16,512]{2,1,0:T(8,128)S(1)}, f32[2,16,512]{2,1,0:T(8,128)S(1)}, u32[]{:S(2)}, u32[]{:S(2)}) collective-permute-start(f32[2,16,512]{2,1,0:T(8,128)S(1)} %get-tuple-element.12), channel_id=1, source_target_pairs={{0,32},{1,33},{2,34},{3,35},{4,36},{5,37},{6,38},{7,39},{8,40},{9,... | collective-permute-start | bytes 196616 | tf_op jit(solution)/shard_map/ppermute | solution.py:38
  98.6 5.8 %collective-permute-start.8 = (f32[2,16,512]{2,1,0:T(8,128)S(1)}, f32[2,16,512]{2,1,0:T(8,128)S(1)}, u32[]{:S(2)}, u32[]{:S(2)}) collective-permute-start(f32[2,16,512]{2,1,0:T(8,128)S(1)} %get-tuple-element.14), channel_id=1, source_target_pairs={{0,64},{1,65},{2,66},{3,67},{4,68},{5,69},{6,70},{7,71},{8,72},{9,... | collective-permute-start | bytes 196616 | tf_op jit(solution)/shard_map/ppermute | solution.py:38
  101.5 4.3 %collective-permute-start.9 = (f32[2,16,512]{2,1,0:T(8,128)S(1)}, f32[2,16,512]{2,1,0:T(8,128)S(1)}, u32[]{:S(2)}, u32[]{:S(2)}) collective-permute-start(f32[2,16,512]{2,1,0:T(8,128)S(1)} %get-tuple-element.13), channel_id=1, source_target_pairs={{0,96},{1,97},{2,98},{3,99},{4,100},{5,101},{6,102},{7,103},{8,104... | collective-permute-start | bytes 196616 | tf_op jit(solution)/shard_map/ppermute | solution.py:38
  107.3 1.2 collective-permute-start.10
  108.6 4.0 %collective-permute-start.11 = (f32[72,16]{1,0:T(8,128)S(1)}, f32[72,16]{1,0:T(8,128)S(1)}, u32[]{:S(2)}, u32[]{:S(2)}) collective-permute-start(f32[72,16]{1,0:T(8,128)S(1)} %fusion.38), channel_id=1, source_target_pairs={{0,2},{1,3},{2,0},{3,1},{4,6},{5,7},{6,4},{7,5},{8,10},{9,11},{10,... | collective-permute-start | bytes 13832 | tf_op jit(solution)/shard_map/ppermute | solution.py:31
  112.6 5.5 %collective-permute-start.12 = (f32[72,16]{1,0:T(8,128)S(1)}, f32[72,16]{1,0:T(8,128)S(1)}, u32[]{:S(2)}, u32[]{:S(2)}) collective-permute-start(f32[72,16]{1,0:T(8,128)S(1)} %add.207), channel_id=1, source_target_pairs={{0,4},{1,5},{2,6},{3,7},{4,0},{5,1},{6,2},{7,3},{8,12},{9,13},{10,... | collective-permute-start | bytes 13832 | tf_op jit(solution)/shard_map/ppermute | solution.py:31
  118.1 4.0 %collective-permute-start.13 = (f32[72,16]{1,0:T(8,128)S(1)}, f32[72,16]{1,0:T(8,128)S(1)}, u32[]{:S(2)}, u32[]{:S(2)}) collective-permute-start(f32[72,16]{1,0:T(8,128)S(1)} %add.208), channel_id=1, source_target_pairs={{0,8},{1,9},{2,10},{3,11},{4,12},{5,13},{6,14},{7,15},{8,0},{9,1},... | collective-permute-start | bytes 13832 | tf_op jit(solution)/shard_map/ppermute | solution.py:31
  122.1 5.5 %collective-permute-start.14 = (f32[72,16]{1,0:T(8,128)S(1)}, f32[72,16]{1,0:T(8,128)S(1)}, u32[]{:S(2)}, u32[]{:S(2)}) collective-permute-start(f32[72,16]{1,0:T(8,128)S(1)} %add.209), channel_id=1, source_target_pairs={{0,16},{1,17},{2,18},{3,19},{4,20},{5,21},{6,22},{7,23},{8,24},{9,... | collective-permute-start | bytes 13832 | tf_op jit(solution)/shard_map/ppermute | solution.py:31
  127.5 4.0 %collective-permute-start.15 = (f32[72,16]{1,0:T(8,128)S(1)}, f32[72,16]{1,0:T(8,128)S(1)}, u32[]{:S(2)}, u32[]{:S(2)}) collective-permute-start(f32[72,16]{1,0:T(8,128)S(1)} %add.210), channel_id=1, source_target_pairs={{0,32},{1,33},{2,34},{3,35},{4,36},{5,37},{6,38},{7,39},{8,40},{9,... | collective-permute-start | bytes 13832 | tf_op jit(solution)/shard_map/ppermute | solution.py:31
  131.5 5.5 %collective-permute-start.16 = (f32[72,16]{1,0:T(8,128)S(1)}, f32[72,16]{1,0:T(8,128)S(1)}, u32[]{:S(2)}, u32[]{:S(2)}) collective-permute-start(f32[72,16]{1,0:T(8,128)S(1)} %add.211), channel_id=1, source_target_pairs={{0,64},{1,65},{2,66},{3,67},{4,68},{5,69},{6,70},{7,71},{8,72},{9,... | collective-permute-start | bytes 13832 | tf_op jit(solution)/shard_map/ppermute | solution.py:31
  138.0 1.2 collective-permute-start.17
  139.3 3.6 %collective-permute-start.18 = (f32[16]{0:T(128)S(1)}, f32[16]{0:T(128)S(1)}, u32[]{:S(2)}, u32[]{:S(2)}) collective-permute-start(f32[16]{0:T(128)S(1)} %add.214), channel_id=1, source_target_pairs={{0,2},{1,3},{2,0},{3,1},{4,6},{5,7},{6,4},{7,5},{8,10},{9,11},{10,... | collective-permute-start | bytes 200 | tf_op jit(solution)/shard_map/ppermute | solution.py:31
  142.8 5.1 %collective-permute-start.19 = (f32[16]{0:T(128)S(1)}, f32[16]{0:T(128)S(1)}, u32[]{:S(2)}, u32[]{:S(2)}) collective-permute-start(f32[16]{0:T(128)S(1)} %add.215), channel_id=1, source_target_pairs={{0,4},{1,5},{2,6},{3,7},{4,0},{5,1},{6,2},{7,3},{8,12},{9,13},{10,... | collective-permute-start | bytes 200 | tf_op jit(solution)/shard_map/ppermute | solution.py:31
  147.9 3.6 %collective-permute-start.20 = (f32[16]{0:T(128)S(1)}, f32[16]{0:T(128)S(1)}, u32[]{:S(2)}, u32[]{:S(2)}) collective-permute-start(f32[16]{0:T(128)S(1)} %add.216), channel_id=1, source_target_pairs={{0,8},{1,9},{2,10},{3,11},{4,12},{5,13},{6,14},{7,15},{8,0},{9,1},... | collective-permute-start | bytes 200 | tf_op jit(solution)/shard_map/ppermute | solution.py:31
  151.5 5.1 %collective-permute-start.21 = (f32[16]{0:T(128)S(1)}, f32[16]{0:T(128)S(1)}, u32[]{:S(2)}, u32[]{:S(2)}) collective-permute-start(f32[16]{0:T(128)S(1)} %add.217), channel_id=1, source_target_pairs={{0,16},{1,17},{2,18},{3,19},{4,20},{5,21},{6,22},{7,23},{8,24},{9,... | collective-permute-start | bytes 200 | tf_op jit(solution)/shard_map/ppermute | solution.py:31
  156.6 3.6 %collective-permute-start.22 = (f32[16]{0:T(128)S(1)}, f32[16]{0:T(128)S(1)}, u32[]{:S(2)}, u32[]{:S(2)}) collective-permute-start(f32[16]{0:T(128)S(1)} %add.218), channel_id=1, source_target_pairs={{0,32},{1,33},{2,34},{3,35},{4,36},{5,37},{6,38},{7,39},{8,40},{9,... | collective-permute-start | bytes 200 | tf_op jit(solution)/shard_map/ppermute | solution.py:31
  160.1 5.1 %collective-permute-start.23 = (f32[16]{0:T(128)S(1)}, f32[16]{0:T(128)S(1)}, u32[]{:S(2)}, u32[]{:S(2)}) collective-permute-start(f32[16]{0:T(128)S(1)} %add.219), channel_id=1, source_target_pairs={{0,64},{1,65},{2,66},{3,67},{4,68},{5,69},{6,70},{7,71},{8,72},{9,... | collective-permute-start | bytes 200 | tf_op jit(solution)/shard_map/ppermute | solution.py:31

commit v4 on v3

--- a/solution.py
+++ b/solution.py
@@ -1,6 +1,8 @@
 import jax
 import jax.numpy as jnp
 from jax import lax
+from jax.experimental import pallas as pl
+from jax.experimental.pallas import tpu as pltpu
 from jax.sharding import PartitionSpec as P
 
 AXES = ("grp", "dev")
@@ -46,6 +48,73 @@
     return spread(d, "y")
 
 
+STEPS = 8
+
+def block_kernel(slot_ref, row_ref, vec_ref, near_ref, u_ref, v_ref, keep_ref, send_ref):
+    i = pl.program_id(0)
+    half = keep_ref.shape[0]
+    near_step = near_ref.shape[0]
+    far_step = u_ref.shape[0]
+    near_total = near_step * pl.num_programs(0)
+
+    @pl.when(i == 0)
+    def _():
+        keep_ref[...] = jnp.zeros_like(keep_ref)
+        send_ref[...] = jnp.zeros_like(send_ref)
+
+    def add(g, part):
+        s = slot_ref[g]
+
+        @pl.when(s < half)
+        def _():
+            keep_ref[s] += part
+
+        @pl.when(s >= half)
+        def _():
+            send_ref[s - half] += part
+
+    for j in range(near_step):
+        g = i * near_step + j
+        a = vec_ref[row_ref[g]]
+        add(g, jnp.dot(a, near_ref[j], preferred_element_type=jnp.float32))
+    for j in range(far_step):
+        g = near_total + i * far_step + j
+        a = vec_ref[row_ref[g]]
+        coeff = lax.dot_general(a, u_ref[j], (((1,), (1,)), ((), ())), preferred_element_type=jnp.float32)
+        add(g, jnp.dot(coeff.astype(jnp.bfloat16), v_ref[j], preferred_element_type=jnp.float32))
+
+
+def block_products(slot, rows, vec_low, near_blocks, far_u, far_v, half):
+    near_count, size, _ = near_blocks.shape
+    far_count, rank, _ = far_u.shape
+    sources = vec_low.shape[1]
+    near_step = near_count // STEPS
+    far_step = far_count // STEPS
+    out = jax.ShapeDtypeStruct((half, sources, size), jnp.float32)
+    grid_spec = pltpu.PrefetchScalarGridSpec(
+        num_scalar_prefetch=2,
+        grid=(STEPS,),
+        in_specs=[
+            pl.BlockSpec(vec_low.shape, lambda i, s, r: (0, 0, 0)),
+            pl.BlockSpec((near_step, size, size), lambda i, s, r: (i, 0, 0)),
+            pl.BlockSpec((far_step, rank, size), lambda i, s, r: (i, 0, 0)),
+            pl.BlockSpec((far_step, rank, size), lambda i, s, r: (i, 0, 0)),
+        ],
+        out_specs=[
+            pl.BlockSpec((half, sources, size), lambda i, s, r: (0, 0, 0)),
+            pl.BlockSpec((half, sources, size), lambda i, s, r: (0, 0, 0)),
+        ],
+    )
+    return pl.pallas_call(
+        block_kernel,
+        grid_spec=grid_spec,
+        out_shape=[out, out],
+        compiler_params=pltpu.CompilerParams(
+            dimension_semantics=("arbitrary",), vmem_limit_bytes=48 * 1024 * 1024
+        ),
+    )(slot, rows, vec_low, near_blocks, far_u, far_v)
+
+
 def on_device(basis, diagonal, near_blocks, far_u, far_v, block_row, block_dest, block_col):
     highest = lax.Precision.HIGHEST
     basis_count = basis.shape[0]
@@ -57,32 +126,15 @@
     me = lax.axis_index(AXES)
     vector = basis[basis_count - 1]
     vec_low = vector.astype(jnp.bfloat16)
-    picked = vec_low[block_row]
-    near_part = jnp.einsum(
-        "snc,scd->snd", picked[:near_count], near_blocks, preferred_element_type=jnp.float32
-    )
-    coeff = jnp.einsum(
-        "snc,skc->snk", picked[near_count:], far_u, preferred_element_type=jnp.float32
-    ).astype(jnp.bfloat16)
-    far_part = jnp.einsum("snk,skc->snc", coeff, far_v, preferred_element_type=jnp.float32)
     dest = block_dest[:, 0]
     rel = {a: (coord(dest, a) - coord(me, a)) % SIZES[a] for a in SIZES}
     to_core = coord(dest, "c")
     order = jnp.where(to_core == 0, rel["x"] * 4 + rel["z"], rel["z"] * 4 + rel["x"])
     slot = ((rel["c"] * 16 + order) * 4 + rel["y"]) * clusters + block_col
-    blocks = slot.shape[0]
-    numbers = jnp.arange(blocks, dtype=jnp.int32)
     spots = devices * clusters
-    lowest = jnp.full((spots,), blocks, jnp.int32).at[slot].min(numbers)
-    highest_block = jnp.full((spots,), -1, jnp.int32).at[slot].max(numbers)
-    second_block = jnp.where(highest_block > lowest, highest_block, blocks)
-    table = jnp.concatenate(
-        [near_part, far_part, jnp.zeros((1, sources, cluster_size), jnp.float32)], axis=0
-    )
-    slab = table[lowest] + table[second_block]
-    shape = (2, 4, 4, 4, clusters, sources, cluster_size)
-    slab = slab.reshape(shape)
-    summed = reduce_to_owner(slab[0], slab[1])
+    keep, send = block_products(slot, block_row, vec_low, near_blocks, far_u, far_v, spots // 2)
+    shape = (4, 4, 4, clusters, sources, cluster_size)
+    summed = reduce_to_owner(keep.reshape(shape), send.reshape(shape))
     image = diagonal[:, None, :] * vector + summed
     panels = clusters * cluster_size * devices
     local_first = jnp.einsum("knjc,njc->kj", basis, image, precision=highest)

time: 167 us -> 170 us (1.018)
  Pallas kernels: 0 us -> 37.2 us
  waiting for transfers between devices: 71.2 us -> 97.2 us
  starting transfers between devices: 41.3 us -> 20 us
  local copies, waits for them, and re-layouts: 21.3 us -> 4.43 us
  other arithmetic: 21.2 us -> 6.15 us
  matrix products: 10.7 us -> 3.6 us
    pallas_call x0 -> x1, Pallas kernels: none -> 37.2 us  [block_products(): pl.pallas_call(block_kernel, grid_spec=grid_spec, out_shape=[out, out], c...]
    ppermute x14, starting transfers between devices: 22.9 us -> 5.32 us  [all_sum(): v = v + lax.ppermute(v, AXES, flipped(bit))]
    ppermute x14, waiting for transfers between devices: 33.8 us -> 51.4 us  [all_sum(): v = v + lax.ppermute(v, AXES, flipped(bit))]
    gather x3 -> x0, local copies, waits for them, and re-layouts: 13.7 us -> none  [the longest x2 13 us: on_device(): slab = table[lowest] + table[second_block]]
    add x1, other arithmetic: 12.1 us -> 0.7 us  [on_device(): slot = ((rel['c'] * 16 + order) * 4 + rel['y']) * clusters + block_col]
    ppermute x9, waiting for transfers between devices: 30.2 us -> 38.4 us  [spread(): acc = acc + lax.ppermute(pieces[k], AXES, moved(axis, k, other))]
    dot_general x3 -> x0, matrix products: 7.09 us -> none  [the longest x1 3.24 us: on_device(): jnp.einsum('snc,skc->snk', picked[near_count:], far_u, preferred_element_...]
    slice x1 -> x0, local copies, waits for them, and re-layouts: 4.53 us -> none  [on_device(): summed = reduce_to_owner(slab[0], slab[1])]
  transfers between devices with their start and end apart: 24 -> 24, of which waited for: 21 -> 22; matrix products, arithmetic and copies ran while one was open for 1% -> 1% of each run, Pallas kernels for 0% -> 0%
where the time goes in v4:
time: 170 us; the launch traced here: 169 us
  waiting for transfers between devices  97.2 us (57%)
  Pallas kernels  37.2 us (22%)
  starting transfers between devices  20 us (12%)
  other arithmetic  6.15 us (4%)
  local copies, waits for them, and re-layouts  4.43 us (3%)
  matrix products  3.6 us (2%)
    ppermute x14, waiting for transfers between devices, all_sum(): v = v + lax.ppermute(v, AXES, flipped(bit))  51.4 us
    ppermute x9, waiting for transfers between devices, spread(): acc = acc + lax.ppermute(pieces[k], AXES, moved(axis, k, other))  38.4 us
    pallas_call x1, Pallas kernels, block_products(): pl.pallas_call(block_kernel, grid_spec=grid_spec, out_shape=[out, out], c...  37.2 us
    ppermute x9, starting transfers between devices, spread(): acc = acc + lax.ppermute(pieces[k], AXES, moved(axis, k, other))  14.7 us
    ppermute x1, waiting for transfers between devices, reduce_to_owner(): d = keep + lax.ppermute(send, AXES, moved('c', 1))  7.37 us
    ppermute x14, starting transfers between devices, all_sum(): v = v + lax.ppermute(v, AXES, flipped(bit))  5.32 us
  transfers between devices with their start and end apart: 24, of which 22 were waited for; matrix products, arithmetic and copies ran while one was open for 1% of the time, Pallas kernels for 0%

profile of v4, /device:TPU:0, one launch (start us, length us, event | category | flops | bytes accessed | tf_op | source)
XLA Modules:
  0.0 169.4 jit_solution(13985940945005356390)
XLA Ops:
  0.7 0.8 bitcast_convert_fusion.vec_ref
  1.6 0.7 multiply_add_fusion.slot_ref
  2.3 2.0 %copy-done = bf16[112,32,512]{2,1,0:T(8,128)(2,1)S(1)} copy-done((bf16[112,32,512]{2,1,0:T(8,128)(2,1)S(1)}, bf16[112,32,512]{2,1,0:T(8,128)(2,1)}, u32[]{:S(2)}) %copy-start) | copy-done | bytes 3670040
  4.3 0.7 copy-done.1
  5.0 37.2 %shard_map.95 = (f32[128,16,512]{2,1,0:T(8,128)}, f32[128,16,512]{2,1,0:T(8,128)}) custom-call(s32[128]{0:T(128)S(1)} %multiply_add_fusion.slot_ref, s32[128]{0:T(128)S(1)} %copy-done.1, bf16[2,16,512]{2,1,0:T(8,128)(2,1)S(1)} %bitcast_convert_fusion.vec_ref, bf16[16,512,512]{2,1,0:T(8,128)(2,1)} %near_ref.1, bf16[112,32,512]{2,1,0:T(8,128)(2,1)S(1)} %copy-done, ...), custom_call_target="tpu_custom_call" | custom-call | tf_op jit(solution)/shard_map/pallas_call | solution.py:108
  42.1 7.4 %collective-permute-done = f32[4,4,4,2,16,512]{5,4,3,2,1,0:T(8,128)S(1)} collective-permute-done((f32[4,4,4,2,16,512]{5,4,3,2,1,0:T(8,128)}, f32[4,4,4,2,16,512]{5,4,3,2,1,0:T(8,128)S(1)}, u32[]{:S(2)}, u32[]{:S(2)}) %collective-permute-start) | collective-permute-done | bytes 4194336 | tf_op jit(solution)/shard_map/ppermute | solution.py:45
  49.5 3.2 %add.174 = f32[4,4,4,2,16,512]{5,4,3,2,1,0:T(8,128)S(1)} add(f32[4,4,4,2,16,512]{5,4,3,2,1,0:T(8,128)} %bitcast.104, f32[4,4,4,2,16,512]{5,4,3,2,1,0:T(8,128)S(1)} %collective-permute-done) | non-fusion elementwise | flops 1048576 | bytes 12582912 | tf_op jit(solution)/shard_map/add | solution.py:45
  52.7 0.6 slice_bitcast_fusion.2
  53.3 2.9 %collective-permute-start.3 = (f32[4,4,2,16,512]{4,3,2,1,0:T(8,128)S(1)}, f32[4,4,2,16,512]{4,3,2,1,0:T(8,128)S(1)}, u32[]{:S(2)}, u32[]{:S(2)}) collective-permute-start(f32[4,4,2,16,512]{4,3,2,1,0:T(8,128)S(1)} %get-tuple-element.9), channel_id=1, source_target_pairs={{0,6},{1,25},{2,0},{3,27},{4,2},{5,29},{6,4},{7,31},{8,14},{9,1},{... | collective-permute-start | bytes 3145736 | tf_op jit(solution)/shard_map/ppermute | solution.py:40
  56.2 0.8 collective-permute-start.2
  57.0 0.9 collective-permute-start.1
  57.9 21.9 %collective-permute-done.3 = f32[4,4,2,16,512]{4,3,2,1,0:T(8,128)S(1)} collective-permute-done((f32[4,4,2,16,512]{4,3,2,1,0:T(8,128)S(1)}, f32[4,4,2,16,512]{4,3,2,1,0:T(8,128)S(1)}, u32[]{:S(2)}, u32[]{:S(2)}) %collective-permute-start.3) | collective-permute-done | bytes 1048608 | tf_op jit(solution)/shard_map/ppermute | solution.py:40
  79.8 4.0 %collective-permute-done.1 = f32[4,4,2,16,512]{4,3,2,1,0:T(8,128)S(1)} collective-permute-done((f32[4,4,2,16,512]{4,3,2,1,0:T(8,128)S(1)}, f32[4,4,2,16,512]{4,3,2,1,0:T(8,128)S(1)}, u32[]{:S(2)}, u32[]{:S(2)}) %collective-permute-start.1) | collective-permute-done | bytes 1048608 | tf_op jit(solution)/shard_map/ppermute | solution.py:40
  83.8 0.6 fusion.2
  84.4 4.1 %collective-permute-start.6 = (f32[4,2,16,512]{3,2,1,0:T(8,128)S(1)}, f32[4,2,16,512]{3,2,1,0:T(8,128)S(1)}, u32[]{:S(2)}, u32[]{:S(2)}) collective-permute-start(f32[4,2,16,512]{3,2,1,0:T(8,128)S(1)} %get-tuple-element.12), channel_id=1, source_target_pairs={{0,24},{1,7},{2,26},{3,1},{4,28},{5,3},{6,30},{7,5},{8,0},{9,15},{... | collective-permute-start | bytes 786440 | tf_op jit(solution)/shard_map/ppermute | solution.py:40
  88.5 1.2 collective-permute-start.4
  89.8 5.5 %collective-permute-done.6 = f32[4,2,16,512]{3,2,1,0:T(8,128)S(1)} collective-permute-done((f32[4,2,16,512]{3,2,1,0:T(8,128)S(1)}, f32[4,2,16,512]{3,2,1,0:T(8,128)S(1)}, u32[]{:S(2)}, u32[]{:S(2)}) %collective-permute-start.6) | collective-permute-done | bytes 262176 | tf_op jit(solution)/shard_map/ppermute | solution.py:40
  95.2 1.3 collective-permute-done.5
  96.5 2.4 %collective-permute-done.4 = f32[4,2,16,512]{3,2,1,0:T(8,128)S(1)} collective-permute-done((f32[4,2,16,512]{3,2,1,0:T(8,128)S(1)}, f32[4,2,16,512]{3,2,1,0:T(8,128)S(1)}, u32[]{:S(2)}, u32[]{:S(2)}) %collective-permute-start.4) | collective-permute-done | bytes 262176 | tf_op jit(solution)/shard_map/ppermute | solution.py:40
  99.0 3.1 %collective-permute-start.9 = (f32[2,16,512]{2,1,0:T(8,128)S(1)}, f32[2,16,512]{2,1,0:T(8,128)S(1)}, u32[]{:S(2)}, u32[]{:S(2)}) collective-permute-start(f32[2,16,512]{2,1,0:T(8,128)S(1)} %get-tuple-element.15), channel_id=1, source_target_pairs={{0,96},{1,97},{2,98},{3,99},{4,100},{5,101},{6,102},{7,103},{8,104... | collective-permute-start | bytes 196616 | tf_op jit(solution)/shard_map/ppermute | solution.py:40
  102.1 0.6 collective-permute-start.8
  102.7 1.0 collective-permute-start.7
  103.7 1.3 convolution_bitcast_fusion
  105.1 2.8 %collective-permute-done.8 = f32[2,16,512]{2,1,0:T(8,128)S(1)} collective-permute-done((f32[2,16,512]{2,1,0:T(8,128)S(1)}, f32[2,16,512]{2,1,0:T(8,128)S(1)}, u32[]{:S(2)}, u32[]{:S(2)}) %collective-permute-start.8) | collective-permute-done | bytes 65568 | tf_op jit(solution)/shard_map/ppermute | solution.py:40
  107.9 0.7 collective-permute-done.7
  108.6 1.5 fusion.5
  110.2 1.2 collective-permute-done.10
  111.5 3.9 %collective-permute-done.11 = f32[72,16]{1,0:T(8,128)S(1)} collective-permute-done((f32[72,16]{1,0:T(8,128)S(1)}, f32[72,16]{1,0:T(8,128)S(1)}, u32[]{:S(2)}, u32[]{:S(2)}) %collective-permute-start.11) | collective-permute-done | bytes 4640 | tf_op jit(solution)/shard_map/ppermute | solution.py:33
  115.4 0.8 collective-permute-start.12
  116.2 4.7 %collective-permute-done.12 = f32[72,16]{1,0:T(8,128)S(1)} collective-permute-done((f32[72,16]{1,0:T(8,128)S(1)}, f32[72,16]{1,0:T(8,128)S(1)}, u32[]{:S(2)}, u32[]{:S(2)}) %collective-permute-start.12) | collective-permute-done | bytes 4640 | tf_op jit(solution)/shard_map/ppermute | solution.py:33
  120.9 3.9 %collective-permute-done.13 = f32[72,16]{1,0:T(8,128)S(1)} collective-permute-done((f32[72,16]{1,0:T(8,128)S(1)}, f32[72,16]{1,0:T(8,128)S(1)}, u32[]{:S(2)}, u32[]{:S(2)}) %collective-permute-start.13) | collective-permute-done | bytes 4640 | tf_op jit(solution)/shard_map/ppermute | solution.py:33
  124.9 0.3 collective-permute-start.14
  125.2 5.1 %collective-permute-done.14 = f32[72,16]{1,0:T(8,128)S(1)} collective-permute-done((f32[72,16]{1,0:T(8,128)S(1)}, f32[72,16]{1,0:T(8,128)S(1)}, u32[]{:S(2)}, u32[]{:S(2)}) %collective-permute-start.14) | collective-permute-done | bytes 4640 | tf_op jit(solution)/shard_map/ppermute | solution.py:33
  130.4 3.9 %collective-permute-done.15 = f32[72,16]{1,0:T(8,128)S(1)} collective-permute-done((f32[72,16]{1,0:T(8,128)S(1)}, f32[72,16]{1,0:T(8,128)S(1)}, u32[]{:S(2)}, u32[]{:S(2)}) %collective-permute-start.15) | collective-permute-done | bytes 4640 | tf_op jit(solution)/shard_map/ppermute | solution.py:33
  134.3 1.3 collective-permute-start.16
  135.6 4.1 %collective-permute-done.16 = f32[72,16]{1,0:T(8,128)S(1)} collective-permute-done((f32[72,16]{1,0:T(8,128)S(1)}, f32[72,16]{1,0:T(8,128)S(1)}, u32[]{:S(2)}, u32[]{:S(2)}) %collective-permute-start.16) | collective-permute-done | bytes 4640 | tf_op jit(solution)/shard_map/ppermute | solution.py:33
  139.9 0.8 fusion.3
  140.9 1.1 collective-permute-done.17
  142.2 3.5 %collective-permute-done.18 = f32[16]{0:T(128)S(1)} collective-permute-done((f32[16]{0:T(128)S(1)}, f32[16]{0:T(128)S(1)}, u32[]{:S(2)}, u32[]{:S(2)}) %collective-permute-start.18) | collective-permute-done | bytes 96 | tf_op jit(solution)/shard_map/ppermute | solution.py:33
  145.7 0.8 collective-permute-start.19
  146.5 4.3 %collective-permute-done.19 = f32[16]{0:T(128)S(1)} collective-permute-done((f32[16]{0:T(128)S(1)}, f32[16]{0:T(128)S(1)}, u32[]{:S(2)}, u32[]{:S(2)}) %collective-permute-start.19) | collective-permute-done | bytes 96 | tf_op jit(solution)/shard_map/ppermute | solution.py:33
  150.9 3.5 %collective-permute-done.20 = f32[16]{0:T(128)S(1)} collective-permute-done((f32[16]{0:T(128)S(1)}, f32[16]{0:T(128)S(1)}, u32[]{:S(2)}, u32[]{:S(2)}) %collective-permute-start.20) | collective-permute-done | bytes 96 | tf_op jit(solution)/shard_map/ppermute | solution.py:33
  154.6 4.7 %collective-permute-done.21 = f32[16]{0:T(128)S(1)} collective-permute-done((f32[16]{0:T(128)S(1)}, f32[16]{0:T(128)S(1)}, u32[]{:S(2)}, u32[]{:S(2)}) %collective-permute-start.21) | collective-permute-done | bytes 96 | tf_op jit(solution)/shard_map/ppermute | solution.py:33
  159.4 3.6 %collective-permute-done.22 = f32[16]{0:T(128)S(1)} collective-permute-done((f32[16]{0:T(128)S(1)}, f32[16]{0:T(128)S(1)}, u32[]{:S(2)}, u32[]{:S(2)}) %collective-permute-start.22) | collective-permute-done | bytes 96 | tf_op jit(solution)/shard_map/ppermute | solution.py:33
  163.0 1.3 collective-permute-start.23
  164.3 3.8 %collective-permute-done.23 = f32[16]{0:T(128)S(1)} collective-permute-done((f32[16]{0:T(128)S(1)}, f32[16]{0:T(128)S(1)}, u32[]{:S(2)}, u32[]{:S(2)}) %collective-permute-start.23) | collective-permute-done | bytes 96 | tf_op jit(solution)/shard_map/ppermute | solution.py:33
  168.0 0.7 broadcast_divide_fusion
  168.8 0.6 pad_maximum_fusion.1
  (45 shorter events, 1.4 us)
Async XLA Ops:
  2.3 2.0 %copy-start = (bf16[112,32,512]{2,1,0:T(8,128)(2,1)S(1)}, bf16[112,32,512]{2,1,0:T(8,128)(2,1)}, u32[]{:S(2)}) copy-start(bf16[112,32,512]{2,1,0:T(8,128)(2,1)} %u_ref.1) | copy-start | bytes 11010052
  4.3 0.7 copy-start.1
  42.1 7.4 %collective-permute-start = (f32[4,4,4,2,16,512]{5,4,3,2,1,0:T(8,128)}, f32[4,4,4,2,16,512]{5,4,3,2,1,0:T(8,128)S(1)}, u32[]{:S(2)}, u32[]{:S(2)}) collective-permute-start(f32[4,4,4,2,16,512]{5,4,3,2,1,0:T(8,128)} %bitcast.112), channel_id=1, source_target_pairs={{0,1},{1,0},{2,3},{3,2},{4,5},{5,4},{6,7},{7,6},{8,9},{9,8},{10,11... | collective-permute-start | bytes 12582920 | tf_op jit(solution)/shard_map/ppermute | solution.py:45
  53.3 26.5 %collective-permute-start.3 = (f32[4,4,2,16,512]{4,3,2,1,0:T(8,128)S(1)}, f32[4,4,2,16,512]{4,3,2,1,0:T(8,128)S(1)}, u32[]{:S(2)}, u32[]{:S(2)}) collective-permute-start(f32[4,4,2,16,512]{4,3,2,1,0:T(8,128)S(1)} %get-tuple-element.9), channel_id=1, source_target_pairs={{0,6},{1,25},{2,0},{3,27},{4,2},{5,29},{6,4},{7,31},{8,14},{9,1},{... | collective-permute-start | bytes 3145736 | tf_op jit(solution)/shard_map/ppermute | solution.py:40
  56.2 23.6 %collective-permute-start.2 = (f32[4,4,2,16,512]{4,3,2,1,0:T(8,128)S(1)}, f32[4,4,2,16,512]{4,3,2,1,0:T(8,128)S(1)}, u32[]{:S(2)}, u32[]{:S(2)}) collective-permute-start(f32[4,4,2,16,512]{4,3,2,1,0:T(8,128)S(1)} %get-tuple-element.10), channel_id=1, source_target_pairs={{0,4},{1,17},{2,6},{3,19},{4,0},{5,21},{6,2},{7,23},{8,12},{9,25},... | collective-permute-start | bytes 3145736 | tf_op jit(solution)/shard_map/ppermute | solution.py:40
  57.0 46.7 %copy-start.2 = (f32[8,2,16,512]{3,2,1,0:T(8,128)S(1)}, f32[8,2,16,512]{3,2,1,0:T(8,128)}, u32[]{:S(2)}) copy-start(f32[8,2,16,512]{3,2,1,0:T(8,128)} %param.8) | copy-start | bytes 1572868
  57.0 51.6 %copy-start.3 = (f32[2,512]{1,0:T(2,128)S(1)}, f32[2,512]{1,0:T(2,128)}, u32[]{:S(2)}) copy-start(f32[2,512]{1,0:T(2,128)} %param.9) | copy-start | bytes 12292
  57.0 26.7 %collective-permute-start.1 = (f32[4,4,2,16,512]{4,3,2,1,0:T(8,128)S(1)}, f32[4,4,2,16,512]{4,3,2,1,0:T(8,128)S(1)}, u32[]{:S(2)}, u32[]{:S(2)}) collective-permute-start(f32[4,4,2,16,512]{4,3,2,1,0:T(8,128)S(1)} %get-tuple-element.8), channel_id=1, source_target_pairs={{0,2},{1,9},{2,4},{3,11},{4,6},{5,13},{6,0},{7,15},{8,10},{9,17},{... | collective-permute-start | bytes 3145736 | tf_op jit(solution)/shard_map/ppermute | solution.py:40
  84.4 10.8 %collective-permute-start.6 = (f32[4,2,16,512]{3,2,1,0:T(8,128)S(1)}, f32[4,2,16,512]{3,2,1,0:T(8,128)S(1)}, u32[]{:S(2)}, u32[]{:S(2)}) collective-permute-start(f32[4,2,16,512]{3,2,1,0:T(8,128)S(1)} %get-tuple-element.12), channel_id=1, source_target_pairs={{0,24},{1,7},{2,26},{3,1},{4,28},{5,3},{6,30},{7,5},{8,0},{9,15},{... | collective-permute-start | bytes 786440 | tf_op jit(solution)/shard_map/ppermute | solution.py:40
  88.5 8.0 %collective-permute-start.5 = (f32[4,2,16,512]{3,2,1,0:T(8,128)S(1)}, f32[4,2,16,512]{3,2,1,0:T(8,128)S(1)}, u32[]{:S(2)}, u32[]{:S(2)}) collective-permute-start(f32[4,2,16,512]{3,2,1,0:T(8,128)S(1)} %get-tuple-element.13), channel_id=1, source_target_pairs={{0,16},{1,5},{2,18},{3,7},{4,20},{5,1},{6,22},{7,3},{8,24},{9,13},... | collective-permute-start | bytes 786440 | tf_op jit(solution)/shard_map/ppermute | solution.py:40
  88.5 10.4 %collective-permute-start.4 = (f32[4,2,16,512]{3,2,1,0:T(8,128)S(1)}, f32[4,2,16,512]{3,2,1,0:T(8,128)S(1)}, u32[]{:S(2)}, u32[]{:S(2)}) collective-permute-start(f32[4,2,16,512]{3,2,1,0:T(8,128)S(1)} %get-tuple-element.11), channel_id=1, source_target_pairs={{0,8},{1,3},{2,10},{3,5},{4,12},{5,7},{6,14},{7,1},{8,16},{9,11},{... | collective-permute-start | bytes 786440 | tf_op jit(solution)/shard_map/ppermute | solution.py:40
  99.0 6.1 %collective-permute-start.9 = (f32[2,16,512]{2,1,0:T(8,128)S(1)}, f32[2,16,512]{2,1,0:T(8,128)S(1)}, u32[]{:S(2)}, u32[]{:S(2)}) collective-permute-start(f32[2,16,512]{2,1,0:T(8,128)S(1)} %get-tuple-element.15), channel_id=1, source_target_pairs={{0,96},{1,97},{2,98},{3,99},{4,100},{5,101},{6,102},{7,103},{8,104... | collective-permute-start | bytes 196616 | tf_op jit(solution)/shard_map/ppermute | solution.py:40
  102.1 5.8 %collective-permute-start.8 = (f32[2,16,512]{2,1,0:T(8,128)S(1)}, f32[2,16,512]{2,1,0:T(8,128)S(1)}, u32[]{:S(2)}, u32[]{:S(2)}) collective-permute-start(f32[2,16,512]{2,1,0:T(8,128)S(1)} %get-tuple-element.16), channel_id=1, source_target_pairs={{0,64},{1,65},{2,66},{3,67},{4,68},{5,69},{6,70},{7,71},{8,72},{9,... | collective-permute-start | bytes 196616 | tf_op jit(solution)/shard_map/ppermute | solution.py:40
  102.7 5.8 %collective-permute-start.7 = (f32[2,16,512]{2,1,0:T(8,128)S(1)}, f32[2,16,512]{2,1,0:T(8,128)S(1)}, u32[]{:S(2)}, u32[]{:S(2)}) collective-permute-start(f32[2,16,512]{2,1,0:T(8,128)S(1)} %get-tuple-element.14), channel_id=1, source_target_pairs={{0,32},{1,33},{2,34},{3,35},{4,36},{5,37},{6,38},{7,39},{8,40},{9,... | collective-permute-start | bytes 196616 | tf_op jit(solution)/shard_map/ppermute | solution.py:40
  110.1 1.2 collective-permute-start.10
  111.4 4.0 %collective-permute-start.11 = (f32[72,16]{1,0:T(8,128)S(1)}, f32[72,16]{1,0:T(8,128)S(1)}, u32[]{:S(2)}, u32[]{:S(2)}) collective-permute-start(f32[72,16]{1,0:T(8,128)S(1)} %fusion.34), channel_id=1, source_target_pairs={{0,2},{1,3},{2,0},{3,1},{4,6},{5,7},{6,4},{7,5},{8,10},{9,11},{10,... | collective-permute-start | bytes 13832 | tf_op jit(solution)/shard_map/ppermute | solution.py:33
  115.4 5.5 %collective-permute-start.12 = (f32[72,16]{1,0:T(8,128)S(1)}, f32[72,16]{1,0:T(8,128)S(1)}, u32[]{:S(2)}, u32[]{:S(2)}) collective-permute-start(f32[72,16]{1,0:T(8,128)S(1)} %add.186), channel_id=1, source_target_pairs={{0,4},{1,5},{2,6},{3,7},{4,0},{5,1},{6,2},{7,3},{8,12},{9,13},{10,... | collective-permute-start | bytes 13832 | tf_op jit(solution)/shard_map/ppermute | solution.py:33
  120.9 4.0 %collective-permute-start.13 = (f32[72,16]{1,0:T(8,128)S(1)}, f32[72,16]{1,0:T(8,128)S(1)}, u32[]{:S(2)}, u32[]{:S(2)}) collective-permute-start(f32[72,16]{1,0:T(8,128)S(1)} %add.187), channel_id=1, source_target_pairs={{0,8},{1,9},{2,10},{3,11},{4,12},{5,13},{6,14},{7,15},{8,0},{9,1},... | collective-permute-start | bytes 13832 | tf_op jit(solution)/shard_map/ppermute | solution.py:33
  124.9 5.5 %collective-permute-start.14 = (f32[72,16]{1,0:T(8,128)S(1)}, f32[72,16]{1,0:T(8,128)S(1)}, u32[]{:S(2)}, u32[]{:S(2)}) collective-permute-start(f32[72,16]{1,0:T(8,128)S(1)} %add.188), channel_id=1, source_target_pairs={{0,16},{1,17},{2,18},{3,19},{4,20},{5,21},{6,22},{7,23},{8,24},{9,... | collective-permute-start | bytes 13832 | tf_op jit(solution)/shard_map/ppermute | solution.py:33
  130.3 4.0 %collective-permute-start.15 = (f32[72,16]{1,0:T(8,128)S(1)}, f32[72,16]{1,0:T(8,128)S(1)}, u32[]{:S(2)}, u32[]{:S(2)}) collective-permute-start(f32[72,16]{1,0:T(8,128)S(1)} %add.189), channel_id=1, source_target_pairs={{0,32},{1,33},{2,34},{3,35},{4,36},{5,37},{6,38},{7,39},{8,40},{9,... | collective-permute-start | bytes 13832 | tf_op jit(solution)/shard_map/ppermute | solution.py:33
  134.3 5.5 %collective-permute-start.16 = (f32[72,16]{1,0:T(8,128)S(1)}, f32[72,16]{1,0:T(8,128)S(1)}, u32[]{:S(2)}, u32[]{:S(2)}) collective-permute-start(f32[72,16]{1,0:T(8,128)S(1)} %add.190), channel_id=1, source_target_pairs={{0,64},{1,65},{2,66},{3,67},{4,68},{5,69},{6,70},{7,71},{8,72},{9,... | collective-permute-start | bytes 13832 | tf_op jit(solution)/shard_map/ppermute | solution.py:33
  140.9 1.2 collective-permute-start.17
  142.1 3.6 %collective-permute-start.18 = (f32[16]{0:T(128)S(1)}, f32[16]{0:T(128)S(1)}, u32[]{:S(2)}, u32[]{:S(2)}) collective-permute-start(f32[16]{0:T(128)S(1)} %add.193), channel_id=1, source_target_pairs={{0,2},{1,3},{2,0},{3,1},{4,6},{5,7},{6,4},{7,5},{8,10},{9,11},{10,... | collective-permute-start | bytes 200 | tf_op jit(solution)/shard_map/ppermute | solution.py:33
  145.7 5.1 %collective-permute-start.19 = (f32[16]{0:T(128)S(1)}, f32[16]{0:T(128)S(1)}, u32[]{:S(2)}, u32[]{:S(2)}) collective-permute-start(f32[16]{0:T(128)S(1)} %add.194), channel_id=1, source_target_pairs={{0,4},{1,5},{2,6},{3,7},{4,0},{5,1},{6,2},{7,3},{8,12},{9,13},{10,... | collective-permute-start | bytes 200 | tf_op jit(solution)/shard_map/ppermute | solution.py:33
  150.7 3.6 %collective-permute-start.20 = (f32[16]{0:T(128)S(1)}, f32[16]{0:T(128)S(1)}, u32[]{:S(2)}, u32[]{:S(2)}) collective-permute-start(f32[16]{0:T(128)S(1)} %add.195), channel_id=1, source_target_pairs={{0,8},{1,9},{2,10},{3,11},{4,12},{5,13},{6,14},{7,15},{8,0},{9,1},... | collective-permute-start | bytes 200 | tf_op jit(solution)/shard_map/ppermute | solution.py:33
  154.3 5.1 %collective-permute-start.21 = (f32[16]{0:T(128)S(1)}, f32[16]{0:T(128)S(1)}, u32[]{:S(2)}, u32[]{:S(2)}) collective-permute-start(f32[16]{0:T(128)S(1)} %add.196), channel_id=1, source_target_pairs={{0,16},{1,17},{2,18},{3,19},{4,20},{5,21},{6,22},{7,23},{8,24},{9,... | collective-permute-start | bytes 200 | tf_op jit(solution)/shard_map/ppermute | solution.py:33
  159.4 3.6 %collective-permute-start.22 = (f32[16]{0:T(128)S(1)}, f32[16]{0:T(128)S(1)}, u32[]{:S(2)}, u32[]{:S(2)}) collective-permute-start(f32[16]{0:T(128)S(1)} %add.197), channel_id=1, source_target_pairs={{0,32},{1,33},{2,34},{3,35},{4,36},{5,37},{6,38},{7,39},{8,40},{9,... | collective-permute-start | bytes 200 | tf_op jit(solution)/shard_map/ppermute | solution.py:33
  163.0 5.1 %collective-permute-start.23 = (f32[16]{0:T(128)S(1)}, f32[16]{0:T(128)S(1)}, u32[]{:S(2)}, u32[]{:S(2)}) collective-permute-start(f32[16]{0:T(128)S(1)} %add.198), channel_id=1, source_target_pairs={{0,64},{1,65},{2,66},{3,67},{4,68},{5,69},{6,70},{7,71},{8,72},{9,... | collective-permute-start | bytes 200 | tf_op jit(solution)/shard_map/ppermute | solution.py:33

commit v5 on v4

--- a/solution.py
+++ b/solution.py
@@ -50,11 +50,12 @@
 
 STEPS = 8
 
-def block_kernel(slot_ref, row_ref, vec_ref, near_ref, u_ref, v_ref, keep_ref, send_ref):
+
+def accumulate_kernel(slot_ref, near_ref, far_ref, keep_ref, send_ref):
     i = pl.program_id(0)
     half = keep_ref.shape[0]
     near_step = near_ref.shape[0]
-    far_step = u_ref.shape[0]
+    far_step = far_ref.shape[0]
     near_total = near_step * pl.num_programs(0)
 
     @pl.when(i == 0)
@@ -74,45 +75,37 @@
             send_ref[s - half] += part
 
     for j in range(near_step):
-        g = i * near_step + j
-        a = vec_ref[row_ref[g]]
-        add(g, jnp.dot(a, near_ref[j], preferred_element_type=jnp.float32))
+        add(i * near_step + j, near_ref[j])
     for j in range(far_step):
-        g = near_total + i * far_step + j
-        a = vec_ref[row_ref[g]]
-        coeff = lax.dot_general(a, u_ref[j], (((1,), (1,)), ((), ())), preferred_element_type=jnp.float32)
-        add(g, jnp.dot(coeff.astype(jnp.bfloat16), v_ref[j], preferred_element_type=jnp.float32))
+        add(near_total + i * far_step + j, far_ref[j])
 
 
-def block_products(slot, rows, vec_low, near_blocks, far_u, far_v, half):
-    near_count, size, _ = near_blocks.shape
-    far_count, rank, _ = far_u.shape
-    sources = vec_low.shape[1]
+def accumulate(slot, near_part, far_part, half):
+    near_count, sources, size = near_part.shape
+    far_count = far_part.shape[0]
     near_step = near_count // STEPS
     far_step = far_count // STEPS
     out = jax.ShapeDtypeStruct((half, sources, size), jnp.float32)
     grid_spec = pltpu.PrefetchScalarGridSpec(
-        num_scalar_prefetch=2,
+        num_scalar_prefetch=1,
         grid=(STEPS,),
         in_specs=[
-            pl.BlockSpec(vec_low.shape, lambda i, s, r: (0, 0, 0)),
-            pl.BlockSpec((near_step, size, size), lambda i, s, r: (i, 0, 0)),
-            pl.BlockSpec((far_step, rank, size), lambda i, s, r: (i, 0, 0)),
-            pl.BlockSpec((far_step, rank, size), lambda i, s, r: (i, 0, 0)),
+            pl.BlockSpec((near_step, sources, size), lambda i, s: (i, 0, 0)),
+            pl.BlockSpec((far_step, sources, size), lambda i, s: (i, 0, 0)),
         ],
         out_specs=[
-            pl.BlockSpec((half, sources, size), lambda i, s, r: (0, 0, 0)),
-            pl.BlockSpec((half, sources, size), lambda i, s, r: (0, 0, 0)),
+            pl.BlockSpec((half, sources, size), lambda i, s: (0, 0, 0)),
+            pl.BlockSpec((half, sources, size), lambda i, s: (0, 0, 0)),
         ],
     )
     return pl.pallas_call(
-        block_kernel,
+        accumulate_kernel,
         grid_spec=grid_spec,
         out_shape=[out, out],
         compiler_params=pltpu.CompilerParams(
             dimension_semantics=("arbitrary",), vmem_limit_bytes=48 * 1024 * 1024
         ),
-    )(slot, rows, vec_low, near_blocks, far_u, far_v)
+    )(slot, near_part, far_part)
 
 
 def on_device(basis, diagonal, near_blocks, far_u, far_v, block_row, block_dest, block_col):
@@ -126,13 +119,21 @@
     me = lax.axis_index(AXES)
     vector = basis[basis_count - 1]
     vec_low = vector.astype(jnp.bfloat16)
+    picked = vec_low[block_row]
+    near_part = jnp.einsum(
+        "snc,scd->snd", picked[:near_count], near_blocks, preferred_element_type=jnp.float32
+    )
+    coeff = jnp.einsum(
+        "snc,skc->snk", picked[near_count:], far_u, preferred_element_type=jnp.float32
+    ).astype(jnp.bfloat16)
+    far_part = jnp.einsum("snk,skc->snc", coeff, far_v, preferred_element_type=jnp.float32)
     dest = block_dest[:, 0]
     rel = {a: (coord(dest, a) - coord(me, a)) % SIZES[a] for a in SIZES}
     to_core = coord(dest, "c")
     order = jnp.where(to_core == 0, rel["x"] * 4 + rel["z"], rel["z"] * 4 + rel["x"])
     slot = ((rel["c"] * 16 + order) * 4 + rel["y"]) * clusters + block_col
     spots = devices * clusters
-    keep, send = block_products(slot, block_row, vec_low, near_blocks, far_u, far_v, spots // 2)
+    keep, send = accumulate(slot, near_part, far_part, spots // 2)
     shape = (4, 4, 4, clusters, sources, cluster_size)
     summed = reduce_to_owner(keep.reshape(shape), send.reshape(shape))
     image = diagonal[:, None, :] * vector + summed

time: 170 us -> 145 us (0.85)
  Pallas kernels: 37.2 us -> 6.42 us
  matrix products: 3.6 us -> 12.1 us
  local copies, waits for them, and re-layouts: 4.43 us -> 2.2 us
    pallas_call x1, Pallas kernels: 37.2 us -> 6.42 us  [accumulate(): pl.pallas_call(accumulate_kernel, grid_spec=grid_spec, out_shape=[out, ou...]
    dot_general x0 -> x3, matrix products: none -> 8.47 us  [the longest x1 4.73 us: on_device(): jnp.einsum('snc,scd->snd', picked[:near_count], near_blocks, preferred_el...]
    unnamed x8 -> x10, local copies, waits for them, and re-layouts: 2.7 us -> 0.03 us
where the time goes in v5:
time: 145 us
  waiting for transfers between devices  97.2 us (67%)
  starting transfers between devices  20 us (14%)
  matrix products  12.1 us (8%)
  Pallas kernels  6.42 us (4%)
  other arithmetic  6.07 us (4%)
  local copies, waits for them, and re-layouts  2.2 us (2%)
    ppermute x14, waiting for transfers between devices, all_sum(): v = v + lax.ppermute(v, AXES, flipped(bit))  51.4 us
    ppermute x9, waiting for transfers between devices, spread(): acc = acc + lax.ppermute(pieces[k], AXES, moved(axis, k, other))  38.4 us
    ppermute x9, starting transfers between devices, spread(): acc = acc + lax.ppermute(pieces[k], AXES, moved(axis, k, other))  14.7 us
    ppermute x1, waiting for transfers between devices, reduce_to_owner(): d = keep + lax.ppermute(send, AXES, moved('c', 1))  7.37 us
    pallas_call x1, Pallas kernels, accumulate(): pl.pallas_call(accumulate_kernel, grid_spec=grid_spec, out_shape=[out, ou...  6.42 us
    ppermute x14, starting transfers between devices, all_sum(): v = v + lax.ppermute(v, AXES, flipped(bit))  5.31 us
    dot_general x1, matrix products, on_device(): jnp.einsum('snc,scd->snd', picked[:near_count], near_blocks, preferred_el...  4.73 us
    add x1, other arithmetic, reduce_to_owner(): d = keep + lax.ppermute(send, AXES, moved('c', 1))  3.2 us
  transfers between devices with their start and end apart: 24, of which 22 were waited for; matrix products, arithmetic and copies ran while one was open for 1% of the time, Pallas kernels for 0%

profile of v5, /device:TPU:0, one launch (start us, length us, event | category | flops | bytes accessed | tf_op | source)
XLA Modules:
  0.0 144.9 jit_solution(4821963234145928225)
XLA Ops:
  0.7 0.8 bitcast_convert_fusion
  1.6 0.7 compare_select_fusion
  2.2 0.7 gather_fusion
  2.9 4.7 %fusion.36.near_ref = f32[16,16,512]{2,1,0:T(8,128)S(1)} fusion(bf16[128,16,512]{2,1,0:T(8,128)(2,1)S(1)} %gather_fusion, bf16[16,512,512]{2,1,0:T(8,128)(2,1)} %param.10), kind=kOutput, calls=%fused_computation.100 | convolution fusion | flops 134217728 | bytes 11010048 | tf_op jit(solution)/shard_map/snc,scd->snd/dot_general | solution.py:123
  7.6 1.1 convolution_convert_fusion
  8.8 2.7 %fusion.35.far_ref = f32[112,16,512]{2,1,0:T(8,128)S(1)} fusion(bf16[112,16,32]{2,1,0:T(8,128)(2,1)S(1)} %convolution_convert_fusion, bf16[112,32,512]{2,1,0:T(8,128)(2,1)} %param.12), kind=kOutput, calls=%fused_computation.99 | convolution fusion | flops 58720256 | bytes 7454720 | tf_op jit(solution)/shard_map/snk,skc->snc/dot_general | solution.py:129
  11.5 6.4 %shard_map.95 = (f32[128,16,512]{2,1,0:T(8,128)}, f32[128,16,512]{2,1,0:T(8,128)}) custom-call(s32[128]{0:T(128)S(1)} %multiply_add_fusion.slot_ref, f32[16,16,512]{2,1,0:T(8,128)S(1)} %fusion.36.near_ref, f32[112,16,512]{2,1,0:T(8,128)S(1)} %fusion.35.far_ref), custom_call_target="tpu_custom_call" | custom-call | tf_op jit(solution)/shard_map/pallas_call | solution.py:101
  17.9 7.4 %collective-permute-done = f32[4,4,4,2,16,512]{5,4,3,2,1,0:T(8,128)S(1)} collective-permute-done((f32[4,4,4,2,16,512]{5,4,3,2,1,0:T(8,128)}, f32[4,4,4,2,16,512]{5,4,3,2,1,0:T(8,128)S(1)}, u32[]{:S(2)}, u32[]{:S(2)}) %collective-permute-start) | collective-permute-done | bytes 4194336 | tf_op jit(solution)/shard_map/ppermute | solution.py:45
  25.3 3.2 %add.178 = f32[4,4,4,2,16,512]{5,4,3,2,1,0:T(8,128)S(1)} add(f32[4,4,4,2,16,512]{5,4,3,2,1,0:T(8,128)} %bitcast.110, f32[4,4,4,2,16,512]{5,4,3,2,1,0:T(8,128)S(1)} %collective-permute-done) | non-fusion elementwise | flops 1048576 | bytes 12582912 | tf_op jit(solution)/shard_map/add | solution.py:45
  28.8 2.9 %collective-permute-start.3 = (f32[4,4,2,16,512]{4,3,2,1,0:T(8,128)S(1)}, f32[4,4,2,16,512]{4,3,2,1,0:T(8,128)S(1)}, u32[]{:S(2)}, u32[]{:S(2)}) collective-permute-start(f32[4,4,2,16,512]{4,3,2,1,0:T(8,128)S(1)} %get-tuple-element.9), channel_id=1, source_target_pairs={{0,6},{1,25},{2,0},{3,27},{4,2},{5,29},{6,4},{7,31},{8,14},{9,1},{... | collective-permute-start | bytes 3145736 | tf_op jit(solution)/shard_map/ppermute | solution.py:40
  31.8 0.8 collective-permute-start.2
  32.6 0.9 collective-permute-start.1
  33.5 21.9 %collective-permute-done.3 = f32[4,4,2,16,512]{4,3,2,1,0:T(8,128)S(1)} collective-permute-done((f32[4,4,2,16,512]{4,3,2,1,0:T(8,128)S(1)}, f32[4,4,2,16,512]{4,3,2,1,0:T(8,128)S(1)}, u32[]{:S(2)}, u32[]{:S(2)}) %collective-permute-start.3) | collective-permute-done | bytes 1048608 | tf_op jit(solution)/shard_map/ppermute | solution.py:40
  55.3 4.0 %collective-permute-done.1 = f32[4,4,2,16,512]{4,3,2,1,0:T(8,128)S(1)} collective-permute-done((f32[4,4,2,16,512]{4,3,2,1,0:T(8,128)S(1)}, f32[4,4,2,16,512]{4,3,2,1,0:T(8,128)S(1)}, u32[]{:S(2)}, u32[]{:S(2)}) %collective-permute-start.1) | collective-permute-done | bytes 1048608 | tf_op jit(solution)/shard_map/ppermute | solution.py:40
  59.3 0.5 fusion.2
  59.9 4.1 %collective-permute-start.6 = (f32[4,2,16,512]{3,2,1,0:T(8,128)S(1)}, f32[4,2,16,512]{3,2,1,0:T(8,128)S(1)}, u32[]{:S(2)}, u32[]{:S(2)}) collective-permute-start(f32[4,2,16,512]{3,2,1,0:T(8,128)S(1)} %get-tuple-element.12), channel_id=1, source_target_pairs={{0,24},{1,7},{2,26},{3,1},{4,28},{5,3},{6,30},{7,5},{8,0},{9,15},{... | collective-permute-start | bytes 786440 | tf_op jit(solution)/shard_map/ppermute | solution.py:40
  64.0 1.3 collective-permute-start.4
  65.3 5.4 %collective-permute-done.6 = f32[4,2,16,512]{3,2,1,0:T(8,128)S(1)} collective-permute-done((f32[4,2,16,512]{3,2,1,0:T(8,128)S(1)}, f32[4,2,16,512]{3,2,1,0:T(8,128)S(1)}, u32[]{:S(2)}, u32[]{:S(2)}) %collective-permute-start.6) | collective-permute-done | bytes 262176 | tf_op jit(solution)/shard_map/ppermute | solution.py:40
  70.7 1.3 collective-permute-done.5
  72.0 2.4 %collective-permute-done.4 = f32[4,2,16,512]{3,2,1,0:T(8,128)S(1)} collective-permute-done((f32[4,2,16,512]{3,2,1,0:T(8,128)S(1)}, f32[4,2,16,512]{3,2,1,0:T(8,128)S(1)}, u32[]{:S(2)}, u32[]{:S(2)}) %collective-permute-start.4) | collective-permute-done | bytes 262176 | tf_op jit(solution)/shard_map/ppermute | solution.py:40
  74.5 3.1 %collective-permute-start.9 = (f32[2,16,512]{2,1,0:T(8,128)S(1)}, f32[2,16,512]{2,1,0:T(8,128)S(1)}, u32[]{:S(2)}, u32[]{:S(2)}) collective-permute-start(f32[2,16,512]{2,1,0:T(8,128)S(1)} %get-tuple-element.15), channel_id=1, source_target_pairs={{0,96},{1,97},{2,98},{3,99},{4,100},{5,101},{6,102},{7,103},{8,104... | collective-permute-start | bytes 196616 | tf_op jit(solution)/shard_map/ppermute | solution.py:40
  77.6 0.6 collective-permute-start.8
  78.2 1.0 collective-permute-start.7
  79.2 1.3 convolution_bitcast_fusion
  80.6 2.8 %collective-permute-done.8 = f32[2,16,512]{2,1,0:T(8,128)S(1)} collective-permute-done((f32[2,16,512]{2,1,0:T(8,128)S(1)}, f32[2,16,512]{2,1,0:T(8,128)S(1)}, u32[]{:S(2)}, u32[]{:S(2)}) %collective-permute-start.8) | collective-permute-done | bytes 65568 | tf_op jit(solution)/shard_map/ppermute | solution.py:40
  83.4 0.7 collective-permute-done.7
  84.1 1.5 %fusion.5 = f32[16,1,8,1]{2,1,3,0:T(1,128)S(1)} fusion(f32[8,2,16,512]{3,2,1,0:T(8,128)S(1)} %copy-done, f32[2,16,512,1]{2,1,0,3:T(8,128)S(1)} %bitcast.111), kind=kOutput, calls=%fused_computation.12 | convolution fusion | flops 1572864 | bytes 590336 | tf_op jit(solution)/shard_map/knjc,njc->kj/dot_general | solution.py:141
  85.7 1.2 collective-permute-done.10
  87.0 3.9 %collective-permute-done.11 = f32[72,16]{1,0:T(8,128)S(1)} collective-permute-done((f32[72,16]{1,0:T(8,128)S(1)}, f32[72,16]{1,0:T(8,128)S(1)}, u32[]{:S(2)}, u32[]{:S(2)}) %collective-permute-start.11) | collective-permute-done | bytes 4640 | tf_op jit(solution)/shard_map/ppermute | solution.py:33
  90.9 0.8 collective-permute-start.12
  91.7 4.7 %collective-permute-done.12 = f32[72,16]{1,0:T(8,128)S(1)} collective-permute-done((f32[72,16]{1,0:T(8,128)S(1)}, f32[72,16]{1,0:T(8,128)S(1)}, u32[]{:S(2)}, u32[]{:S(2)}) %collective-permute-start.12) | collective-permute-done | bytes 4640 | tf_op jit(solution)/shard_map/ppermute | solution.py:33
  96.4 3.9 %collective-permute-done.13 = f32[72,16]{1,0:T(8,128)S(1)} collective-permute-done((f32[72,16]{1,0:T(8,128)S(1)}, f32[72,16]{1,0:T(8,128)S(1)}, u32[]{:S(2)}, u32[]{:S(2)}) %collective-permute-start.13) | collective-permute-done | bytes 4640 | tf_op jit(solution)/shard_map/ppermute | solution.py:33
  100.7 5.1 %collective-permute-done.14 = f32[72,16]{1,0:T(8,128)S(1)} collective-permute-done((f32[72,16]{1,0:T(8,128)S(1)}, f32[72,16]{1,0:T(8,128)S(1)}, u32[]{:S(2)}, u32[]{:S(2)}) %collective-permute-start.14) | collective-permute-done | bytes 4640 | tf_op jit(solution)/shard_map/ppermute | solution.py:33
  105.9 3.9 %collective-permute-done.15 = f32[72,16]{1,0:T(8,128)S(1)} collective-permute-done((f32[72,16]{1,0:T(8,128)S(1)}, f32[72,16]{1,0:T(8,128)S(1)}, u32[]{:S(2)}, u32[]{:S(2)}) %collective-permute-start.15) | collective-permute-done | bytes 4640 | tf_op jit(solution)/shard_map/ppermute | solution.py:33
  109.8 1.3 collective-permute-start.16
  111.1 4.1 %collective-permute-done.16 = f32[72,16]{1,0:T(8,128)S(1)} collective-permute-done((f32[72,16]{1,0:T(8,128)S(1)}, f32[72,16]{1,0:T(8,128)S(1)}, u32[]{:S(2)}, u32[]{:S(2)}) %collective-permute-start.16) | collective-permute-done | bytes 4640 | tf_op jit(solution)/shard_map/ppermute | solution.py:33
  115.4 0.8 fusion.3
  116.4 1.1 collective-permute-done.17
  117.7 3.5 %collective-permute-done.18 = f32[16]{0:T(128)S(1)} collective-permute-done((f32[16]{0:T(128)S(1)}, f32[16]{0:T(128)S(1)}, u32[]{:S(2)}, u32[]{:S(2)}) %collective-permute-start.18) | collective-permute-done | bytes 96 | tf_op jit(solution)/shard_map/ppermute | solution.py:33
  121.2 0.8 collective-permute-start.19
  122.0 4.3 %collective-permute-done.19 = f32[16]{0:T(128)S(1)} collective-permute-done((f32[16]{0:T(128)S(1)}, f32[16]{0:T(128)S(1)}, u32[]{:S(2)}, u32[]{:S(2)}) %collective-permute-start.19) | collective-permute-done | bytes 96 | tf_op jit(solution)/shard_map/ppermute | solution.py:33
  126.4 3.5 %collective-permute-done.20 = f32[16]{0:T(128)S(1)} collective-permute-done((f32[16]{0:T(128)S(1)}, f32[16]{0:T(128)S(1)}, u32[]{:S(2)}, u32[]{:S(2)}) %collective-permute-start.20) | collective-permute-done | bytes 96 | tf_op jit(solution)/shard_map/ppermute | solution.py:33
  130.1 4.7 %collective-permute-done.21 = f32[16]{0:T(128)S(1)} collective-permute-done((f32[16]{0:T(128)S(1)}, f32[16]{0:T(128)S(1)}, u32[]{:S(2)}, u32[]{:S(2)}) %collective-permute-start.21) | collective-permute-done | bytes 96 | tf_op jit(solution)/shard_map/ppermute | solution.py:33
  134.9 3.6 %collective-permute-done.22 = f32[16]{0:T(128)S(1)} collective-permute-done((f32[16]{0:T(128)S(1)}, f32[16]{0:T(128)S(1)}, u32[]{:S(2)}, u32[]{:S(2)}) %collective-permute-start.22) | collective-permute-done | bytes 96 | tf_op jit(solution)/shard_map/ppermute | solution.py:33
  138.5 1.3 collective-permute-start.23
  139.8 3.8 %collective-permute-done.23 = f32[16]{0:T(128)S(1)} collective-permute-done((f32[16]{0:T(128)S(1)}, f32[16]{0:T(128)S(1)}, u32[]{:S(2)}, u32[]{:S(2)}) %collective-permute-start.23) | collective-permute-done | bytes 96 | tf_op jit(solution)/shard_map/ppermute | solution.py:33
  143.5 0.7 broadcast_divide_fusion
  144.3 0.6 pad_maximum_fusion.1
  (53 shorter events, 2.2 us)
Async XLA Ops:
  2.9 4.7 %copy-start.1 = (bf16[112,32,512]{2,1,0:T(8,128)(2,1)S(1)}, bf16[112,32,512]{2,1,0:T(8,128)(2,1)}, u32[]{:S(2)}) copy-start(bf16[112,32,512]{2,1,0:T(8,128)(2,1)} %param.11) | copy-start | bytes 11010052
  8.8 2.7 %copy-start.3 = (s32[128]{0:T(128)S(1)}, s32[128]{0:T(128)}, u32[]{:S(2)}) copy-start(s32[128]{0:T(128)} %param.15) | copy-start | bytes 1540
  8.8 2.7 %copy-start.4 = (s32[128,1]{0,1:T(1,128)S(1)}, s32[128,1]{0,1:T(1,128)}, u32[]{:S(2)}) copy-start(s32[128,1]{0,1:T(1,128)} %param.14) | copy-start | bytes 1540
  17.9 7.4 %collective-permute-start = (f32[4,4,4,2,16,512]{5,4,3,2,1,0:T(8,128)}, f32[4,4,4,2,16,512]{5,4,3,2,1,0:T(8,128)S(1)}, u32[]{:S(2)}, u32[]{:S(2)}) collective-permute-start(f32[4,4,4,2,16,512]{5,4,3,2,1,0:T(8,128)} %bitcast.118), channel_id=1, source_target_pairs={{0,1},{1,0},{2,3},{3,2},{4,5},{5,4},{6,7},{7,6},{8,9},{9,8},{10,11... | collective-permute-start | bytes 12582920 | tf_op jit(solution)/shard_map/ppermute | solution.py:45
  28.8 26.5 %collective-permute-start.3 = (f32[4,4,2,16,512]{4,3,2,1,0:T(8,128)S(1)}, f32[4,4,2,16,512]{4,3,2,1,0:T(8,128)S(1)}, u32[]{:S(2)}, u32[]{:S(2)}) collective-permute-start(f32[4,4,2,16,512]{4,3,2,1,0:T(8,128)S(1)} %get-tuple-element.9), channel_id=1, source_target_pairs={{0,6},{1,25},{2,0},{3,27},{4,2},{5,29},{6,4},{7,31},{8,14},{9,1},{... | collective-permute-start | bytes 3145736 | tf_op jit(solution)/shard_map/ppermute | solution.py:40
  31.8 23.6 %collective-permute-start.2 = (f32[4,4,2,16,512]{4,3,2,1,0:T(8,128)S(1)}, f32[4,4,2,16,512]{4,3,2,1,0:T(8,128)S(1)}, u32[]{:S(2)}, u32[]{:S(2)}) collective-permute-start(f32[4,4,2,16,512]{4,3,2,1,0:T(8,128)S(1)} %get-tuple-element.10), channel_id=1, source_target_pairs={{0,4},{1,17},{2,6},{3,19},{4,0},{5,21},{6,2},{7,23},{8,12},{9,25},... | collective-permute-start | bytes 3145736 | tf_op jit(solution)/shard_map/ppermute | solution.py:40
  32.6 46.6 %copy-start = (f32[8,2,16,512]{3,2,1,0:T(8,128)S(1)}, f32[8,2,16,512]{3,2,1,0:T(8,128)}, u32[]{:S(2)}) copy-start(f32[8,2,16,512]{3,2,1,0:T(8,128)} %param.8) | copy-start | bytes 1572868
  32.6 51.5 %copy-start.2 = (f32[2,512]{1,0:T(2,128)S(1)}, f32[2,512]{1,0:T(2,128)}, u32[]{:S(2)}) copy-start(f32[2,512]{1,0:T(2,128)} %param.9) | copy-start | bytes 12292
  32.6 26.7 %collective-permute-start.1 = (f32[4,4,2,16,512]{4,3,2,1,0:T(8,128)S(1)}, f32[4,4,2,16,512]{4,3,2,1,0:T(8,128)S(1)}, u32[]{:S(2)}, u32[]{:S(2)}) collective-permute-start(f32[4,4,2,16,512]{4,3,2,1,0:T(8,128)S(1)} %get-tuple-element.8), channel_id=1, source_target_pairs={{0,2},{1,9},{2,4},{3,11},{4,6},{5,13},{6,0},{7,15},{8,10},{9,17},{... | collective-permute-start | bytes 3145736 | tf_op jit(solution)/shard_map/ppermute | solution.py:40
  59.9 10.8 %collective-permute-start.6 = (f32[4,2,16,512]{3,2,1,0:T(8,128)S(1)}, f32[4,2,16,512]{3,2,1,0:T(8,128)S(1)}, u32[]{:S(2)}, u32[]{:S(2)}) collective-permute-start(f32[4,2,16,512]{3,2,1,0:T(8,128)S(1)} %get-tuple-element.12), channel_id=1, source_target_pairs={{0,24},{1,7},{2,26},{3,1},{4,28},{5,3},{6,30},{7,5},{8,0},{9,15},{... | collective-permute-start | bytes 786440 | tf_op jit(solution)/shard_map/ppermute | solution.py:40
  64.0 8.0 %collective-permute-start.5 = (f32[4,2,16,512]{3,2,1,0:T(8,128)S(1)}, f32[4,2,16,512]{3,2,1,0:T(8,128)S(1)}, u32[]{:S(2)}, u32[]{:S(2)}) collective-permute-start(f32[4,2,16,512]{3,2,1,0:T(8,128)S(1)} %get-tuple-element.13), channel_id=1, source_target_pairs={{0,16},{1,5},{2,18},{3,7},{4,20},{5,1},{6,22},{7,3},{8,24},{9,13},... | collective-permute-start | bytes 786440 | tf_op jit(solution)/shard_map/ppermute | solution.py:40
  64.0 10.4 %collective-permute-start.4 = (f32[4,2,16,512]{3,2,1,0:T(8,128)S(1)}, f32[4,2,16,512]{3,2,1,0:T(8,128)S(1)}, u32[]{:S(2)}, u32[]{:S(2)}) collective-permute-start(f32[4,2,16,512]{3,2,1,0:T(8,128)S(1)} %get-tuple-element.11), channel_id=1, source_target_pairs={{0,8},{1,3},{2,10},{3,5},{4,12},{5,7},{6,14},{7,1},{8,16},{9,11},{... | collective-permute-start | bytes 786440 | tf_op jit(solution)/shard_map/ppermute | solution.py:40
  74.5 6.1 %collective-permute-start.9 = (f32[2,16,512]{2,1,0:T(8,128)S(1)}, f32[2,16,512]{2,1,0:T(8,128)S(1)}, u32[]{:S(2)}, u32[]{:S(2)}) collective-permute-start(f32[2,16,512]{2,1,0:T(8,128)S(1)} %get-tuple-element.15), channel_id=1, source_target_pairs={{0,96},{1,97},{2,98},{3,99},{4,100},{5,101},{6,102},{7,103},{8,104... | collective-permute-start | bytes 196616 | tf_op jit(solution)/shard_map/ppermute | solution.py:40
  77.6 5.8 %collective-permute-start.8 = (f32[2,16,512]{2,1,0:T(8,128)S(1)}, f32[2,16,512]{2,1,0:T(8,128)S(1)}, u32[]{:S(2)}, u32[]{:S(2)}) collective-permute-start(f32[2,16,512]{2,1,0:T(8,128)S(1)} %get-tuple-element.16), channel_id=1, source_target_pairs={{0,64},{1,65},{2,66},{3,67},{4,68},{5,69},{6,70},{7,71},{8,72},{9,... | collective-permute-start | bytes 196616 | tf_op jit(solution)/shard_map/ppermute | solution.py:40
  78.2 5.8 %collective-permute-start.7 = (f32[2,16,512]{2,1,0:T(8,128)S(1)}, f32[2,16,512]{2,1,0:T(8,128)S(1)}, u32[]{:S(2)}, u32[]{:S(2)}) collective-permute-start(f32[2,16,512]{2,1,0:T(8,128)S(1)} %get-tuple-element.14), channel_id=1, source_target_pairs={{0,32},{1,33},{2,34},{3,35},{4,36},{5,37},{6,38},{7,39},{8,40},{9,... | collective-permute-start | bytes 196616 | tf_op jit(solution)/shard_map/ppermute | solution.py:40
  85.6 1.2 collective-permute-start.10
  86.9 4.0 %collective-permute-start.11 = (f32[72,16]{1,0:T(8,128)S(1)}, f32[72,16]{1,0:T(8,128)S(1)}, u32[]{:S(2)}, u32[]{:S(2)}) collective-permute-start(f32[72,16]{1,0:T(8,128)S(1)} %fusion.34), channel_id=1, source_target_pairs={{0,2},{1,3},{2,0},{3,1},{4,6},{5,7},{6,4},{7,5},{8,10},{9,11},{10,... | collective-permute-start | bytes 13832 | tf_op jit(solution)/shard_map/ppermute | solution.py:33
  90.9 5.5 %collective-permute-start.12 = (f32[72,16]{1,0:T(8,128)S(1)}, f32[72,16]{1,0:T(8,128)S(1)}, u32[]{:S(2)}, u32[]{:S(2)}) collective-permute-start(f32[72,16]{1,0:T(8,128)S(1)} %add.190), channel_id=1, source_target_pairs={{0,4},{1,5},{2,6},{3,7},{4,0},{5,1},{6,2},{7,3},{8,12},{9,13},{10,... | collective-permute-start | bytes 13832 | tf_op jit(solution)/shard_map/ppermute | solution.py:33
  96.4 4.0 %collective-permute-start.13 = (f32[72,16]{1,0:T(8,128)S(1)}, f32[72,16]{1,0:T(8,128)S(1)}, u32[]{:S(2)}, u32[]{:S(2)}) collective-permute-start(f32[72,16]{1,0:T(8,128)S(1)} %add.191), channel_id=1, source_target_pairs={{0,8},{1,9},{2,10},{3,11},{4,12},{5,13},{6,14},{7,15},{8,0},{9,1},... | collective-permute-start | bytes 13832 | tf_op jit(solution)/shard_map/ppermute | solution.py:33
  100.4 5.5 %collective-permute-start.14 = (f32[72,16]{1,0:T(8,128)S(1)}, f32[72,16]{1,0:T(8,128)S(1)}, u32[]{:S(2)}, u32[]{:S(2)}) collective-permute-start(f32[72,16]{1,0:T(8,128)S(1)} %add.192), channel_id=1, source_target_pairs={{0,16},{1,17},{2,18},{3,19},{4,20},{5,21},{6,22},{7,23},{8,24},{9,... | collective-permute-start | bytes 13832 | tf_op jit(solution)/shard_map/ppermute | solution.py:33
  105.8 4.0 %collective-permute-start.15 = (f32[72,16]{1,0:T(8,128)S(1)}, f32[72,16]{1,0:T(8,128)S(1)}, u32[]{:S(2)}, u32[]{:S(2)}) collective-permute-start(f32[72,16]{1,0:T(8,128)S(1)} %add.193), channel_id=1, source_target_pairs={{0,32},{1,33},{2,34},{3,35},{4,36},{5,37},{6,38},{7,39},{8,40},{9,... | collective-permute-start | bytes 13832 | tf_op jit(solution)/shard_map/ppermute | solution.py:33
  109.8 5.5 %collective-permute-start.16 = (f32[72,16]{1,0:T(8,128)S(1)}, f32[72,16]{1,0:T(8,128)S(1)}, u32[]{:S(2)}, u32[]{:S(2)}) collective-permute-start(f32[72,16]{1,0:T(8,128)S(1)} %add.194), channel_id=1, source_target_pairs={{0,64},{1,65},{2,66},{3,67},{4,68},{5,69},{6,70},{7,71},{8,72},{9,... | collective-permute-start | bytes 13832 | tf_op jit(solution)/shard_map/ppermute | solution.py:33
  116.3 1.2 collective-permute-start.17
  117.6 3.6 %collective-permute-start.18 = (f32[16]{0:T(128)S(1)}, f32[16]{0:T(128)S(1)}, u32[]{:S(2)}, u32[]{:S(2)}) collective-permute-start(f32[16]{0:T(128)S(1)} %add.197), channel_id=1, source_target_pairs={{0,2},{1,3},{2,0},{3,1},{4,6},{5,7},{6,4},{7,5},{8,10},{9,11},{10,... | collective-permute-start | bytes 200 | tf_op jit(solution)/shard_map/ppermute | solution.py:33
  121.2 5.1 %collective-permute-start.19 = (f32[16]{0:T(128)S(1)}, f32[16]{0:T(128)S(1)}, u32[]{:S(2)}, u32[]{:S(2)}) collective-permute-start(f32[16]{0:T(128)S(1)} %add.198), channel_id=1, source_target_pairs={{0,4},{1,5},{2,6},{3,7},{4,0},{5,1},{6,2},{7,3},{8,12},{9,13},{10,... | collective-permute-start | bytes 200 | tf_op jit(solution)/shard_map/ppermute | solution.py:33
  126.2 3.6 %collective-permute-start.20 = (f32[16]{0:T(128)S(1)}, f32[16]{0:T(128)S(1)}, u32[]{:S(2)}, u32[]{:S(2)}) collective-permute-start(f32[16]{0:T(128)S(1)} %add.199), channel_id=1, source_target_pairs={{0,8},{1,9},{2,10},{3,11},{4,12},{5,13},{6,14},{7,15},{8,0},{9,1},... | collective-permute-start | bytes 200 | tf_op jit(solution)/shard_map/ppermute | solution.py:33
  129.8 5.1 %collective-permute-start.21 = (f32[16]{0:T(128)S(1)}, f32[16]{0:T(128)S(1)}, u32[]{:S(2)}, u32[]{:S(2)}) collective-permute-start(f32[16]{0:T(128)S(1)} %add.200), channel_id=1, source_target_pairs={{0,16},{1,17},{2,18},{3,19},{4,20},{5,21},{6,22},{7,23},{8,24},{9,... | collective-permute-start | bytes 200 | tf_op jit(solution)/shard_map/ppermute | solution.py:33
  134.9 3.6 %collective-permute-start.22 = (f32[16]{0:T(128)S(1)}, f32[16]{0:T(128)S(1)}, u32[]{:S(2)}, u32[]{:S(2)}) collective-permute-start(f32[16]{0:T(128)S(1)} %add.201), channel_id=1, source_target_pairs={{0,32},{1,33},{2,34},{3,35},{4,36},{5,37},{6,38},{7,39},{8,40},{9,... | collective-permute-start | bytes 200 | tf_op jit(solution)/shard_map/ppermute | solution.py:33
  138.5 5.1 %collective-permute-start.23 = (f32[16]{0:T(128)S(1)}, f32[16]{0:T(128)S(1)}, u32[]{:S(2)}, u32[]{:S(2)}) collective-permute-start(f32[16]{0:T(128)S(1)} %add.202), channel_id=1, source_target_pairs={{0,64},{1,65},{2,66},{3,67},{4,68},{5,69},{6,70},{7,71},{8,72},{9,... | collective-permute-start | bytes 200 | tf_op jit(solution)/shard_map/ppermute | solution.py:33

commit v6 on v5

--- a/solution.py
+++ b/solution.py
@@ -24,13 +24,15 @@
     return pairs
 
 
-def flipped(bit):
-    return [(g, g ^ (1 << bit)) for g in range(128)]
+def flipped(mask):
+    return [(g, g ^ mask) for g in range(128)]
 
 
 def all_sum(v):
-    for bit in range(7):
-        v = v + lax.ppermute(v, AXES, flipped(bit))
+    v = v + lax.ppermute(v, AXES, flipped(1))
+    for axis in ("x", "z", "y"):
+        for step in (1, 3):
+            v = v + lax.ppermute(v, AXES, flipped(step * STRIDE[axis]))
     return v
 
 
@@ -42,9 +44,11 @@
 
 
 def reduce_to_owner(keep, send):
-    d = keep + lax.ppermute(send, AXES, moved("c", 1))
-    d = spread(d, "x", "z")
-    d = spread(d, "z", "x")
+    pieces = [keep[k] + lax.ppermute(send[k], AXES, moved("c", 1)) for k in range(4)]
+    acc = pieces[0]
+    for k in (1, 2, 3):
+        acc = acc + lax.ppermute(pieces[k], AXES, moved("x", k, "z"))
+    d = spread(acc, "z", "x")
     return spread(d, "y")
 
 

time: 145 us -> 136 us (0.938)
  waiting for transfers between devices: 97.2 us -> 68.1 us
  starting transfers between devices: 20 us -> 38.6 us
  local copies, waits for them, and re-layouts: 2.2 us -> 7.57 us
  other arithmetic: 6.07 us -> 3.7 us
    ppermute x9 -> x6, waiting for transfers between devices: 38.4 us -> 7.63 us  [spread(): acc = acc + lax.ppermute(pieces[k], AXES, moved(axis, k, other))]
    ppermute x15 -> x21, starting transfers between devices: 5.31 us -> 26.2 us  [the longest x12 19 us: all_sum(): v = v + lax.ppermute(v, AXES, flipped(step * STRIDE[axis]))]
    slice x0 -> x1, local copies, waits for them, and re-layouts: none -> 4.46 us  [reduce_to_owner(): send[k]]
    dot_general x1, matrix products: 4.73 us -> 1.19 us  [on_device(): jnp.einsum('snc,scd->snd', picked[:near_count], near_blocks, preferred_el...]
    ppermute x9 -> x6, starting transfers between devices: 14.7 us -> 12.5 us  [spread(): acc = acc + lax.ppermute(pieces[k], AXES, moved(axis, k, other))]
    dot_general x1, matrix products: 1.08 us -> 3.24 us  [on_device(): jnp.einsum('snc,skc->snk', picked[near_count:], far_u, preferred_element_...]
    add x14 -> x17, other arithmetic: 3.27 us -> 1.4 us  [the longest x1 0.7 us: reduce_to_owner(): acc = acc + lax.ppermute(pieces[k], AXES, moved('x', k, 'z'))]
    ppermute x15 -> x21, waiting for transfers between devices: 58.8 us -> 60.5 us  [the longest x12 33.5 us: all_sum(): v = v + lax.ppermute(v, AXES, flipped(step * STRIDE[axis]))]
  transfers between devices with their start and end apart: 24 -> 27, of which waited for: 22 -> 22; matrix products, arithmetic and copies ran while one was open for 1% -> 2% of each run, Pallas kernels for 0% -> 0%
where the time goes in v6:
time: 136 us
  waiting for transfers between devices  68.1 us (50%)
  starting transfers between devices  38.6 us (28%)
  matrix products  10.7 us (8%)
  local copies, waits for them, and re-layouts  7.57 us (6%)
  Pallas kernels  6.43 us (5%)
  other arithmetic  3.7 us (3%)
    ppermute x12, waiting for transfers between devices, all_sum(): v = v + lax.ppermute(v, AXES, flipped(step * STRIDE[axis]))  33.5 us
    ppermute x3, waiting for transfers between devices, reduce_to_owner(): acc = acc + lax.ppermute(pieces[k], AXES, moved('x', k, 'z'))  22.9 us
    ppermute x12, starting transfers between devices, all_sum(): v = v + lax.ppermute(v, AXES, flipped(step * STRIDE[axis]))  19 us
    ppermute x6, starting transfers between devices, spread(): acc = acc + lax.ppermute(pieces[k], AXES, moved(axis, k, other))  12.5 us
    ppermute x6, waiting for transfers between devices, spread(): acc = acc + lax.ppermute(pieces[k], AXES, moved(axis, k, other))  7.63 us
    pallas_call x1, Pallas kernels, accumulate(): pl.pallas_call(accumulate_kernel, grid_spec=grid_spec, out_shape=[out, ou...  6.43 us
    ppermute x3, starting transfers between devices, reduce_to_owner(): acc = acc + lax.ppermute(pieces[k], AXES, moved('x', k, 'z'))  5.99 us
    slice x1, local copies, waits for them, and re-layouts, reduce_to_owner(): send[k]  4.46 us
  transfers between devices with their start and end apart: 27, of which 22 were waited for; matrix products, arithmetic and copies ran while one was open for 2% of the time, Pallas kernels for 0%

profile of v6, /device:TPU:0, one launch (start us, length us, event | category | flops | bytes accessed | tf_op | source)
XLA Modules:
  0.0 136.0 jit_solution(10102432913431490631)
XLA Ops:
  0.7 0.8 bitcast_convert_fusion
  2.9 3.2 %convolution_convert_fusion = bf16[112,16,32]{2,1,0:T(8,128)(2,1)S(1)} fusion(bf16[128,16,512]{2,1,0:T(8,128)(2,1)S(1)} %gather_fusion, bf16[112,32,512]{2,1,0:T(8,128)(2,1)} %param.11), kind=kOutput, calls=%fused_computation.1 | convolution fusion | flops 58777600 | bytes 5881856 | tf_op jit(solution)/shard_map/snc,skc->snk/dot_general | solution.py:130
  6.2 1.2 copy-done.4
  7.4 1.2 fusion.35.near_ref
  8.6 2.7 %fusion.34.far_ref = f32[112,16,512]{2,1,0:T(8,128)S(1)} fusion(bf16[112,16,32]{2,1,0:T(8,128)(2,1)S(1)} %convolution_convert_fusion, bf16[112,32,512]{2,1,0:T(8,128)(2,1)} %param.12), kind=kOutput, calls=%fused_computation.95 | convolution fusion | flops 58720256 | bytes 7454720 | tf_op jit(solution)/shard_map/snk,skc->snc/dot_general | solution.py:133
  11.3 6.4 %shard_map.95 = (f32[128,16,512]{2,1,0:T(8,128)}, f32[128,16,512]{2,1,0:T(8,128)}) custom-call(s32[128]{0:T(128)S(1)} %multiply_add_fusion.slot_ref, f32[16,16,512]{2,1,0:T(8,128)S(1)} %fusion.35.near_ref, f32[112,16,512]{2,1,0:T(8,128)S(1)} %fusion.34.far_ref), custom_call_target="tpu_custom_call" | custom-call | tf_op jit(solution)/shard_map/pallas_call | solution.py:105
  17.8 4.5 %fusion.32 = (f32[32,16,512]{2,1,0:T(8,128)S(1)}, f32[32,16,512]{2,1,0:T(8,128)S(1)}, f32[32,16,512]{2,1,0:T(8,128)S(1)}, f32[32,16,512]{2,1,0:T(8,128)S(1)}, f3...) fusion(f32[128,16,512]{2,1,0:T(8,128)} %get-tuple-element.5, ...), kind=kLoop, calls=%fused_computation.93 | loop fusion | bytes 16777216 | tf_op jit(solution)/shard_map/slice | solution.py:47
  23.3 1.6 %collective-permute-done.1 = f32[4,4,2,16,512]{4,3,2,1,0:T(8,128)S(1)} collective-permute-done((f32[4,4,2,16,512]{4,3,2,1,0:T(8,128)S(1)}, f32[4,4,2,16,512]{4,3,2,1,0:T(8,128)S(1)}, u32[]{:S(2)}, u32[]{:S(2)}) %collective-permute-start.1) | collective-permute-done | bytes 1048608 | tf_op jit(solution)/shard_map/ppermute | solution.py:47
  25.2 1.7 %collective-permute-start.2 = (f32[4,4,2,16,512]{4,3,2,1,0:T(8,128)S(1)}, f32[4,4,2,16,512]{4,3,2,1,0:T(8,128)S(1)}, u32[]{:S(2)}, u32[]{:S(2)}) collective-permute-start(f32[4,4,2,16,512]{4,3,2,1,0:T(8,128)S(1)} %add.188), channel_id=1, source_target_pairs={{0,2},{1,9},{2,4},{3,11},{4,6},{5,13},{6,0},{7,15},{8,10},{9,17},{... | collective-permute-start | bytes 3145736 | tf_op jit(solution)/shard_map/ppermute | solution.py:50
  27.1 2.8 %collective-permute-start.4 = (f32[4,4,2,16,512]{4,3,2,1,0:T(8,128)S(1)}, f32[4,4,2,16,512]{4,3,2,1,0:T(8,128)S(1)}, u32[]{:S(2)}, u32[]{:S(2)}) collective-permute-start(f32[4,4,2,16,512]{4,3,2,1,0:T(8,128)S(1)} %add.190), channel_id=1, source_target_pairs={{0,4},{1,17},{2,6},{3,19},{4,0},{5,21},{6,2},{7,23},{8,12},{9,25},... | collective-permute-start | bytes 3145736 | tf_op jit(solution)/shard_map/ppermute | solution.py:50
  30.1 1.5 %collective-permute-start.6 = (f32[4,4,2,16,512]{4,3,2,1,0:T(8,128)S(1)}, f32[4,4,2,16,512]{4,3,2,1,0:T(8,128)S(1)}, u32[]{:S(2)}, u32[]{:S(2)}) collective-permute-start(f32[4,4,2,16,512]{4,3,2,1,0:T(8,128)S(1)} %add.192), channel_id=1, source_target_pairs={{0,6},{1,25},{2,0},{3,27},{4,2},{5,29},{6,4},{7,31},{8,14},{9,1},{... | collective-permute-start | bytes 3145736 | tf_op jit(solution)/shard_map/ppermute | solution.py:50
  31.6 9.7 %collective-permute-done.2 = f32[4,4,2,16,512]{4,3,2,1,0:T(8,128)S(1)} collective-permute-done((f32[4,4,2,16,512]{4,3,2,1,0:T(8,128)S(1)}, f32[4,4,2,16,512]{4,3,2,1,0:T(8,128)S(1)}, u32[]{:S(2)}, u32[]{:S(2)}) %collective-permute-start.2) | collective-permute-done | bytes 1048608 | tf_op jit(solution)/shard_map/ppermute | solution.py:50
  41.3 12.3 %collective-permute-done.4 = f32[4,4,2,16,512]{4,3,2,1,0:T(8,128)S(1)} collective-permute-done((f32[4,4,2,16,512]{4,3,2,1,0:T(8,128)S(1)}, f32[4,4,2,16,512]{4,3,2,1,0:T(8,128)S(1)}, u32[]{:S(2)}, u32[]{:S(2)}) %collective-permute-start.4) | collective-permute-done | bytes 1048608 | tf_op jit(solution)/shard_map/ppermute | solution.py:50
  53.6 0.9 collective-permute-done.6
  55.4 2.0 %collective-permute-start.7 = (f32[4,2,16,512]{3,2,1,0:T(8,128)S(1)}, f32[4,2,16,512]{3,2,1,0:T(8,128)S(1)}, u32[]{:S(2)}, u32[]{:S(2)}) collective-permute-start(f32[4,2,16,512]{3,2,1,0:T(8,128)S(1)} %get-tuple-element.16), channel_id=1, source_target_pairs={{0,8},{1,3},{2,10},{3,5},{4,12},{5,7},{6,14},{7,1},{8,16},{9,11},{... | collective-permute-start | bytes 786440 | tf_op jit(solution)/shard_map/ppermute | solution.py:42
  57.3 3.6 %collective-permute-start.8 = (f32[4,2,16,512]{3,2,1,0:T(8,128)S(1)}, f32[4,2,16,512]{3,2,1,0:T(8,128)S(1)}, u32[]{:S(2)}, u32[]{:S(2)}) collective-permute-start(f32[4,2,16,512]{3,2,1,0:T(8,128)S(1)} %get-tuple-element.18), channel_id=1, source_target_pairs={{0,16},{1,5},{2,18},{3,7},{4,20},{5,1},{6,22},{7,3},{8,24},{9,13},... | collective-permute-start | bytes 786440 | tf_op jit(solution)/shard_map/ppermute | solution.py:42
  60.9 1.0 collective-permute-start.9
  61.9 1.9 %collective-permute-done.7 = f32[4,2,16,512]{3,2,1,0:T(8,128)S(1)} collective-permute-done((f32[4,2,16,512]{3,2,1,0:T(8,128)S(1)}, f32[4,2,16,512]{3,2,1,0:T(8,128)S(1)}, u32[]{:S(2)}, u32[]{:S(2)}) %collective-permute-start.7) | collective-permute-done | bytes 262176 | tf_op jit(solution)/shard_map/ppermute | solution.py:42
  63.8 4.3 %collective-permute-done.8 = f32[4,2,16,512]{3,2,1,0:T(8,128)S(1)} collective-permute-done((f32[4,2,16,512]{3,2,1,0:T(8,128)S(1)}, f32[4,2,16,512]{3,2,1,0:T(8,128)S(1)}, u32[]{:S(2)}, u32[]{:S(2)}) %collective-permute-start.8) | collective-permute-done | bytes 262176 | tf_op jit(solution)/shard_map/ppermute | solution.py:42
  68.2 1.6 %collective-permute-start.10 = (f32[2,16,512]{2,1,0:T(8,128)S(1)}, f32[2,16,512]{2,1,0:T(8,128)S(1)}, u32[]{:S(2)}, u32[]{:S(2)}) collective-permute-start(f32[2,16,512]{2,1,0:T(8,128)S(1)} %get-tuple-element.19), channel_id=1, source_target_pairs={{0,32},{1,33},{2,34},{3,35},{4,36},{5,37},{6,38},{7,39},{8,40},{9,... | collective-permute-start | bytes 196616 | tf_op jit(solution)/shard_map/ppermute | solution.py:42
  69.8 2.9 %collective-permute-start.11 = (f32[2,16,512]{2,1,0:T(8,128)S(1)}, f32[2,16,512]{2,1,0:T(8,128)S(1)}, u32[]{:S(2)}, u32[]{:S(2)}) collective-permute-start(f32[2,16,512]{2,1,0:T(8,128)S(1)} %get-tuple-element.21), channel_id=1, source_target_pairs={{0,64},{1,65},{2,66},{3,67},{4,68},{5,69},{6,70},{7,71},{8,72},{9,... | collective-permute-start | bytes 196616 | tf_op jit(solution)/shard_map/ppermute | solution.py:42
  72.7 1.3 collective-permute-start.12
  74.1 1.3 convolution_bitcast_fusion
  75.7 1.3 collective-permute-done.12
  77.0 1.5 %fusion.2 = f32[16,1,8,1]{2,1,3,0:T(1,128)S(1)} fusion(f32[8,2,16,512]{3,2,1,0:T(8,128)S(1)} %copy-done, f32[2,16,512,1]{2,1,0,3:T(8,128)S(1)} %bitcast.110), kind=kOutput, calls=%fused_computation.6 | convolution fusion | flops 1572864 | bytes 590336 | tf_op jit(solution)/shard_map/knjc,njc->kj/dot_general | solution.py:145
  78.6 1.2 collective-permute-done.13
  79.8 1.7 %collective-permute-start.14 = (f32[72,16]{1,0:T(8,128)S(1)}, f32[72,16]{1,0:T(8,128)S(1)}, u32[]{:S(2)}, u32[]{:S(2)}) collective-permute-start(f32[72,16]{1,0:T(8,128)S(1)} %fusion.31), channel_id=1, source_target_pairs={{0,2},{1,3},{2,0},{3,1},{4,6},{5,7},{6,4},{7,5},{8,10},{9,11},{10,... | collective-permute-start | bytes 13832 | tf_op jit(solution)/shard_map/ppermute | solution.py:35
  81.6 2.3 %collective-permute-done.14 = f32[72,16]{1,0:T(8,128)S(1)} collective-permute-done((f32[72,16]{1,0:T(8,128)S(1)}, f32[72,16]{1,0:T(8,128)S(1)}, u32[]{:S(2)}, u32[]{:S(2)}) %collective-permute-start.14) | collective-permute-done | bytes 4640 | tf_op jit(solution)/shard_map/ppermute | solution.py:35
  83.9 2.6 %collective-permute-start.15 = (f32[72,16]{1,0:T(8,128)S(1)}, f32[72,16]{1,0:T(8,128)S(1)}, u32[]{:S(2)}, u32[]{:S(2)}) collective-permute-start(f32[72,16]{1,0:T(8,128)S(1)} %add.202), channel_id=1, source_target_pairs={{0,6},{1,7},{2,4},{3,5},{4,2},{5,3},{6,0},{7,1},{8,14},{9,15},{10,... | collective-permute-start | bytes 13832 | tf_op jit(solution)/shard_map/ppermute | solution.py:35
  86.5 2.5 %collective-permute-done.15 = f32[72,16]{1,0:T(8,128)S(1)} collective-permute-done((f32[72,16]{1,0:T(8,128)S(1)}, f32[72,16]{1,0:T(8,128)S(1)}, u32[]{:S(2)}, u32[]{:S(2)}) %collective-permute-start.15) | collective-permute-done | bytes 4640 | tf_op jit(solution)/shard_map/ppermute | solution.py:35
  89.1 1.5 %collective-permute-start.16 = (f32[72,16]{1,0:T(8,128)S(1)}, f32[72,16]{1,0:T(8,128)S(1)}, u32[]{:S(2)}, u32[]{:S(2)}) collective-permute-start(f32[72,16]{1,0:T(8,128)S(1)} %add.203), channel_id=1, source_target_pairs={{0,8},{1,9},{2,10},{3,11},{4,12},{5,13},{6,14},{7,15},{8,0},{9,1},... | collective-permute-start | bytes 13832 | tf_op jit(solution)/shard_map/ppermute | solution.py:35
  90.6 2.4 %collective-permute-done.16 = f32[72,16]{1,0:T(8,128)S(1)} collective-permute-done((f32[72,16]{1,0:T(8,128)S(1)}, f32[72,16]{1,0:T(8,128)S(1)}, u32[]{:S(2)}, u32[]{:S(2)}) %collective-permute-start.16) | collective-permute-done | bytes 4640 | tf_op jit(solution)/shard_map/ppermute | solution.py:35
  93.0 2.2 %collective-permute-start.17 = (f32[72,16]{1,0:T(8,128)S(1)}, f32[72,16]{1,0:T(8,128)S(1)}, u32[]{:S(2)}, u32[]{:S(2)}) collective-permute-start(f32[72,16]{1,0:T(8,128)S(1)} %add.204), channel_id=1, source_target_pairs={{0,24},{1,25},{2,26},{3,27},{4,28},{5,29},{6,30},{7,31},{8,16},{9,... | collective-permute-start | bytes 13832 | tf_op jit(solution)/shard_map/ppermute | solution.py:35
  95.2 3.0 %collective-permute-done.17 = f32[72,16]{1,0:T(8,128)S(1)} collective-permute-done((f32[72,16]{1,0:T(8,128)S(1)}, f32[72,16]{1,0:T(8,128)S(1)}, u32[]{:S(2)}, u32[]{:S(2)}) %collective-permute-start.17) | collective-permute-done | bytes 4640 | tf_op jit(solution)/shard_map/ppermute | solution.py:35
  98.5 3.6 %collective-permute-done.18 = f32[72,16]{1,0:T(8,128)S(1)} collective-permute-done((f32[72,16]{1,0:T(8,128)S(1)}, f32[72,16]{1,0:T(8,128)S(1)}, u32[]{:S(2)}, u32[]{:S(2)}) %collective-permute-start.18) | collective-permute-done | bytes 4640 | tf_op jit(solution)/shard_map/ppermute | solution.py:35
  102.2 2.6 %collective-permute-start.19 = (f32[72,16]{1,0:T(8,128)S(1)}, f32[72,16]{1,0:T(8,128)S(1)}, u32[]{:S(2)}, u32[]{:S(2)}) collective-permute-start(f32[72,16]{1,0:T(8,128)S(1)} %add.206), channel_id=1, source_target_pairs={{0,96},{1,97},{2,98},{3,99},{4,100},{5,101},{6,102},{7,103},{8,104... | collective-permute-start | bytes 13832 | tf_op jit(solution)/shard_map/ppermute | solution.py:35
  104.7 2.6 %collective-permute-done.19 = f32[72,16]{1,0:T(8,128)S(1)} collective-permute-done((f32[72,16]{1,0:T(8,128)S(1)}, f32[72,16]{1,0:T(8,128)S(1)}, u32[]{:S(2)}, u32[]{:S(2)}) %collective-permute-start.19) | collective-permute-done | bytes 4640 | tf_op jit(solution)/shard_map/ppermute | solution.py:35
  107.5 0.8 fusion
  108.5 1.1 collective-permute-done.20
  110.1 3.1 %collective-permute-done.21 = f32[16]{0:T(128)S(1)} collective-permute-done((f32[16]{0:T(128)S(1)}, f32[16]{0:T(128)S(1)}, u32[]{:S(2)}, u32[]{:S(2)}) %collective-permute-start.21) | collective-permute-done | bytes 96 | tf_op jit(solution)/shard_map/ppermute | solution.py:35
  113.2 2.6 %collective-permute-start.22 = (f32[16]{0:T(128)S(1)}, f32[16]{0:T(128)S(1)}, u32[]{:S(2)}, u32[]{:S(2)}) collective-permute-start(f32[16]{0:T(128)S(1)} %add.210), channel_id=1, source_target_pairs={{0,6},{1,7},{2,4},{3,5},{4,2},{5,3},{6,0},{7,1},{8,14},{9,15},{10,... | collective-permute-start | bytes 200 | tf_op jit(solution)/shard_map/ppermute | solution.py:35
  115.8 2.1 %collective-permute-done.22 = f32[16]{0:T(128)S(1)} collective-permute-done((f32[16]{0:T(128)S(1)}, f32[16]{0:T(128)S(1)}, u32[]{:S(2)}, u32[]{:S(2)}) %collective-permute-start.22) | collective-permute-done | bytes 96 | tf_op jit(solution)/shard_map/ppermute | solution.py:35
  118.3 3.3 %collective-permute-done.23 = f32[16]{0:T(128)S(1)} collective-permute-done((f32[16]{0:T(128)S(1)}, f32[16]{0:T(128)S(1)}, u32[]{:S(2)}, u32[]{:S(2)}) %collective-permute-start.23) | collective-permute-done | bytes 96 | tf_op jit(solution)/shard_map/ppermute | solution.py:35
  121.6 2.2 %collective-permute-start.24 = (f32[16]{0:T(128)S(1)}, f32[16]{0:T(128)S(1)}, u32[]{:S(2)}, u32[]{:S(2)}) collective-permute-start(f32[16]{0:T(128)S(1)} %add.212), channel_id=1, source_target_pairs={{0,24},{1,25},{2,26},{3,27},{4,28},{5,29},{6,30},{7,31},{8,16},{9,... | collective-permute-start | bytes 200 | tf_op jit(solution)/shard_map/ppermute | solution.py:35
  123.7 2.6 %collective-permute-done.24 = f32[16]{0:T(128)S(1)} collective-permute-done((f32[16]{0:T(128)S(1)}, f32[16]{0:T(128)S(1)}, u32[]{:S(2)}, u32[]{:S(2)}) %collective-permute-start.24) | collective-permute-done | bytes 96 | tf_op jit(solution)/shard_map/ppermute | solution.py:35
  126.4 3.6 %collective-permute-done.25 = f32[16]{0:T(128)S(1)} collective-permute-done((f32[16]{0:T(128)S(1)}, f32[16]{0:T(128)S(1)}, u32[]{:S(2)}, u32[]{:S(2)}) %collective-permute-start.25) | collective-permute-done | bytes 96 | tf_op jit(solution)/shard_map/ppermute | solution.py:35
  129.9 2.6 %collective-permute-start.26 = (f32[16]{0:T(128)S(1)}, f32[16]{0:T(128)S(1)}, u32[]{:S(2)}, u32[]{:S(2)}) collective-permute-start(f32[16]{0:T(128)S(1)} %add.214), channel_id=1, source_target_pairs={{0,96},{1,97},{2,98},{3,99},{4,100},{5,101},{6,102},{7,103},{8,104... | collective-permute-start | bytes 200 | tf_op jit(solution)/shard_map/ppermute | solution.py:35
  132.5 2.2 %collective-permute-done.26 = f32[16]{0:T(128)S(1)} collective-permute-done((f32[16]{0:T(128)S(1)}, f32[16]{0:T(128)S(1)}, u32[]{:S(2)}, u32[]{:S(2)}) %collective-permute-start.26) | collective-permute-done | bytes 96 | tf_op jit(solution)/shard_map/ppermute | solution.py:35
  (61 shorter events, 7.1 us)
Async XLA Ops:
  2.9 4.5 %copy-start.4 = (bf16[16,512,512]{2,1,0:T(8,128)(2,1)S(1)}, bf16[16,512,512]{2,1,0:T(8,128)(2,1)}, u32[]{:S(2)}) copy-start(bf16[16,512,512]{2,1,0:T(8,128)(2,1)} %param.10) | copy-start | bytes 25165828
  8.6 2.7 %copy-start.2 = (s32[128]{0:T(128)S(1)}, s32[128]{0:T(128)}, u32[]{:S(2)}) copy-start(s32[128]{0:T(128)} %param.15) | copy-start | bytes 1540
  8.6 2.7 %copy-start.3 = (s32[128,1]{0,1:T(1,128)S(1)}, s32[128,1]{0,1:T(1,128)}, u32[]{:S(2)}) copy-start(s32[128,1]{0,1:T(1,128)} %param.14) | copy-start | bytes 1540
  22.2 2.7 %collective-permute-start.1 = (f32[4,4,2,16,512]{4,3,2,1,0:T(8,128)S(1)}, f32[4,4,2,16,512]{4,3,2,1,0:T(8,128)S(1)}, u32[]{:S(2)}, u32[]{:S(2)}) collective-permute-start(f32[4,4,2,16,512]{4,3,2,1,0:T(8,128)S(1)} %bitcast.109), channel_id=1, source_target_pairs={{0,1},{1,0},{2,3},{3,2},{4,5},{5,4},{6,7},{7,6},{8,9},{9,8},{10,11... | collective-permute-start | bytes 3145736 | tf_op jit(solution)/shard_map/ppermute | solution.py:47
  22.3 4.5 %collective-permute-start.3 = (f32[4,4,2,16,512]{4,3,2,1,0:T(8,128)S(1)}, f32[4,4,2,16,512]{4,3,2,1,0:T(8,128)S(1)}, u32[]{:S(2)}, u32[]{:S(2)}) collective-permute-start(f32[4,4,2,16,512]{4,3,2,1,0:T(8,128)S(1)} %bitcast.108), channel_id=1, source_target_pairs={{0,1},{1,0},{2,3},{3,2},{4,5},{5,4},{6,7},{7,6},{8,9},{9,8},{10,11... | collective-permute-start | bytes 3145736 | tf_op jit(solution)/shard_map/ppermute | solution.py:47
  22.8 7.1 %collective-permute-start.5 = (f32[4,4,2,16,512]{4,3,2,1,0:T(8,128)S(1)}, f32[4,4,2,16,512]{4,3,2,1,0:T(8,128)S(1)}, u32[]{:S(2)}, u32[]{:S(2)}) collective-permute-start(f32[4,4,2,16,512]{4,3,2,1,0:T(8,128)S(1)} %bitcast.107), channel_id=1, source_target_pairs={{0,1},{1,0},{2,3},{3,2},{4,5},{5,4},{6,7},{7,6},{8,9},{9,8},{10,11... | collective-permute-start | bytes 3145736 | tf_op jit(solution)/shard_map/ppermute | solution.py:47
  22.9 8.7 %collective-permute-start = (f32[4,4,2,16,512]{4,3,2,1,0:T(8,128)S(1)}, f32[4,4,2,16,512]{4,3,2,1,0:T(8,128)S(1)}, u32[]{:S(2)}, u32[]{:S(2)}) collective-permute-start(f32[4,4,2,16,512]{4,3,2,1,0:T(8,128)S(1)} %bitcast.106), channel_id=1, source_target_pairs={{0,1},{1,0},{2,3},{3,2},{4,5},{5,4},{6,7},{7,6},{8,9},{9,8},{10,11... | collective-permute-start | bytes 3145736 | tf_op jit(solution)/shard_map/ppermute | solution.py:47
  25.2 16.1 %collective-permute-start.2 = (f32[4,4,2,16,512]{4,3,2,1,0:T(8,128)S(1)}, f32[4,4,2,16,512]{4,3,2,1,0:T(8,128)S(1)}, u32[]{:S(2)}, u32[]{:S(2)}) collective-permute-start(f32[4,4,2,16,512]{4,3,2,1,0:T(8,128)S(1)} %add.188), channel_id=1, source_target_pairs={{0,2},{1,9},{2,4},{3,11},{4,6},{5,13},{6,0},{7,15},{8,10},{9,17},{... | collective-permute-start | bytes 3145736 | tf_op jit(solution)/shard_map/ppermute | solution.py:50
  27.1 26.5 %collective-permute-start.4 = (f32[4,4,2,16,512]{4,3,2,1,0:T(8,128)S(1)}, f32[4,4,2,16,512]{4,3,2,1,0:T(8,128)S(1)}, u32[]{:S(2)}, u32[]{:S(2)}) collective-permute-start(f32[4,4,2,16,512]{4,3,2,1,0:T(8,128)S(1)} %add.190), channel_id=1, source_target_pairs={{0,4},{1,17},{2,6},{3,19},{4,0},{5,21},{6,2},{7,23},{8,12},{9,25},... | collective-permute-start | bytes 3145736 | tf_op jit(solution)/shard_map/ppermute | solution.py:50
  30.1 24.4 %collective-permute-start.6 = (f32[4,4,2,16,512]{4,3,2,1,0:T(8,128)S(1)}, f32[4,4,2,16,512]{4,3,2,1,0:T(8,128)S(1)}, u32[]{:S(2)}, u32[]{:S(2)}) collective-permute-start(f32[4,4,2,16,512]{4,3,2,1,0:T(8,128)S(1)} %add.192), channel_id=1, source_target_pairs={{0,6},{1,25},{2,0},{3,27},{4,2},{5,29},{6,4},{7,31},{8,14},{9,1},{... | collective-permute-start | bytes 3145736 | tf_op jit(solution)/shard_map/ppermute | solution.py:50
  54.6 19.5 %copy-start = (f32[8,2,16,512]{3,2,1,0:T(8,128)S(1)}, f32[8,2,16,512]{3,2,1,0:T(8,128)}, u32[]{:S(2)}) copy-start(f32[8,2,16,512]{3,2,1,0:T(8,128)} %param.8) | copy-start | bytes 1572868
  54.6 22.4 %copy-start.1 = (f32[2,512]{1,0:T(2,128)S(1)}, f32[2,512]{1,0:T(2,128)}, u32[]{:S(2)}) copy-start(f32[2,512]{1,0:T(2,128)} %param.9) | copy-start | bytes 12292
  55.4 8.5 %collective-permute-start.7 = (f32[4,2,16,512]{3,2,1,0:T(8,128)S(1)}, f32[4,2,16,512]{3,2,1,0:T(8,128)S(1)}, u32[]{:S(2)}, u32[]{:S(2)}) collective-permute-start(f32[4,2,16,512]{3,2,1,0:T(8,128)S(1)} %get-tuple-element.16), channel_id=1, source_target_pairs={{0,8},{1,3},{2,10},{3,5},{4,12},{5,7},{6,14},{7,1},{8,16},{9,11},{... | collective-permute-start | bytes 786440 | tf_op jit(solution)/shard_map/ppermute | solution.py:42
  57.3 10.7 %collective-permute-start.8 = (f32[4,2,16,512]{3,2,1,0:T(8,128)S(1)}, f32[4,2,16,512]{3,2,1,0:T(8,128)S(1)}, u32[]{:S(2)}, u32[]{:S(2)}) collective-permute-start(f32[4,2,16,512]{3,2,1,0:T(8,128)S(1)} %get-tuple-element.18), channel_id=1, source_target_pairs={{0,16},{1,5},{2,18},{3,7},{4,20},{5,1},{6,22},{7,3},{8,24},{9,13},... | collective-permute-start | bytes 786440 | tf_op jit(solution)/shard_map/ppermute | solution.py:42
  60.9 7.2 %collective-permute-start.9 = (f32[4,2,16,512]{3,2,1,0:T(8,128)S(1)}, f32[4,2,16,512]{3,2,1,0:T(8,128)S(1)}, u32[]{:S(2)}, u32[]{:S(2)}) collective-permute-start(f32[4,2,16,512]{3,2,1,0:T(8,128)S(1)} %get-tuple-element.17), channel_id=1, source_target_pairs={{0,24},{1,7},{2,26},{3,1},{4,28},{5,3},{6,30},{7,5},{8,0},{9,15},{... | collective-permute-start | bytes 786440 | tf_op jit(solution)/shard_map/ppermute | solution.py:42
  68.2 7.3 %collective-permute-start.10 = (f32[2,16,512]{2,1,0:T(8,128)S(1)}, f32[2,16,512]{2,1,0:T(8,128)S(1)}, u32[]{:S(2)}, u32[]{:S(2)}) collective-permute-start(f32[2,16,512]{2,1,0:T(8,128)S(1)} %get-tuple-element.19), channel_id=1, source_target_pairs={{0,32},{1,33},{2,34},{3,35},{4,36},{5,37},{6,38},{7,39},{8,40},{9,... | collective-permute-start | bytes 196616 | tf_op jit(solution)/shard_map/ppermute | solution.py:42
  69.8 5.8 %collective-permute-start.11 = (f32[2,16,512]{2,1,0:T(8,128)S(1)}, f32[2,16,512]{2,1,0:T(8,128)S(1)}, u32[]{:S(2)}, u32[]{:S(2)}) collective-permute-start(f32[2,16,512]{2,1,0:T(8,128)S(1)} %get-tuple-element.21), channel_id=1, source_target_pairs={{0,64},{1,65},{2,66},{3,67},{4,68},{5,69},{6,70},{7,71},{8,72},{9,... | collective-permute-start | bytes 196616 | tf_op jit(solution)/shard_map/ppermute | solution.py:42
  72.7 4.3 %collective-permute-start.12 = (f32[2,16,512]{2,1,0:T(8,128)S(1)}, f32[2,16,512]{2,1,0:T(8,128)S(1)}, u32[]{:S(2)}, u32[]{:S(2)}) collective-permute-start(f32[2,16,512]{2,1,0:T(8,128)S(1)} %get-tuple-element.20), channel_id=1, source_target_pairs={{0,96},{1,97},{2,98},{3,99},{4,100},{5,101},{6,102},{7,103},{8,104... | collective-permute-start | bytes 196616 | tf_op jit(solution)/shard_map/ppermute | solution.py:42
  78.6 1.2 collective-permute-start.13
  79.8 4.0 %collective-permute-start.14 = (f32[72,16]{1,0:T(8,128)S(1)}, f32[72,16]{1,0:T(8,128)S(1)}, u32[]{:S(2)}, u32[]{:S(2)}) collective-permute-start(f32[72,16]{1,0:T(8,128)S(1)} %fusion.31), channel_id=1, source_target_pairs={{0,2},{1,3},{2,0},{3,1},{4,6},{5,7},{6,4},{7,5},{8,10},{9,11},{10,... | collective-permute-start | bytes 13832 | tf_op jit(solution)/shard_map/ppermute | solution.py:35
  83.9 5.2 %collective-permute-start.15 = (f32[72,16]{1,0:T(8,128)S(1)}, f32[72,16]{1,0:T(8,128)S(1)}, u32[]{:S(2)}, u32[]{:S(2)}) collective-permute-start(f32[72,16]{1,0:T(8,128)S(1)} %add.202), channel_id=1, source_target_pairs={{0,6},{1,7},{2,4},{3,5},{4,2},{5,3},{6,0},{7,1},{8,14},{9,15},{10,... | collective-permute-start | bytes 13832 | tf_op jit(solution)/shard_map/ppermute | solution.py:35
  89.1 4.0 %collective-permute-start.16 = (f32[72,16]{1,0:T(8,128)S(1)}, f32[72,16]{1,0:T(8,128)S(1)}, u32[]{:S(2)}, u32[]{:S(2)}) collective-permute-start(f32[72,16]{1,0:T(8,128)S(1)} %add.203), channel_id=1, source_target_pairs={{0,8},{1,9},{2,10},{3,11},{4,12},{5,13},{6,14},{7,15},{8,0},{9,1},... | collective-permute-start | bytes 13832 | tf_op jit(solution)/shard_map/ppermute | solution.py:35
  93.0 5.2 %collective-permute-start.17 = (f32[72,16]{1,0:T(8,128)S(1)}, f32[72,16]{1,0:T(8,128)S(1)}, u32[]{:S(2)}, u32[]{:S(2)}) collective-permute-start(f32[72,16]{1,0:T(8,128)S(1)} %add.204), channel_id=1, source_target_pairs={{0,24},{1,25},{2,26},{3,27},{4,28},{5,29},{6,30},{7,31},{8,16},{9,... | collective-permute-start | bytes 13832 | tf_op jit(solution)/shard_map/ppermute | solution.py:35
  98.2 4.0 %collective-permute-start.18 = (f32[72,16]{1,0:T(8,128)S(1)}, f32[72,16]{1,0:T(8,128)S(1)}, u32[]{:S(2)}, u32[]{:S(2)}) collective-permute-start(f32[72,16]{1,0:T(8,128)S(1)} %add.205), channel_id=1, source_target_pairs={{0,32},{1,33},{2,34},{3,35},{4,36},{5,37},{6,38},{7,39},{8,40},{9,... | collective-permute-start | bytes 13832 | tf_op jit(solution)/shard_map/ppermute | solution.py:35
  102.2 5.2 %collective-permute-start.19 = (f32[72,16]{1,0:T(8,128)S(1)}, f32[72,16]{1,0:T(8,128)S(1)}, u32[]{:S(2)}, u32[]{:S(2)}) collective-permute-start(f32[72,16]{1,0:T(8,128)S(1)} %add.206), channel_id=1, source_target_pairs={{0,96},{1,97},{2,98},{3,99},{4,100},{5,101},{6,102},{7,103},{8,104... | collective-permute-start | bytes 13832 | tf_op jit(solution)/shard_map/ppermute | solution.py:35
  108.4 1.2 collective-permute-start.20
  109.6 3.6 %collective-permute-start.21 = (f32[16]{0:T(128)S(1)}, f32[16]{0:T(128)S(1)}, u32[]{:S(2)}, u32[]{:S(2)}) collective-permute-start(f32[16]{0:T(128)S(1)} %add.209), channel_id=1, source_target_pairs={{0,2},{1,3},{2,0},{3,1},{4,6},{5,7},{6,4},{7,5},{8,10},{9,11},{10,... | collective-permute-start | bytes 200 | tf_op jit(solution)/shard_map/ppermute | solution.py:35
  113.2 4.8 %collective-permute-start.22 = (f32[16]{0:T(128)S(1)}, f32[16]{0:T(128)S(1)}, u32[]{:S(2)}, u32[]{:S(2)}) collective-permute-start(f32[16]{0:T(128)S(1)} %add.210), channel_id=1, source_target_pairs={{0,6},{1,7},{2,4},{3,5},{4,2},{5,3},{6,0},{7,1},{8,14},{9,15},{10,... | collective-permute-start | bytes 200 | tf_op jit(solution)/shard_map/ppermute | solution.py:35
  118.0 3.6 %collective-permute-start.23 = (f32[16]{0:T(128)S(1)}, f32[16]{0:T(128)S(1)}, u32[]{:S(2)}, u32[]{:S(2)}) collective-permute-start(f32[16]{0:T(128)S(1)} %add.211), channel_id=1, source_target_pairs={{0,8},{1,9},{2,10},{3,11},{4,12},{5,13},{6,14},{7,15},{8,0},{9,1},... | collective-permute-start | bytes 200 | tf_op jit(solution)/shard_map/ppermute | solution.py:35
  121.6 4.8 %collective-permute-start.24 = (f32[16]{0:T(128)S(1)}, f32[16]{0:T(128)S(1)}, u32[]{:S(2)}, u32[]{:S(2)}) collective-permute-start(f32[16]{0:T(128)S(1)} %add.212), channel_id=1, source_target_pairs={{0,24},{1,25},{2,26},{3,27},{4,28},{5,29},{6,30},{7,31},{8,16},{9,... | collective-permute-start | bytes 200 | tf_op jit(solution)/shard_map/ppermute | solution.py:35
  126.4 3.6 %collective-permute-start.25 = (f32[16]{0:T(128)S(1)}, f32[16]{0:T(128)S(1)}, u32[]{:S(2)}, u32[]{:S(2)}) collective-permute-start(f32[16]{0:T(128)S(1)} %add.213), channel_id=1, source_target_pairs={{0,32},{1,33},{2,34},{3,35},{4,36},{5,37},{6,38},{7,39},{8,40},{9,... | collective-permute-start | bytes 200 | tf_op jit(solution)/shard_map/ppermute | solution.py:35
  129.9 4.8 %collective-permute-start.26 = (f32[16]{0:T(128)S(1)}, f32[16]{0:T(128)S(1)}, u32[]{:S(2)}, u32[]{:S(2)}) collective-permute-start(f32[16]{0:T(128)S(1)} %add.214), channel_id=1, source_target_pairs={{0,96},{1,97},{2,98},{3,99},{4,100},{5,101},{6,102},{7,103},{8,104... | collective-permute-start | bytes 200 | tf_op jit(solution)/shard_map/ppermute | solution.py:35

commit v7 on v6

--- a/solution.py
+++ b/solution.py
@@ -55,28 +55,25 @@
 STEPS = 8
 
 
-def accumulate_kernel(slot_ref, near_ref, far_ref, keep_ref, send_ref):
+def accumulate_kernel(slot_ref, near_ref, far_ref, *out_refs):
     i = pl.program_id(0)
-    half = keep_ref.shape[0]
+    piece = out_refs[0].shape[0]
     near_step = near_ref.shape[0]
     far_step = far_ref.shape[0]
     near_total = near_step * pl.num_programs(0)
 
     @pl.when(i == 0)
     def _():
-        keep_ref[...] = jnp.zeros_like(keep_ref)
-        send_ref[...] = jnp.zeros_like(send_ref)
+        for ref in out_refs:
+            ref[...] = jnp.zeros_like(ref)
 
     def add(g, part):
         s = slot_ref[g]
+        for number, ref in enumerate(out_refs):
 
-        @pl.when(s < half)
-        def _():
-            keep_ref[s] += part
-
-        @pl.when(s >= half)
-        def _():
-            send_ref[s - half] += part
+            @pl.when(s // piece == number)
+            def _():
+                ref[s % piece] += part
 
     for j in range(near_step):
         add(i * near_step + j, near_ref[j])
@@ -84,12 +81,13 @@
         add(near_total + i * far_step + j, far_ref[j])
 
 
-def accumulate(slot, near_part, far_part, half):
+def accumulate(slot, near_part, far_part, spots, pieces):
     near_count, sources, size = near_part.shape
     far_count = far_part.shape[0]
     near_step = near_count // STEPS
     far_step = far_count // STEPS
-    out = jax.ShapeDtypeStruct((half, sources, size), jnp.float32)
+    length = spots // pieces
+    out = jax.ShapeDtypeStruct((length, sources, size), jnp.float32)
     grid_spec = pltpu.PrefetchScalarGridSpec(
         num_scalar_prefetch=1,
         grid=(STEPS,),
@@ -97,15 +95,12 @@
             pl.BlockSpec((near_step, sources, size), lambda i, s: (i, 0, 0)),
             pl.BlockSpec((far_step, sources, size), lambda i, s: (i, 0, 0)),
         ],
-        out_specs=[
-            pl.BlockSpec((half, sources, size), lambda i, s: (0, 0, 0)),
-            pl.BlockSpec((half, sources, size), lambda i, s: (0, 0, 0)),
-        ],
+        out_specs=[pl.BlockSpec((length, sources, size), lambda i, s: (0, 0, 0))] * pieces,
     )
     return pl.pallas_call(
         accumulate_kernel,
         grid_spec=grid_spec,
-        out_shape=[out, out],
+        out_shape=[out] * pieces,
         compiler_params=pltpu.CompilerParams(
             dimension_semantics=("arbitrary",), vmem_limit_bytes=48 * 1024 * 1024
         ),
@@ -137,9 +132,10 @@
     order = jnp.where(to_core == 0, rel["x"] * 4 + rel["z"], rel["z"] * 4 + rel["x"])
     slot = ((rel["c"] * 16 + order) * 4 + rel["y"]) * clusters + block_col
     spots = devices * clusters
-    keep, send = accumulate(slot, near_part, far_part, spots // 2)
-    shape = (4, 4, 4, clusters, sources, cluster_size)
-    summed = reduce_to_owner(keep.reshape(shape), send.reshape(shape))
+    parts = accumulate(slot, near_part, far_part, spots, 8)
+    shape = (4, 4, clusters, sources, cluster_size)
+    parts = [p.reshape(shape) for p in parts]
+    summed = reduce_to_owner(parts[:4], parts[4:])
     image = diagonal[:, None, :] * vector + summed
     panels = clusters * cluster_size * devices
     local_first = jnp.einsum("knjc,njc->kj", basis, image, precision=highest)

time: 136 us -> 138 us (1.015)
  Pallas kernels: 6.43 us -> 11.1 us
  local copies, waits for them, and re-layouts: 7.57 us -> 3.11 us
  matrix products: 10.7 us -> 12.5 us
    pallas_call x1, Pallas kernels: 6.43 us -> 11.1 us  [accumulate(): pl.pallas_call(accumulate_kernel, grid_spec=grid_spec, out_shape=[out] *...]
    slice x1 -> x0, local copies, waits for them, and re-layouts: 4.46 us -> none  [reduce_to_owner(): send[k]]
    dot_general x1, matrix products: 2.69 us -> 4.47 us  [on_device(): jnp.einsum('snk,skc->snc', coeff, far_v, preferred_element_type=jnp.float32)]
  transfers between devices with their start and end apart: 27 -> 27, of which waited for: 22 -> 22; matrix products, arithmetic and copies ran while one was open for 2% -> 1% of each run, Pallas kernels for 0% -> 0%
where the time goes in v7:
time: 138 us
  waiting for transfers between devices  68.2 us (49%)
  starting transfers between devices  38.6 us (28%)
  matrix products  12.5 us (9%)
  Pallas kernels  11.1 us (8%)
  other arithmetic  3.69 us (3%)
  local copies, waits for them, and re-layouts  3.11 us (2%)
    ppermute x12, waiting for transfers between devices, all_sum(): v = v + lax.ppermute(v, AXES, flipped(step * STRIDE[axis]))  33.5 us
    ppermute x3, waiting for transfers between devices, reduce_to_owner(): acc = acc + lax.ppermute(pieces[k], AXES, moved('x', k, 'z'))  22.9 us
    ppermute x12, starting transfers between devices, all_sum(): v = v + lax.ppermute(v, AXES, flipped(step * STRIDE[axis]))  19 us
    ppermute x6, starting transfers between devices, spread(): acc = acc + lax.ppermute(pieces[k], AXES, moved(axis, k, other))  12.5 us
    pallas_call x1, Pallas kernels, accumulate(): pl.pallas_call(accumulate_kernel, grid_spec=grid_spec, out_shape=[out] *...  11.1 us
    ppermute x6, waiting for transfers between devices, spread(): acc = acc + lax.ppermute(pieces[k], AXES, moved(axis, k, other))  7.6 us
    ppermute x3, starting transfers between devices, reduce_to_owner(): acc = acc + lax.ppermute(pieces[k], AXES, moved('x', k, 'z'))  5.97 us
    dot_general x1, matrix products, on_device(): jnp.einsum('snk,skc->snc', coeff, far_v, preferred_element_type=jnp.float32)  4.47 us
  transfers between devices with their start and end apart: 27, of which 22 were waited for; matrix products, arithmetic and copies ran while one was open for 1% of the time, Pallas kernels for 0%

profile of v7, /device:TPU:0, one launch (start us, length us, event | category | flops | bytes accessed | tf_op | source)
XLA Modules:
  0.0 138.1 jit_solution(13314593058087772433)
XLA Ops:
  0.7 0.8 bitcast_convert_fusion
  2.9 3.2 %convolution_convert_fusion = bf16[112,16,32]{2,1,0:T(8,128)(2,1)S(1)} fusion(bf16[128,16,512]{2,1,0:T(8,128)(2,1)S(1)} %gather_fusion, bf16[112,32,512]{2,1,0:T(8,128)(2,1)} %param.11), kind=kOutput, calls=%fused_computation.1 | convolution fusion | flops 58777600 | bytes 5881856 | tf_op jit(solution)/shard_map/snc,skc->snk/dot_general | solution.py:125
  6.2 1.2 copy-done.4
  7.4 1.2 fusion.33.near_ref
  8.6 4.5 %fusion.32.far_ref = f32[112,16,512]{2,1,0:T(8,128)} fusion(bf16[112,16,32]{2,1,0:T(8,128)(2,1)S(1)} %convolution_convert_fusion, bf16[112,32,512]{2,1,0:T(8,128)(2,1)} %param.12), kind=kOutput, calls=%fused_computation.93 | convolution fusion | flops 58720256 | bytes 7454720 | tf_op jit(solution)/shard_map/snk,skc->snc/dot_general | solution.py:128
  13.1 11.1 %shard_map.95 = (f32[32,16,512]{2,1,0:T(8,128)S(1)}, f32[32,16,512]{2,1,0:T(8,128)S(1)}, f32[32,16,512]{2,1,0:T(8,128)S(1)}, f32[32,16,512]{2,1,0:T(8,128)S(1)},...) custom-call(s32[128]{0:T(128)S(1)} %multiply_add_fusion.slot_ref, ...), custom_call_target="tpu_custom_call" | custom-call | tf_op jit(solution)/shard_map/pallas_call | solution.py:100
  25.2 1.8 %collective-permute-done.1 = f32[4,4,2,16,512]{4,3,2,1,0:T(8,128)S(1)} collective-permute-done((f32[4,4,2,16,512]{4,3,2,1,0:T(8,128)}, f32[4,4,2,16,512]{4,3,2,1,0:T(8,128)S(1)}, u32[]{:S(2)}, u32[]{:S(2)}) %collective-permute-start.1) | collective-permute-done | bytes 1048608 | tf_op jit(solution)/shard_map/ppermute | solution.py:47
  27.3 1.7 %collective-permute-start.2 = (f32[4,4,2,16,512]{4,3,2,1,0:T(8,128)S(1)}, f32[4,4,2,16,512]{4,3,2,1,0:T(8,128)S(1)}, u32[]{:S(2)}, u32[]{:S(2)}) collective-permute-start(f32[4,4,2,16,512]{4,3,2,1,0:T(8,128)S(1)} %add.188), channel_id=1, source_target_pairs={{0,2},{1,9},{2,4},{3,11},{4,6},{5,13},{6,0},{7,15},{8,10},{9,17},{... | collective-permute-start | bytes 3145736 | tf_op jit(solution)/shard_map/ppermute | solution.py:50
  29.2 2.8 %collective-permute-start.4 = (f32[4,4,2,16,512]{4,3,2,1,0:T(8,128)S(1)}, f32[4,4,2,16,512]{4,3,2,1,0:T(8,128)S(1)}, u32[]{:S(2)}, u32[]{:S(2)}) collective-permute-start(f32[4,4,2,16,512]{4,3,2,1,0:T(8,128)S(1)} %add.190), channel_id=1, source_target_pairs={{0,4},{1,17},{2,6},{3,19},{4,0},{5,21},{6,2},{7,23},{8,12},{9,25},... | collective-permute-start | bytes 3145736 | tf_op jit(solution)/shard_map/ppermute | solution.py:50
  32.2 1.5 %collective-permute-start.6 = (f32[4,4,2,16,512]{4,3,2,1,0:T(8,128)S(1)}, f32[4,4,2,16,512]{4,3,2,1,0:T(8,128)S(1)}, u32[]{:S(2)}, u32[]{:S(2)}) collective-permute-start(f32[4,4,2,16,512]{4,3,2,1,0:T(8,128)S(1)} %add.192), channel_id=1, source_target_pairs={{0,6},{1,25},{2,0},{3,27},{4,2},{5,29},{6,4},{7,31},{8,14},{9,1},{... | collective-permute-start | bytes 3145736 | tf_op jit(solution)/shard_map/ppermute | solution.py:50
  33.7 9.7 %collective-permute-done.2 = f32[4,4,2,16,512]{4,3,2,1,0:T(8,128)S(1)} collective-permute-done((f32[4,4,2,16,512]{4,3,2,1,0:T(8,128)S(1)}, f32[4,4,2,16,512]{4,3,2,1,0:T(8,128)S(1)}, u32[]{:S(2)}, u32[]{:S(2)}) %collective-permute-start.2) | collective-permute-done | bytes 1048608 | tf_op jit(solution)/shard_map/ppermute | solution.py:50
  43.3 12.3 %collective-permute-done.4 = f32[4,4,2,16,512]{4,3,2,1,0:T(8,128)S(1)} collective-permute-done((f32[4,4,2,16,512]{4,3,2,1,0:T(8,128)S(1)}, f32[4,4,2,16,512]{4,3,2,1,0:T(8,128)S(1)}, u32[]{:S(2)}, u32[]{:S(2)}) %collective-permute-start.4) | collective-permute-done | bytes 1048608 | tf_op jit(solution)/shard_map/ppermute | solution.py:50
  55.7 0.9 collective-permute-done.6
  57.4 2.0 %collective-permute-start.7 = (f32[4,2,16,512]{3,2,1,0:T(8,128)S(1)}, f32[4,2,16,512]{3,2,1,0:T(8,128)S(1)}, u32[]{:S(2)}, u32[]{:S(2)}) collective-permute-start(f32[4,2,16,512]{3,2,1,0:T(8,128)S(1)} %get-tuple-element.20), channel_id=1, source_target_pairs={{0,8},{1,3},{2,10},{3,5},{4,12},{5,7},{6,14},{7,1},{8,16},{9,11},{... | collective-permute-start | bytes 786440 | tf_op jit(solution)/shard_map/ppermute | solution.py:42
  59.4 3.6 %collective-permute-start.8 = (f32[4,2,16,512]{3,2,1,0:T(8,128)S(1)}, f32[4,2,16,512]{3,2,1,0:T(8,128)S(1)}, u32[]{:S(2)}, u32[]{:S(2)}) collective-permute-start(f32[4,2,16,512]{3,2,1,0:T(8,128)S(1)} %get-tuple-element.22), channel_id=1, source_target_pairs={{0,16},{1,5},{2,18},{3,7},{4,20},{5,1},{6,22},{7,3},{8,24},{9,13},... | collective-permute-start | bytes 786440 | tf_op jit(solution)/shard_map/ppermute | solution.py:42
  63.0 1.0 collective-permute-start.9
  64.0 1.9 %collective-permute-done.7 = f32[4,2,16,512]{3,2,1,0:T(8,128)S(1)} collective-permute-done((f32[4,2,16,512]{3,2,1,0:T(8,128)S(1)}, f32[4,2,16,512]{3,2,1,0:T(8,128)S(1)}, u32[]{:S(2)}, u32[]{:S(2)}) %collective-permute-start.7) | collective-permute-done | bytes 262176 | tf_op jit(solution)/shard_map/ppermute | solution.py:42
  65.9 4.3 %collective-permute-done.8 = f32[4,2,16,512]{3,2,1,0:T(8,128)S(1)} collective-permute-done((f32[4,2,16,512]{3,2,1,0:T(8,128)S(1)}, f32[4,2,16,512]{3,2,1,0:T(8,128)S(1)}, u32[]{:S(2)}, u32[]{:S(2)}) %collective-permute-start.8) | collective-permute-done | bytes 262176 | tf_op jit(solution)/shard_map/ppermute | solution.py:42
  70.2 1.7 %collective-permute-start.10 = (f32[2,16,512]{2,1,0:T(8,128)S(1)}, f32[2,16,512]{2,1,0:T(8,128)S(1)}, u32[]{:S(2)}, u32[]{:S(2)}) collective-permute-start(f32[2,16,512]{2,1,0:T(8,128)S(1)} %get-tuple-element.23), channel_id=1, source_target_pairs={{0,32},{1,33},{2,34},{3,35},{4,36},{5,37},{6,38},{7,39},{8,40},{9,... | collective-permute-start | bytes 196616 | tf_op jit(solution)/shard_map/ppermute | solution.py:42
  71.9 2.9 %collective-permute-start.11 = (f32[2,16,512]{2,1,0:T(8,128)S(1)}, f32[2,16,512]{2,1,0:T(8,128)S(1)}, u32[]{:S(2)}, u32[]{:S(2)}) collective-permute-start(f32[2,16,512]{2,1,0:T(8,128)S(1)} %get-tuple-element.25), channel_id=1, source_target_pairs={{0,64},{1,65},{2,66},{3,67},{4,68},{5,69},{6,70},{7,71},{8,72},{9,... | collective-permute-start | bytes 196616 | tf_op jit(solution)/shard_map/ppermute | solution.py:42
  74.8 1.4 collective-permute-start.12
  76.2 1.3 convolution_bitcast_fusion
  77.7 1.3 collective-permute-done.12
  79.1 1.5 %fusion.2 = f32[16,1,8,1]{2,1,3,0:T(1,128)S(1)} fusion(f32[8,2,16,512]{3,2,1,0:T(8,128)S(1)} %copy-done, f32[2,16,512,1]{2,1,0,3:T(8,128)S(1)} %bitcast.107), kind=kOutput, calls=%fused_computation.6 | convolution fusion | flops 1572864 | bytes 590336 | tf_op jit(solution)/shard_map/knjc,njc->kj/dot_general | solution.py:141
  80.7 1.2 collective-permute-done.13
  81.9 1.7 %collective-permute-start.14 = (f32[72,16]{1,0:T(8,128)S(1)}, f32[72,16]{1,0:T(8,128)S(1)}, u32[]{:S(2)}, u32[]{:S(2)}) collective-permute-start(f32[72,16]{1,0:T(8,128)S(1)} %fusion.31), channel_id=1, source_target_pairs={{0,2},{1,3},{2,0},{3,1},{4,6},{5,7},{6,4},{7,5},{8,10},{9,11},{10,... | collective-permute-start | bytes 13832 | tf_op jit(solution)/shard_map/ppermute | solution.py:35
  83.6 2.3 %collective-permute-done.14 = f32[72,16]{1,0:T(8,128)S(1)} collective-permute-done((f32[72,16]{1,0:T(8,128)S(1)}, f32[72,16]{1,0:T(8,128)S(1)}, u32[]{:S(2)}, u32[]{:S(2)}) %collective-permute-start.14) | collective-permute-done | bytes 4640 | tf_op jit(solution)/shard_map/ppermute | solution.py:35
  85.9 2.6 %collective-permute-start.15 = (f32[72,16]{1,0:T(8,128)S(1)}, f32[72,16]{1,0:T(8,128)S(1)}, u32[]{:S(2)}, u32[]{:S(2)}) collective-permute-start(f32[72,16]{1,0:T(8,128)S(1)} %add.202), channel_id=1, source_target_pairs={{0,6},{1,7},{2,4},{3,5},{4,2},{5,3},{6,0},{7,1},{8,14},{9,15},{10,... | collective-permute-start | bytes 13832 | tf_op jit(solution)/shard_map/ppermute | solution.py:35
  88.6 2.5 %collective-permute-done.15 = f32[72,16]{1,0:T(8,128)S(1)} collective-permute-done((f32[72,16]{1,0:T(8,128)S(1)}, f32[72,16]{1,0:T(8,128)S(1)}, u32[]{:S(2)}, u32[]{:S(2)}) %collective-permute-start.15) | collective-permute-done | bytes 4640 | tf_op jit(solution)/shard_map/ppermute | solution.py:35
  91.1 1.5 %collective-permute-start.16 = (f32[72,16]{1,0:T(8,128)S(1)}, f32[72,16]{1,0:T(8,128)S(1)}, u32[]{:S(2)}, u32[]{:S(2)}) collective-permute-start(f32[72,16]{1,0:T(8,128)S(1)} %add.203), channel_id=1, source_target_pairs={{0,8},{1,9},{2,10},{3,11},{4,12},{5,13},{6,14},{7,15},{8,0},{9,1},... | collective-permute-start | bytes 13832 | tf_op jit(solution)/shard_map/ppermute | solution.py:35
  92.6 2.4 %collective-permute-done.16 = f32[72,16]{1,0:T(8,128)S(1)} collective-permute-done((f32[72,16]{1,0:T(8,128)S(1)}, f32[72,16]{1,0:T(8,128)S(1)}, u32[]{:S(2)}, u32[]{:S(2)}) %collective-permute-start.16) | collective-permute-done | bytes 4640 | tf_op jit(solution)/shard_map/ppermute | solution.py:35
  95.1 2.2 %collective-permute-start.17 = (f32[72,16]{1,0:T(8,128)S(1)}, f32[72,16]{1,0:T(8,128)S(1)}, u32[]{:S(2)}, u32[]{:S(2)}) collective-permute-start(f32[72,16]{1,0:T(8,128)S(1)} %add.204), channel_id=1, source_target_pairs={{0,24},{1,25},{2,26},{3,27},{4,28},{5,29},{6,30},{7,31},{8,16},{9,... | collective-permute-start | bytes 13832 | tf_op jit(solution)/shard_map/ppermute | solution.py:35
  97.2 3.0 %collective-permute-done.17 = f32[72,16]{1,0:T(8,128)S(1)} collective-permute-done((f32[72,16]{1,0:T(8,128)S(1)}, f32[72,16]{1,0:T(8,128)S(1)}, u32[]{:S(2)}, u32[]{:S(2)}) %collective-permute-start.17) | collective-permute-done | bytes 4640 | tf_op jit(solution)/shard_map/ppermute | solution.py:35
  100.6 3.6 %collective-permute-done.18 = f32[72,16]{1,0:T(8,128)S(1)} collective-permute-done((f32[72,16]{1,0:T(8,128)S(1)}, f32[72,16]{1,0:T(8,128)S(1)}, u32[]{:S(2)}, u32[]{:S(2)}) %collective-permute-start.18) | collective-permute-done | bytes 4640 | tf_op jit(solution)/shard_map/ppermute | solution.py:35
  104.2 2.6 %collective-permute-start.19 = (f32[72,16]{1,0:T(8,128)S(1)}, f32[72,16]{1,0:T(8,128)S(1)}, u32[]{:S(2)}, u32[]{:S(2)}) collective-permute-start(f32[72,16]{1,0:T(8,128)S(1)} %add.206), channel_id=1, source_target_pairs={{0,96},{1,97},{2,98},{3,99},{4,100},{5,101},{6,102},{7,103},{8,104... | collective-permute-start | bytes 13832 | tf_op jit(solution)/shard_map/ppermute | solution.py:35
  106.8 2.6 %collective-permute-done.19 = f32[72,16]{1,0:T(8,128)S(1)} collective-permute-done((f32[72,16]{1,0:T(8,128)S(1)}, f32[72,16]{1,0:T(8,128)S(1)}, u32[]{:S(2)}, u32[]{:S(2)}) %collective-permute-start.19) | collective-permute-done | bytes 4640 | tf_op jit(solution)/shard_map/ppermute | solution.py:35
  109.5 0.8 fusion
  110.5 1.1 collective-permute-done.20
  112.1 3.1 %collective-permute-done.21 = f32[16]{0:T(128)S(1)} collective-permute-done((f32[16]{0:T(128)S(1)}, f32[16]{0:T(128)S(1)}, u32[]{:S(2)}, u32[]{:S(2)}) %collective-permute-start.21) | collective-permute-done | bytes 96 | tf_op jit(solution)/shard_map/ppermute | solution.py:35
  115.3 2.6 %collective-permute-start.22 = (f32[16]{0:T(128)S(1)}, f32[16]{0:T(128)S(1)}, u32[]{:S(2)}, u32[]{:S(2)}) collective-permute-start(f32[16]{0:T(128)S(1)} %add.210), channel_id=1, source_target_pairs={{0,6},{1,7},{2,4},{3,5},{4,2},{5,3},{6,0},{7,1},{8,14},{9,15},{10,... | collective-permute-start | bytes 200 | tf_op jit(solution)/shard_map/ppermute | solution.py:35
  117.9 2.1 %collective-permute-done.22 = f32[16]{0:T(128)S(1)} collective-permute-done((f32[16]{0:T(128)S(1)}, f32[16]{0:T(128)S(1)}, u32[]{:S(2)}, u32[]{:S(2)}) %collective-permute-start.22) | collective-permute-done | bytes 96 | tf_op jit(solution)/shard_map/ppermute | solution.py:35
  120.4 3.3 %collective-permute-done.23 = f32[16]{0:T(128)S(1)} collective-permute-done((f32[16]{0:T(128)S(1)}, f32[16]{0:T(128)S(1)}, u32[]{:S(2)}, u32[]{:S(2)}) %collective-permute-start.23) | collective-permute-done | bytes 96 | tf_op jit(solution)/shard_map/ppermute | solution.py:35
  123.6 2.2 %collective-permute-start.24 = (f32[16]{0:T(128)S(1)}, f32[16]{0:T(128)S(1)}, u32[]{:S(2)}, u32[]{:S(2)}) collective-permute-start(f32[16]{0:T(128)S(1)} %add.212), channel_id=1, source_target_pairs={{0,24},{1,25},{2,26},{3,27},{4,28},{5,29},{6,30},{7,31},{8,16},{9,... | collective-permute-start | bytes 200 | tf_op jit(solution)/shard_map/ppermute | solution.py:35
  125.8 2.6 %collective-permute-done.24 = f32[16]{0:T(128)S(1)} collective-permute-done((f32[16]{0:T(128)S(1)}, f32[16]{0:T(128)S(1)}, u32[]{:S(2)}, u32[]{:S(2)}) %collective-permute-start.24) | collective-permute-done | bytes 96 | tf_op jit(solution)/shard_map/ppermute | solution.py:35
  128.4 3.6 %collective-permute-done.25 = f32[16]{0:T(128)S(1)} collective-permute-done((f32[16]{0:T(128)S(1)}, f32[16]{0:T(128)S(1)}, u32[]{:S(2)}, u32[]{:S(2)}) %collective-permute-start.25) | collective-permute-done | bytes 96 | tf_op jit(solution)/shard_map/ppermute | solution.py:35
  132.0 2.6 %collective-permute-start.26 = (f32[16]{0:T(128)S(1)}, f32[16]{0:T(128)S(1)}, u32[]{:S(2)}, u32[]{:S(2)}) collective-permute-start(f32[16]{0:T(128)S(1)} %add.214), channel_id=1, source_target_pairs={{0,96},{1,97},{2,98},{3,99},{4,100},{5,101},{6,102},{7,103},{8,104... | collective-permute-start | bytes 200 | tf_op jit(solution)/shard_map/ppermute | solution.py:35
  134.6 2.2 %collective-permute-done.26 = f32[16]{0:T(128)S(1)} collective-permute-done((f32[16]{0:T(128)S(1)}, f32[16]{0:T(128)S(1)}, u32[]{:S(2)}, u32[]{:S(2)}) %collective-permute-start.26) | collective-permute-done | bytes 96 | tf_op jit(solution)/shard_map/ppermute | solution.py:35
  136.8 0.7 broadcast_divide_fusion
  (60 shorter events, 6.4 us)
Async XLA Ops:
  2.9 4.5 %copy-start.4 = (bf16[16,512,512]{2,1,0:T(8,128)(2,1)S(1)}, bf16[16,512,512]{2,1,0:T(8,128)(2,1)}, u32[]{:S(2)}) copy-start(bf16[16,512,512]{2,1,0:T(8,128)(2,1)} %param.10) | copy-start | bytes 25165828
  8.6 4.5 %copy-start.2 = (s32[128]{0:T(128)S(1)}, s32[128]{0:T(128)}, u32[]{:S(2)}) copy-start(s32[128]{0:T(128)} %param.15) | copy-start | bytes 1540
  8.6 4.5 %copy-start.3 = (s32[128,1]{0,1:T(1,128)S(1)}, s32[128,1]{0,1:T(1,128)}, u32[]{:S(2)}) copy-start(s32[128,1]{0,1:T(1,128)} %param.14) | copy-start | bytes 1540
  24.2 2.9 %collective-permute-start.1 = (f32[4,4,2,16,512]{4,3,2,1,0:T(8,128)}, f32[4,4,2,16,512]{4,3,2,1,0:T(8,128)S(1)}, u32[]{:S(2)}, u32[]{:S(2)}) collective-permute-start(f32[4,4,2,16,512]{4,3,2,1,0:T(8,128)} %bitcast.116), channel_id=1, source_target_pairs={{0,1},{1,0},{2,3},{3,2},{4,5},{5,4},{6,7},{7,6},{8,9},{9,8},{10,11... | collective-permute-start | bytes 3145736 | tf_op jit(solution)/shard_map/ppermute | solution.py:47
  24.2 4.8 %collective-permute-start.3 = (f32[4,4,2,16,512]{4,3,2,1,0:T(8,128)}, f32[4,4,2,16,512]{4,3,2,1,0:T(8,128)S(1)}, u32[]{:S(2)}, u32[]{:S(2)}) collective-permute-start(f32[4,4,2,16,512]{4,3,2,1,0:T(8,128)} %bitcast.115), channel_id=1, source_target_pairs={{0,1},{1,0},{2,3},{3,2},{4,5},{5,4},{6,7},{7,6},{8,9},{9,8},{10,11... | collective-permute-start | bytes 3145736 | tf_op jit(solution)/shard_map/ppermute | solution.py:47
  24.7 7.3 %collective-permute-start.5 = (f32[4,4,2,16,512]{4,3,2,1,0:T(8,128)}, f32[4,4,2,16,512]{4,3,2,1,0:T(8,128)S(1)}, u32[]{:S(2)}, u32[]{:S(2)}) collective-permute-start(f32[4,4,2,16,512]{4,3,2,1,0:T(8,128)} %bitcast.114), channel_id=1, source_target_pairs={{0,1},{1,0},{2,3},{3,2},{4,5},{5,4},{6,7},{7,6},{8,9},{9,8},{10,11... | collective-permute-start | bytes 3145736 | tf_op jit(solution)/shard_map/ppermute | solution.py:47
  24.7 9.0 %collective-permute-start = (f32[4,4,2,16,512]{4,3,2,1,0:T(8,128)S(1)}, f32[4,4,2,16,512]{4,3,2,1,0:T(8,128)S(1)}, u32[]{:S(2)}, u32[]{:S(2)}) collective-permute-start(f32[4,4,2,16,512]{4,3,2,1,0:T(8,128)S(1)} %bitcast.106), channel_id=1, source_target_pairs={{0,1},{1,0},{2,3},{3,2},{4,5},{5,4},{6,7},{7,6},{8,9},{9,8},{10,11... | collective-permute-start | bytes 3145736 | tf_op jit(solution)/shard_map/ppermute | solution.py:47
  27.3 16.1 %collective-permute-start.2 = (f32[4,4,2,16,512]{4,3,2,1,0:T(8,128)S(1)}, f32[4,4,2,16,512]{4,3,2,1,0:T(8,128)S(1)}, u32[]{:S(2)}, u32[]{:S(2)}) collective-permute-start(f32[4,4,2,16,512]{4,3,2,1,0:T(8,128)S(1)} %add.188), channel_id=1, source_target_pairs={{0,2},{1,9},{2,4},{3,11},{4,6},{5,13},{6,0},{7,15},{8,10},{9,17},{... | collective-permute-start | bytes 3145736 | tf_op jit(solution)/shard_map/ppermute | solution.py:50
  29.2 26.5 %collective-permute-start.4 = (f32[4,4,2,16,512]{4,3,2,1,0:T(8,128)S(1)}, f32[4,4,2,16,512]{4,3,2,1,0:T(8,128)S(1)}, u32[]{:S(2)}, u32[]{:S(2)}) collective-permute-start(f32[4,4,2,16,512]{4,3,2,1,0:T(8,128)S(1)} %add.190), channel_id=1, source_target_pairs={{0,4},{1,17},{2,6},{3,19},{4,0},{5,21},{6,2},{7,23},{8,12},{9,25},... | collective-permute-start | bytes 3145736 | tf_op jit(solution)/shard_map/ppermute | solution.py:50
  32.2 24.4 %collective-permute-start.6 = (f32[4,4,2,16,512]{4,3,2,1,0:T(8,128)S(1)}, f32[4,4,2,16,512]{4,3,2,1,0:T(8,128)S(1)}, u32[]{:S(2)}, u32[]{:S(2)}) collective-permute-start(f32[4,4,2,16,512]{4,3,2,1,0:T(8,128)S(1)} %add.192), channel_id=1, source_target_pairs={{0,6},{1,25},{2,0},{3,27},{4,2},{5,29},{6,4},{7,31},{8,14},{9,1},{... | collective-permute-start | bytes 3145736 | tf_op jit(solution)/shard_map/ppermute | solution.py:50
  56.6 19.5 %copy-start = (f32[8,2,16,512]{3,2,1,0:T(8,128)S(1)}, f32[8,2,16,512]{3,2,1,0:T(8,128)}, u32[]{:S(2)}) copy-start(f32[8,2,16,512]{3,2,1,0:T(8,128)} %param.8) | copy-start | bytes 1572868
  56.6 22.4 %copy-start.1 = (f32[2,512]{1,0:T(2,128)S(1)}, f32[2,512]{1,0:T(2,128)}, u32[]{:S(2)}) copy-start(f32[2,512]{1,0:T(2,128)} %param.9) | copy-start | bytes 12292
  57.4 8.5 %collective-permute-start.7 = (f32[4,2,16,512]{3,2,1,0:T(8,128)S(1)}, f32[4,2,16,512]{3,2,1,0:T(8,128)S(1)}, u32[]{:S(2)}, u32[]{:S(2)}) collective-permute-start(f32[4,2,16,512]{3,2,1,0:T(8,128)S(1)} %get-tuple-element.20), channel_id=1, source_target_pairs={{0,8},{1,3},{2,10},{3,5},{4,12},{5,7},{6,14},{7,1},{8,16},{9,11},{... | collective-permute-start | bytes 786440 | tf_op jit(solution)/shard_map/ppermute | solution.py:42
  59.4 10.7 %collective-permute-start.8 = (f32[4,2,16,512]{3,2,1,0:T(8,128)S(1)}, f32[4,2,16,512]{3,2,1,0:T(8,128)S(1)}, u32[]{:S(2)}, u32[]{:S(2)}) collective-permute-start(f32[4,2,16,512]{3,2,1,0:T(8,128)S(1)} %get-tuple-element.22), channel_id=1, source_target_pairs={{0,16},{1,5},{2,18},{3,7},{4,20},{5,1},{6,22},{7,3},{8,24},{9,13},... | collective-permute-start | bytes 786440 | tf_op jit(solution)/shard_map/ppermute | solution.py:42
  63.0 7.2 %collective-permute-start.9 = (f32[4,2,16,512]{3,2,1,0:T(8,128)S(1)}, f32[4,2,16,512]{3,2,1,0:T(8,128)S(1)}, u32[]{:S(2)}, u32[]{:S(2)}) collective-permute-start(f32[4,2,16,512]{3,2,1,0:T(8,128)S(1)} %get-tuple-element.21), channel_id=1, source_target_pairs={{0,24},{1,7},{2,26},{3,1},{4,28},{5,3},{6,30},{7,5},{8,0},{9,15},{... | collective-permute-start | bytes 786440 | tf_op jit(solution)/shard_map/ppermute | solution.py:42
  70.2 7.3 %collective-permute-start.10 = (f32[2,16,512]{2,1,0:T(8,128)S(1)}, f32[2,16,512]{2,1,0:T(8,128)S(1)}, u32[]{:S(2)}, u32[]{:S(2)}) collective-permute-start(f32[2,16,512]{2,1,0:T(8,128)S(1)} %get-tuple-element.23), channel_id=1, source_target_pairs={{0,32},{1,33},{2,34},{3,35},{4,36},{5,37},{6,38},{7,39},{8,40},{9,... | collective-permute-start | bytes 196616 | tf_op jit(solution)/shard_map/ppermute | solution.py:42
  71.9 5.8 %collective-permute-start.11 = (f32[2,16,512]{2,1,0:T(8,128)S(1)}, f32[2,16,512]{2,1,0:T(8,128)S(1)}, u32[]{:S(2)}, u32[]{:S(2)}) collective-permute-start(f32[2,16,512]{2,1,0:T(8,128)S(1)} %get-tuple-element.25), channel_id=1, source_target_pairs={{0,64},{1,65},{2,66},{3,67},{4,68},{5,69},{6,70},{7,71},{8,72},{9,... | collective-permute-start | bytes 196616 | tf_op jit(solution)/shard_map/ppermute | solution.py:42
  74.8 4.3 %collective-permute-start.12 = (f32[2,16,512]{2,1,0:T(8,128)S(1)}, f32[2,16,512]{2,1,0:T(8,128)S(1)}, u32[]{:S(2)}, u32[]{:S(2)}) collective-permute-start(f32[2,16,512]{2,1,0:T(8,128)S(1)} %get-tuple-element.24), channel_id=1, source_target_pairs={{0,96},{1,97},{2,98},{3,99},{4,100},{5,101},{6,102},{7,103},{8,104... | collective-permute-start | bytes 196616 | tf_op jit(solution)/shard_map/ppermute | solution.py:42
  80.6 1.2 collective-permute-start.13
  81.9 4.0 %collective-permute-start.14 = (f32[72,16]{1,0:T(8,128)S(1)}, f32[72,16]{1,0:T(8,128)S(1)}, u32[]{:S(2)}, u32[]{:S(2)}) collective-permute-start(f32[72,16]{1,0:T(8,128)S(1)} %fusion.31), channel_id=1, source_target_pairs={{0,2},{1,3},{2,0},{3,1},{4,6},{5,7},{6,4},{7,5},{8,10},{9,11},{10,... | collective-permute-start | bytes 13832 | tf_op jit(solution)/shard_map/ppermute | solution.py:35
  85.9 5.2 %collective-permute-start.15 = (f32[72,16]{1,0:T(8,128)S(1)}, f32[72,16]{1,0:T(8,128)S(1)}, u32[]{:S(2)}, u32[]{:S(2)}) collective-permute-start(f32[72,16]{1,0:T(8,128)S(1)} %add.202), channel_id=1, source_target_pairs={{0,6},{1,7},{2,4},{3,5},{4,2},{5,3},{6,0},{7,1},{8,14},{9,15},{10,... | collective-permute-start | bytes 13832 | tf_op jit(solution)/shard_map/ppermute | solution.py:35
  91.1 4.0 %collective-permute-start.16 = (f32[72,16]{1,0:T(8,128)S(1)}, f32[72,16]{1,0:T(8,128)S(1)}, u32[]{:S(2)}, u32[]{:S(2)}) collective-permute-start(f32[72,16]{1,0:T(8,128)S(1)} %add.203), channel_id=1, source_target_pairs={{0,8},{1,9},{2,10},{3,11},{4,12},{5,13},{6,14},{7,15},{8,0},{9,1},... | collective-permute-start | bytes 13832 | tf_op jit(solution)/shard_map/ppermute | solution.py:35
  95.1 5.2 %collective-permute-start.17 = (f32[72,16]{1,0:T(8,128)S(1)}, f32[72,16]{1,0:T(8,128)S(1)}, u32[]{:S(2)}, u32[]{:S(2)}) collective-permute-start(f32[72,16]{1,0:T(8,128)S(1)} %add.204), channel_id=1, source_target_pairs={{0,24},{1,25},{2,26},{3,27},{4,28},{5,29},{6,30},{7,31},{8,16},{9,... | collective-permute-start | bytes 13832 | tf_op jit(solution)/shard_map/ppermute | solution.py:35
  100.2 4.0 %collective-permute-start.18 = (f32[72,16]{1,0:T(8,128)S(1)}, f32[72,16]{1,0:T(8,128)S(1)}, u32[]{:S(2)}, u32[]{:S(2)}) collective-permute-start(f32[72,16]{1,0:T(8,128)S(1)} %add.205), channel_id=1, source_target_pairs={{0,32},{1,33},{2,34},{3,35},{4,36},{5,37},{6,38},{7,39},{8,40},{9,... | collective-permute-start | bytes 13832 | tf_op jit(solution)/shard_map/ppermute | solution.py:35
  104.2 5.2 %collective-permute-start.19 = (f32[72,16]{1,0:T(8,128)S(1)}, f32[72,16]{1,0:T(8,128)S(1)}, u32[]{:S(2)}, u32[]{:S(2)}) collective-permute-start(f32[72,16]{1,0:T(8,128)S(1)} %add.206), channel_id=1, source_target_pairs={{0,96},{1,97},{2,98},{3,99},{4,100},{5,101},{6,102},{7,103},{8,104... | collective-permute-start | bytes 13832 | tf_op jit(solution)/shard_map/ppermute | solution.py:35
  110.5 1.2 collective-permute-start.20
  111.7 3.6 %collective-permute-start.21 = (f32[16]{0:T(128)S(1)}, f32[16]{0:T(128)S(1)}, u32[]{:S(2)}, u32[]{:S(2)}) collective-permute-start(f32[16]{0:T(128)S(1)} %add.209), channel_id=1, source_target_pairs={{0,2},{1,3},{2,0},{3,1},{4,6},{5,7},{6,4},{7,5},{8,10},{9,11},{10,... | collective-permute-start | bytes 200 | tf_op jit(solution)/shard_map/ppermute | solution.py:35
  115.3 4.8 %collective-permute-start.22 = (f32[16]{0:T(128)S(1)}, f32[16]{0:T(128)S(1)}, u32[]{:S(2)}, u32[]{:S(2)}) collective-permute-start(f32[16]{0:T(128)S(1)} %add.210), channel_id=1, source_target_pairs={{0,6},{1,7},{2,4},{3,5},{4,2},{5,3},{6,0},{7,1},{8,14},{9,15},{10,... | collective-permute-start | bytes 200 | tf_op jit(solution)/shard_map/ppermute | solution.py:35
  120.0 3.6 %collective-permute-start.23 = (f32[16]{0:T(128)S(1)}, f32[16]{0:T(128)S(1)}, u32[]{:S(2)}, u32[]{:S(2)}) collective-permute-start(f32[16]{0:T(128)S(1)} %add.211), channel_id=1, source_target_pairs={{0,8},{1,9},{2,10},{3,11},{4,12},{5,13},{6,14},{7,15},{8,0},{9,1},... | collective-permute-start | bytes 200 | tf_op jit(solution)/shard_map/ppermute | solution.py:35
  123.6 4.8 %collective-permute-start.24 = (f32[16]{0:T(128)S(1)}, f32[16]{0:T(128)S(1)}, u32[]{:S(2)}, u32[]{:S(2)}) collective-permute-start(f32[16]{0:T(128)S(1)} %add.212), channel_id=1, source_target_pairs={{0,24},{1,25},{2,26},{3,27},{4,28},{5,29},{6,30},{7,31},{8,16},{9,... | collective-permute-start | bytes 200 | tf_op jit(solution)/shard_map/ppermute | solution.py:35
  128.4 3.6 %collective-permute-start.25 = (f32[16]{0:T(128)S(1)}, f32[16]{0:T(128)S(1)}, u32[]{:S(2)}, u32[]{:S(2)}) collective-permute-start(f32[16]{0:T(128)S(1)} %add.213), channel_id=1, source_target_pairs={{0,32},{1,33},{2,34},{3,35},{4,36},{5,37},{6,38},{7,39},{8,40},{9,... | collective-permute-start | bytes 200 | tf_op jit(solution)/shard_map/ppermute | solution.py:35
  132.0 4.8 %collective-permute-start.26 = (f32[16]{0:T(128)S(1)}, f32[16]{0:T(128)S(1)}, u32[]{:S(2)}, u32[]{:S(2)}) collective-permute-start(f32[16]{0:T(128)S(1)} %add.214), channel_id=1, source_target_pairs={{0,96},{1,97},{2,98},{3,99},{4,100},{5,101},{6,102},{7,103},{8,104... | collective-permute-start | bytes 200 | tf_op jit(solution)/shard_map/ppermute | solution.py:35

commit v8 on v6

--- a/solution.py
+++ b/solution.py
@@ -144,13 +144,25 @@
     panels = clusters * cluster_size * devices
     local_first = jnp.einsum("knjc,njc->kj", basis, image, precision=highest)
     local_gram = jnp.einsum("knjc,mnjc->kmj", basis, basis, precision=highest)
-    both = all_sum(jnp.concatenate([local_first, local_gram.reshape(-1, sources)], axis=0))
+    local_size = jnp.sum(image * image, axis=(0, 2))[None, :]
+    both = all_sum(
+        jnp.concatenate([local_first, local_gram.reshape(-1, sources), local_size], axis=0)
+    )
     first = both[:basis_count] / panels
-    gram = both[basis_count:].reshape(basis_count, basis_count, sources) / panels
+    gram = both[basis_count:-1].reshape(basis_count, basis_count, sources) / panels
+    size = both[-1] / panels
     second = first - jnp.einsum("kmj,mj->kj", gram, first, precision=highest)
     total = first + second
     twice = image - jnp.einsum("kj,knjc->njc", total, basis, precision=highest)
-    square = all_sum(jnp.sum(twice * twice, axis=(0, 2))) / panels
+    cross = jnp.sum(total * first, axis=0)
+    curve = jnp.sum(total * jnp.einsum("kmj,mj->kj", gram, total, precision=highest), axis=0)
+    formula = size - 2.0 * cross + curve
+    trusted = jnp.all(formula >= 0.01 * (size + 2.0 * jnp.abs(cross) + jnp.abs(curve)))
+    square = lax.cond(
+        trusted,
+        lambda: formula,
+        lambda: all_sum(jnp.sum(twice * twice, axis=(0, 2))) / panels,
+    )
     beta = jnp.sqrt(square + 1e-06)
     next_vector = twice / beta[None, :, None]
     hess_column = jnp.concatenate([total, beta[None, :]], axis=0)

time: 136 us -> 112 us (0.82)
  waiting for transfers between devices: 68.1 us -> 50.2 us
  starting transfers between devices: 38.6 us -> 30.5 us
    ppermute x12 -> x6, waiting for transfers between devices: 33.5 us -> 16.8 us  [all_sum(): v = v + lax.ppermute(v, AXES, flipped(step * STRIDE[axis]))]
    ppermute x12 -> x6, starting transfers between devices: 19 us -> 10.9 us  [all_sum(): v = v + lax.ppermute(v, AXES, flipped(step * STRIDE[axis]))]
  transfers between devices with their start and end apart: 27 -> 20, of which waited for: 22 -> 15; matrix products, arithmetic and copies ran while one was open for 2% -> 2% of each run, Pallas kernels for 0% -> 0%
where the time goes in v8:
time: 112 us; the launch traced here: 111 us
  waiting for transfers between devices  50.2 us (45%)
  starting transfers between devices  30.5 us (27%)
  matrix products  10.7 us (10%)
  local copies, waits for them, and re-layouts  7.57 us (7%)
  Pallas kernels  6.39 us (6%)
  other arithmetic  4.36 us (4%)
  between operations  1.56 us (1%)
    ppermute x3, waiting for transfers between devices, reduce_to_owner(): acc = acc + lax.ppermute(pieces[k], AXES, moved('x', k, 'z'))  22.9 us
    ppermute x6, waiting for transfers between devices, all_sum(): v = v + lax.ppermute(v, AXES, flipped(step * STRIDE[axis]))  16.8 us
    ppermute x6, starting transfers between devices, spread(): acc = acc + lax.ppermute(pieces[k], AXES, moved(axis, k, other))  12.5 us
    ppermute x6, starting transfers between devices, all_sum(): v = v + lax.ppermute(v, AXES, flipped(step * STRIDE[axis]))  10.9 us
    ppermute x6, waiting for transfers between devices, spread(): acc = acc + lax.ppermute(pieces[k], AXES, moved(axis, k, other))  7.63 us
    pallas_call x1, Pallas kernels, accumulate(): pl.pallas_call(accumulate_kernel, grid_spec=grid_spec, out_shape=[out, ou...  6.39 us
    ppermute x3, starting transfers between devices, reduce_to_owner(): acc = acc + lax.ppermute(pieces[k], AXES, moved('x', k, 'z'))  5.99 us
    slice x1, local copies, waits for them, and re-layouts, reduce_to_owner(): send[k]  4.46 us
  transfers between devices with their start and end apart: 20, of which 15 were waited for; matrix products, arithmetic and copies ran while one was open for 2% of the time, Pallas kernels for 0%

profile of v8, /device:TPU:0, one launch (start us, length us, event | category | flops | bytes accessed | tf_op | source)
XLA Modules:
  0.0 111.3 jit_solution(16316530793509271119)
XLA Ops:
  0.7 0.8 bitcast_convert_fusion
  1.6 0.7 compare_select_fusion
  2.2 0.7 gather_fusion
  2.9 3.2 %convolution_convert_fusion = bf16[112,16,32]{2,1,0:T(8,128)(2,1)S(1)} fusion(bf16[128,16,512]{2,1,0:T(8,128)(2,1)S(1)} %gather_fusion, bf16[112,32,512]{2,1,0:T(8,128)(2,1)} %param.13), kind=kOutput, calls=%fused_computation.3 | convolution fusion | flops 58777600 | bytes 5881856 | tf_op jit(solution)/shard_map/snc,skc->snk/dot_general | solution.py:130
  6.2 1.2 %copy-done.4 = bf16[16,512,512]{2,1,0:T(8,128)(2,1)S(1)} copy-done((bf16[16,512,512]{2,1,0:T(8,128)(2,1)S(1)}, bf16[16,512,512]{2,1,0:T(8,128)(2,1)}, u32[]{:S(2)}) %copy-start.4) | copy-done | bytes 8388632
  7.4 1.2 %fusion.37.near_ref = f32[16,16,512]{2,1,0:T(8,128)S(1)} fusion(bf16[128,16,512]{2,1,0:T(8,128)(2,1)S(1)} %gather_fusion, bf16[16,512,512]{2,1,0:T(8,128)(2,1)S(1)} %copy-done.4), kind=kOutput, calls=%fused_computation.106 | convolution fusion | flops 134217728 | bytes 11010048 | tf_op jit(solution)/shard_map/snc,scd->snd/dot_general | solution.py:127
  8.6 2.7 %fusion.36.far_ref = f32[112,16,512]{2,1,0:T(8,128)S(1)} fusion(bf16[112,16,32]{2,1,0:T(8,128)(2,1)S(1)} %convolution_convert_fusion, bf16[112,32,512]{2,1,0:T(8,128)(2,1)} %param.14), kind=kOutput, calls=%fused_computation.105 | convolution fusion | flops 58720256 | bytes 7454720 | tf_op jit(solution)/shard_map/snk,skc->snc/dot_general | solution.py:133
  11.3 6.4 %shard_map.95 = (f32[128,16,512]{2,1,0:T(8,128)}, f32[128,16,512]{2,1,0:T(8,128)}) custom-call(s32[128]{0:T(128)S(1)} %multiply_add_fusion.slot_ref, f32[16,16,512]{2,1,0:T(8,128)S(1)} %fusion.37.near_ref, f32[112,16,512]{2,1,0:T(8,128)S(1)} %fusion.36.far_ref), custom_call_target="tpu_custom_call" | custom-call | tf_op jit(solution)/shard_map/pallas_call | solution.py:105
  17.7 4.5 %fusion.34 = (f32[32,16,512]{2,1,0:T(8,128)S(1)}, f32[32,16,512]{2,1,0:T(8,128)S(1)}, f32[32,16,512]{2,1,0:T(8,128)S(1)}, f32[32,16,512]{2,1,0:T(8,128)S(1)}, f3...) fusion(f32[128,16,512]{2,1,0:T(8,128)} %get-tuple-element.10, ...), kind=kLoop, calls=%fused_computation.103 | loop fusion | bytes 16777216 | tf_op jit(solution)/shard_map/slice | solution.py:47
  22.3 0.5 collective-permute-start.10
  22.9 0.4 collective-permute-start.7
  23.3 1.6 %collective-permute-done.8 = f32[4,4,2,16,512]{4,3,2,1,0:T(8,128)S(1)} collective-permute-done((f32[4,4,2,16,512]{4,3,2,1,0:T(8,128)S(1)}, f32[4,4,2,16,512]{4,3,2,1,0:T(8,128)S(1)}, u32[]{:S(2)}, u32[]{:S(2)}) %collective-permute-start.8) | collective-permute-done | bytes 1048608 | tf_op jit(solution)/shard_map/ppermute | solution.py:47
  25.2 1.7 %collective-permute-start.9 = (f32[4,4,2,16,512]{4,3,2,1,0:T(8,128)S(1)}, f32[4,4,2,16,512]{4,3,2,1,0:T(8,128)S(1)}, u32[]{:S(2)}, u32[]{:S(2)}) collective-permute-start(f32[4,4,2,16,512]{4,3,2,1,0:T(8,128)S(1)} %add.200), channel_id=1, source_target_pairs={{0,2},{1,9},{2,4},{3,11},{4,6},{5,13},{6,0},{7,15},{8,10},{9,17},{... | collective-permute-start | bytes 3145736 | tf_op jit(solution)/shard_map/ppermute | solution.py:50
  27.1 2.8 %collective-permute-start.11 = (f32[4,4,2,16,512]{4,3,2,1,0:T(8,128)S(1)}, f32[4,4,2,16,512]{4,3,2,1,0:T(8,128)S(1)}, u32[]{:S(2)}, u32[]{:S(2)}) collective-permute-start(f32[4,4,2,16,512]{4,3,2,1,0:T(8,128)S(1)} %add.202), channel_id=1, source_target_pairs={{0,4},{1,17},{2,6},{3,19},{4,0},{5,21},{6,2},{7,23},{8,12},{9,25},... | collective-permute-start | bytes 3145736 | tf_op jit(solution)/shard_map/ppermute | solution.py:50
  29.9 0.2 add.204
  30.1 1.5 %collective-permute-start.13 = (f32[4,4,2,16,512]{4,3,2,1,0:T(8,128)S(1)}, f32[4,4,2,16,512]{4,3,2,1,0:T(8,128)S(1)}, u32[]{:S(2)}, u32[]{:S(2)}) collective-permute-start(f32[4,4,2,16,512]{4,3,2,1,0:T(8,128)S(1)} %add.204), channel_id=1, source_target_pairs={{0,6},{1,25},{2,0},{3,27},{4,2},{5,29},{6,4},{7,31},{8,14},{9,1},{... | collective-permute-start | bytes 3145736 | tf_op jit(solution)/shard_map/ppermute | solution.py:50
  31.6 9.7 %collective-permute-done.9 = f32[4,4,2,16,512]{4,3,2,1,0:T(8,128)S(1)} collective-permute-done((f32[4,4,2,16,512]{4,3,2,1,0:T(8,128)S(1)}, f32[4,4,2,16,512]{4,3,2,1,0:T(8,128)S(1)}, u32[]{:S(2)}, u32[]{:S(2)}) %collective-permute-start.9) | collective-permute-done | bytes 1048608 | tf_op jit(solution)/shard_map/ppermute | solution.py:50
  41.2 12.3 %collective-permute-done.11 = f32[4,4,2,16,512]{4,3,2,1,0:T(8,128)S(1)} collective-permute-done((f32[4,4,2,16,512]{4,3,2,1,0:T(8,128)S(1)}, f32[4,4,2,16,512]{4,3,2,1,0:T(8,128)S(1)}, u32[]{:S(2)}, u32[]{:S(2)}) %collective-permute-start.11) | collective-permute-done | bytes 1048608 | tf_op jit(solution)/shard_map/ppermute | solution.py:50
  53.6 0.9 collective-permute-done.13
  54.5 0.7 add_add_fusion
  55.3 2.0 %collective-permute-start.14 = (f32[4,2,16,512]{3,2,1,0:T(8,128)S(1)}, f32[4,2,16,512]{3,2,1,0:T(8,128)S(1)}, u32[]{:S(2)}, u32[]{:S(2)}) collective-permute-start(f32[4,2,16,512]{3,2,1,0:T(8,128)S(1)} %get-tuple-element.25), channel_id=1, source_target_pairs={{0,8},{1,3},{2,10},{3,5},{4,12},{5,7},{6,14},{7,1},{8,16},{9,11},{... | collective-permute-start | bytes 786440 | tf_op jit(solution)/shard_map/ppermute | solution.py:42
  57.3 3.6 %collective-permute-start.15 = (f32[4,2,16,512]{3,2,1,0:T(8,128)S(1)}, f32[4,2,16,512]{3,2,1,0:T(8,128)S(1)}, u32[]{:S(2)}, u32[]{:S(2)}) collective-permute-start(f32[4,2,16,512]{3,2,1,0:T(8,128)S(1)} %get-tuple-element.27), channel_id=1, source_target_pairs={{0,16},{1,5},{2,18},{3,7},{4,20},{5,1},{6,22},{7,3},{8,24},{9,13},... | collective-permute-start | bytes 786440 | tf_op jit(solution)/shard_map/ppermute | solution.py:42
  60.9 1.0 collective-permute-start.16
  61.9 1.9 %collective-permute-done.14 = f32[4,2,16,512]{3,2,1,0:T(8,128)S(1)} collective-permute-done((f32[4,2,16,512]{3,2,1,0:T(8,128)S(1)}, f32[4,2,16,512]{3,2,1,0:T(8,128)S(1)}, u32[]{:S(2)}, u32[]{:S(2)}) %collective-permute-start.14) | collective-permute-done | bytes 262176 | tf_op jit(solution)/shard_map/ppermute | solution.py:42
  63.8 4.3 %collective-permute-done.15 = f32[4,2,16,512]{3,2,1,0:T(8,128)S(1)} collective-permute-done((f32[4,2,16,512]{3,2,1,0:T(8,128)S(1)}, f32[4,2,16,512]{3,2,1,0:T(8,128)S(1)}, u32[]{:S(2)}, u32[]{:S(2)}) %collective-permute-start.15) | collective-permute-done | bytes 262176 | tf_op jit(solution)/shard_map/ppermute | solution.py:42
  68.2 1.6 %collective-permute-start.17 = (f32[2,16,512]{2,1,0:T(8,128)S(1)}, f32[2,16,512]{2,1,0:T(8,128)S(1)}, u32[]{:S(2)}, u32[]{:S(2)}) collective-permute-start(f32[2,16,512]{2,1,0:T(8,128)S(1)} %get-tuple-element.28), channel_id=1, source_target_pairs={{0,32},{1,33},{2,34},{3,35},{4,36},{5,37},{6,38},{7,39},{8,40},{9,... | collective-permute-start | bytes 196616 | tf_op jit(solution)/shard_map/ppermute | solution.py:42
  69.8 2.9 %collective-permute-start.18 = (f32[2,16,512]{2,1,0:T(8,128)S(1)}, f32[2,16,512]{2,1,0:T(8,128)S(1)}, u32[]{:S(2)}, u32[]{:S(2)}) collective-permute-start(f32[2,16,512]{2,1,0:T(8,128)S(1)} %get-tuple-element.30), channel_id=1, source_target_pairs={{0,64},{1,65},{2,66},{3,67},{4,68},{5,69},{6,70},{7,71},{8,72},{9,... | collective-permute-start | bytes 196616 | tf_op jit(solution)/shard_map/ppermute | solution.py:42
  72.7 1.3 %collective-permute-start.19 = (f32[2,16,512]{2,1,0:T(8,128)S(1)}, f32[2,16,512]{2,1,0:T(8,128)S(1)}, u32[]{:S(2)}, u32[]{:S(2)}) collective-permute-start(f32[2,16,512]{2,1,0:T(8,128)S(1)} %get-tuple-element.29), channel_id=1, source_target_pairs={{0,96},{1,97},{2,98},{3,99},{4,100},{5,101},{6,102},{7,103},{8,104... | collective-permute-start | bytes 196616 | tf_op jit(solution)/shard_map/ppermute | solution.py:42
  74.1 1.3 %convolution_bitcast_fusion = f32[8,8,16]{0,1,2:T(8,128)S(1)} fusion(f32[8,2,16,512]{3,2,1,0:T(8,128)S(1)} %copy-done), kind=kOutput, calls=%fused_computation.4 | convolution fusion | flops 12582912 | bytes 528384 | tf_op jit(solution)/shard_map/knjc,mnjc->kmj/dot_general | solution.py:146
  75.6 1.3 %collective-permute-done.19 = f32[2,16,512]{2,1,0:T(8,128)S(1)} collective-permute-done((f32[2,16,512]{2,1,0:T(8,128)S(1)}, f32[2,16,512]{2,1,0:T(8,128)S(1)}, u32[]{:S(2)}, u32[]{:S(2)}) %collective-permute-start.19) | collective-permute-done | bytes 65568 | tf_op jit(solution)/shard_map/ppermute | solution.py:42
  77.1 1.5 %fusion.2 = f32[16,1,8,1]{2,1,3,0:T(1,128)S(1)} fusion(f32[8,2,16,512]{3,2,1,0:T(8,128)S(1)} %copy-done, f32[2,16,512,1]{2,1,0,3:T(8,128)S(1)} %bitcast.125), kind=kOutput, calls=%fused_computation.8 | convolution fusion | flops 1572864 | bytes 590336 | tf_op jit(solution)/shard_map/knjc,njc->kj/dot_general | solution.py:145
  78.7 1.2 %collective-permute-done.20 = f32[73,16]{1,0:T(8,128)S(1)} collective-permute-done((f32[73,16]{1,0:T(8,128)S(1)}, f32[73,16]{1,0:T(8,128)S(1)}, u32[]{:S(2)}, u32[]{:S(2)}) %collective-permute-start.20) | collective-permute-done | bytes 4704 | tf_op jit(solution)/shard_map/ppermute | solution.py:32
  79.9 1.7 %collective-permute-start.21 = (f32[73,16]{1,0:T(8,128)S(1)}, f32[73,16]{1,0:T(8,128)S(1)}, u32[]{:S(2)}, u32[]{:S(2)}) collective-permute-start(f32[73,16]{1,0:T(8,128)S(1)} %fusion.32), channel_id=1, source_target_pairs={{0,2},{1,3},{2,0},{3,1},{4,6},{5,7},{6,4},{7,5},{8,10},{9,11},{10,... | collective-permute-start | bytes 14024 | tf_op jit(solution)/shard_map/ppermute | solution.py:35
  81.6 2.4 %collective-permute-done.21 = f32[73,16]{1,0:T(8,128)S(1)} collective-permute-done((f32[73,16]{1,0:T(8,128)S(1)}, f32[73,16]{1,0:T(8,128)S(1)}, u32[]{:S(2)}, u32[]{:S(2)}) %collective-permute-start.21) | collective-permute-done | bytes 4704 | tf_op jit(solution)/shard_map/ppermute | solution.py:35
  84.0 2.6 %collective-permute-start.22 = (f32[73,16]{1,0:T(8,128)S(1)}, f32[73,16]{1,0:T(8,128)S(1)}, u32[]{:S(2)}, u32[]{:S(2)}) collective-permute-start(f32[73,16]{1,0:T(8,128)S(1)} %add.214), channel_id=1, source_target_pairs={{0,6},{1,7},{2,4},{3,5},{4,2},{5,3},{6,0},{7,1},{8,14},{9,15},{10,... | collective-permute-start | bytes 14024 | tf_op jit(solution)/shard_map/ppermute | solution.py:35
  86.6 2.6 %collective-permute-done.22 = f32[73,16]{1,0:T(8,128)S(1)} collective-permute-done((f32[73,16]{1,0:T(8,128)S(1)}, f32[73,16]{1,0:T(8,128)S(1)}, u32[]{:S(2)}, u32[]{:S(2)}) %collective-permute-start.22) | collective-permute-done | bytes 4704 | tf_op jit(solution)/shard_map/ppermute | solution.py:35
  89.2 1.5 %collective-permute-start.23 = (f32[73,16]{1,0:T(8,128)S(1)}, f32[73,16]{1,0:T(8,128)S(1)}, u32[]{:S(2)}, u32[]{:S(2)}) collective-permute-start(f32[73,16]{1,0:T(8,128)S(1)} %add.215), channel_id=1, source_target_pairs={{0,8},{1,9},{2,10},{3,11},{4,12},{5,13},{6,14},{7,15},{8,0},{9,1},... | collective-permute-start | bytes 14024 | tf_op jit(solution)/shard_map/ppermute | solution.py:35
  90.7 2.5 %collective-permute-done.23 = f32[73,16]{1,0:T(8,128)S(1)} collective-permute-done((f32[73,16]{1,0:T(8,128)S(1)}, f32[73,16]{1,0:T(8,128)S(1)}, u32[]{:S(2)}, u32[]{:S(2)}) %collective-permute-start.23) | collective-permute-done | bytes 4704 | tf_op jit(solution)/shard_map/ppermute | solution.py:35
  93.2 2.2 %collective-permute-start.24 = (f32[73,16]{1,0:T(8,128)S(1)}, f32[73,16]{1,0:T(8,128)S(1)}, u32[]{:S(2)}, u32[]{:S(2)}) collective-permute-start(f32[73,16]{1,0:T(8,128)S(1)} %add.216), channel_id=1, source_target_pairs={{0,24},{1,25},{2,26},{3,27},{4,28},{5,29},{6,30},{7,31},{8,16},{9,... | collective-permute-start | bytes 14024 | tf_op jit(solution)/shard_map/ppermute | solution.py:35
  95.4 3.1 %collective-permute-done.24 = f32[73,16]{1,0:T(8,128)S(1)} collective-permute-done((f32[73,16]{1,0:T(8,128)S(1)}, f32[73,16]{1,0:T(8,128)S(1)}, u32[]{:S(2)}, u32[]{:S(2)}) %collective-permute-start.24) | collective-permute-done | bytes 4704 | tf_op jit(solution)/shard_map/ppermute | solution.py:35
  98.4 0.3 collective-permute-start.25
  98.8 3.7 %collective-permute-done.25 = f32[73,16]{1,0:T(8,128)S(1)} collective-permute-done((f32[73,16]{1,0:T(8,128)S(1)}, f32[73,16]{1,0:T(8,128)S(1)}, u32[]{:S(2)}, u32[]{:S(2)}) %collective-permute-start.25) | collective-permute-done | bytes 4704 | tf_op jit(solution)/shard_map/ppermute | solution.py:35
  102.5 2.6 %collective-permute-start.26 = (f32[73,16]{1,0:T(8,128)S(1)}, f32[73,16]{1,0:T(8,128)S(1)}, u32[]{:S(2)}, u32[]{:S(2)}) collective-permute-start(f32[73,16]{1,0:T(8,128)S(1)} %add.218), channel_id=1, source_target_pairs={{0,96},{1,97},{2,98},{3,99},{4,100},{5,101},{6,102},{7,103},{8,104... | collective-permute-start | bytes 14024 | tf_op jit(solution)/shard_map/ppermute | solution.py:35
  105.0 2.7 %collective-permute-done.26 = f32[73,16]{1,0:T(8,128)S(1)} collective-permute-done((f32[73,16]{1,0:T(8,128)S(1)}, f32[73,16]{1,0:T(8,128)S(1)}, u32[]{:S(2)}, u32[]{:S(2)}) %collective-permute-start.26) | collective-permute-done | bytes 4704 | tf_op jit(solution)/shard_map/ppermute | solution.py:35
  107.8 0.6 compare_reduce_fusion
  109.1 0.8 fusion
  110.0 0.6 pad_maximum_fusion.1
  110.6 0.7 broadcast_divide_fusion
  (46 shorter events, 1.6 us)
Async XLA Ops:
  2.9 4.5 %copy-start.4 = (bf16[16,512,512]{2,1,0:T(8,128)(2,1)S(1)}, bf16[16,512,512]{2,1,0:T(8,128)(2,1)}, u32[]{:S(2)}) copy-start(bf16[16,512,512]{2,1,0:T(8,128)(2,1)} %param.12) | copy-start | bytes 25165828
  8.6 2.7 %copy-start.2 = (s32[128]{0:T(128)S(1)}, s32[128]{0:T(128)}, u32[]{:S(2)}) copy-start(s32[128]{0:T(128)} %param.17) | copy-start | bytes 1540
  8.6 2.7 %copy-start.3 = (s32[128,1]{0,1:T(1,128)S(1)}, s32[128,1]{0,1:T(1,128)}, u32[]{:S(2)}) copy-start(s32[128,1]{0,1:T(1,128)} %param.16) | copy-start | bytes 1540
  22.2 2.7 %collective-permute-start.8 = (f32[4,4,2,16,512]{4,3,2,1,0:T(8,128)S(1)}, f32[4,4,2,16,512]{4,3,2,1,0:T(8,128)S(1)}, u32[]{:S(2)}, u32[]{:S(2)}) collective-permute-start(f32[4,4,2,16,512]{4,3,2,1,0:T(8,128)S(1)} %bitcast.124), channel_id=1, source_target_pairs={{0,1},{1,0},{2,3},{3,2},{4,5},{5,4},{6,7},{7,6},{8,9},{9,8},{10,11... | collective-permute-start | bytes 3145736 | tf_op jit(solution)/shard_map/ppermute | solution.py:47
  22.3 4.5 %collective-permute-start.10 = (f32[4,4,2,16,512]{4,3,2,1,0:T(8,128)S(1)}, f32[4,4,2,16,512]{4,3,2,1,0:T(8,128)S(1)}, u32[]{:S(2)}, u32[]{:S(2)}) collective-permute-start(f32[4,4,2,16,512]{4,3,2,1,0:T(8,128)S(1)} %bitcast.123), channel_id=1, source_target_pairs={{0,1},{1,0},{2,3},{3,2},{4,5},{5,4},{6,7},{7,6},{8,9},{9,8},{10,11... | collective-permute-start | bytes 3145736 | tf_op jit(solution)/shard_map/ppermute | solution.py:47
  22.8 7.1 %collective-permute-start.12 = (f32[4,4,2,16,512]{4,3,2,1,0:T(8,128)S(1)}, f32[4,4,2,16,512]{4,3,2,1,0:T(8,128)S(1)}, u32[]{:S(2)}, u32[]{:S(2)}) collective-permute-start(f32[4,4,2,16,512]{4,3,2,1,0:T(8,128)S(1)} %bitcast.122), channel_id=1, source_target_pairs={{0,1},{1,0},{2,3},{3,2},{4,5},{5,4},{6,7},{7,6},{8,9},{9,8},{10,11... | collective-permute-start | bytes 3145736 | tf_op jit(solution)/shard_map/ppermute | solution.py:47
  22.9 8.7 %collective-permute-start.7 = (f32[4,4,2,16,512]{4,3,2,1,0:T(8,128)S(1)}, f32[4,4,2,16,512]{4,3,2,1,0:T(8,128)S(1)}, u32[]{:S(2)}, u32[]{:S(2)}) collective-permute-start(f32[4,4,2,16,512]{4,3,2,1,0:T(8,128)S(1)} %bitcast.121), channel_id=1, source_target_pairs={{0,1},{1,0},{2,3},{3,2},{4,5},{5,4},{6,7},{7,6},{8,9},{9,8},{10,11... | collective-permute-start | bytes 3145736 | tf_op jit(solution)/shard_map/ppermute | solution.py:47
  25.2 16.1 %collective-permute-start.9 = (f32[4,4,2,16,512]{4,3,2,1,0:T(8,128)S(1)}, f32[4,4,2,16,512]{4,3,2,1,0:T(8,128)S(1)}, u32[]{:S(2)}, u32[]{:S(2)}) collective-permute-start(f32[4,4,2,16,512]{4,3,2,1,0:T(8,128)S(1)} %add.200), channel_id=1, source_target_pairs={{0,2},{1,9},{2,4},{3,11},{4,6},{5,13},{6,0},{7,15},{8,10},{9,17},{... | collective-permute-start | bytes 3145736 | tf_op jit(solution)/shard_map/ppermute | solution.py:50
  27.1 26.5 %collective-permute-start.11 = (f32[4,4,2,16,512]{4,3,2,1,0:T(8,128)S(1)}, f32[4,4,2,16,512]{4,3,2,1,0:T(8,128)S(1)}, u32[]{:S(2)}, u32[]{:S(2)}) collective-permute-start(f32[4,4,2,16,512]{4,3,2,1,0:T(8,128)S(1)} %add.202), channel_id=1, source_target_pairs={{0,4},{1,17},{2,6},{3,19},{4,0},{5,21},{6,2},{7,23},{8,12},{9,25},... | collective-permute-start | bytes 3145736 | tf_op jit(solution)/shard_map/ppermute | solution.py:50
  30.1 24.4 %collective-permute-start.13 = (f32[4,4,2,16,512]{4,3,2,1,0:T(8,128)S(1)}, f32[4,4,2,16,512]{4,3,2,1,0:T(8,128)S(1)}, u32[]{:S(2)}, u32[]{:S(2)}) collective-permute-start(f32[4,4,2,16,512]{4,3,2,1,0:T(8,128)S(1)} %add.204), channel_id=1, source_target_pairs={{0,6},{1,25},{2,0},{3,27},{4,2},{5,29},{6,4},{7,31},{8,14},{9,1},{... | collective-permute-start | bytes 3145736 | tf_op jit(solution)/shard_map/ppermute | solution.py:50
  54.5 19.5 %copy-start = (f32[8,2,16,512]{3,2,1,0:T(8,128)S(1)}, f32[8,2,16,512]{3,2,1,0:T(8,128)}, u32[]{:S(2)}) copy-start(f32[8,2,16,512]{3,2,1,0:T(8,128)} %param.10) | copy-start | bytes 1572868
  54.5 22.4 %copy-start.1 = (f32[2,512]{1,0:T(2,128)S(1)}, f32[2,512]{1,0:T(2,128)}, u32[]{:S(2)}) copy-start(f32[2,512]{1,0:T(2,128)} %param.11) | copy-start | bytes 12292
  55.3 8.5 %collective-permute-start.14 = (f32[4,2,16,512]{3,2,1,0:T(8,128)S(1)}, f32[4,2,16,512]{3,2,1,0:T(8,128)S(1)}, u32[]{:S(2)}, u32[]{:S(2)}) collective-permute-start(f32[4,2,16,512]{3,2,1,0:T(8,128)S(1)} %get-tuple-element.25), channel_id=1, source_target_pairs={{0,8},{1,3},{2,10},{3,5},{4,12},{5,7},{6,14},{7,1},{8,16},{9,11},{... | collective-permute-start | bytes 786440 | tf_op jit(solution)/shard_map/ppermute | solution.py:42
  57.3 10.7 %collective-permute-start.15 = (f32[4,2,16,512]{3,2,1,0:T(8,128)S(1)}, f32[4,2,16,512]{3,2,1,0:T(8,128)S(1)}, u32[]{:S(2)}, u32[]{:S(2)}) collective-permute-start(f32[4,2,16,512]{3,2,1,0:T(8,128)S(1)} %get-tuple-element.27), channel_id=1, source_target_pairs={{0,16},{1,5},{2,18},{3,7},{4,20},{5,1},{6,22},{7,3},{8,24},{9,13},... | collective-permute-start | bytes 786440 | tf_op jit(solution)/shard_map/ppermute | solution.py:42
  60.9 7.2 %collective-permute-start.16 = (f32[4,2,16,512]{3,2,1,0:T(8,128)S(1)}, f32[4,2,16,512]{3,2,1,0:T(8,128)S(1)}, u32[]{:S(2)}, u32[]{:S(2)}) collective-permute-start(f32[4,2,16,512]{3,2,1,0:T(8,128)S(1)} %get-tuple-element.26), channel_id=1, source_target_pairs={{0,24},{1,7},{2,26},{3,1},{4,28},{5,3},{6,30},{7,5},{8,0},{9,15},{... | collective-permute-start | bytes 786440 | tf_op jit(solution)/shard_map/ppermute | solution.py:42
  68.2 7.3 %collective-permute-start.17 = (f32[2,16,512]{2,1,0:T(8,128)S(1)}, f32[2,16,512]{2,1,0:T(8,128)S(1)}, u32[]{:S(2)}, u32[]{:S(2)}) collective-permute-start(f32[2,16,512]{2,1,0:T(8,128)S(1)} %get-tuple-element.28), channel_id=1, source_target_pairs={{0,32},{1,33},{2,34},{3,35},{4,36},{5,37},{6,38},{7,39},{8,40},{9,... | collective-permute-start | bytes 196616 | tf_op jit(solution)/shard_map/ppermute | solution.py:42
  69.8 5.8 %collective-permute-start.18 = (f32[2,16,512]{2,1,0:T(8,128)S(1)}, f32[2,16,512]{2,1,0:T(8,128)S(1)}, u32[]{:S(2)}, u32[]{:S(2)}) collective-permute-start(f32[2,16,512]{2,1,0:T(8,128)S(1)} %get-tuple-element.30), channel_id=1, source_target_pairs={{0,64},{1,65},{2,66},{3,67},{4,68},{5,69},{6,70},{7,71},{8,72},{9,... | collective-permute-start | bytes 196616 | tf_op jit(solution)/shard_map/ppermute | solution.py:42
  72.7 4.3 %collective-permute-start.19 = (f32[2,16,512]{2,1,0:T(8,128)S(1)}, f32[2,16,512]{2,1,0:T(8,128)S(1)}, u32[]{:S(2)}, u32[]{:S(2)}) collective-permute-start(f32[2,16,512]{2,1,0:T(8,128)S(1)} %get-tuple-element.29), channel_id=1, source_target_pairs={{0,96},{1,97},{2,98},{3,99},{4,100},{5,101},{6,102},{7,103},{8,104... | collective-permute-start | bytes 196616 | tf_op jit(solution)/shard_map/ppermute | solution.py:42
  78.6 1.3 %collective-permute-start.20 = (f32[73,16]{1,0:T(8,128)S(1)}, f32[73,16]{1,0:T(8,128)S(1)}, u32[]{:S(2)}, u32[]{:S(2)}) collective-permute-start(f32[73,16]{1,0:T(8,128)S(1)} %pad_maximum_fusion), channel_id=1, source_target_pairs={{0,1},{1,0},{2,3},{3,2},{4,5},{5,4},{6,7},{7,6},{8,9},{9,8},{10,11... | collective-permute-start | bytes 14024 | tf_op jit(solution)/shard_map/ppermute | solution.py:32
  79.9 4.1 %collective-permute-start.21 = (f32[73,16]{1,0:T(8,128)S(1)}, f32[73,16]{1,0:T(8,128)S(1)}, u32[]{:S(2)}, u32[]{:S(2)}) collective-permute-start(f32[73,16]{1,0:T(8,128)S(1)} %fusion.32), channel_id=1, source_target_pairs={{0,2},{1,3},{2,0},{3,1},{4,6},{5,7},{6,4},{7,5},{8,10},{9,11},{10,... | collective-permute-start | bytes 14024 | tf_op jit(solution)/shard_map/ppermute | solution.py:35
  84.0 5.2 %collective-permute-start.22 = (f32[73,16]{1,0:T(8,128)S(1)}, f32[73,16]{1,0:T(8,128)S(1)}, u32[]{:S(2)}, u32[]{:S(2)}) collective-permute-start(f32[73,16]{1,0:T(8,128)S(1)} %add.214), channel_id=1, source_target_pairs={{0,6},{1,7},{2,4},{3,5},{4,2},{5,3},{6,0},{7,1},{8,14},{9,15},{10,... | collective-permute-start | bytes 14024 | tf_op jit(solution)/shard_map/ppermute | solution.py:35
  89.2 4.0 %collective-permute-start.23 = (f32[73,16]{1,0:T(8,128)S(1)}, f32[73,16]{1,0:T(8,128)S(1)}, u32[]{:S(2)}, u32[]{:S(2)}) collective-permute-start(f32[73,16]{1,0:T(8,128)S(1)} %add.215), channel_id=1, source_target_pairs={{0,8},{1,9},{2,10},{3,11},{4,12},{5,13},{6,14},{7,15},{8,0},{9,1},... | collective-permute-start | bytes 14024 | tf_op jit(solution)/shard_map/ppermute | solution.py:35
  93.2 5.2 %collective-permute-start.24 = (f32[73,16]{1,0:T(8,128)S(1)}, f32[73,16]{1,0:T(8,128)S(1)}, u32[]{:S(2)}, u32[]{:S(2)}) collective-permute-start(f32[73,16]{1,0:T(8,128)S(1)} %add.216), channel_id=1, source_target_pairs={{0,24},{1,25},{2,26},{3,27},{4,28},{5,29},{6,30},{7,31},{8,16},{9,... | collective-permute-start | bytes 14024 | tf_op jit(solution)/shard_map/ppermute | solution.py:35
  98.4 4.0 %collective-permute-start.25 = (f32[73,16]{1,0:T(8,128)S(1)}, f32[73,16]{1,0:T(8,128)S(1)}, u32[]{:S(2)}, u32[]{:S(2)}) collective-permute-start(f32[73,16]{1,0:T(8,128)S(1)} %add.217), channel_id=1, source_target_pairs={{0,32},{1,33},{2,34},{3,35},{4,36},{5,37},{6,38},{7,39},{8,40},{9,... | collective-permute-start | bytes 14024 | tf_op jit(solution)/shard_map/ppermute | solution.py:35
  102.5 5.2 %collective-permute-start.26 = (f32[73,16]{1,0:T(8,128)S(1)}, f32[73,16]{1,0:T(8,128)S(1)}, u32[]{:S(2)}, u32[]{:S(2)}) collective-permute-start(f32[73,16]{1,0:T(8,128)S(1)} %add.218), channel_id=1, source_target_pairs={{0,96},{1,97},{2,98},{3,99},{4,100},{5,101},{6,102},{7,103},{8,104... | collective-permute-start | bytes 14024 | tf_op jit(solution)/shard_map/ppermute | solution.py:35

commit v9 on v7

--- a/solution.py
+++ b/solution.py
@@ -55,7 +55,8 @@
 STEPS = 8
 
 
-def accumulate_kernel(slot_ref, near_ref, far_ref, *out_refs):
+def accumulate_kernel(slot_ref, near_ref, far_ref, *refs):
+    *out_refs, total_ref = refs
     i = pl.program_id(0)
     piece = out_refs[0].shape[0]
     near_step = near_ref.shape[0]
@@ -64,21 +65,17 @@
 
     @pl.when(i == 0)
     def _():
-        for ref in out_refs:
-            ref[...] = jnp.zeros_like(ref)
-
-    def add(g, part):
-        s = slot_ref[g]
-        for number, ref in enumerate(out_refs):
-
-            @pl.when(s // piece == number)
-            def _():
-                ref[s % piece] += part
+        total_ref[...] = jnp.zeros_like(total_ref)
 
     for j in range(near_step):
-        add(i * near_step + j, near_ref[j])
+        total_ref[slot_ref[i * near_step + j]] += near_ref[j]
     for j in range(far_step):
-        add(near_total + i * far_step + j, far_ref[j])
+        total_ref[slot_ref[near_total + i * far_step + j]] += far_ref[j]
+
+    @pl.when(i == pl.num_programs(0) - 1)
+    def _():
+        for number, ref in enumerate(out_refs):
+            ref[...] = total_ref[number * piece:(number + 1) * piece]
 
 
 def accumulate(slot, near_part, far_part, spots, pieces):
@@ -96,6 +93,7 @@
             pl.BlockSpec((far_step, sources, size), lambda i, s: (i, 0, 0)),
         ],
         out_specs=[pl.BlockSpec((length, sources, size), lambda i, s: (0, 0, 0))] * pieces,
+        scratch_shapes=[pltpu.VMEM((spots, sources, size), jnp.float32)],
     )
     return pl.pallas_call(
         accumulate_kernel,
@@ -140,13 +138,25 @@
     panels = clusters * cluster_size * devices
     local_first = jnp.einsum("knjc,njc->kj", basis, image, precision=highest)
     local_gram = jnp.einsum("knjc,mnjc->kmj", basis, basis, precision=highest)
-    both = all_sum(jnp.concatenate([local_first, local_gram.reshape(-1, sources)], axis=0))
+    local_size = jnp.sum(image * image, axis=(0, 2))[None, :]
+    both = all_sum(
+        jnp.concatenate([local_first, local_gram.reshape(-1, sources), local_size], axis=0)
+    )
     first = both[:basis_count] / panels
-    gram = both[basis_count:].reshape(basis_count, basis_count, sources) / panels
+    gram = both[basis_count:-1].reshape(basis_count, basis_count, sources) / panels
+    size = both[-1] / panels
     second = first - jnp.einsum("kmj,mj->kj", gram, first, precision=highest)
     total = first + second
     twice = image - jnp.einsum("kj,knjc->njc", total, basis, precision=highest)
-    square = all_sum(jnp.sum(twice * twice, axis=(0, 2))) / panels
+    cross = jnp.sum(total * first, axis=0)
+    curve = jnp.sum(total * jnp.einsum("kmj,mj->kj", gram, total, precision=highest), axis=0)
+    formula = size - 2.0 * cross + curve
+    trusted = jnp.all(formula >= 0.01 * (size + 2.0 * jnp.abs(cross) + jnp.abs(curve)))
+    square = lax.cond(
+        trusted,
+        lambda: formula,
+        lambda: all_sum(jnp.sum(twice * twice, axis=(0, 2))) / panels,
+    )
     beta = jnp.sqrt(square + 1e-06)
     next_vector = twice / beta[None, :, None]
     hess_column = jnp.concatenate([total, beta[None, :]], axis=0)

time: 138 us -> 111 us (0.80)
  waiting for transfers between devices: 68.2 us -> 50.5 us
  starting transfers between devices: 38.6 us -> 30.6 us
  Pallas kernels: 11.1 us -> 8.03 us
    ppermute x12 -> x6, waiting for transfers between devices: 33.5 us -> 16.8 us  [all_sum(): v = v + lax.ppermute(v, AXES, flipped(step * STRIDE[axis]))]
    ppermute x12 -> x6, starting transfers between devices: 19 us -> 10.9 us  [all_sum(): v = v + lax.ppermute(v, AXES, flipped(step * STRIDE[axis]))]
    pallas_call x1, Pallas kernels: 11.1 us -> 8.03 us  [accumulate(): pl.pallas_call(accumulate_kernel, grid_spec=grid_spec, out_shape=[out] *...]
  transfers between devices with their start and end apart: 27 -> 20, of which waited for: 22 -> 15; matrix products, arithmetic and copies ran while one was open for 1% -> 2% of each run, Pallas kernels for 0% -> 0%
where the time goes in v9:
time: 111 us
  waiting for transfers between devices  50.5 us (45%)
  starting transfers between devices  30.6 us (28%)
  matrix products  12.5 us (11%)
  Pallas kernels  8.03 us (7%)
  other arithmetic  4.35 us (4%)
  local copies, waits for them, and re-layouts  3.11 us (3%)
  between operations  1.52 us (1%)
    ppermute x3, waiting for transfers between devices, reduce_to_owner(): acc = acc + lax.ppermute(pieces[k], AXES, moved('x', k, 'z'))  22.9 us
    ppermute x6, waiting for transfers between devices, all_sum(): v = v + lax.ppermute(v, AXES, flipped(step * STRIDE[axis]))  16.8 us
    ppermute x6, starting transfers between devices, spread(): acc = acc + lax.ppermute(pieces[k], AXES, moved(axis, k, other))  12.5 us
    ppermute x6, starting transfers between devices, all_sum(): v = v + lax.ppermute(v, AXES, flipped(step * STRIDE[axis]))  10.9 us
    pallas_call x1, Pallas kernels, accumulate(): pl.pallas_call(accumulate_kernel, grid_spec=grid_spec, out_shape=[out] *...  8.03 us
    ppermute x6, waiting for transfers between devices, spread(): acc = acc + lax.ppermute(pieces[k], AXES, moved(axis, k, other))  7.63 us
    ppermute x3, starting transfers between devices, reduce_to_owner(): acc = acc + lax.ppermute(pieces[k], AXES, moved('x', k, 'z'))  5.99 us
    dot_general x1, matrix products, on_device(): jnp.einsum('snk,skc->snc', coeff, far_v, preferred_element_type=jnp.float32)  4.48 us
  transfers between devices with their start and end apart: 20, of which 15 were waited for; matrix products, arithmetic and copies ran while one was open for 2% of the time, Pallas kernels for 0%

profile of v9, /device:TPU:0, one launch (start us, length us, event | category | flops | bytes accessed | tf_op | source)
XLA Modules:
  0.0 110.6 jit_solution(11630546543605661762)
XLA Ops:
  0.7 0.8 bitcast_convert_fusion
  1.6 0.7 compare_select_fusion
  2.2 0.7 gather_fusion
  2.9 3.2 %convolution_convert_fusion = bf16[112,16,32]{2,1,0:T(8,128)(2,1)S(1)} fusion(bf16[128,16,512]{2,1,0:T(8,128)(2,1)S(1)} %gather_fusion, bf16[112,32,512]{2,1,0:T(8,128)(2,1)} %param.13), kind=kOutput, calls=%fused_computation.3 | convolution fusion | flops 58777600 | bytes 5881856 | tf_op jit(solution)/shard_map/snc,skc->snk/dot_general | solution.py:123
  6.2 1.2 %copy-done.4 = bf16[16,512,512]{2,1,0:T(8,128)(2,1)S(1)} copy-done((bf16[16,512,512]{2,1,0:T(8,128)(2,1)S(1)}, bf16[16,512,512]{2,1,0:T(8,128)(2,1)}, u32[]{:S(2)}) %copy-start.4) | copy-done | bytes 8388632
  7.4 1.2 %fusion.35.near_ref = f32[16,16,512]{2,1,0:T(8,128)S(1)} fusion(bf16[128,16,512]{2,1,0:T(8,128)(2,1)S(1)} %gather_fusion, bf16[16,512,512]{2,1,0:T(8,128)(2,1)S(1)} %copy-done.4), kind=kOutput, calls=%fused_computation.104 | convolution fusion | flops 134217728 | bytes 11010048 | tf_op jit(solution)/shard_map/snc,scd->snd/dot_general | solution.py:120
  8.6 4.5 %fusion.34.far_ref = f32[112,16,512]{2,1,0:T(8,128)} fusion(bf16[112,16,32]{2,1,0:T(8,128)(2,1)S(1)} %convolution_convert_fusion, bf16[112,32,512]{2,1,0:T(8,128)(2,1)} %param.14), kind=kOutput, calls=%fused_computation.103 | convolution fusion | flops 58720256 | bytes 7454720 | tf_op jit(solution)/shard_map/snk,skc->snc/dot_general | solution.py:126
  13.1 8.0 %shard_map.95 = (f32[32,16,512]{2,1,0:T(8,128)S(1)}, f32[32,16,512]{2,1,0:T(8,128)S(1)}, f32[32,16,512]{2,1,0:T(8,128)S(1)}, f32[32,16,512]{2,1,0:T(8,128)S(1)},...) custom-call(s32[128]{0:T(128)S(1)} %multiply_add_fusion.slot_ref, ...), custom_call_target="tpu_custom_call" | custom-call | tf_op jit(solution)/shard_map/pallas_call | solution.py:98
  21.1 0.5 collective-permute-start.10
  21.7 0.5 collective-permute-start.7
  22.2 1.8 %collective-permute-done.8 = f32[4,4,2,16,512]{4,3,2,1,0:T(8,128)S(1)} collective-permute-done((f32[4,4,2,16,512]{4,3,2,1,0:T(8,128)}, f32[4,4,2,16,512]{4,3,2,1,0:T(8,128)S(1)}, u32[]{:S(2)}, u32[]{:S(2)}) %collective-permute-start.8) | collective-permute-done | bytes 1048608 | tf_op jit(solution)/shard_map/ppermute | solution.py:47
  24.0 0.2 add.200
  24.2 1.7 %collective-permute-start.9 = (f32[4,4,2,16,512]{4,3,2,1,0:T(8,128)S(1)}, f32[4,4,2,16,512]{4,3,2,1,0:T(8,128)S(1)}, u32[]{:S(2)}, u32[]{:S(2)}) collective-permute-start(f32[4,4,2,16,512]{4,3,2,1,0:T(8,128)S(1)} %add.200), channel_id=1, source_target_pairs={{0,2},{1,9},{2,4},{3,11},{4,6},{5,13},{6,0},{7,15},{8,10},{9,17},{... | collective-permute-start | bytes 3145736 | tf_op jit(solution)/shard_map/ppermute | solution.py:50
  26.1 2.8 %collective-permute-start.11 = (f32[4,4,2,16,512]{4,3,2,1,0:T(8,128)S(1)}, f32[4,4,2,16,512]{4,3,2,1,0:T(8,128)S(1)}, u32[]{:S(2)}, u32[]{:S(2)}) collective-permute-start(f32[4,4,2,16,512]{4,3,2,1,0:T(8,128)S(1)} %add.202), channel_id=1, source_target_pairs={{0,4},{1,17},{2,6},{3,19},{4,0},{5,21},{6,2},{7,23},{8,12},{9,25},... | collective-permute-start | bytes 3145736 | tf_op jit(solution)/shard_map/ppermute | solution.py:50
  29.2 1.5 %collective-permute-start.13 = (f32[4,4,2,16,512]{4,3,2,1,0:T(8,128)S(1)}, f32[4,4,2,16,512]{4,3,2,1,0:T(8,128)S(1)}, u32[]{:S(2)}, u32[]{:S(2)}) collective-permute-start(f32[4,4,2,16,512]{4,3,2,1,0:T(8,128)S(1)} %add.204), channel_id=1, source_target_pairs={{0,6},{1,25},{2,0},{3,27},{4,2},{5,29},{6,4},{7,31},{8,14},{9,1},{... | collective-permute-start | bytes 3145736 | tf_op jit(solution)/shard_map/ppermute | solution.py:50
  30.6 9.7 %collective-permute-done.9 = f32[4,4,2,16,512]{4,3,2,1,0:T(8,128)S(1)} collective-permute-done((f32[4,4,2,16,512]{4,3,2,1,0:T(8,128)S(1)}, f32[4,4,2,16,512]{4,3,2,1,0:T(8,128)S(1)}, u32[]{:S(2)}, u32[]{:S(2)}) %collective-permute-start.9) | collective-permute-done | bytes 1048608 | tf_op jit(solution)/shard_map/ppermute | solution.py:50
  40.3 12.3 %collective-permute-done.11 = f32[4,4,2,16,512]{4,3,2,1,0:T(8,128)S(1)} collective-permute-done((f32[4,4,2,16,512]{4,3,2,1,0:T(8,128)S(1)}, f32[4,4,2,16,512]{4,3,2,1,0:T(8,128)S(1)}, u32[]{:S(2)}, u32[]{:S(2)}) %collective-permute-start.11) | collective-permute-done | bytes 1048608 | tf_op jit(solution)/shard_map/ppermute | solution.py:50
  52.6 0.9 collective-permute-done.13
  53.6 0.7 add_add_fusion
  54.4 2.0 %collective-permute-start.14 = (f32[4,2,16,512]{3,2,1,0:T(8,128)S(1)}, f32[4,2,16,512]{3,2,1,0:T(8,128)S(1)}, u32[]{:S(2)}, u32[]{:S(2)}) collective-permute-start(f32[4,2,16,512]{3,2,1,0:T(8,128)S(1)} %get-tuple-element.29), channel_id=1, source_target_pairs={{0,8},{1,3},{2,10},{3,5},{4,12},{5,7},{6,14},{7,1},{8,16},{9,11},{... | collective-permute-start | bytes 786440 | tf_op jit(solution)/shard_map/ppermute | solution.py:42
  56.4 3.6 %collective-permute-start.15 = (f32[4,2,16,512]{3,2,1,0:T(8,128)S(1)}, f32[4,2,16,512]{3,2,1,0:T(8,128)S(1)}, u32[]{:S(2)}, u32[]{:S(2)}) collective-permute-start(f32[4,2,16,512]{3,2,1,0:T(8,128)S(1)} %get-tuple-element.31), channel_id=1, source_target_pairs={{0,16},{1,5},{2,18},{3,7},{4,20},{5,1},{6,22},{7,3},{8,24},{9,13},... | collective-permute-start | bytes 786440 | tf_op jit(solution)/shard_map/ppermute | solution.py:42
  59.9 1.0 collective-permute-start.16
  61.0 1.9 %collective-permute-done.14 = f32[4,2,16,512]{3,2,1,0:T(8,128)S(1)} collective-permute-done((f32[4,2,16,512]{3,2,1,0:T(8,128)S(1)}, f32[4,2,16,512]{3,2,1,0:T(8,128)S(1)}, u32[]{:S(2)}, u32[]{:S(2)}) %collective-permute-start.14) | collective-permute-done | bytes 262176 | tf_op jit(solution)/shard_map/ppermute | solution.py:42
  62.8 4.3 %collective-permute-done.15 = f32[4,2,16,512]{3,2,1,0:T(8,128)S(1)} collective-permute-done((f32[4,2,16,512]{3,2,1,0:T(8,128)S(1)}, f32[4,2,16,512]{3,2,1,0:T(8,128)S(1)}, u32[]{:S(2)}, u32[]{:S(2)}) %collective-permute-start.15) | collective-permute-done | bytes 262176 | tf_op jit(solution)/shard_map/ppermute | solution.py:42
  67.2 1.6 %collective-permute-start.17 = (f32[2,16,512]{2,1,0:T(8,128)S(1)}, f32[2,16,512]{2,1,0:T(8,128)S(1)}, u32[]{:S(2)}, u32[]{:S(2)}) collective-permute-start(f32[2,16,512]{2,1,0:T(8,128)S(1)} %get-tuple-element.32), channel_id=1, source_target_pairs={{0,32},{1,33},{2,34},{3,35},{4,36},{5,37},{6,38},{7,39},{8,40},{9,... | collective-permute-start | bytes 196616 | tf_op jit(solution)/shard_map/ppermute | solution.py:42
  68.9 2.9 %collective-permute-start.18 = (f32[2,16,512]{2,1,0:T(8,128)S(1)}, f32[2,16,512]{2,1,0:T(8,128)S(1)}, u32[]{:S(2)}, u32[]{:S(2)}) collective-permute-start(f32[2,16,512]{2,1,0:T(8,128)S(1)} %get-tuple-element.34), channel_id=1, source_target_pairs={{0,64},{1,65},{2,66},{3,67},{4,68},{5,69},{6,70},{7,71},{8,72},{9,... | collective-permute-start | bytes 196616 | tf_op jit(solution)/shard_map/ppermute | solution.py:42
  71.8 1.3 %collective-permute-start.19 = (f32[2,16,512]{2,1,0:T(8,128)S(1)}, f32[2,16,512]{2,1,0:T(8,128)S(1)}, u32[]{:S(2)}, u32[]{:S(2)}) collective-permute-start(f32[2,16,512]{2,1,0:T(8,128)S(1)} %get-tuple-element.33), channel_id=1, source_target_pairs={{0,96},{1,97},{2,98},{3,99},{4,100},{5,101},{6,102},{7,103},{8,104... | collective-permute-start | bytes 196616 | tf_op jit(solution)/shard_map/ppermute | solution.py:42
  73.1 1.3 %convolution_bitcast_fusion = f32[8,8,16]{0,1,2:T(8,128)S(1)} fusion(f32[8,2,16,512]{3,2,1,0:T(8,128)S(1)} %copy-done), kind=kOutput, calls=%fused_computation.4 | convolution fusion | flops 12582912 | bytes 528384 | tf_op jit(solution)/shard_map/knjc,mnjc->kmj/dot_general | solution.py:140
  74.7 1.3 %collective-permute-done.19 = f32[2,16,512]{2,1,0:T(8,128)S(1)} collective-permute-done((f32[2,16,512]{2,1,0:T(8,128)S(1)}, f32[2,16,512]{2,1,0:T(8,128)S(1)}, u32[]{:S(2)}, u32[]{:S(2)}) %collective-permute-start.19) | collective-permute-done | bytes 65568 | tf_op jit(solution)/shard_map/ppermute | solution.py:42
  76.2 1.5 %fusion.2 = f32[16,1,8,1]{2,1,3,0:T(1,128)S(1)} fusion(f32[8,2,16,512]{3,2,1,0:T(8,128)S(1)} %copy-done, f32[2,16,512,1]{2,1,0,3:T(8,128)S(1)} %bitcast.122), kind=kOutput, calls=%fused_computation.8 | convolution fusion | flops 1572864 | bytes 590336 | tf_op jit(solution)/shard_map/knjc,njc->kj/dot_general | solution.py:139
  77.7 0.2 collective-permute-start.20
  77.9 1.2 %collective-permute-done.20 = f32[73,16]{1,0:T(8,128)S(1)} collective-permute-done((f32[73,16]{1,0:T(8,128)S(1)}, f32[73,16]{1,0:T(8,128)S(1)}, u32[]{:S(2)}, u32[]{:S(2)}) %collective-permute-start.20) | collective-permute-done | bytes 4704 | tf_op jit(solution)/shard_map/ppermute | solution.py:32
  79.1 1.7 %collective-permute-start.21 = (f32[73,16]{1,0:T(8,128)S(1)}, f32[73,16]{1,0:T(8,128)S(1)}, u32[]{:S(2)}, u32[]{:S(2)}) collective-permute-start(f32[73,16]{1,0:T(8,128)S(1)} %fusion.32), channel_id=1, source_target_pairs={{0,2},{1,3},{2,0},{3,1},{4,6},{5,7},{6,4},{7,5},{8,10},{9,11},{10,... | collective-permute-start | bytes 14024 | tf_op jit(solution)/shard_map/ppermute | solution.py:35
  80.9 2.4 %collective-permute-done.21 = f32[73,16]{1,0:T(8,128)S(1)} collective-permute-done((f32[73,16]{1,0:T(8,128)S(1)}, f32[73,16]{1,0:T(8,128)S(1)}, u32[]{:S(2)}, u32[]{:S(2)}) %collective-permute-start.21) | collective-permute-done | bytes 4704 | tf_op jit(solution)/shard_map/ppermute | solution.py:35
  83.2 2.6 %collective-permute-start.22 = (f32[73,16]{1,0:T(8,128)S(1)}, f32[73,16]{1,0:T(8,128)S(1)}, u32[]{:S(2)}, u32[]{:S(2)}) collective-permute-start(f32[73,16]{1,0:T(8,128)S(1)} %add.214), channel_id=1, source_target_pairs={{0,6},{1,7},{2,4},{3,5},{4,2},{5,3},{6,0},{7,1},{8,14},{9,15},{10,... | collective-permute-start | bytes 14024 | tf_op jit(solution)/shard_map/ppermute | solution.py:35
  85.9 2.6 %collective-permute-done.22 = f32[73,16]{1,0:T(8,128)S(1)} collective-permute-done((f32[73,16]{1,0:T(8,128)S(1)}, f32[73,16]{1,0:T(8,128)S(1)}, u32[]{:S(2)}, u32[]{:S(2)}) %collective-permute-start.22) | collective-permute-done | bytes 4704 | tf_op jit(solution)/shard_map/ppermute | solution.py:35
  88.5 1.5 %collective-permute-start.23 = (f32[73,16]{1,0:T(8,128)S(1)}, f32[73,16]{1,0:T(8,128)S(1)}, u32[]{:S(2)}, u32[]{:S(2)}) collective-permute-start(f32[73,16]{1,0:T(8,128)S(1)} %add.215), channel_id=1, source_target_pairs={{0,8},{1,9},{2,10},{3,11},{4,12},{5,13},{6,14},{7,15},{8,0},{9,1},... | collective-permute-start | bytes 14024 | tf_op jit(solution)/shard_map/ppermute | solution.py:35
  90.0 2.5 %collective-permute-done.23 = f32[73,16]{1,0:T(8,128)S(1)} collective-permute-done((f32[73,16]{1,0:T(8,128)S(1)}, f32[73,16]{1,0:T(8,128)S(1)}, u32[]{:S(2)}, u32[]{:S(2)}) %collective-permute-start.23) | collective-permute-done | bytes 4704 | tf_op jit(solution)/shard_map/ppermute | solution.py:35
  92.5 2.2 %collective-permute-start.24 = (f32[73,16]{1,0:T(8,128)S(1)}, f32[73,16]{1,0:T(8,128)S(1)}, u32[]{:S(2)}, u32[]{:S(2)}) collective-permute-start(f32[73,16]{1,0:T(8,128)S(1)} %add.216), channel_id=1, source_target_pairs={{0,24},{1,25},{2,26},{3,27},{4,28},{5,29},{6,30},{7,31},{8,16},{9,... | collective-permute-start | bytes 14024 | tf_op jit(solution)/shard_map/ppermute | solution.py:35
  94.6 3.1 %collective-permute-done.24 = f32[73,16]{1,0:T(8,128)S(1)} collective-permute-done((f32[73,16]{1,0:T(8,128)S(1)}, f32[73,16]{1,0:T(8,128)S(1)}, u32[]{:S(2)}, u32[]{:S(2)}) %collective-permute-start.24) | collective-permute-done | bytes 4704 | tf_op jit(solution)/shard_map/ppermute | solution.py:35
  97.7 0.3 collective-permute-start.25
  98.0 3.7 %collective-permute-done.25 = f32[73,16]{1,0:T(8,128)S(1)} collective-permute-done((f32[73,16]{1,0:T(8,128)S(1)}, f32[73,16]{1,0:T(8,128)S(1)}, u32[]{:S(2)}, u32[]{:S(2)}) %collective-permute-start.25) | collective-permute-done | bytes 4704 | tf_op jit(solution)/shard_map/ppermute | solution.py:35
  101.7 2.6 %collective-permute-start.26 = (f32[73,16]{1,0:T(8,128)S(1)}, f32[73,16]{1,0:T(8,128)S(1)}, u32[]{:S(2)}, u32[]{:S(2)}) collective-permute-start(f32[73,16]{1,0:T(8,128)S(1)} %add.218), channel_id=1, source_target_pairs={{0,96},{1,97},{2,98},{3,99},{4,100},{5,101},{6,102},{7,103},{8,104... | collective-permute-start | bytes 14024 | tf_op jit(solution)/shard_map/ppermute | solution.py:35
  104.2 2.7 %collective-permute-done.26 = f32[73,16]{1,0:T(8,128)S(1)} collective-permute-done((f32[73,16]{1,0:T(8,128)S(1)}, f32[73,16]{1,0:T(8,128)S(1)}, u32[]{:S(2)}, u32[]{:S(2)}) %collective-permute-start.26) | collective-permute-done | bytes 4704 | tf_op jit(solution)/shard_map/ppermute | solution.py:35
  107.0 0.6 compare_reduce_fusion
  108.4 0.8 fusion
  109.3 0.6 pad_maximum_fusion.1
  109.9 0.7 broadcast_divide_fusion
  (45 shorter events, 1.4 us)
Async XLA Ops:
  2.9 4.5 %copy-start.4 = (bf16[16,512,512]{2,1,0:T(8,128)(2,1)S(1)}, bf16[16,512,512]{2,1,0:T(8,128)(2,1)}, u32[]{:S(2)}) copy-start(bf16[16,512,512]{2,1,0:T(8,128)(2,1)} %param.12) | copy-start | bytes 25165828
  8.6 4.5 %copy-start.2 = (s32[128]{0:T(128)S(1)}, s32[128]{0:T(128)}, u32[]{:S(2)}) copy-start(s32[128]{0:T(128)} %param.17) | copy-start | bytes 1540
  8.6 4.5 %copy-start.3 = (s32[128,1]{0,1:T(1,128)S(1)}, s32[128,1]{0,1:T(1,128)}, u32[]{:S(2)}) copy-start(s32[128,1]{0,1:T(1,128)} %param.16) | copy-start | bytes 1540
  21.1 2.9 %collective-permute-start.8 = (f32[4,4,2,16,512]{4,3,2,1,0:T(8,128)}, f32[4,4,2,16,512]{4,3,2,1,0:T(8,128)S(1)}, u32[]{:S(2)}, u32[]{:S(2)}) collective-permute-start(f32[4,4,2,16,512]{4,3,2,1,0:T(8,128)} %bitcast.133), channel_id=1, source_target_pairs={{0,1},{1,0},{2,3},{3,2},{4,5},{5,4},{6,7},{7,6},{8,9},{9,8},{10,11... | collective-permute-start | bytes 3145736 | tf_op jit(solution)/shard_map/ppermute | solution.py:47
  21.1 4.8 %collective-permute-start.10 = (f32[4,4,2,16,512]{4,3,2,1,0:T(8,128)}, f32[4,4,2,16,512]{4,3,2,1,0:T(8,128)S(1)}, u32[]{:S(2)}, u32[]{:S(2)}) collective-permute-start(f32[4,4,2,16,512]{4,3,2,1,0:T(8,128)} %bitcast.132), channel_id=1, source_target_pairs={{0,1},{1,0},{2,3},{3,2},{4,5},{5,4},{6,7},{7,6},{8,9},{9,8},{10,11... | collective-permute-start | bytes 3145736 | tf_op jit(solution)/shard_map/ppermute | solution.py:47
  21.6 7.3 %collective-permute-start.12 = (f32[4,4,2,16,512]{4,3,2,1,0:T(8,128)}, f32[4,4,2,16,512]{4,3,2,1,0:T(8,128)S(1)}, u32[]{:S(2)}, u32[]{:S(2)}) collective-permute-start(f32[4,4,2,16,512]{4,3,2,1,0:T(8,128)} %bitcast.131), channel_id=1, source_target_pairs={{0,1},{1,0},{2,3},{3,2},{4,5},{5,4},{6,7},{7,6},{8,9},{9,8},{10,11... | collective-permute-start | bytes 3145736 | tf_op jit(solution)/shard_map/ppermute | solution.py:47
  21.7 9.0 %collective-permute-start.7 = (f32[4,4,2,16,512]{4,3,2,1,0:T(8,128)S(1)}, f32[4,4,2,16,512]{4,3,2,1,0:T(8,128)S(1)}, u32[]{:S(2)}, u32[]{:S(2)}) collective-permute-start(f32[4,4,2,16,512]{4,3,2,1,0:T(8,128)S(1)} %bitcast.121), channel_id=1, source_target_pairs={{0,1},{1,0},{2,3},{3,2},{4,5},{5,4},{6,7},{7,6},{8,9},{9,8},{10,11... | collective-permute-start | bytes 3145736 | tf_op jit(solution)/shard_map/ppermute | solution.py:47
  24.2 16.1 %collective-permute-start.9 = (f32[4,4,2,16,512]{4,3,2,1,0:T(8,128)S(1)}, f32[4,4,2,16,512]{4,3,2,1,0:T(8,128)S(1)}, u32[]{:S(2)}, u32[]{:S(2)}) collective-permute-start(f32[4,4,2,16,512]{4,3,2,1,0:T(8,128)S(1)} %add.200), channel_id=1, source_target_pairs={{0,2},{1,9},{2,4},{3,11},{4,6},{5,13},{6,0},{7,15},{8,10},{9,17},{... | collective-permute-start | bytes 3145736 | tf_op jit(solution)/shard_map/ppermute | solution.py:50
  26.1 26.5 %collective-permute-start.11 = (f32[4,4,2,16,512]{4,3,2,1,0:T(8,128)S(1)}, f32[4,4,2,16,512]{4,3,2,1,0:T(8,128)S(1)}, u32[]{:S(2)}, u32[]{:S(2)}) collective-permute-start(f32[4,4,2,16,512]{4,3,2,1,0:T(8,128)S(1)} %add.202), channel_id=1, source_target_pairs={{0,4},{1,17},{2,6},{3,19},{4,0},{5,21},{6,2},{7,23},{8,12},{9,25},... | collective-permute-start | bytes 3145736 | tf_op jit(solution)/shard_map/ppermute | solution.py:50
  29.2 24.4 %collective-permute-start.13 = (f32[4,4,2,16,512]{4,3,2,1,0:T(8,128)S(1)}, f32[4,4,2,16,512]{4,3,2,1,0:T(8,128)S(1)}, u32[]{:S(2)}, u32[]{:S(2)}) collective-permute-start(f32[4,4,2,16,512]{4,3,2,1,0:T(8,128)S(1)} %add.204), channel_id=1, source_target_pairs={{0,6},{1,25},{2,0},{3,27},{4,2},{5,29},{6,4},{7,31},{8,14},{9,1},{... | collective-permute-start | bytes 3145736 | tf_op jit(solution)/shard_map/ppermute | solution.py:50
  53.6 19.5 %copy-start = (f32[8,2,16,512]{3,2,1,0:T(8,128)S(1)}, f32[8,2,16,512]{3,2,1,0:T(8,128)}, u32[]{:S(2)}) copy-start(f32[8,2,16,512]{3,2,1,0:T(8,128)} %param.10) | copy-start | bytes 1572868
  53.6 22.4 %copy-start.1 = (f32[2,512]{1,0:T(2,128)S(1)}, f32[2,512]{1,0:T(2,128)}, u32[]{:S(2)}) copy-start(f32[2,512]{1,0:T(2,128)} %param.11) | copy-start | bytes 12292
  54.4 8.5 %collective-permute-start.14 = (f32[4,2,16,512]{3,2,1,0:T(8,128)S(1)}, f32[4,2,16,512]{3,2,1,0:T(8,128)S(1)}, u32[]{:S(2)}, u32[]{:S(2)}) collective-permute-start(f32[4,2,16,512]{3,2,1,0:T(8,128)S(1)} %get-tuple-element.29), channel_id=1, source_target_pairs={{0,8},{1,3},{2,10},{3,5},{4,12},{5,7},{6,14},{7,1},{8,16},{9,11},{... | collective-permute-start | bytes 786440 | tf_op jit(solution)/shard_map/ppermute | solution.py:42
  56.4 10.7 %collective-permute-start.15 = (f32[4,2,16,512]{3,2,1,0:T(8,128)S(1)}, f32[4,2,16,512]{3,2,1,0:T(8,128)S(1)}, u32[]{:S(2)}, u32[]{:S(2)}) collective-permute-start(f32[4,2,16,512]{3,2,1,0:T(8,128)S(1)} %get-tuple-element.31), channel_id=1, source_target_pairs={{0,16},{1,5},{2,18},{3,7},{4,20},{5,1},{6,22},{7,3},{8,24},{9,13},... | collective-permute-start | bytes 786440 | tf_op jit(solution)/shard_map/ppermute | solution.py:42
  59.9 7.2 %collective-permute-start.16 = (f32[4,2,16,512]{3,2,1,0:T(8,128)S(1)}, f32[4,2,16,512]{3,2,1,0:T(8,128)S(1)}, u32[]{:S(2)}, u32[]{:S(2)}) collective-permute-start(f32[4,2,16,512]{3,2,1,0:T(8,128)S(1)} %get-tuple-element.30), channel_id=1, source_target_pairs={{0,24},{1,7},{2,26},{3,1},{4,28},{5,3},{6,30},{7,5},{8,0},{9,15},{... | collective-permute-start | bytes 786440 | tf_op jit(solution)/shard_map/ppermute | solution.py:42
  67.2 7.3 %collective-permute-start.17 = (f32[2,16,512]{2,1,0:T(8,128)S(1)}, f32[2,16,512]{2,1,0:T(8,128)S(1)}, u32[]{:S(2)}, u32[]{:S(2)}) collective-permute-start(f32[2,16,512]{2,1,0:T(8,128)S(1)} %get-tuple-element.32), channel_id=1, source_target_pairs={{0,32},{1,33},{2,34},{3,35},{4,36},{5,37},{6,38},{7,39},{8,40},{9,... | collective-permute-start | bytes 196616 | tf_op jit(solution)/shard_map/ppermute | solution.py:42
  68.9 5.8 %collective-permute-start.18 = (f32[2,16,512]{2,1,0:T(8,128)S(1)}, f32[2,16,512]{2,1,0:T(8,128)S(1)}, u32[]{:S(2)}, u32[]{:S(2)}) collective-permute-start(f32[2,16,512]{2,1,0:T(8,128)S(1)} %get-tuple-element.34), channel_id=1, source_target_pairs={{0,64},{1,65},{2,66},{3,67},{4,68},{5,69},{6,70},{7,71},{8,72},{9,... | collective-permute-start | bytes 196616 | tf_op jit(solution)/shard_map/ppermute | solution.py:42
  71.8 4.3 %collective-permute-start.19 = (f32[2,16,512]{2,1,0:T(8,128)S(1)}, f32[2,16,512]{2,1,0:T(8,128)S(1)}, u32[]{:S(2)}, u32[]{:S(2)}) collective-permute-start(f32[2,16,512]{2,1,0:T(8,128)S(1)} %get-tuple-element.33), channel_id=1, source_target_pairs={{0,96},{1,97},{2,98},{3,99},{4,100},{5,101},{6,102},{7,103},{8,104... | collective-permute-start | bytes 196616 | tf_op jit(solution)/shard_map/ppermute | solution.py:42
  77.7 1.4 %collective-permute-start.20 = (f32[73,16]{1,0:T(8,128)S(1)}, f32[73,16]{1,0:T(8,128)S(1)}, u32[]{:S(2)}, u32[]{:S(2)}) collective-permute-start(f32[73,16]{1,0:T(8,128)S(1)} %pad_maximum_fusion), channel_id=1, source_target_pairs={{0,1},{1,0},{2,3},{3,2},{4,5},{5,4},{6,7},{7,6},{8,9},{9,8},{10,11... | collective-permute-start | bytes 14024 | tf_op jit(solution)/shard_map/ppermute | solution.py:32
  79.1 4.1 %collective-permute-start.21 = (f32[73,16]{1,0:T(8,128)S(1)}, f32[73,16]{1,0:T(8,128)S(1)}, u32[]{:S(2)}, u32[]{:S(2)}) collective-permute-start(f32[73,16]{1,0:T(8,128)S(1)} %fusion.32), channel_id=1, source_target_pairs={{0,2},{1,3},{2,0},{3,1},{4,6},{5,7},{6,4},{7,5},{8,10},{9,11},{10,... | collective-permute-start | bytes 14024 | tf_op jit(solution)/shard_map/ppermute | solution.py:35
  83.2 5.2 %collective-permute-start.22 = (f32[73,16]{1,0:T(8,128)S(1)}, f32[73,16]{1,0:T(8,128)S(1)}, u32[]{:S(2)}, u32[]{:S(2)}) collective-permute-start(f32[73,16]{1,0:T(8,128)S(1)} %add.214), channel_id=1, source_target_pairs={{0,6},{1,7},{2,4},{3,5},{4,2},{5,3},{6,0},{7,1},{8,14},{9,15},{10,... | collective-permute-start | bytes 14024 | tf_op jit(solution)/shard_map/ppermute | solution.py:35
  88.5 4.0 %collective-permute-start.23 = (f32[73,16]{1,0:T(8,128)S(1)}, f32[73,16]{1,0:T(8,128)S(1)}, u32[]{:S(2)}, u32[]{:S(2)}) collective-permute-start(f32[73,16]{1,0:T(8,128)S(1)} %add.215), channel_id=1, source_target_pairs={{0,8},{1,9},{2,10},{3,11},{4,12},{5,13},{6,14},{7,15},{8,0},{9,1},... | collective-permute-start | bytes 14024 | tf_op jit(solution)/shard_map/ppermute | solution.py:35
  92.5 5.2 %collective-permute-start.24 = (f32[73,16]{1,0:T(8,128)S(1)}, f32[73,16]{1,0:T(8,128)S(1)}, u32[]{:S(2)}, u32[]{:S(2)}) collective-permute-start(f32[73,16]{1,0:T(8,128)S(1)} %add.216), channel_id=1, source_target_pairs={{0,24},{1,25},{2,26},{3,27},{4,28},{5,29},{6,30},{7,31},{8,16},{9,... | collective-permute-start | bytes 14024 | tf_op jit(solution)/shard_map/ppermute | solution.py:35
  97.7 4.0 %collective-permute-start.25 = (f32[73,16]{1,0:T(8,128)S(1)}, f32[73,16]{1,0:T(8,128)S(1)}, u32[]{:S(2)}, u32[]{:S(2)}) collective-permute-start(f32[73,16]{1,0:T(8,128)S(1)} %add.217), channel_id=1, source_target_pairs={{0,32},{1,33},{2,34},{3,35},{4,36},{5,37},{6,38},{7,39},{8,40},{9,... | collective-permute-start | bytes 14024 | tf_op jit(solution)/shard_map/ppermute | solution.py:35
  101.7 5.2 %collective-permute-start.26 = (f32[73,16]{1,0:T(8,128)S(1)}, f32[73,16]{1,0:T(8,128)S(1)}, u32[]{:S(2)}, u32[]{:S(2)}) collective-permute-start(f32[73,16]{1,0:T(8,128)S(1)} %add.218), channel_id=1, source_target_pairs={{0,96},{1,97},{2,98},{3,99},{4,100},{5,101},{6,102},{7,103},{8,104... | collective-permute-start | bytes 14024 | tf_op jit(solution)/shard_map/ppermute | solution.py:35

commit v10 on v9

--- a/solution.py
+++ b/solution.py
@@ -100,7 +100,7 @@
         grid_spec=grid_spec,
         out_shape=[out] * pieces,
         compiler_params=pltpu.CompilerParams(
-            dimension_semantics=("arbitrary",), vmem_limit_bytes=48 * 1024 * 1024
+            dimension_semantics=("arbitrary",), vmem_limit_bytes=28 * 1024 * 1024
         ),
     )(slot, near_part, far_part)
 

time: 111 us -> 103 us (0.928)
  Pallas kernels: 8.03 us -> 2.36 us
  matrix products: 12.5 us -> 10.7 us
    pallas_call x1, Pallas kernels: 8.03 us -> 2.36 us  [accumulate(): pl.pallas_call(accumulate_kernel, grid_spec=grid_spec, out_shape=[out] *...]
    dot_general x1, matrix products: 4.48 us -> 2.69 us  [on_device(): jnp.einsum('snk,skc->snc', coeff, far_v, preferred_element_type=jnp.float32)]
where the time goes in v10:
time: 103 us
  waiting for transfers between devices  50.2 us (49%)
  starting transfers between devices  30.7 us (30%)
  matrix products  10.7 us (10%)
  other arithmetic  4.28 us (4%)
  local copies, waits for them, and re-layouts  3.09 us (3%)
  Pallas kernels  2.36 us (2%)
  between operations  1.55 us (2%)
    ppermute x3, waiting for transfers between devices, reduce_to_owner(): acc = acc + lax.ppermute(pieces[k], AXES, moved('x', k, 'z'))  22.9 us
    ppermute x6, waiting for transfers between devices, all_sum(): v = v + lax.ppermute(v, AXES, flipped(step * STRIDE[axis]))  16.8 us
    ppermute x6, starting transfers between devices, spread(): acc = acc + lax.ppermute(pieces[k], AXES, moved(axis, k, other))  12.5 us
    ppermute x6, starting transfers between devices, all_sum(): v = v + lax.ppermute(v, AXES, flipped(step * STRIDE[axis]))  10.9 us
    ppermute x6, waiting for transfers between devices, spread(): acc = acc + lax.ppermute(pieces[k], AXES, moved(axis, k, other))  7.63 us
    ppermute x3, starting transfers between devices, reduce_to_owner(): acc = acc + lax.ppermute(pieces[k], AXES, moved('x', k, 'z'))  5.99 us
    dot_general x1, matrix products, on_device(): jnp.einsum('snc,skc->snk', picked[near_count:], far_u, preferred_element_...  3.24 us
    dot_general x1, matrix products, on_device(): jnp.einsum('snk,skc->snc', coeff, far_v, preferred_element_type=jnp.float32)  2.69 us
  transfers between devices with their start and end apart: 20, of which 15 were waited for; matrix products, arithmetic and copies ran while one was open for 2% of the time, Pallas kernels for 0%

profile of v10, /device:TPU:0, one launch (start us, length us, event | category | flops | bytes accessed | tf_op | source)
XLA Modules:
  0.0 102.9 jit_solution(8716098934090164775)
XLA Ops:
  0.7 0.8 bitcast_convert_fusion
  1.6 0.7 compare_select_fusion
  2.2 0.7 gather_fusion
  2.9 3.2 %convolution_convert_fusion = bf16[112,16,32]{2,1,0:T(8,128)(2,1)S(1)} fusion(bf16[128,16,512]{2,1,0:T(8,128)(2,1)S(1)} %gather_fusion, bf16[112,32,512]{2,1,0:T(8,128)(2,1)} %param.13), kind=kOutput, calls=%fused_computation.3 | convolution fusion | flops 58777600 | bytes 5881856 | tf_op jit(solution)/shard_map/snc,skc->snk/dot_general | solution.py:123
  6.2 1.2 %copy-done.4 = bf16[16,512,512]{2,1,0:T(8,128)(2,1)S(1)} copy-done((bf16[16,512,512]{2,1,0:T(8,128)(2,1)S(1)}, bf16[16,512,512]{2,1,0:T(8,128)(2,1)}, u32[]{:S(2)}) %copy-start.4) | copy-done | bytes 8388632
  7.4 1.2 %fusion.35.near_ref = f32[16,16,512]{2,1,0:T(8,128)S(1)} fusion(bf16[128,16,512]{2,1,0:T(8,128)(2,1)S(1)} %gather_fusion, bf16[16,512,512]{2,1,0:T(8,128)(2,1)S(1)} %copy-done.4), kind=kOutput, calls=%fused_computation.104 | convolution fusion | flops 134217728 | bytes 11010048 | tf_op jit(solution)/shard_map/snc,scd->snd/dot_general | solution.py:120
  8.6 2.7 %fusion.34.far_ref = f32[112,16,512]{2,1,0:T(8,128)S(1)} fusion(bf16[112,16,32]{2,1,0:T(8,128)(2,1)S(1)} %convolution_convert_fusion, bf16[112,32,512]{2,1,0:T(8,128)(2,1)} %param.14), kind=kOutput, calls=%fused_computation.103 | convolution fusion | flops 58720256 | bytes 7454720 | tf_op jit(solution)/shard_map/snk,skc->snc/dot_general | solution.py:126
  11.3 2.4 %shard_map.95 = (f32[32,16,512]{2,1,0:T(8,128)S(1)}, f32[32,16,512]{2,1,0:T(8,128)S(1)}, f32[32,16,512]{2,1,0:T(8,128)S(1)}, f32[32,16,512]{2,1,0:T(8,128)S(1)},...) custom-call(s32[128]{0:T(128)S(1)} %multiply_add_fusion.slot_ref, ...), custom_call_target="tpu_custom_call" | custom-call | tf_op jit(solution)/shard_map/pallas_call | solution.py:98
  13.8 0.5 collective-permute-start.10
  14.4 0.4 collective-permute-start.7
  14.8 1.6 %collective-permute-done.8 = f32[4,4,2,16,512]{4,3,2,1,0:T(8,128)S(1)} collective-permute-done((f32[4,4,2,16,512]{4,3,2,1,0:T(8,128)S(1)}, f32[4,4,2,16,512]{4,3,2,1,0:T(8,128)S(1)}, u32[]{:S(2)}, u32[]{:S(2)}) %collective-permute-start.8) | collective-permute-done | bytes 1048608 | tf_op jit(solution)/shard_map/ppermute | solution.py:47
  16.5 0.2 add.200
  16.7 1.7 %collective-permute-start.9 = (f32[4,4,2,16,512]{4,3,2,1,0:T(8,128)S(1)}, f32[4,4,2,16,512]{4,3,2,1,0:T(8,128)S(1)}, u32[]{:S(2)}, u32[]{:S(2)}) collective-permute-start(f32[4,4,2,16,512]{4,3,2,1,0:T(8,128)S(1)} %add.200), channel_id=1, source_target_pairs={{0,2},{1,9},{2,4},{3,11},{4,6},{5,13},{6,0},{7,15},{8,10},{9,17},{... | collective-permute-start | bytes 3145736 | tf_op jit(solution)/shard_map/ppermute | solution.py:50
  18.6 2.8 %collective-permute-start.11 = (f32[4,4,2,16,512]{4,3,2,1,0:T(8,128)S(1)}, f32[4,4,2,16,512]{4,3,2,1,0:T(8,128)S(1)}, u32[]{:S(2)}, u32[]{:S(2)}) collective-permute-start(f32[4,4,2,16,512]{4,3,2,1,0:T(8,128)S(1)} %add.202), channel_id=1, source_target_pairs={{0,4},{1,17},{2,6},{3,19},{4,0},{5,21},{6,2},{7,23},{8,12},{9,25},... | collective-permute-start | bytes 3145736 | tf_op jit(solution)/shard_map/ppermute | solution.py:50
  21.6 1.5 %collective-permute-start.13 = (f32[4,4,2,16,512]{4,3,2,1,0:T(8,128)S(1)}, f32[4,4,2,16,512]{4,3,2,1,0:T(8,128)S(1)}, u32[]{:S(2)}, u32[]{:S(2)}) collective-permute-start(f32[4,4,2,16,512]{4,3,2,1,0:T(8,128)S(1)} %add.204), channel_id=1, source_target_pairs={{0,6},{1,25},{2,0},{3,27},{4,2},{5,29},{6,4},{7,31},{8,14},{9,1},{... | collective-permute-start | bytes 3145736 | tf_op jit(solution)/shard_map/ppermute | solution.py:50
  23.1 9.7 %collective-permute-done.9 = f32[4,4,2,16,512]{4,3,2,1,0:T(8,128)S(1)} collective-permute-done((f32[4,4,2,16,512]{4,3,2,1,0:T(8,128)S(1)}, f32[4,4,2,16,512]{4,3,2,1,0:T(8,128)S(1)}, u32[]{:S(2)}, u32[]{:S(2)}) %collective-permute-start.9) | collective-permute-done | bytes 1048608 | tf_op jit(solution)/shard_map/ppermute | solution.py:50
  32.7 12.3 %collective-permute-done.11 = f32[4,4,2,16,512]{4,3,2,1,0:T(8,128)S(1)} collective-permute-done((f32[4,4,2,16,512]{4,3,2,1,0:T(8,128)S(1)}, f32[4,4,2,16,512]{4,3,2,1,0:T(8,128)S(1)}, u32[]{:S(2)}, u32[]{:S(2)}) %collective-permute-start.11) | collective-permute-done | bytes 1048608 | tf_op jit(solution)/shard_map/ppermute | solution.py:50
  45.1 0.9 collective-permute-done.13
  46.0 0.6 add_add_fusion
  46.7 2.0 %collective-permute-start.14 = (f32[4,2,16,512]{3,2,1,0:T(8,128)S(1)}, f32[4,2,16,512]{3,2,1,0:T(8,128)S(1)}, u32[]{:S(2)}, u32[]{:S(2)}) collective-permute-start(f32[4,2,16,512]{3,2,1,0:T(8,128)S(1)} %get-tuple-element.29), channel_id=1, source_target_pairs={{0,8},{1,3},{2,10},{3,5},{4,12},{5,7},{6,14},{7,1},{8,16},{9,11},{... | collective-permute-start | bytes 786440 | tf_op jit(solution)/shard_map/ppermute | solution.py:42
  48.7 3.6 %collective-permute-start.15 = (f32[4,2,16,512]{3,2,1,0:T(8,128)S(1)}, f32[4,2,16,512]{3,2,1,0:T(8,128)S(1)}, u32[]{:S(2)}, u32[]{:S(2)}) collective-permute-start(f32[4,2,16,512]{3,2,1,0:T(8,128)S(1)} %get-tuple-element.31), channel_id=1, source_target_pairs={{0,16},{1,5},{2,18},{3,7},{4,20},{5,1},{6,22},{7,3},{8,24},{9,13},... | collective-permute-start | bytes 786440 | tf_op jit(solution)/shard_map/ppermute | solution.py:42
  52.3 1.0 collective-permute-start.16
  53.3 1.9 %collective-permute-done.14 = f32[4,2,16,512]{3,2,1,0:T(8,128)S(1)} collective-permute-done((f32[4,2,16,512]{3,2,1,0:T(8,128)S(1)}, f32[4,2,16,512]{3,2,1,0:T(8,128)S(1)}, u32[]{:S(2)}, u32[]{:S(2)}) %collective-permute-start.14) | collective-permute-done | bytes 262176 | tf_op jit(solution)/shard_map/ppermute | solution.py:42
  55.2 4.3 %collective-permute-done.15 = f32[4,2,16,512]{3,2,1,0:T(8,128)S(1)} collective-permute-done((f32[4,2,16,512]{3,2,1,0:T(8,128)S(1)}, f32[4,2,16,512]{3,2,1,0:T(8,128)S(1)}, u32[]{:S(2)}, u32[]{:S(2)}) %collective-permute-start.15) | collective-permute-done | bytes 262176 | tf_op jit(solution)/shard_map/ppermute | solution.py:42
  59.6 1.6 %collective-permute-start.17 = (f32[2,16,512]{2,1,0:T(8,128)S(1)}, f32[2,16,512]{2,1,0:T(8,128)S(1)}, u32[]{:S(2)}, u32[]{:S(2)}) collective-permute-start(f32[2,16,512]{2,1,0:T(8,128)S(1)} %get-tuple-element.32), channel_id=1, source_target_pairs={{0,32},{1,33},{2,34},{3,35},{4,36},{5,37},{6,38},{7,39},{8,40},{9,... | collective-permute-start | bytes 196616 | tf_op jit(solution)/shard_map/ppermute | solution.py:42
  61.2 2.9 %collective-permute-start.18 = (f32[2,16,512]{2,1,0:T(8,128)S(1)}, f32[2,16,512]{2,1,0:T(8,128)S(1)}, u32[]{:S(2)}, u32[]{:S(2)}) collective-permute-start(f32[2,16,512]{2,1,0:T(8,128)S(1)} %get-tuple-element.34), channel_id=1, source_target_pairs={{0,64},{1,65},{2,66},{3,67},{4,68},{5,69},{6,70},{7,71},{8,72},{9,... | collective-permute-start | bytes 196616 | tf_op jit(solution)/shard_map/ppermute | solution.py:42
  64.1 1.3 %collective-permute-start.19 = (f32[2,16,512]{2,1,0:T(8,128)S(1)}, f32[2,16,512]{2,1,0:T(8,128)S(1)}, u32[]{:S(2)}, u32[]{:S(2)}) collective-permute-start(f32[2,16,512]{2,1,0:T(8,128)S(1)} %get-tuple-element.33), channel_id=1, source_target_pairs={{0,96},{1,97},{2,98},{3,99},{4,100},{5,101},{6,102},{7,103},{8,104... | collective-permute-start | bytes 196616 | tf_op jit(solution)/shard_map/ppermute | solution.py:42
  65.5 1.3 %convolution_bitcast_fusion = f32[8,8,16]{0,1,2:T(8,128)S(1)} fusion(f32[8,2,16,512]{3,2,1,0:T(8,128)S(1)} %copy-done), kind=kOutput, calls=%fused_computation.4 | convolution fusion | flops 12582912 | bytes 528384 | tf_op jit(solution)/shard_map/knjc,mnjc->kmj/dot_general | solution.py:140
  67.0 1.3 %collective-permute-done.19 = f32[2,16,512]{2,1,0:T(8,128)S(1)} collective-permute-done((f32[2,16,512]{2,1,0:T(8,128)S(1)}, f32[2,16,512]{2,1,0:T(8,128)S(1)}, u32[]{:S(2)}, u32[]{:S(2)}) %collective-permute-start.19) | collective-permute-done | bytes 65568 | tf_op jit(solution)/shard_map/ppermute | solution.py:42
  68.5 1.5 %fusion.2 = f32[16,1,8,1]{2,1,3,0:T(1,128)S(1)} fusion(f32[8,2,16,512]{3,2,1,0:T(8,128)S(1)} %copy-done, f32[2,16,512,1]{2,1,0,3:T(8,128)S(1)} %bitcast.125), kind=kOutput, calls=%fused_computation.8 | convolution fusion | flops 1572864 | bytes 590336 | tf_op jit(solution)/shard_map/knjc,njc->kj/dot_general | solution.py:139
  70.0 0.2 collective-permute-start.20
  70.3 1.2 %collective-permute-done.20 = f32[73,16]{1,0:T(8,128)S(1)} collective-permute-done((f32[73,16]{1,0:T(8,128)S(1)}, f32[73,16]{1,0:T(8,128)S(1)}, u32[]{:S(2)}, u32[]{:S(2)}) %collective-permute-start.20) | collective-permute-done | bytes 4704 | tf_op jit(solution)/shard_map/ppermute | solution.py:32
  71.5 1.7 %collective-permute-start.21 = (f32[73,16]{1,0:T(8,128)S(1)}, f32[73,16]{1,0:T(8,128)S(1)}, u32[]{:S(2)}, u32[]{:S(2)}) collective-permute-start(f32[73,16]{1,0:T(8,128)S(1)} %fusion.32), channel_id=1, source_target_pairs={{0,2},{1,3},{2,0},{3,1},{4,6},{5,7},{6,4},{7,5},{8,10},{9,11},{10,... | collective-permute-start | bytes 14024 | tf_op jit(solution)/shard_map/ppermute | solution.py:35
  73.2 2.4 %collective-permute-done.21 = f32[73,16]{1,0:T(8,128)S(1)} collective-permute-done((f32[73,16]{1,0:T(8,128)S(1)}, f32[73,16]{1,0:T(8,128)S(1)}, u32[]{:S(2)}, u32[]{:S(2)}) %collective-permute-start.21) | collective-permute-done | bytes 4704 | tf_op jit(solution)/shard_map/ppermute | solution.py:35
  75.6 2.6 %collective-permute-start.22 = (f32[73,16]{1,0:T(8,128)S(1)}, f32[73,16]{1,0:T(8,128)S(1)}, u32[]{:S(2)}, u32[]{:S(2)}) collective-permute-start(f32[73,16]{1,0:T(8,128)S(1)} %add.214), channel_id=1, source_target_pairs={{0,6},{1,7},{2,4},{3,5},{4,2},{5,3},{6,0},{7,1},{8,14},{9,15},{10,... | collective-permute-start | bytes 14024 | tf_op jit(solution)/shard_map/ppermute | solution.py:35
  78.2 2.6 %collective-permute-done.22 = f32[73,16]{1,0:T(8,128)S(1)} collective-permute-done((f32[73,16]{1,0:T(8,128)S(1)}, f32[73,16]{1,0:T(8,128)S(1)}, u32[]{:S(2)}, u32[]{:S(2)}) %collective-permute-start.22) | collective-permute-done | bytes 4704 | tf_op jit(solution)/shard_map/ppermute | solution.py:35
  80.8 1.5 %collective-permute-start.23 = (f32[73,16]{1,0:T(8,128)S(1)}, f32[73,16]{1,0:T(8,128)S(1)}, u32[]{:S(2)}, u32[]{:S(2)}) collective-permute-start(f32[73,16]{1,0:T(8,128)S(1)} %add.215), channel_id=1, source_target_pairs={{0,8},{1,9},{2,10},{3,11},{4,12},{5,13},{6,14},{7,15},{8,0},{9,1},... | collective-permute-start | bytes 14024 | tf_op jit(solution)/shard_map/ppermute | solution.py:35
  82.3 2.5 %collective-permute-done.23 = f32[73,16]{1,0:T(8,128)S(1)} collective-permute-done((f32[73,16]{1,0:T(8,128)S(1)}, f32[73,16]{1,0:T(8,128)S(1)}, u32[]{:S(2)}, u32[]{:S(2)}) %collective-permute-start.23) | collective-permute-done | bytes 4704 | tf_op jit(solution)/shard_map/ppermute | solution.py:35
  84.8 2.2 %collective-permute-start.24 = (f32[73,16]{1,0:T(8,128)S(1)}, f32[73,16]{1,0:T(8,128)S(1)}, u32[]{:S(2)}, u32[]{:S(2)}) collective-permute-start(f32[73,16]{1,0:T(8,128)S(1)} %add.216), channel_id=1, source_target_pairs={{0,24},{1,25},{2,26},{3,27},{4,28},{5,29},{6,30},{7,31},{8,16},{9,... | collective-permute-start | bytes 14024 | tf_op jit(solution)/shard_map/ppermute | solution.py:35
  87.0 3.1 %collective-permute-done.24 = f32[73,16]{1,0:T(8,128)S(1)} collective-permute-done((f32[73,16]{1,0:T(8,128)S(1)}, f32[73,16]{1,0:T(8,128)S(1)}, u32[]{:S(2)}, u32[]{:S(2)}) %collective-permute-start.24) | collective-permute-done | bytes 4704 | tf_op jit(solution)/shard_map/ppermute | solution.py:35
  90.0 0.3 collective-permute-start.25
  90.4 3.7 %collective-permute-done.25 = f32[73,16]{1,0:T(8,128)S(1)} collective-permute-done((f32[73,16]{1,0:T(8,128)S(1)}, f32[73,16]{1,0:T(8,128)S(1)}, u32[]{:S(2)}, u32[]{:S(2)}) %collective-permute-start.25) | collective-permute-done | bytes 4704 | tf_op jit(solution)/shard_map/ppermute | solution.py:35
  94.0 2.6 %collective-permute-start.26 = (f32[73,16]{1,0:T(8,128)S(1)}, f32[73,16]{1,0:T(8,128)S(1)}, u32[]{:S(2)}, u32[]{:S(2)}) collective-permute-start(f32[73,16]{1,0:T(8,128)S(1)} %add.218), channel_id=1, source_target_pairs={{0,96},{1,97},{2,98},{3,99},{4,100},{5,101},{6,102},{7,103},{8,104... | collective-permute-start | bytes 14024 | tf_op jit(solution)/shard_map/ppermute | solution.py:35
  96.6 2.7 %collective-permute-done.26 = f32[73,16]{1,0:T(8,128)S(1)} collective-permute-done((f32[73,16]{1,0:T(8,128)S(1)}, f32[73,16]{1,0:T(8,128)S(1)}, u32[]{:S(2)}, u32[]{:S(2)}) %collective-permute-start.26) | collective-permute-done | bytes 4704 | tf_op jit(solution)/shard_map/ppermute | solution.py:35
  99.4 0.6 compare_reduce_fusion
  100.7 0.8 fusion
  101.6 0.6 pad_maximum_fusion.1
  102.2 0.7 broadcast_divide_fusion
  (45 shorter events, 1.5 us)
Async XLA Ops:
  2.9 4.5 %copy-start.4 = (bf16[16,512,512]{2,1,0:T(8,128)(2,1)S(1)}, bf16[16,512,512]{2,1,0:T(8,128)(2,1)}, u32[]{:S(2)}) copy-start(bf16[16,512,512]{2,1,0:T(8,128)(2,1)} %param.12) | copy-start | bytes 25165828
  8.6 2.7 %copy-start.2 = (s32[128]{0:T(128)S(1)}, s32[128]{0:T(128)}, u32[]{:S(2)}) copy-start(s32[128]{0:T(128)} %param.17) | copy-start | bytes 1540
  8.6 2.7 %copy-start.3 = (s32[128,1]{0,1:T(1,128)S(1)}, s32[128,1]{0,1:T(1,128)}, u32[]{:S(2)}) copy-start(s32[128,1]{0,1:T(1,128)} %param.16) | copy-start | bytes 1540
  13.7 2.7 %collective-permute-start.8 = (f32[4,4,2,16,512]{4,3,2,1,0:T(8,128)S(1)}, f32[4,4,2,16,512]{4,3,2,1,0:T(8,128)S(1)}, u32[]{:S(2)}, u32[]{:S(2)}) collective-permute-start(f32[4,4,2,16,512]{4,3,2,1,0:T(8,128)S(1)} %bitcast.124), channel_id=1, source_target_pairs={{0,1},{1,0},{2,3},{3,2},{4,5},{5,4},{6,7},{7,6},{8,9},{9,8},{10,11... | collective-permute-start | bytes 3145736 | tf_op jit(solution)/shard_map/ppermute | solution.py:47
  13.8 4.5 %collective-permute-start.10 = (f32[4,4,2,16,512]{4,3,2,1,0:T(8,128)S(1)}, f32[4,4,2,16,512]{4,3,2,1,0:T(8,128)S(1)}, u32[]{:S(2)}, u32[]{:S(2)}) collective-permute-start(f32[4,4,2,16,512]{4,3,2,1,0:T(8,128)S(1)} %bitcast.123), channel_id=1, source_target_pairs={{0,1},{1,0},{2,3},{3,2},{4,5},{5,4},{6,7},{7,6},{8,9},{9,8},{10,11... | collective-permute-start | bytes 3145736 | tf_op jit(solution)/shard_map/ppermute | solution.py:47
  14.3 7.1 %collective-permute-start.12 = (f32[4,4,2,16,512]{4,3,2,1,0:T(8,128)S(1)}, f32[4,4,2,16,512]{4,3,2,1,0:T(8,128)S(1)}, u32[]{:S(2)}, u32[]{:S(2)}) collective-permute-start(f32[4,4,2,16,512]{4,3,2,1,0:T(8,128)S(1)} %bitcast.122), channel_id=1, source_target_pairs={{0,1},{1,0},{2,3},{3,2},{4,5},{5,4},{6,7},{7,6},{8,9},{9,8},{10,11... | collective-permute-start | bytes 3145736 | tf_op jit(solution)/shard_map/ppermute | solution.py:47
  14.4 8.7 %collective-permute-start.7 = (f32[4,4,2,16,512]{4,3,2,1,0:T(8,128)S(1)}, f32[4,4,2,16,512]{4,3,2,1,0:T(8,128)S(1)}, u32[]{:S(2)}, u32[]{:S(2)}) collective-permute-start(f32[4,4,2,16,512]{4,3,2,1,0:T(8,128)S(1)} %bitcast.121), channel_id=1, source_target_pairs={{0,1},{1,0},{2,3},{3,2},{4,5},{5,4},{6,7},{7,6},{8,9},{9,8},{10,11... | collective-permute-start | bytes 3145736 | tf_op jit(solution)/shard_map/ppermute | solution.py:47
  16.7 16.1 %collective-permute-start.9 = (f32[4,4,2,16,512]{4,3,2,1,0:T(8,128)S(1)}, f32[4,4,2,16,512]{4,3,2,1,0:T(8,128)S(1)}, u32[]{:S(2)}, u32[]{:S(2)}) collective-permute-start(f32[4,4,2,16,512]{4,3,2,1,0:T(8,128)S(1)} %add.200), channel_id=1, source_target_pairs={{0,2},{1,9},{2,4},{3,11},{4,6},{5,13},{6,0},{7,15},{8,10},{9,17},{... | collective-permute-start | bytes 3145736 | tf_op jit(solution)/shard_map/ppermute | solution.py:50
  18.6 26.5 %collective-permute-start.11 = (f32[4,4,2,16,512]{4,3,2,1,0:T(8,128)S(1)}, f32[4,4,2,16,512]{4,3,2,1,0:T(8,128)S(1)}, u32[]{:S(2)}, u32[]{:S(2)}) collective-permute-start(f32[4,4,2,16,512]{4,3,2,1,0:T(8,128)S(1)} %add.202), channel_id=1, source_target_pairs={{0,4},{1,17},{2,6},{3,19},{4,0},{5,21},{6,2},{7,23},{8,12},{9,25},... | collective-permute-start | bytes 3145736 | tf_op jit(solution)/shard_map/ppermute | solution.py:50
  21.6 24.4 %collective-permute-start.13 = (f32[4,4,2,16,512]{4,3,2,1,0:T(8,128)S(1)}, f32[4,4,2,16,512]{4,3,2,1,0:T(8,128)S(1)}, u32[]{:S(2)}, u32[]{:S(2)}) collective-permute-start(f32[4,4,2,16,512]{4,3,2,1,0:T(8,128)S(1)} %add.204), channel_id=1, source_target_pairs={{0,6},{1,25},{2,0},{3,27},{4,2},{5,29},{6,4},{7,31},{8,14},{9,1},{... | collective-permute-start | bytes 3145736 | tf_op jit(solution)/shard_map/ppermute | solution.py:50
  46.0 19.4 %copy-start = (f32[8,2,16,512]{3,2,1,0:T(8,128)S(1)}, f32[8,2,16,512]{3,2,1,0:T(8,128)}, u32[]{:S(2)}) copy-start(f32[8,2,16,512]{3,2,1,0:T(8,128)} %param.10) | copy-start | bytes 1572868
  46.0 22.3 %copy-start.1 = (f32[2,512]{1,0:T(2,128)S(1)}, f32[2,512]{1,0:T(2,128)}, u32[]{:S(2)}) copy-start(f32[2,512]{1,0:T(2,128)} %param.11) | copy-start | bytes 12292
  46.7 8.5 %collective-permute-start.14 = (f32[4,2,16,512]{3,2,1,0:T(8,128)S(1)}, f32[4,2,16,512]{3,2,1,0:T(8,128)S(1)}, u32[]{:S(2)}, u32[]{:S(2)}) collective-permute-start(f32[4,2,16,512]{3,2,1,0:T(8,128)S(1)} %get-tuple-element.29), channel_id=1, source_target_pairs={{0,8},{1,3},{2,10},{3,5},{4,12},{5,7},{6,14},{7,1},{8,16},{9,11},{... | collective-permute-start | bytes 786440 | tf_op jit(solution)/shard_map/ppermute | solution.py:42
  48.7 10.7 %collective-permute-start.15 = (f32[4,2,16,512]{3,2,1,0:T(8,128)S(1)}, f32[4,2,16,512]{3,2,1,0:T(8,128)S(1)}, u32[]{:S(2)}, u32[]{:S(2)}) collective-permute-start(f32[4,2,16,512]{3,2,1,0:T(8,128)S(1)} %get-tuple-element.31), channel_id=1, source_target_pairs={{0,16},{1,5},{2,18},{3,7},{4,20},{5,1},{6,22},{7,3},{8,24},{9,13},... | collective-permute-start | bytes 786440 | tf_op jit(solution)/shard_map/ppermute | solution.py:42
  52.3 7.2 %collective-permute-start.16 = (f32[4,2,16,512]{3,2,1,0:T(8,128)S(1)}, f32[4,2,16,512]{3,2,1,0:T(8,128)S(1)}, u32[]{:S(2)}, u32[]{:S(2)}) collective-permute-start(f32[4,2,16,512]{3,2,1,0:T(8,128)S(1)} %get-tuple-element.30), channel_id=1, source_target_pairs={{0,24},{1,7},{2,26},{3,1},{4,28},{5,3},{6,30},{7,5},{8,0},{9,15},{... | collective-permute-start | bytes 786440 | tf_op jit(solution)/shard_map/ppermute | solution.py:42
  59.6 7.3 %collective-permute-start.17 = (f32[2,16,512]{2,1,0:T(8,128)S(1)}, f32[2,16,512]{2,1,0:T(8,128)S(1)}, u32[]{:S(2)}, u32[]{:S(2)}) collective-permute-start(f32[2,16,512]{2,1,0:T(8,128)S(1)} %get-tuple-element.32), channel_id=1, source_target_pairs={{0,32},{1,33},{2,34},{3,35},{4,36},{5,37},{6,38},{7,39},{8,40},{9,... | collective-permute-start | bytes 196616 | tf_op jit(solution)/shard_map/ppermute | solution.py:42
  61.2 5.8 %collective-permute-start.18 = (f32[2,16,512]{2,1,0:T(8,128)S(1)}, f32[2,16,512]{2,1,0:T(8,128)S(1)}, u32[]{:S(2)}, u32[]{:S(2)}) collective-permute-start(f32[2,16,512]{2,1,0:T(8,128)S(1)} %get-tuple-element.34), channel_id=1, source_target_pairs={{0,64},{1,65},{2,66},{3,67},{4,68},{5,69},{6,70},{7,71},{8,72},{9,... | collective-permute-start | bytes 196616 | tf_op jit(solution)/shard_map/ppermute | solution.py:42
  64.1 4.3 %collective-permute-start.19 = (f32[2,16,512]{2,1,0:T(8,128)S(1)}, f32[2,16,512]{2,1,0:T(8,128)S(1)}, u32[]{:S(2)}, u32[]{:S(2)}) collective-permute-start(f32[2,16,512]{2,1,0:T(8,128)S(1)} %get-tuple-element.33), channel_id=1, source_target_pairs={{0,96},{1,97},{2,98},{3,99},{4,100},{5,101},{6,102},{7,103},{8,104... | collective-permute-start | bytes 196616 | tf_op jit(solution)/shard_map/ppermute | solution.py:42
  70.0 1.4 %collective-permute-start.20 = (f32[73,16]{1,0:T(8,128)S(1)}, f32[73,16]{1,0:T(8,128)S(1)}, u32[]{:S(2)}, u32[]{:S(2)}) collective-permute-start(f32[73,16]{1,0:T(8,128)S(1)} %pad_maximum_fusion), channel_id=1, source_target_pairs={{0,1},{1,0},{2,3},{3,2},{4,5},{5,4},{6,7},{7,6},{8,9},{9,8},{10,11... | collective-permute-start | bytes 14024 | tf_op jit(solution)/shard_map/ppermute | solution.py:32
  71.5 4.1 %collective-permute-start.21 = (f32[73,16]{1,0:T(8,128)S(1)}, f32[73,16]{1,0:T(8,128)S(1)}, u32[]{:S(2)}, u32[]{:S(2)}) collective-permute-start(f32[73,16]{1,0:T(8,128)S(1)} %fusion.32), channel_id=1, source_target_pairs={{0,2},{1,3},{2,0},{3,1},{4,6},{5,7},{6,4},{7,5},{8,10},{9,11},{10,... | collective-permute-start | bytes 14024 | tf_op jit(solution)/shard_map/ppermute | solution.py:35
  75.6 5.2 %collective-permute-start.22 = (f32[73,16]{1,0:T(8,128)S(1)}, f32[73,16]{1,0:T(8,128)S(1)}, u32[]{:S(2)}, u32[]{:S(2)}) collective-permute-start(f32[73,16]{1,0:T(8,128)S(1)} %add.214), channel_id=1, source_target_pairs={{0,6},{1,7},{2,4},{3,5},{4,2},{5,3},{6,0},{7,1},{8,14},{9,15},{10,... | collective-permute-start | bytes 14024 | tf_op jit(solution)/shard_map/ppermute | solution.py:35
  80.8 4.0 %collective-permute-start.23 = (f32[73,16]{1,0:T(8,128)S(1)}, f32[73,16]{1,0:T(8,128)S(1)}, u32[]{:S(2)}, u32[]{:S(2)}) collective-permute-start(f32[73,16]{1,0:T(8,128)S(1)} %add.215), channel_id=1, source_target_pairs={{0,8},{1,9},{2,10},{3,11},{4,12},{5,13},{6,14},{7,15},{8,0},{9,1},... | collective-permute-start | bytes 14024 | tf_op jit(solution)/shard_map/ppermute | solution.py:35
  84.8 5.2 %collective-permute-start.24 = (f32[73,16]{1,0:T(8,128)S(1)}, f32[73,16]{1,0:T(8,128)S(1)}, u32[]{:S(2)}, u32[]{:S(2)}) collective-permute-start(f32[73,16]{1,0:T(8,128)S(1)} %add.216), channel_id=1, source_target_pairs={{0,24},{1,25},{2,26},{3,27},{4,28},{5,29},{6,30},{7,31},{8,16},{9,... | collective-permute-start | bytes 14024 | tf_op jit(solution)/shard_map/ppermute | solution.py:35
  90.0 4.0 %collective-permute-start.25 = (f32[73,16]{1,0:T(8,128)S(1)}, f32[73,16]{1,0:T(8,128)S(1)}, u32[]{:S(2)}, u32[]{:S(2)}) collective-permute-start(f32[73,16]{1,0:T(8,128)S(1)} %add.217), channel_id=1, source_target_pairs={{0,32},{1,33},{2,34},{3,35},{4,36},{5,37},{6,38},{7,39},{8,40},{9,... | collective-permute-start | bytes 14024 | tf_op jit(solution)/shard_map/ppermute | solution.py:35
  94.0 5.2 %collective-permute-start.26 = (f32[73,16]{1,0:T(8,128)S(1)}, f32[73,16]{1,0:T(8,128)S(1)}, u32[]{:S(2)}, u32[]{:S(2)}) collective-permute-start(f32[73,16]{1,0:T(8,128)S(1)} %add.218), channel_id=1, source_target_pairs={{0,96},{1,97},{2,98},{3,99},{4,100},{5,101},{6,102},{7,103},{8,104... | collective-permute-start | bytes 14024 | tf_op jit(solution)/shard_map/ppermute | solution.py:35

commit v11 on v10

--- a/solution.py
+++ b/solution.py
@@ -120,8 +120,10 @@
     near_part = jnp.einsum(
         "snc,scd->snd", picked[:near_count], near_blocks, preferred_element_type=jnp.float32
     )
-    coeff = jnp.einsum(
-        "snc,skc->snk", picked[near_count:], far_u, preferred_element_type=jnp.float32
+    both_rows = jnp.einsum("rnc,skc->srnk", vec_low, far_u, preferred_element_type=jnp.float32)
+    far_rows = block_row[near_count:]
+    coeff = jnp.where(
+        (far_rows == 0)[:, None, None], both_rows[:, 0], both_rows[:, 1]
     ).astype(jnp.bfloat16)
     far_part = jnp.einsum("snk,skc->snc", coeff, far_v, preferred_element_type=jnp.float32)
     dest = block_dest[:, 0]

time: 103 us -> 106 us (1.029)
  matrix products: 10.7 us -> 14 us
  local copies, waits for them, and re-layouts: 3.09 us -> 1.86 us
    dot_general x1, matrix products: 1.19 us -> 4.73 us  [on_device(): jnp.einsum('snc,scd->snd', picked[:near_count], near_blocks, preferred_el...]
    dot_general x1, matrix products: 2.69 us -> 0.72 us  [on_device(): jnp.einsum('snk,skc->snc', coeff, far_v, preferred_element_type=jnp.float32)]
    dot_general x1, matrix products: 3.24 us -> 4.96 us  [on_device(): jnp.einsum('rnc,skc->srnk', vec_low, far_u, preferred_element_type=jnp.fl...]
    unnamed x10, local copies, waits for them, and re-layouts: 1.26 us -> 0.02 us
where the time goes in v11:
time: 106 us
  waiting for transfers between devices  50.2 us (47%)
  starting transfers between devices  30.5 us (29%)
  matrix products  14 us (13%)
  other arithmetic  5.02 us (5%)
  Pallas kernels  2.36 us (2%)
  local copies, waits for them, and re-layouts  1.86 us (2%)
  between operations  1.61 us (2%)
    ppermute x3, waiting for transfers between devices, reduce_to_owner(): acc = acc + lax.ppermute(pieces[k], AXES, moved('x', k, 'z'))  22.9 us
    ppermute x6, waiting for transfers between devices, all_sum(): v = v + lax.ppermute(v, AXES, flipped(step * STRIDE[axis]))  16.8 us
    ppermute x6, starting transfers between devices, spread(): acc = acc + lax.ppermute(pieces[k], AXES, moved(axis, k, other))  12.5 us
    ppermute x6, starting transfers between devices, all_sum(): v = v + lax.ppermute(v, AXES, flipped(step * STRIDE[axis]))  10.9 us
    ppermute x6, waiting for transfers between devices, spread(): acc = acc + lax.ppermute(pieces[k], AXES, moved(axis, k, other))  7.62 us
    ppermute x3, starting transfers between devices, reduce_to_owner(): acc = acc + lax.ppermute(pieces[k], AXES, moved('x', k, 'z'))  5.99 us
    dot_general x1, matrix products, on_device(): jnp.einsum('rnc,skc->srnk', vec_low, far_u, preferred_element_type=jnp.fl...  4.96 us
    dot_general x1, matrix products, on_device(): jnp.einsum('snc,scd->snd', picked[:near_count], near_blocks, preferred_el...  4.73 us
  transfers between devices with their start and end apart: 20, of which 15 were waited for; matrix products, arithmetic and copies ran while one was open for 2% of the time, Pallas kernels for 0%

profile of v11, /device:TPU:0, one launch (start us, length us, event | category | flops | bytes accessed | tf_op | source)
XLA Modules:
  0.0 105.6 jit_solution(4599209458123281900)
XLA Ops:
  0.7 0.7 slice_compare_fusion
  1.4 0.7 compare_select_fusion
  2.1 0.8 bitcast_convert_fusion
  2.9 5.0 %fusion.2 = bf16[112,2,16,32]{3,2,1,0:T(8,128)(2,1)S(1)} fusion(bf16[112,32,512]{2,1,0:T(8,128)(2,1)} %param.13, f32[8,2,16,512]{3,2,1,0:T(8,128)} %param.10), kind=kOutput, calls=%fused_computation.5 | convolution fusion | flops 117440512 | bytes 3932160 | tf_op jit(solution)/shard_map/rnc,skc->srnk/dot_general | solution.py:123
  8.0 0.7 gather_fusion
  8.7 4.7 %fusion.45.near_ref = f32[16,16,512]{2,1,0:T(8,128)S(1)} fusion(bf16[128,16,512]{2,1,0:T(8,128)(2,1)S(1)} %gather_fusion, bf16[16,512,512]{2,1,0:T(8,128)(2,1)} %param.12), kind=kOutput, calls=%fused_computation.113 | convolution fusion | flops 134217728 | bytes 11010048 | tf_op jit(solution)/shard_map/snc,scd->snd/dot_general | solution.py:120
  13.4 0.7 fusion.12.far_ref
  14.2 2.4 %shard_map.95 = (f32[32,16,512]{2,1,0:T(8,128)S(1)}, f32[32,16,512]{2,1,0:T(8,128)S(1)}, f32[32,16,512]{2,1,0:T(8,128)S(1)}, f32[32,16,512]{2,1,0:T(8,128)S(1)},...) custom-call(s32[128]{0:T(128)S(1)} %multiply_add_fusion.slot_ref, ...), custom_call_target="tpu_custom_call" | custom-call | tf_op jit(solution)/shard_map/pallas_call | solution.py:98
  16.7 0.5 collective-permute-start.10
  17.3 0.4 collective-permute-start.7
  17.7 1.6 %collective-permute-done.8 = f32[4,4,2,16,512]{4,3,2,1,0:T(8,128)S(1)} collective-permute-done((f32[4,4,2,16,512]{4,3,2,1,0:T(8,128)S(1)}, f32[4,4,2,16,512]{4,3,2,1,0:T(8,128)S(1)}, u32[]{:S(2)}, u32[]{:S(2)}) %collective-permute-start.8) | collective-permute-done | bytes 1048608 | tf_op jit(solution)/shard_map/ppermute | solution.py:47
  19.3 0.2 add.200
  19.5 1.7 %collective-permute-start.9 = (f32[4,4,2,16,512]{4,3,2,1,0:T(8,128)S(1)}, f32[4,4,2,16,512]{4,3,2,1,0:T(8,128)S(1)}, u32[]{:S(2)}, u32[]{:S(2)}) collective-permute-start(f32[4,4,2,16,512]{4,3,2,1,0:T(8,128)S(1)} %add.200), channel_id=1, source_target_pairs={{0,2},{1,9},{2,4},{3,11},{4,6},{5,13},{6,0},{7,15},{8,10},{9,17},{... | collective-permute-start | bytes 3145736 | tf_op jit(solution)/shard_map/ppermute | solution.py:50
  21.2 0.2 add.202
  21.4 2.8 %collective-permute-start.11 = (f32[4,4,2,16,512]{4,3,2,1,0:T(8,128)S(1)}, f32[4,4,2,16,512]{4,3,2,1,0:T(8,128)S(1)}, u32[]{:S(2)}, u32[]{:S(2)}) collective-permute-start(f32[4,4,2,16,512]{4,3,2,1,0:T(8,128)S(1)} %add.202), channel_id=1, source_target_pairs={{0,4},{1,17},{2,6},{3,19},{4,0},{5,21},{6,2},{7,23},{8,12},{9,25},... | collective-permute-start | bytes 3145736 | tf_op jit(solution)/shard_map/ppermute | solution.py:50
  24.4 1.5 %collective-permute-start.13 = (f32[4,4,2,16,512]{4,3,2,1,0:T(8,128)S(1)}, f32[4,4,2,16,512]{4,3,2,1,0:T(8,128)S(1)}, u32[]{:S(2)}, u32[]{:S(2)}) collective-permute-start(f32[4,4,2,16,512]{4,3,2,1,0:T(8,128)S(1)} %add.204), channel_id=1, source_target_pairs={{0,6},{1,25},{2,0},{3,27},{4,2},{5,29},{6,4},{7,31},{8,14},{9,1},{... | collective-permute-start | bytes 3145736 | tf_op jit(solution)/shard_map/ppermute | solution.py:50
  25.9 9.7 %collective-permute-done.9 = f32[4,4,2,16,512]{4,3,2,1,0:T(8,128)S(1)} collective-permute-done((f32[4,4,2,16,512]{4,3,2,1,0:T(8,128)S(1)}, f32[4,4,2,16,512]{4,3,2,1,0:T(8,128)S(1)}, u32[]{:S(2)}, u32[]{:S(2)}) %collective-permute-start.9) | collective-permute-done | bytes 1048608 | tf_op jit(solution)/shard_map/ppermute | solution.py:50
  35.6 12.3 %collective-permute-done.11 = f32[4,4,2,16,512]{4,3,2,1,0:T(8,128)S(1)} collective-permute-done((f32[4,4,2,16,512]{4,3,2,1,0:T(8,128)S(1)}, f32[4,4,2,16,512]{4,3,2,1,0:T(8,128)S(1)}, u32[]{:S(2)}, u32[]{:S(2)}) %collective-permute-start.11) | collective-permute-done | bytes 1048608 | tf_op jit(solution)/shard_map/ppermute | solution.py:50
  47.9 0.9 collective-permute-done.13
  48.9 0.6 add_add_fusion
  49.6 2.0 %collective-permute-start.14 = (f32[4,2,16,512]{3,2,1,0:T(8,128)S(1)}, f32[4,2,16,512]{3,2,1,0:T(8,128)S(1)}, u32[]{:S(2)}, u32[]{:S(2)}) collective-permute-start(f32[4,2,16,512]{3,2,1,0:T(8,128)S(1)} %get-tuple-element.29), channel_id=1, source_target_pairs={{0,8},{1,3},{2,10},{3,5},{4,12},{5,7},{6,14},{7,1},{8,16},{9,11},{... | collective-permute-start | bytes 786440 | tf_op jit(solution)/shard_map/ppermute | solution.py:42
  51.6 3.6 %collective-permute-start.15 = (f32[4,2,16,512]{3,2,1,0:T(8,128)S(1)}, f32[4,2,16,512]{3,2,1,0:T(8,128)S(1)}, u32[]{:S(2)}, u32[]{:S(2)}) collective-permute-start(f32[4,2,16,512]{3,2,1,0:T(8,128)S(1)} %get-tuple-element.31), channel_id=1, source_target_pairs={{0,16},{1,5},{2,18},{3,7},{4,20},{5,1},{6,22},{7,3},{8,24},{9,13},... | collective-permute-start | bytes 786440 | tf_op jit(solution)/shard_map/ppermute | solution.py:42
  55.1 1.0 collective-permute-start.16
  56.1 1.9 %collective-permute-done.14 = f32[4,2,16,512]{3,2,1,0:T(8,128)S(1)} collective-permute-done((f32[4,2,16,512]{3,2,1,0:T(8,128)S(1)}, f32[4,2,16,512]{3,2,1,0:T(8,128)S(1)}, u32[]{:S(2)}, u32[]{:S(2)}) %collective-permute-start.14) | collective-permute-done | bytes 262176 | tf_op jit(solution)/shard_map/ppermute | solution.py:42
  58.0 4.3 %collective-permute-done.15 = f32[4,2,16,512]{3,2,1,0:T(8,128)S(1)} collective-permute-done((f32[4,2,16,512]{3,2,1,0:T(8,128)S(1)}, f32[4,2,16,512]{3,2,1,0:T(8,128)S(1)}, u32[]{:S(2)}, u32[]{:S(2)}) %collective-permute-start.15) | collective-permute-done | bytes 262176 | tf_op jit(solution)/shard_map/ppermute | solution.py:42
  62.4 1.6 %collective-permute-start.17 = (f32[2,16,512]{2,1,0:T(8,128)S(1)}, f32[2,16,512]{2,1,0:T(8,128)S(1)}, u32[]{:S(2)}, u32[]{:S(2)}) collective-permute-start(f32[2,16,512]{2,1,0:T(8,128)S(1)} %get-tuple-element.32), channel_id=1, source_target_pairs={{0,32},{1,33},{2,34},{3,35},{4,36},{5,37},{6,38},{7,39},{8,40},{9,... | collective-permute-start | bytes 196616 | tf_op jit(solution)/shard_map/ppermute | solution.py:42
  64.1 2.9 %collective-permute-start.18 = (f32[2,16,512]{2,1,0:T(8,128)S(1)}, f32[2,16,512]{2,1,0:T(8,128)S(1)}, u32[]{:S(2)}, u32[]{:S(2)}) collective-permute-start(f32[2,16,512]{2,1,0:T(8,128)S(1)} %get-tuple-element.34), channel_id=1, source_target_pairs={{0,64},{1,65},{2,66},{3,67},{4,68},{5,69},{6,70},{7,71},{8,72},{9,... | collective-permute-start | bytes 196616 | tf_op jit(solution)/shard_map/ppermute | solution.py:42
  67.0 1.3 %collective-permute-start.19 = (f32[2,16,512]{2,1,0:T(8,128)S(1)}, f32[2,16,512]{2,1,0:T(8,128)S(1)}, u32[]{:S(2)}, u32[]{:S(2)}) collective-permute-start(f32[2,16,512]{2,1,0:T(8,128)S(1)} %get-tuple-element.33), channel_id=1, source_target_pairs={{0,96},{1,97},{2,98},{3,99},{4,100},{5,101},{6,102},{7,103},{8,104... | collective-permute-start | bytes 196616 | tf_op jit(solution)/shard_map/ppermute | solution.py:42
  68.3 1.3 %convolution_bitcast_fusion = f32[8,8,16]{0,1,2:T(8,128)S(1)} fusion(f32[8,2,16,512]{3,2,1,0:T(8,128)S(1)} %copy-done), kind=kOutput, calls=%fused_computation.6 | convolution fusion | flops 12582912 | bytes 528384 | tf_op jit(solution)/shard_map/knjc,mnjc->kmj/dot_general | solution.py:142
  69.9 1.3 %collective-permute-done.19 = f32[2,16,512]{2,1,0:T(8,128)S(1)} collective-permute-done((f32[2,16,512]{2,1,0:T(8,128)S(1)}, f32[2,16,512]{2,1,0:T(8,128)S(1)}, u32[]{:S(2)}, u32[]{:S(2)}) %collective-permute-start.19) | collective-permute-done | bytes 65568 | tf_op jit(solution)/shard_map/ppermute | solution.py:42
  71.4 1.5 %fusion.9 = f32[16,1,8,1]{2,1,3,0:T(1,128)S(1)} fusion(f32[8,2,16,512]{3,2,1,0:T(8,128)S(1)} %copy-done, f32[2,16,512,1]{2,1,0,3:T(8,128)S(1)} %bitcast.151), kind=kOutput, calls=%fused_computation.14 | convolution fusion | flops 1572864 | bytes 590336 | tf_op jit(solution)/shard_map/knjc,njc->kj/dot_general | solution.py:141
  73.0 1.2 %collective-permute-done.20 = f32[73,16]{1,0:T(8,128)S(1)} collective-permute-done((f32[73,16]{1,0:T(8,128)S(1)}, f32[73,16]{1,0:T(8,128)S(1)}, u32[]{:S(2)}, u32[]{:S(2)}) %collective-permute-start.20) | collective-permute-done | bytes 4704 | tf_op jit(solution)/shard_map/ppermute | solution.py:32
  74.2 1.7 %collective-permute-start.21 = (f32[73,16]{1,0:T(8,128)S(1)}, f32[73,16]{1,0:T(8,128)S(1)}, u32[]{:S(2)}, u32[]{:S(2)}) collective-permute-start(f32[73,16]{1,0:T(8,128)S(1)} %fusion.43), channel_id=1, source_target_pairs={{0,2},{1,3},{2,0},{3,1},{4,6},{5,7},{6,4},{7,5},{8,10},{9,11},{10,... | collective-permute-start | bytes 14024 | tf_op jit(solution)/shard_map/ppermute | solution.py:35
  75.9 2.4 %collective-permute-done.21 = f32[73,16]{1,0:T(8,128)S(1)} collective-permute-done((f32[73,16]{1,0:T(8,128)S(1)}, f32[73,16]{1,0:T(8,128)S(1)}, u32[]{:S(2)}, u32[]{:S(2)}) %collective-permute-start.21) | collective-permute-done | bytes 4704 | tf_op jit(solution)/shard_map/ppermute | solution.py:35
  78.3 2.6 %collective-permute-start.22 = (f32[73,16]{1,0:T(8,128)S(1)}, f32[73,16]{1,0:T(8,128)S(1)}, u32[]{:S(2)}, u32[]{:S(2)}) collective-permute-start(f32[73,16]{1,0:T(8,128)S(1)} %add.214), channel_id=1, source_target_pairs={{0,6},{1,7},{2,4},{3,5},{4,2},{5,3},{6,0},{7,1},{8,14},{9,15},{10,... | collective-permute-start | bytes 14024 | tf_op jit(solution)/shard_map/ppermute | solution.py:35
  80.9 2.6 %collective-permute-done.22 = f32[73,16]{1,0:T(8,128)S(1)} collective-permute-done((f32[73,16]{1,0:T(8,128)S(1)}, f32[73,16]{1,0:T(8,128)S(1)}, u32[]{:S(2)}, u32[]{:S(2)}) %collective-permute-start.22) | collective-permute-done | bytes 4704 | tf_op jit(solution)/shard_map/ppermute | solution.py:35
  83.5 1.5 %collective-permute-start.23 = (f32[73,16]{1,0:T(8,128)S(1)}, f32[73,16]{1,0:T(8,128)S(1)}, u32[]{:S(2)}, u32[]{:S(2)}) collective-permute-start(f32[73,16]{1,0:T(8,128)S(1)} %add.215), channel_id=1, source_target_pairs={{0,8},{1,9},{2,10},{3,11},{4,12},{5,13},{6,14},{7,15},{8,0},{9,1},... | collective-permute-start | bytes 14024 | tf_op jit(solution)/shard_map/ppermute | solution.py:35
  85.0 2.5 %collective-permute-done.23 = f32[73,16]{1,0:T(8,128)S(1)} collective-permute-done((f32[73,16]{1,0:T(8,128)S(1)}, f32[73,16]{1,0:T(8,128)S(1)}, u32[]{:S(2)}, u32[]{:S(2)}) %collective-permute-start.23) | collective-permute-done | bytes 4704 | tf_op jit(solution)/shard_map/ppermute | solution.py:35
  87.5 2.2 %collective-permute-start.24 = (f32[73,16]{1,0:T(8,128)S(1)}, f32[73,16]{1,0:T(8,128)S(1)}, u32[]{:S(2)}, u32[]{:S(2)}) collective-permute-start(f32[73,16]{1,0:T(8,128)S(1)} %add.216), channel_id=1, source_target_pairs={{0,24},{1,25},{2,26},{3,27},{4,28},{5,29},{6,30},{7,31},{8,16},{9,... | collective-permute-start | bytes 14024 | tf_op jit(solution)/shard_map/ppermute | solution.py:35
  89.6 3.1 %collective-permute-done.24 = f32[73,16]{1,0:T(8,128)S(1)} collective-permute-done((f32[73,16]{1,0:T(8,128)S(1)}, f32[73,16]{1,0:T(8,128)S(1)}, u32[]{:S(2)}, u32[]{:S(2)}) %collective-permute-start.24) | collective-permute-done | bytes 4704 | tf_op jit(solution)/shard_map/ppermute | solution.py:35
  92.7 0.3 collective-permute-start.25
  93.0 3.7 %collective-permute-done.25 = f32[73,16]{1,0:T(8,128)S(1)} collective-permute-done((f32[73,16]{1,0:T(8,128)S(1)}, f32[73,16]{1,0:T(8,128)S(1)}, u32[]{:S(2)}, u32[]{:S(2)}) %collective-permute-start.25) | collective-permute-done | bytes 4704 | tf_op jit(solution)/shard_map/ppermute | solution.py:35
  96.7 2.6 %collective-permute-start.26 = (f32[73,16]{1,0:T(8,128)S(1)}, f32[73,16]{1,0:T(8,128)S(1)}, u32[]{:S(2)}, u32[]{:S(2)}) collective-permute-start(f32[73,16]{1,0:T(8,128)S(1)} %add.218), channel_id=1, source_target_pairs={{0,96},{1,97},{2,98},{3,99},{4,100},{5,101},{6,102},{7,103},{8,104... | collective-permute-start | bytes 14024 | tf_op jit(solution)/shard_map/ppermute | solution.py:35
  99.3 2.7 %collective-permute-done.26 = f32[73,16]{1,0:T(8,128)S(1)} collective-permute-done((f32[73,16]{1,0:T(8,128)S(1)}, f32[73,16]{1,0:T(8,128)S(1)}, u32[]{:S(2)}, u32[]{:S(2)}) %collective-permute-start.26) | collective-permute-done | bytes 4704 | tf_op jit(solution)/shard_map/ppermute | solution.py:35
  102.0 0.6 compare_reduce_fusion
  103.4 0.8 fusion.7
  104.3 0.6 pad_maximum_fusion.1
  104.9 0.7 broadcast_divide_fusion
  (46 shorter events, 1.4 us)
Async XLA Ops:
  8.7 4.7 %copy-start.1 = (bf16[112,32,512]{2,1,0:T(8,128)(2,1)S(1)}, bf16[112,32,512]{2,1,0:T(8,128)(2,1)}, u32[]{:S(2)}) copy-start(bf16[112,32,512]{2,1,0:T(8,128)(2,1)} %param.14) | copy-start | bytes 11010052
  13.4 0.7 copy-start.3
  13.4 0.8 copy-start.4
  16.6 2.7 %collective-permute-start.8 = (f32[4,4,2,16,512]{4,3,2,1,0:T(8,128)S(1)}, f32[4,4,2,16,512]{4,3,2,1,0:T(8,128)S(1)}, u32[]{:S(2)}, u32[]{:S(2)}) collective-permute-start(f32[4,4,2,16,512]{4,3,2,1,0:T(8,128)S(1)} %bitcast.150), channel_id=1, source_target_pairs={{0,1},{1,0},{2,3},{3,2},{4,5},{5,4},{6,7},{7,6},{8,9},{9,8},{10,11... | collective-permute-start | bytes 3145736 | tf_op jit(solution)/shard_map/ppermute | solution.py:47
  16.7 4.5 %collective-permute-start.10 = (f32[4,4,2,16,512]{4,3,2,1,0:T(8,128)S(1)}, f32[4,4,2,16,512]{4,3,2,1,0:T(8,128)S(1)}, u32[]{:S(2)}, u32[]{:S(2)}) collective-permute-start(f32[4,4,2,16,512]{4,3,2,1,0:T(8,128)S(1)} %bitcast.149), channel_id=1, source_target_pairs={{0,1},{1,0},{2,3},{3,2},{4,5},{5,4},{6,7},{7,6},{8,9},{9,8},{10,11... | collective-permute-start | bytes 3145736 | tf_op jit(solution)/shard_map/ppermute | solution.py:47
  17.2 7.1 %collective-permute-start.12 = (f32[4,4,2,16,512]{4,3,2,1,0:T(8,128)S(1)}, f32[4,4,2,16,512]{4,3,2,1,0:T(8,128)S(1)}, u32[]{:S(2)}, u32[]{:S(2)}) collective-permute-start(f32[4,4,2,16,512]{4,3,2,1,0:T(8,128)S(1)} %bitcast.148), channel_id=1, source_target_pairs={{0,1},{1,0},{2,3},{3,2},{4,5},{5,4},{6,7},{7,6},{8,9},{9,8},{10,11... | collective-permute-start | bytes 3145736 | tf_op jit(solution)/shard_map/ppermute | solution.py:47
  17.3 8.7 %collective-permute-start.7 = (f32[4,4,2,16,512]{4,3,2,1,0:T(8,128)S(1)}, f32[4,4,2,16,512]{4,3,2,1,0:T(8,128)S(1)}, u32[]{:S(2)}, u32[]{:S(2)}) collective-permute-start(f32[4,4,2,16,512]{4,3,2,1,0:T(8,128)S(1)} %bitcast.147), channel_id=1, source_target_pairs={{0,1},{1,0},{2,3},{3,2},{4,5},{5,4},{6,7},{7,6},{8,9},{9,8},{10,11... | collective-permute-start | bytes 3145736 | tf_op jit(solution)/shard_map/ppermute | solution.py:47
  19.5 16.1 %collective-permute-start.9 = (f32[4,4,2,16,512]{4,3,2,1,0:T(8,128)S(1)}, f32[4,4,2,16,512]{4,3,2,1,0:T(8,128)S(1)}, u32[]{:S(2)}, u32[]{:S(2)}) collective-permute-start(f32[4,4,2,16,512]{4,3,2,1,0:T(8,128)S(1)} %add.200), channel_id=1, source_target_pairs={{0,2},{1,9},{2,4},{3,11},{4,6},{5,13},{6,0},{7,15},{8,10},{9,17},{... | collective-permute-start | bytes 3145736 | tf_op jit(solution)/shard_map/ppermute | solution.py:50
  21.4 26.5 %collective-permute-start.11 = (f32[4,4,2,16,512]{4,3,2,1,0:T(8,128)S(1)}, f32[4,4,2,16,512]{4,3,2,1,0:T(8,128)S(1)}, u32[]{:S(2)}, u32[]{:S(2)}) collective-permute-start(f32[4,4,2,16,512]{4,3,2,1,0:T(8,128)S(1)} %add.202), channel_id=1, source_target_pairs={{0,4},{1,17},{2,6},{3,19},{4,0},{5,21},{6,2},{7,23},{8,12},{9,25},... | collective-permute-start | bytes 3145736 | tf_op jit(solution)/shard_map/ppermute | solution.py:50
  24.4 24.4 %collective-permute-start.13 = (f32[4,4,2,16,512]{4,3,2,1,0:T(8,128)S(1)}, f32[4,4,2,16,512]{4,3,2,1,0:T(8,128)S(1)}, u32[]{:S(2)}, u32[]{:S(2)}) collective-permute-start(f32[4,4,2,16,512]{4,3,2,1,0:T(8,128)S(1)} %add.204), channel_id=1, source_target_pairs={{0,6},{1,25},{2,0},{3,27},{4,2},{5,29},{6,4},{7,31},{8,14},{9,1},{... | collective-permute-start | bytes 3145736 | tf_op jit(solution)/shard_map/ppermute | solution.py:50
  48.9 19.4 %copy-start = (f32[8,2,16,512]{3,2,1,0:T(8,128)S(1)}, f32[8,2,16,512]{3,2,1,0:T(8,128)}, u32[]{:S(2)}) copy-start(f32[8,2,16,512]{3,2,1,0:T(8,128)} %param.10) | copy-start | bytes 1572868
  48.9 22.3 %copy-start.2 = (f32[2,512]{1,0:T(2,128)S(1)}, f32[2,512]{1,0:T(2,128)}, u32[]{:S(2)}) copy-start(f32[2,512]{1,0:T(2,128)} %param.11) | copy-start | bytes 12292
  49.6 8.5 %collective-permute-start.14 = (f32[4,2,16,512]{3,2,1,0:T(8,128)S(1)}, f32[4,2,16,512]{3,2,1,0:T(8,128)S(1)}, u32[]{:S(2)}, u32[]{:S(2)}) collective-permute-start(f32[4,2,16,512]{3,2,1,0:T(8,128)S(1)} %get-tuple-element.29), channel_id=1, source_target_pairs={{0,8},{1,3},{2,10},{3,5},{4,12},{5,7},{6,14},{7,1},{8,16},{9,11},{... | collective-permute-start | bytes 786440 | tf_op jit(solution)/shard_map/ppermute | solution.py:42
  51.6 10.7 %collective-permute-start.15 = (f32[4,2,16,512]{3,2,1,0:T(8,128)S(1)}, f32[4,2,16,512]{3,2,1,0:T(8,128)S(1)}, u32[]{:S(2)}, u32[]{:S(2)}) collective-permute-start(f32[4,2,16,512]{3,2,1,0:T(8,128)S(1)} %get-tuple-element.31), channel_id=1, source_target_pairs={{0,16},{1,5},{2,18},{3,7},{4,20},{5,1},{6,22},{7,3},{8,24},{9,13},... | collective-permute-start | bytes 786440 | tf_op jit(solution)/shard_map/ppermute | solution.py:42
  55.1 7.2 %collective-permute-start.16 = (f32[4,2,16,512]{3,2,1,0:T(8,128)S(1)}, f32[4,2,16,512]{3,2,1,0:T(8,128)S(1)}, u32[]{:S(2)}, u32[]{:S(2)}) collective-permute-start(f32[4,2,16,512]{3,2,1,0:T(8,128)S(1)} %get-tuple-element.30), channel_id=1, source_target_pairs={{0,24},{1,7},{2,26},{3,1},{4,28},{5,3},{6,30},{7,5},{8,0},{9,15},{... | collective-permute-start | bytes 786440 | tf_op jit(solution)/shard_map/ppermute | solution.py:42
  62.4 7.3 %collective-permute-start.17 = (f32[2,16,512]{2,1,0:T(8,128)S(1)}, f32[2,16,512]{2,1,0:T(8,128)S(1)}, u32[]{:S(2)}, u32[]{:S(2)}) collective-permute-start(f32[2,16,512]{2,1,0:T(8,128)S(1)} %get-tuple-element.32), channel_id=1, source_target_pairs={{0,32},{1,33},{2,34},{3,35},{4,36},{5,37},{6,38},{7,39},{8,40},{9,... | collective-permute-start | bytes 196616 | tf_op jit(solution)/shard_map/ppermute | solution.py:42
  64.1 5.8 %collective-permute-start.18 = (f32[2,16,512]{2,1,0:T(8,128)S(1)}, f32[2,16,512]{2,1,0:T(8,128)S(1)}, u32[]{:S(2)}, u32[]{:S(2)}) collective-permute-start(f32[2,16,512]{2,1,0:T(8,128)S(1)} %get-tuple-element.34), channel_id=1, source_target_pairs={{0,64},{1,65},{2,66},{3,67},{4,68},{5,69},{6,70},{7,71},{8,72},{9,... | collective-permute-start | bytes 196616 | tf_op jit(solution)/shard_map/ppermute | solution.py:42
  67.0 4.3 %collective-permute-start.19 = (f32[2,16,512]{2,1,0:T(8,128)S(1)}, f32[2,16,512]{2,1,0:T(8,128)S(1)}, u32[]{:S(2)}, u32[]{:S(2)}) collective-permute-start(f32[2,16,512]{2,1,0:T(8,128)S(1)} %get-tuple-element.33), channel_id=1, source_target_pairs={{0,96},{1,97},{2,98},{3,99},{4,100},{5,101},{6,102},{7,103},{8,104... | collective-permute-start | bytes 196616 | tf_op jit(solution)/shard_map/ppermute | solution.py:42
  72.9 1.3 %collective-permute-start.20 = (f32[73,16]{1,0:T(8,128)S(1)}, f32[73,16]{1,0:T(8,128)S(1)}, u32[]{:S(2)}, u32[]{:S(2)}) collective-permute-start(f32[73,16]{1,0:T(8,128)S(1)} %pad_maximum_fusion), channel_id=1, source_target_pairs={{0,1},{1,0},{2,3},{3,2},{4,5},{5,4},{6,7},{7,6},{8,9},{9,8},{10,11... | collective-permute-start | bytes 14024 | tf_op jit(solution)/shard_map/ppermute | solution.py:32
  74.2 4.1 %collective-permute-start.21 = (f32[73,16]{1,0:T(8,128)S(1)}, f32[73,16]{1,0:T(8,128)S(1)}, u32[]{:S(2)}, u32[]{:S(2)}) collective-permute-start(f32[73,16]{1,0:T(8,128)S(1)} %fusion.43), channel_id=1, source_target_pairs={{0,2},{1,3},{2,0},{3,1},{4,6},{5,7},{6,4},{7,5},{8,10},{9,11},{10,... | collective-permute-start | bytes 14024 | tf_op jit(solution)/shard_map/ppermute | solution.py:35
  78.3 5.2 %collective-permute-start.22 = (f32[73,16]{1,0:T(8,128)S(1)}, f32[73,16]{1,0:T(8,128)S(1)}, u32[]{:S(2)}, u32[]{:S(2)}) collective-permute-start(f32[73,16]{1,0:T(8,128)S(1)} %add.214), channel_id=1, source_target_pairs={{0,6},{1,7},{2,4},{3,5},{4,2},{5,3},{6,0},{7,1},{8,14},{9,15},{10,... | collective-permute-start | bytes 14024 | tf_op jit(solution)/shard_map/ppermute | solution.py:35
  83.5 4.0 %collective-permute-start.23 = (f32[73,16]{1,0:T(8,128)S(1)}, f32[73,16]{1,0:T(8,128)S(1)}, u32[]{:S(2)}, u32[]{:S(2)}) collective-permute-start(f32[73,16]{1,0:T(8,128)S(1)} %add.215), channel_id=1, source_target_pairs={{0,8},{1,9},{2,10},{3,11},{4,12},{5,13},{6,14},{7,15},{8,0},{9,1},... | collective-permute-start | bytes 14024 | tf_op jit(solution)/shard_map/ppermute | solution.py:35
  87.5 5.2 %collective-permute-start.24 = (f32[73,16]{1,0:T(8,128)S(1)}, f32[73,16]{1,0:T(8,128)S(1)}, u32[]{:S(2)}, u32[]{:S(2)}) collective-permute-start(f32[73,16]{1,0:T(8,128)S(1)} %add.216), channel_id=1, source_target_pairs={{0,24},{1,25},{2,26},{3,27},{4,28},{5,29},{6,30},{7,31},{8,16},{9,... | collective-permute-start | bytes 14024 | tf_op jit(solution)/shard_map/ppermute | solution.py:35
  92.7 4.0 %collective-permute-start.25 = (f32[73,16]{1,0:T(8,128)S(1)}, f32[73,16]{1,0:T(8,128)S(1)}, u32[]{:S(2)}, u32[]{:S(2)}) collective-permute-start(f32[73,16]{1,0:T(8,128)S(1)} %add.217), channel_id=1, source_target_pairs={{0,32},{1,33},{2,34},{3,35},{4,36},{5,37},{6,38},{7,39},{8,40},{9,... | collective-permute-start | bytes 14024 | tf_op jit(solution)/shard_map/ppermute | solution.py:35
  96.7 5.2 %collective-permute-start.26 = (f32[73,16]{1,0:T(8,128)S(1)}, f32[73,16]{1,0:T(8,128)S(1)}, u32[]{:S(2)}, u32[]{:S(2)}) collective-permute-start(f32[73,16]{1,0:T(8,128)S(1)} %add.218), channel_id=1, source_target_pairs={{0,96},{1,97},{2,98},{3,99},{4,100},{5,101},{6,102},{7,103},{8,104... | collective-permute-start | bytes 14024 | tf_op jit(solution)/shard_map/ppermute | solution.py:35

commit v12 on v10

--- a/solution.py
+++ b/solution.py
@@ -4,6 +4,7 @@
 from jax.experimental import pallas as pl
 from jax.experimental.pallas import tpu as pltpu
 from jax.sharding import PartitionSpec as P
+
 
 AXES = ("grp", "dev")
 SIZES = {"y": 4, "z": 4, "x": 4, "c": 2}
@@ -45,9 +46,9 @@
 
 def reduce_to_owner(keep, send):
     pieces = [keep[k] + lax.ppermute(send[k], AXES, moved("c", 1)) for k in range(4)]
-    acc = pieces[0]
-    for k in (1, 2, 3):
-        acc = acc + lax.ppermute(pieces[k], AXES, moved("x", k, "z"))
+    far = lax.ppermute(pieces[2], AXES, moved("x", 2, "z"))
+    near = [lax.ppermute(pieces[k], AXES, moved("x", k, "z")) for k in (1, 3)]
+    acc = pieces[0] + near[0] + far + near[1]
     d = spread(acc, "z", "x")
     return spread(d, "y")
 
@@ -105,7 +106,7 @@
     )(slot, near_part, far_part)
 
 
-def on_device(basis, diagonal, near_blocks, far_u, far_v, block_row, block_dest, block_col):
+def step(basis, diagonal, near_blocks, far_u, far_v, block_row, block_dest, block_col):
     highest = lax.Precision.HIGHEST
     basis_count = basis.shape[0]
     clusters = basis.shape[1]
@@ -175,6 +176,4 @@
         P(AXES),
     )
     out_specs = (P(AXES, None, None), P())
-    return jax.shard_map(
-        on_device, mesh=mesh, in_specs=in_specs, out_specs=out_specs, check_vma=False
-    )
+    return jax.shard_map(step, mesh=mesh, in_specs=in_specs, out_specs=out_specs, check_vma=False)

time: 103 us -> 103 us (level)
  no operation moved by 1% of the time
where the time goes in v12:
time: 103 us
  waiting for transfers between devices  50.2 us (49%)
  starting transfers between devices  30.7 us (30%)
  matrix products  10.7 us (10%)
  other arithmetic  4.28 us (4%)
  local copies, waits for them, and re-layouts  3.09 us (3%)
  Pallas kernels  2.36 us (2%)
  between operations  1.55 us (2%)
    ppermute x6, waiting for transfers between devices, all_sum(): v = v + lax.ppermute(v, AXES, flipped(step * STRIDE[axis]))  16.8 us
    ppermute x6, starting transfers between devices, spread(): acc = acc + lax.ppermute(pieces[k], AXES, moved(axis, k, other))  12.5 us
    ppermute x1, waiting for transfers between devices, reduce_to_owner(): far = lax.ppermute(pieces[2], AXES, moved('x', 2, 'z'))  12.3 us
    ppermute x6, starting transfers between devices, all_sum(): v = v + lax.ppermute(v, AXES, flipped(step * STRIDE[axis]))  10.9 us
    ppermute x2, waiting for transfers between devices, reduce_to_owner(): near = [lax.ppermute(pieces[k], AXES, moved('x', k, 'z')) for k in (1, 3)]  10.6 us
    ppermute x6, waiting for transfers between devices, spread(): acc = acc + lax.ppermute(pieces[k], AXES, moved(axis, k, other))  7.63 us
    dot_general x1, matrix products, step(): jnp.einsum('snc,skc->snk', picked[near_count:], far_u, preferred_element_...  3.24 us
    ppermute x2, starting transfers between devices, reduce_to_owner(): near = [lax.ppermute(pieces[k], AXES, moved('x', k, 'z')) for k in (1, 3)]  3.16 us
  transfers between devices with their start and end apart: 20, of which 15 were waited for; matrix products, arithmetic and copies ran while one was open for 2% of the time, Pallas kernels for 0%

profile of v12, /device:TPU:0, one launch (start us, length us, event | category | flops | bytes accessed | tf_op | source)
XLA Modules:
  0.0 102.9 jit_solution(8716098934090164775)
XLA Ops:
  0.7 0.8 bitcast_convert_fusion
  1.6 0.7 compare_select_fusion
  2.2 0.7 gather_fusion
  2.9 3.2 %convolution_convert_fusion = bf16[112,16,32]{2,1,0:T(8,128)(2,1)S(1)} fusion(bf16[128,16,512]{2,1,0:T(8,128)(2,1)S(1)} %gather_fusion, bf16[112,32,512]{2,1,0:T(8,128)(2,1)} %param.13), kind=kOutput, calls=%fused_computation.3 | convolution fusion | flops 58777600 | bytes 5881856 | tf_op jit(solution)/shard_map/snc,skc->snk/dot_general | solution.py:124
  6.2 1.2 %copy-done.4 = bf16[16,512,512]{2,1,0:T(8,128)(2,1)S(1)} copy-done((bf16[16,512,512]{2,1,0:T(8,128)(2,1)S(1)}, bf16[16,512,512]{2,1,0:T(8,128)(2,1)}, u32[]{:S(2)}) %copy-start.4) | copy-done | bytes 8388632
  7.4 1.2 %fusion.35.near_ref = f32[16,16,512]{2,1,0:T(8,128)S(1)} fusion(bf16[128,16,512]{2,1,0:T(8,128)(2,1)S(1)} %gather_fusion, bf16[16,512,512]{2,1,0:T(8,128)(2,1)S(1)} %copy-done.4), kind=kOutput, calls=%fused_computation.104 | convolution fusion | flops 134217728 | bytes 11010048 | tf_op jit(solution)/shard_map/snc,scd->snd/dot_general | solution.py:121
  8.6 2.7 %fusion.34.far_ref = f32[112,16,512]{2,1,0:T(8,128)S(1)} fusion(bf16[112,16,32]{2,1,0:T(8,128)(2,1)S(1)} %convolution_convert_fusion, bf16[112,32,512]{2,1,0:T(8,128)(2,1)} %param.14), kind=kOutput, calls=%fused_computation.103 | convolution fusion | flops 58720256 | bytes 7454720 | tf_op jit(solution)/shard_map/snk,skc->snc/dot_general | solution.py:127
  11.3 2.4 %shard_map.95 = (f32[32,16,512]{2,1,0:T(8,128)S(1)}, f32[32,16,512]{2,1,0:T(8,128)S(1)}, f32[32,16,512]{2,1,0:T(8,128)S(1)}, f32[32,16,512]{2,1,0:T(8,128)S(1)},...) custom-call(s32[128]{0:T(128)S(1)} %multiply_add_fusion.slot_ref, ...), custom_call_target="tpu_custom_call" | custom-call | tf_op jit(solution)/shard_map/pallas_call | solution.py:99
  13.8 0.5 collective-permute-start.10
  14.4 0.4 collective-permute-start.7
  14.8 1.6 %collective-permute-done.8 = f32[4,4,2,16,512]{4,3,2,1,0:T(8,128)S(1)} collective-permute-done((f32[4,4,2,16,512]{4,3,2,1,0:T(8,128)S(1)}, f32[4,4,2,16,512]{4,3,2,1,0:T(8,128)S(1)}, u32[]{:S(2)}, u32[]{:S(2)}) %collective-permute-start.8) | collective-permute-done | bytes 1048608 | tf_op jit(solution)/shard_map/ppermute | solution.py:48
  16.5 0.2 add.200
  16.7 1.7 %collective-permute-start.9 = (f32[4,4,2,16,512]{4,3,2,1,0:T(8,128)S(1)}, f32[4,4,2,16,512]{4,3,2,1,0:T(8,128)S(1)}, u32[]{:S(2)}, u32[]{:S(2)}) collective-permute-start(f32[4,4,2,16,512]{4,3,2,1,0:T(8,128)S(1)} %add.200), channel_id=1, source_target_pairs={{0,2},{1,9},{2,4},{3,11},{4,6},{5,13},{6,0},{7,15},{8,10},{9,17},{... | collective-permute-start | bytes 3145736 | tf_op jit(solution)/shard_map/ppermute | solution.py:50
  18.6 2.8 %collective-permute-start.11 = (f32[4,4,2,16,512]{4,3,2,1,0:T(8,128)S(1)}, f32[4,4,2,16,512]{4,3,2,1,0:T(8,128)S(1)}, u32[]{:S(2)}, u32[]{:S(2)}) collective-permute-start(f32[4,4,2,16,512]{4,3,2,1,0:T(8,128)S(1)} %add.202), channel_id=1, source_target_pairs={{0,4},{1,17},{2,6},{3,19},{4,0},{5,21},{6,2},{7,23},{8,12},{9,25},... | collective-permute-start | bytes 3145736 | tf_op jit(solution)/shard_map/ppermute | solution.py:49
  21.6 1.5 %collective-permute-start.13 = (f32[4,4,2,16,512]{4,3,2,1,0:T(8,128)S(1)}, f32[4,4,2,16,512]{4,3,2,1,0:T(8,128)S(1)}, u32[]{:S(2)}, u32[]{:S(2)}) collective-permute-start(f32[4,4,2,16,512]{4,3,2,1,0:T(8,128)S(1)} %add.204), channel_id=1, source_target_pairs={{0,6},{1,25},{2,0},{3,27},{4,2},{5,29},{6,4},{7,31},{8,14},{9,1},{... | collective-permute-start | bytes 3145736 | tf_op jit(solution)/shard_map/ppermute | solution.py:50
  23.1 9.7 %collective-permute-done.9 = f32[4,4,2,16,512]{4,3,2,1,0:T(8,128)S(1)} collective-permute-done((f32[4,4,2,16,512]{4,3,2,1,0:T(8,128)S(1)}, f32[4,4,2,16,512]{4,3,2,1,0:T(8,128)S(1)}, u32[]{:S(2)}, u32[]{:S(2)}) %collective-permute-start.9) | collective-permute-done | bytes 1048608 | tf_op jit(solution)/shard_map/ppermute | solution.py:50
  32.7 12.3 %collective-permute-done.11 = f32[4,4,2,16,512]{4,3,2,1,0:T(8,128)S(1)} collective-permute-done((f32[4,4,2,16,512]{4,3,2,1,0:T(8,128)S(1)}, f32[4,4,2,16,512]{4,3,2,1,0:T(8,128)S(1)}, u32[]{:S(2)}, u32[]{:S(2)}) %collective-permute-start.11) | collective-permute-done | bytes 1048608 | tf_op jit(solution)/shard_map/ppermute | solution.py:49
  45.1 0.9 collective-permute-done.13
  46.0 0.6 add_add_fusion
  46.7 2.0 %collective-permute-start.14 = (f32[4,2,16,512]{3,2,1,0:T(8,128)S(1)}, f32[4,2,16,512]{3,2,1,0:T(8,128)S(1)}, u32[]{:S(2)}, u32[]{:S(2)}) collective-permute-start(f32[4,2,16,512]{3,2,1,0:T(8,128)S(1)} %get-tuple-element.29), channel_id=1, source_target_pairs={{0,8},{1,3},{2,10},{3,5},{4,12},{5,7},{6,14},{7,1},{8,16},{9,11},{... | collective-permute-start | bytes 786440 | tf_op jit(solution)/shard_map/ppermute | solution.py:43
  48.7 3.6 %collective-permute-start.15 = (f32[4,2,16,512]{3,2,1,0:T(8,128)S(1)}, f32[4,2,16,512]{3,2,1,0:T(8,128)S(1)}, u32[]{:S(2)}, u32[]{:S(2)}) collective-permute-start(f32[4,2,16,512]{3,2,1,0:T(8,128)S(1)} %get-tuple-element.31), channel_id=1, source_target_pairs={{0,16},{1,5},{2,18},{3,7},{4,20},{5,1},{6,22},{7,3},{8,24},{9,13},... | collective-permute-start | bytes 786440 | tf_op jit(solution)/shard_map/ppermute | solution.py:43
  52.3 1.0 collective-permute-start.16
  53.3 1.9 %collective-permute-done.14 = f32[4,2,16,512]{3,2,1,0:T(8,128)S(1)} collective-permute-done((f32[4,2,16,512]{3,2,1,0:T(8,128)S(1)}, f32[4,2,16,512]{3,2,1,0:T(8,128)S(1)}, u32[]{:S(2)}, u32[]{:S(2)}) %collective-permute-start.14) | collective-permute-done | bytes 262176 | tf_op jit(solution)/shard_map/ppermute | solution.py:43
  55.2 4.3 %collective-permute-done.15 = f32[4,2,16,512]{3,2,1,0:T(8,128)S(1)} collective-permute-done((f32[4,2,16,512]{3,2,1,0:T(8,128)S(1)}, f32[4,2,16,512]{3,2,1,0:T(8,128)S(1)}, u32[]{:S(2)}, u32[]{:S(2)}) %collective-permute-start.15) | collective-permute-done | bytes 262176 | tf_op jit(solution)/shard_map/ppermute | solution.py:43
  59.6 1.6 %collective-permute-start.17 = (f32[2,16,512]{2,1,0:T(8,128)S(1)}, f32[2,16,512]{2,1,0:T(8,128)S(1)}, u32[]{:S(2)}, u32[]{:S(2)}) collective-permute-start(f32[2,16,512]{2,1,0:T(8,128)S(1)} %get-tuple-element.32), channel_id=1, source_target_pairs={{0,32},{1,33},{2,34},{3,35},{4,36},{5,37},{6,38},{7,39},{8,40},{9,... | collective-permute-start | bytes 196616 | tf_op jit(solution)/shard_map/ppermute | solution.py:43
  61.2 2.9 %collective-permute-start.18 = (f32[2,16,512]{2,1,0:T(8,128)S(1)}, f32[2,16,512]{2,1,0:T(8,128)S(1)}, u32[]{:S(2)}, u32[]{:S(2)}) collective-permute-start(f32[2,16,512]{2,1,0:T(8,128)S(1)} %get-tuple-element.34), channel_id=1, source_target_pairs={{0,64},{1,65},{2,66},{3,67},{4,68},{5,69},{6,70},{7,71},{8,72},{9,... | collective-permute-start | bytes 196616 | tf_op jit(solution)/shard_map/ppermute | solution.py:43
  64.1 1.3 %collective-permute-start.19 = (f32[2,16,512]{2,1,0:T(8,128)S(1)}, f32[2,16,512]{2,1,0:T(8,128)S(1)}, u32[]{:S(2)}, u32[]{:S(2)}) collective-permute-start(f32[2,16,512]{2,1,0:T(8,128)S(1)} %get-tuple-element.33), channel_id=1, source_target_pairs={{0,96},{1,97},{2,98},{3,99},{4,100},{5,101},{6,102},{7,103},{8,104... | collective-permute-start | bytes 196616 | tf_op jit(solution)/shard_map/ppermute | solution.py:43
  65.5 1.3 %convolution_bitcast_fusion = f32[8,8,16]{0,1,2:T(8,128)S(1)} fusion(f32[8,2,16,512]{3,2,1,0:T(8,128)S(1)} %copy-done), kind=kOutput, calls=%fused_computation.4 | convolution fusion | flops 12582912 | bytes 528384 | tf_op jit(solution)/shard_map/knjc,mnjc->kmj/dot_general | solution.py:141
  67.0 1.3 %collective-permute-done.19 = f32[2,16,512]{2,1,0:T(8,128)S(1)} collective-permute-done((f32[2,16,512]{2,1,0:T(8,128)S(1)}, f32[2,16,512]{2,1,0:T(8,128)S(1)}, u32[]{:S(2)}, u32[]{:S(2)}) %collective-permute-start.19) | collective-permute-done | bytes 65568 | tf_op jit(solution)/shard_map/ppermute | solution.py:43
  68.5 1.5 %fusion.2 = f32[16,1,8,1]{2,1,3,0:T(1,128)S(1)} fusion(f32[8,2,16,512]{3,2,1,0:T(8,128)S(1)} %copy-done, f32[2,16,512,1]{2,1,0,3:T(8,128)S(1)} %bitcast.125), kind=kOutput, calls=%fused_computation.8 | convolution fusion | flops 1572864 | bytes 590336 | tf_op jit(solution)/shard_map/knjc,njc->kj/dot_general | solution.py:140
  70.0 0.2 collective-permute-start.20
  70.3 1.2 %collective-permute-done.20 = f32[73,16]{1,0:T(8,128)S(1)} collective-permute-done((f32[73,16]{1,0:T(8,128)S(1)}, f32[73,16]{1,0:T(8,128)S(1)}, u32[]{:S(2)}, u32[]{:S(2)}) %collective-permute-start.20) | collective-permute-done | bytes 4704 | tf_op jit(solution)/shard_map/ppermute | solution.py:33
  71.5 1.7 %collective-permute-start.21 = (f32[73,16]{1,0:T(8,128)S(1)}, f32[73,16]{1,0:T(8,128)S(1)}, u32[]{:S(2)}, u32[]{:S(2)}) collective-permute-start(f32[73,16]{1,0:T(8,128)S(1)} %fusion.32), channel_id=1, source_target_pairs={{0,2},{1,3},{2,0},{3,1},{4,6},{5,7},{6,4},{7,5},{8,10},{9,11},{10,... | collective-permute-start | bytes 14024 | tf_op jit(solution)/shard_map/ppermute | solution.py:36
  73.2 2.4 %collective-permute-done.21 = f32[73,16]{1,0:T(8,128)S(1)} collective-permute-done((f32[73,16]{1,0:T(8,128)S(1)}, f32[73,16]{1,0:T(8,128)S(1)}, u32[]{:S(2)}, u32[]{:S(2)}) %collective-permute-start.21) | collective-permute-done | bytes 4704 | tf_op jit(solution)/shard_map/ppermute | solution.py:36
  75.6 2.6 %collective-permute-start.22 = (f32[73,16]{1,0:T(8,128)S(1)}, f32[73,16]{1,0:T(8,128)S(1)}, u32[]{:S(2)}, u32[]{:S(2)}) collective-permute-start(f32[73,16]{1,0:T(8,128)S(1)} %add.214), channel_id=1, source_target_pairs={{0,6},{1,7},{2,4},{3,5},{4,2},{5,3},{6,0},{7,1},{8,14},{9,15},{10,... | collective-permute-start | bytes 14024 | tf_op jit(solution)/shard_map/ppermute | solution.py:36
  78.2 2.6 %collective-permute-done.22 = f32[73,16]{1,0:T(8,128)S(1)} collective-permute-done((f32[73,16]{1,0:T(8,128)S(1)}, f32[73,16]{1,0:T(8,128)S(1)}, u32[]{:S(2)}, u32[]{:S(2)}) %collective-permute-start.22) | collective-permute-done | bytes 4704 | tf_op jit(solution)/shard_map/ppermute | solution.py:36
  80.8 1.5 %collective-permute-start.23 = (f32[73,16]{1,0:T(8,128)S(1)}, f32[73,16]{1,0:T(8,128)S(1)}, u32[]{:S(2)}, u32[]{:S(2)}) collective-permute-start(f32[73,16]{1,0:T(8,128)S(1)} %add.215), channel_id=1, source_target_pairs={{0,8},{1,9},{2,10},{3,11},{4,12},{5,13},{6,14},{7,15},{8,0},{9,1},... | collective-permute-start | bytes 14024 | tf_op jit(solution)/shard_map/ppermute | solution.py:36
  82.3 2.5 %collective-permute-done.23 = f32[73,16]{1,0:T(8,128)S(1)} collective-permute-done((f32[73,16]{1,0:T(8,128)S(1)}, f32[73,16]{1,0:T(8,128)S(1)}, u32[]{:S(2)}, u32[]{:S(2)}) %collective-permute-start.23) | collective-permute-done | bytes 4704 | tf_op jit(solution)/shard_map/ppermute | solution.py:36
  84.8 2.2 %collective-permute-start.24 = (f32[73,16]{1,0:T(8,128)S(1)}, f32[73,16]{1,0:T(8,128)S(1)}, u32[]{:S(2)}, u32[]{:S(2)}) collective-permute-start(f32[73,16]{1,0:T(8,128)S(1)} %add.216), channel_id=1, source_target_pairs={{0,24},{1,25},{2,26},{3,27},{4,28},{5,29},{6,30},{7,31},{8,16},{9,... | collective-permute-start | bytes 14024 | tf_op jit(solution)/shard_map/ppermute | solution.py:36
  87.0 3.1 %collective-permute-done.24 = f32[73,16]{1,0:T(8,128)S(1)} collective-permute-done((f32[73,16]{1,0:T(8,128)S(1)}, f32[73,16]{1,0:T(8,128)S(1)}, u32[]{:S(2)}, u32[]{:S(2)}) %collective-permute-start.24) | collective-permute-done | bytes 4704 | tf_op jit(solution)/shard_map/ppermute | solution.py:36
  90.0 0.3 collective-permute-start.25
  90.4 3.7 %collective-permute-done.25 = f32[73,16]{1,0:T(8,128)S(1)} collective-permute-done((f32[73,16]{1,0:T(8,128)S(1)}, f32[73,16]{1,0:T(8,128)S(1)}, u32[]{:S(2)}, u32[]{:S(2)}) %collective-permute-start.25) | collective-permute-done | bytes 4704 | tf_op jit(solution)/shard_map/ppermute | solution.py:36
  94.0 2.6 %collective-permute-start.26 = (f32[73,16]{1,0:T(8,128)S(1)}, f32[73,16]{1,0:T(8,128)S(1)}, u32[]{:S(2)}, u32[]{:S(2)}) collective-permute-start(f32[73,16]{1,0:T(8,128)S(1)} %add.218), channel_id=1, source_target_pairs={{0,96},{1,97},{2,98},{3,99},{4,100},{5,101},{6,102},{7,103},{8,104... | collective-permute-start | bytes 14024 | tf_op jit(solution)/shard_map/ppermute | solution.py:36
  96.6 2.7 %collective-permute-done.26 = f32[73,16]{1,0:T(8,128)S(1)} collective-permute-done((f32[73,16]{1,0:T(8,128)S(1)}, f32[73,16]{1,0:T(8,128)S(1)}, u32[]{:S(2)}, u32[]{:S(2)}) %collective-permute-start.26) | collective-permute-done | bytes 4704 | tf_op jit(solution)/shard_map/ppermute | solution.py:36
  99.4 0.6 compare_reduce_fusion
  100.7 0.8 fusion
  101.6 0.6 pad_maximum_fusion.1
  102.2 0.7 broadcast_divide_fusion
  (45 shorter events, 1.5 us)
Async XLA Ops:
  2.9 4.5 %copy-start.4 = (bf16[16,512,512]{2,1,0:T(8,128)(2,1)S(1)}, bf16[16,512,512]{2,1,0:T(8,128)(2,1)}, u32[]{:S(2)}) copy-start(bf16[16,512,512]{2,1,0:T(8,128)(2,1)} %param.12) | copy-start | bytes 25165828
  8.6 2.7 %copy-start.2 = (s32[128]{0:T(128)S(1)}, s32[128]{0:T(128)}, u32[]{:S(2)}) copy-start(s32[128]{0:T(128)} %param.17) | copy-start | bytes 1540
  8.6 2.7 %copy-start.3 = (s32[128,1]{0,1:T(1,128)S(1)}, s32[128,1]{0,1:T(1,128)}, u32[]{:S(2)}) copy-start(s32[128,1]{0,1:T(1,128)} %param.16) | copy-start | bytes 1540
  13.7 2.7 %collective-permute-start.8 = (f32[4,4,2,16,512]{4,3,2,1,0:T(8,128)S(1)}, f32[4,4,2,16,512]{4,3,2,1,0:T(8,128)S(1)}, u32[]{:S(2)}, u32[]{:S(2)}) collective-permute-start(f32[4,4,2,16,512]{4,3,2,1,0:T(8,128)S(1)} %bitcast.124), channel_id=1, source_target_pairs={{0,1},{1,0},{2,3},{3,2},{4,5},{5,4},{6,7},{7,6},{8,9},{9,8},{10,11... | collective-permute-start | bytes 3145736 | tf_op jit(solution)/shard_map/ppermute | solution.py:48
  13.8 4.5 %collective-permute-start.10 = (f32[4,4,2,16,512]{4,3,2,1,0:T(8,128)S(1)}, f32[4,4,2,16,512]{4,3,2,1,0:T(8,128)S(1)}, u32[]{:S(2)}, u32[]{:S(2)}) collective-permute-start(f32[4,4,2,16,512]{4,3,2,1,0:T(8,128)S(1)} %bitcast.123), channel_id=1, source_target_pairs={{0,1},{1,0},{2,3},{3,2},{4,5},{5,4},{6,7},{7,6},{8,9},{9,8},{10,11... | collective-permute-start | bytes 3145736 | tf_op jit(solution)/shard_map/ppermute | solution.py:48
  14.3 7.1 %collective-permute-start.12 = (f32[4,4,2,16,512]{4,3,2,1,0:T(8,128)S(1)}, f32[4,4,2,16,512]{4,3,2,1,0:T(8,128)S(1)}, u32[]{:S(2)}, u32[]{:S(2)}) collective-permute-start(f32[4,4,2,16,512]{4,3,2,1,0:T(8,128)S(1)} %bitcast.122), channel_id=1, source_target_pairs={{0,1},{1,0},{2,3},{3,2},{4,5},{5,4},{6,7},{7,6},{8,9},{9,8},{10,11... | collective-permute-start | bytes 3145736 | tf_op jit(solution)/shard_map/ppermute | solution.py:48
  14.4 8.7 %collective-permute-start.7 = (f32[4,4,2,16,512]{4,3,2,1,0:T(8,128)S(1)}, f32[4,4,2,16,512]{4,3,2,1,0:T(8,128)S(1)}, u32[]{:S(2)}, u32[]{:S(2)}) collective-permute-start(f32[4,4,2,16,512]{4,3,2,1,0:T(8,128)S(1)} %bitcast.121), channel_id=1, source_target_pairs={{0,1},{1,0},{2,3},{3,2},{4,5},{5,4},{6,7},{7,6},{8,9},{9,8},{10,11... | collective-permute-start | bytes 3145736 | tf_op jit(solution)/shard_map/ppermute | solution.py:48
  16.7 16.1 %collective-permute-start.9 = (f32[4,4,2,16,512]{4,3,2,1,0:T(8,128)S(1)}, f32[4,4,2,16,512]{4,3,2,1,0:T(8,128)S(1)}, u32[]{:S(2)}, u32[]{:S(2)}) collective-permute-start(f32[4,4,2,16,512]{4,3,2,1,0:T(8,128)S(1)} %add.200), channel_id=1, source_target_pairs={{0,2},{1,9},{2,4},{3,11},{4,6},{5,13},{6,0},{7,15},{8,10},{9,17},{... | collective-permute-start | bytes 3145736 | tf_op jit(solution)/shard_map/ppermute | solution.py:50
  18.6 26.5 %collective-permute-start.11 = (f32[4,4,2,16,512]{4,3,2,1,0:T(8,128)S(1)}, f32[4,4,2,16,512]{4,3,2,1,0:T(8,128)S(1)}, u32[]{:S(2)}, u32[]{:S(2)}) collective-permute-start(f32[4,4,2,16,512]{4,3,2,1,0:T(8,128)S(1)} %add.202), channel_id=1, source_target_pairs={{0,4},{1,17},{2,6},{3,19},{4,0},{5,21},{6,2},{7,23},{8,12},{9,25},... | collective-permute-start | bytes 3145736 | tf_op jit(solution)/shard_map/ppermute | solution.py:49
  21.6 24.4 %collective-permute-start.13 = (f32[4,4,2,16,512]{4,3,2,1,0:T(8,128)S(1)}, f32[4,4,2,16,512]{4,3,2,1,0:T(8,128)S(1)}, u32[]{:S(2)}, u32[]{:S(2)}) collective-permute-start(f32[4,4,2,16,512]{4,3,2,1,0:T(8,128)S(1)} %add.204), channel_id=1, source_target_pairs={{0,6},{1,25},{2,0},{3,27},{4,2},{5,29},{6,4},{7,31},{8,14},{9,1},{... | collective-permute-start | bytes 3145736 | tf_op jit(solution)/shard_map/ppermute | solution.py:50
  46.0 19.4 %copy-start = (f32[8,2,16,512]{3,2,1,0:T(8,128)S(1)}, f32[8,2,16,512]{3,2,1,0:T(8,128)}, u32[]{:S(2)}) copy-start(f32[8,2,16,512]{3,2,1,0:T(8,128)} %param.10) | copy-start | bytes 1572868
  46.0 22.3 %copy-start.1 = (f32[2,512]{1,0:T(2,128)S(1)}, f32[2,512]{1,0:T(2,128)}, u32[]{:S(2)}) copy-start(f32[2,512]{1,0:T(2,128)} %param.11) | copy-start | bytes 12292
  46.7 8.5 %collective-permute-start.14 = (f32[4,2,16,512]{3,2,1,0:T(8,128)S(1)}, f32[4,2,16,512]{3,2,1,0:T(8,128)S(1)}, u32[]{:S(2)}, u32[]{:S(2)}) collective-permute-start(f32[4,2,16,512]{3,2,1,0:T(8,128)S(1)} %get-tuple-element.29), channel_id=1, source_target_pairs={{0,8},{1,3},{2,10},{3,5},{4,12},{5,7},{6,14},{7,1},{8,16},{9,11},{... | collective-permute-start | bytes 786440 | tf_op jit(solution)/shard_map/ppermute | solution.py:43
  48.7 10.7 %collective-permute-start.15 = (f32[4,2,16,512]{3,2,1,0:T(8,128)S(1)}, f32[4,2,16,512]{3,2,1,0:T(8,128)S(1)}, u32[]{:S(2)}, u32[]{:S(2)}) collective-permute-start(f32[4,2,16,512]{3,2,1,0:T(8,128)S(1)} %get-tuple-element.31), channel_id=1, source_target_pairs={{0,16},{1,5},{2,18},{3,7},{4,20},{5,1},{6,22},{7,3},{8,24},{9,13},... | collective-permute-start | bytes 786440 | tf_op jit(solution)/shard_map/ppermute | solution.py:43
  52.3 7.2 %collective-permute-start.16 = (f32[4,2,16,512]{3,2,1,0:T(8,128)S(1)}, f32[4,2,16,512]{3,2,1,0:T(8,128)S(1)}, u32[]{:S(2)}, u32[]{:S(2)}) collective-permute-start(f32[4,2,16,512]{3,2,1,0:T(8,128)S(1)} %get-tuple-element.30), channel_id=1, source_target_pairs={{0,24},{1,7},{2,26},{3,1},{4,28},{5,3},{6,30},{7,5},{8,0},{9,15},{... | collective-permute-start | bytes 786440 | tf_op jit(solution)/shard_map/ppermute | solution.py:43
  59.6 7.3 %collective-permute-start.17 = (f32[2,16,512]{2,1,0:T(8,128)S(1)}, f32[2,16,512]{2,1,0:T(8,128)S(1)}, u32[]{:S(2)}, u32[]{:S(2)}) collective-permute-start(f32[2,16,512]{2,1,0:T(8,128)S(1)} %get-tuple-element.32), channel_id=1, source_target_pairs={{0,32},{1,33},{2,34},{3,35},{4,36},{5,37},{6,38},{7,39},{8,40},{9,... | collective-permute-start | bytes 196616 | tf_op jit(solution)/shard_map/ppermute | solution.py:43
  61.2 5.8 %collective-permute-start.18 = (f32[2,16,512]{2,1,0:T(8,128)S(1)}, f32[2,16,512]{2,1,0:T(8,128)S(1)}, u32[]{:S(2)}, u32[]{:S(2)}) collective-permute-start(f32[2,16,512]{2,1,0:T(8,128)S(1)} %get-tuple-element.34), channel_id=1, source_target_pairs={{0,64},{1,65},{2,66},{3,67},{4,68},{5,69},{6,70},{7,71},{8,72},{9,... | collective-permute-start | bytes 196616 | tf_op jit(solution)/shard_map/ppermute | solution.py:43
  64.1 4.3 %collective-permute-start.19 = (f32[2,16,512]{2,1,0:T(8,128)S(1)}, f32[2,16,512]{2,1,0:T(8,128)S(1)}, u32[]{:S(2)}, u32[]{:S(2)}) collective-permute-start(f32[2,16,512]{2,1,0:T(8,128)S(1)} %get-tuple-element.33), channel_id=1, source_target_pairs={{0,96},{1,97},{2,98},{3,99},{4,100},{5,101},{6,102},{7,103},{8,104... | collective-permute-start | bytes 196616 | tf_op jit(solution)/shard_map/ppermute | solution.py:43
  70.0 1.4 %collective-permute-start.20 = (f32[73,16]{1,0:T(8,128)S(1)}, f32[73,16]{1,0:T(8,128)S(1)}, u32[]{:S(2)}, u32[]{:S(2)}) collective-permute-start(f32[73,16]{1,0:T(8,128)S(1)} %pad_maximum_fusion), channel_id=1, source_target_pairs={{0,1},{1,0},{2,3},{3,2},{4,5},{5,4},{6,7},{7,6},{8,9},{9,8},{10,11... | collective-permute-start | bytes 14024 | tf_op jit(solution)/shard_map/ppermute | solution.py:33
  71.5 4.1 %collective-permute-start.21 = (f32[73,16]{1,0:T(8,128)S(1)}, f32[73,16]{1,0:T(8,128)S(1)}, u32[]{:S(2)}, u32[]{:S(2)}) collective-permute-start(f32[73,16]{1,0:T(8,128)S(1)} %fusion.32), channel_id=1, source_target_pairs={{0,2},{1,3},{2,0},{3,1},{4,6},{5,7},{6,4},{7,5},{8,10},{9,11},{10,... | collective-permute-start | bytes 14024 | tf_op jit(solution)/shard_map/ppermute | solution.py:36
  75.6 5.2 %collective-permute-start.22 = (f32[73,16]{1,0:T(8,128)S(1)}, f32[73,16]{1,0:T(8,128)S(1)}, u32[]{:S(2)}, u32[]{:S(2)}) collective-permute-start(f32[73,16]{1,0:T(8,128)S(1)} %add.214), channel_id=1, source_target_pairs={{0,6},{1,7},{2,4},{3,5},{4,2},{5,3},{6,0},{7,1},{8,14},{9,15},{10,... | collective-permute-start | bytes 14024 | tf_op jit(solution)/shard_map/ppermute | solution.py:36
  80.8 4.0 %collective-permute-start.23 = (f32[73,16]{1,0:T(8,128)S(1)}, f32[73,16]{1,0:T(8,128)S(1)}, u32[]{:S(2)}, u32[]{:S(2)}) collective-permute-start(f32[73,16]{1,0:T(8,128)S(1)} %add.215), channel_id=1, source_target_pairs={{0,8},{1,9},{2,10},{3,11},{4,12},{5,13},{6,14},{7,15},{8,0},{9,1},... | collective-permute-start | bytes 14024 | tf_op jit(solution)/shard_map/ppermute | solution.py:36
  84.8 5.2 %collective-permute-start.24 = (f32[73,16]{1,0:T(8,128)S(1)}, f32[73,16]{1,0:T(8,128)S(1)}, u32[]{:S(2)}, u32[]{:S(2)}) collective-permute-start(f32[73,16]{1,0:T(8,128)S(1)} %add.216), channel_id=1, source_target_pairs={{0,24},{1,25},{2,26},{3,27},{4,28},{5,29},{6,30},{7,31},{8,16},{9,... | collective-permute-start | bytes 14024 | tf_op jit(solution)/shard_map/ppermute | solution.py:36
  90.0 4.0 %collective-permute-start.25 = (f32[73,16]{1,0:T(8,128)S(1)}, f32[73,16]{1,0:T(8,128)S(1)}, u32[]{:S(2)}, u32[]{:S(2)}) collective-permute-start(f32[73,16]{1,0:T(8,128)S(1)} %add.217), channel_id=1, source_target_pairs={{0,32},{1,33},{2,34},{3,35},{4,36},{5,37},{6,38},{7,39},{8,40},{9,... | collective-permute-start | bytes 14024 | tf_op jit(solution)/shard_map/ppermute | solution.py:36
  94.0 5.2 %collective-permute-start.26 = (f32[73,16]{1,0:T(8,128)S(1)}, f32[73,16]{1,0:T(8,128)S(1)}, u32[]{:S(2)}, u32[]{:S(2)}) collective-permute-start(f32[73,16]{1,0:T(8,128)S(1)} %add.218), channel_id=1, source_target_pairs={{0,96},{1,97},{2,98},{3,99},{4,100},{5,101},{6,102},{7,103},{8,104... | collective-permute-start | bytes 14024 | tf_op jit(solution)/shard_map/ppermute | solution.py:36

commit v13 on v12

--- a/solution.py
+++ b/solution.py
@@ -38,10 +38,9 @@
 
 
 def spread(pieces, axis, other=None):
-    acc = pieces[0]
-    for k in (1, 2, 3):
-        acc = acc + lax.ppermute(pieces[k], AXES, moved(axis, k, other))
-    return acc
+    far = lax.ppermute(pieces[2], AXES, moved(axis, 2, other))
+    near = [lax.ppermute(pieces[k], AXES, moved(axis, k, other)) for k in (1, 3)]
+    return pieces[0] + near[0] + far + near[1]
 
 
 def reduce_to_owner(keep, send):

time: 103 us -> 103 us (level)
  no operation moved by 1% of the time
where the time goes in v13:
time: 103 us
  waiting for transfers between devices  50.2 us (49%)
  starting transfers between devices  30.7 us (30%)
  matrix products  10.7 us (10%)
  other arithmetic  4.28 us (4%)
  local copies, waits for them, and re-layouts  3.09 us (3%)
  Pallas kernels  2.36 us (2%)
  between operations  1.55 us (2%)
    ppermute x6, waiting for transfers between devices, all_sum(): v = v + lax.ppermute(v, AXES, flipped(step * STRIDE[axis]))  16.8 us
    ppermute x1, waiting for transfers between devices, reduce_to_owner(): far = lax.ppermute(pieces[2], AXES, moved('x', 2, 'z'))  12.3 us
    ppermute x6, starting transfers between devices, all_sum(): v = v + lax.ppermute(v, AXES, flipped(step * STRIDE[axis]))  10.9 us
    ppermute x2, waiting for transfers between devices, reduce_to_owner(): near = [lax.ppermute(pieces[k], AXES, moved('x', k, 'z')) for k in (1, 3)]  10.6 us
    ppermute x2, starting transfers between devices, spread(): far = lax.ppermute(pieces[2], AXES, moved(axis, 2, other))  6.48 us
    ppermute x4, starting transfers between devices, spread(): lax.ppermute(pieces[k], AXES, moved(axis, k, other))  5.99 us
    ppermute x2, waiting for transfers between devices, spread(): far = lax.ppermute(pieces[2], AXES, moved(axis, 2, other))  4.42 us
    dot_general x1, matrix products, step(): jnp.einsum('snc,skc->snk', picked[near_count:], far_u, preferred_element_...  3.24 us
  transfers between devices with their start and end apart: 20, of which 15 were waited for; matrix products, arithmetic and copies ran while one was open for 2% of the time, Pallas kernels for 0%

profile of v13, /device:TPU:0, one launch (start us, length us, event | category | flops | bytes accessed | tf_op | source)
XLA Modules:
  0.0 102.9 jit_solution(8716098934090164775)
XLA Ops:
  0.7 0.8 bitcast_convert_fusion
  1.6 0.7 compare_select_fusion
  2.2 0.7 gather_fusion
  2.9 3.2 %convolution_convert_fusion = bf16[112,16,32]{2,1,0:T(8,128)(2,1)S(1)} fusion(bf16[128,16,512]{2,1,0:T(8,128)(2,1)S(1)} %gather_fusion, bf16[112,32,512]{2,1,0:T(8,128)(2,1)} %param.13), kind=kOutput, calls=%fused_computation.3 | convolution fusion | flops 58777600 | bytes 5881856 | tf_op jit(solution)/shard_map/snc,skc->snk/dot_general | solution.py:123
  6.2 1.2 %copy-done.4 = bf16[16,512,512]{2,1,0:T(8,128)(2,1)S(1)} copy-done((bf16[16,512,512]{2,1,0:T(8,128)(2,1)S(1)}, bf16[16,512,512]{2,1,0:T(8,128)(2,1)}, u32[]{:S(2)}) %copy-start.4) | copy-done | bytes 8388632
  7.4 1.2 %fusion.35.near_ref = f32[16,16,512]{2,1,0:T(8,128)S(1)} fusion(bf16[128,16,512]{2,1,0:T(8,128)(2,1)S(1)} %gather_fusion, bf16[16,512,512]{2,1,0:T(8,128)(2,1)S(1)} %copy-done.4), kind=kOutput, calls=%fused_computation.104 | convolution fusion | flops 134217728 | bytes 11010048 | tf_op jit(solution)/shard_map/snc,scd->snd/dot_general | solution.py:120
  8.6 2.7 %fusion.34.far_ref = f32[112,16,512]{2,1,0:T(8,128)S(1)} fusion(bf16[112,16,32]{2,1,0:T(8,128)(2,1)S(1)} %convolution_convert_fusion, bf16[112,32,512]{2,1,0:T(8,128)(2,1)} %param.14), kind=kOutput, calls=%fused_computation.103 | convolution fusion | flops 58720256 | bytes 7454720 | tf_op jit(solution)/shard_map/snk,skc->snc/dot_general | solution.py:126
  11.3 2.4 %shard_map.95 = (f32[32,16,512]{2,1,0:T(8,128)S(1)}, f32[32,16,512]{2,1,0:T(8,128)S(1)}, f32[32,16,512]{2,1,0:T(8,128)S(1)}, f32[32,16,512]{2,1,0:T(8,128)S(1)},...) custom-call(s32[128]{0:T(128)S(1)} %multiply_add_fusion.slot_ref, ...), custom_call_target="tpu_custom_call" | custom-call | tf_op jit(solution)/shard_map/pallas_call | solution.py:98
  13.8 0.5 collective-permute-start.10
  14.4 0.4 collective-permute-start.7
  14.8 1.6 %collective-permute-done.8 = f32[4,4,2,16,512]{4,3,2,1,0:T(8,128)S(1)} collective-permute-done((f32[4,4,2,16,512]{4,3,2,1,0:T(8,128)S(1)}, f32[4,4,2,16,512]{4,3,2,1,0:T(8,128)S(1)}, u32[]{:S(2)}, u32[]{:S(2)}) %collective-permute-start.8) | collective-permute-done | bytes 1048608 | tf_op jit(solution)/shard_map/ppermute | solution.py:47
  16.5 0.2 add.200
  16.7 1.7 %collective-permute-start.9 = (f32[4,4,2,16,512]{4,3,2,1,0:T(8,128)S(1)}, f32[4,4,2,16,512]{4,3,2,1,0:T(8,128)S(1)}, u32[]{:S(2)}, u32[]{:S(2)}) collective-permute-start(f32[4,4,2,16,512]{4,3,2,1,0:T(8,128)S(1)} %add.200), channel_id=1, source_target_pairs={{0,2},{1,9},{2,4},{3,11},{4,6},{5,13},{6,0},{7,15},{8,10},{9,17},{... | collective-permute-start | bytes 3145736 | tf_op jit(solution)/shard_map/ppermute | solution.py:49
  18.6 2.8 %collective-permute-start.11 = (f32[4,4,2,16,512]{4,3,2,1,0:T(8,128)S(1)}, f32[4,4,2,16,512]{4,3,2,1,0:T(8,128)S(1)}, u32[]{:S(2)}, u32[]{:S(2)}) collective-permute-start(f32[4,4,2,16,512]{4,3,2,1,0:T(8,128)S(1)} %add.202), channel_id=1, source_target_pairs={{0,4},{1,17},{2,6},{3,19},{4,0},{5,21},{6,2},{7,23},{8,12},{9,25},... | collective-permute-start | bytes 3145736 | tf_op jit(solution)/shard_map/ppermute | solution.py:48
  21.6 1.5 %collective-permute-start.13 = (f32[4,4,2,16,512]{4,3,2,1,0:T(8,128)S(1)}, f32[4,4,2,16,512]{4,3,2,1,0:T(8,128)S(1)}, u32[]{:S(2)}, u32[]{:S(2)}) collective-permute-start(f32[4,4,2,16,512]{4,3,2,1,0:T(8,128)S(1)} %add.204), channel_id=1, source_target_pairs={{0,6},{1,25},{2,0},{3,27},{4,2},{5,29},{6,4},{7,31},{8,14},{9,1},{... | collective-permute-start | bytes 3145736 | tf_op jit(solution)/shard_map/ppermute | solution.py:49
  23.1 9.7 %collective-permute-done.9 = f32[4,4,2,16,512]{4,3,2,1,0:T(8,128)S(1)} collective-permute-done((f32[4,4,2,16,512]{4,3,2,1,0:T(8,128)S(1)}, f32[4,4,2,16,512]{4,3,2,1,0:T(8,128)S(1)}, u32[]{:S(2)}, u32[]{:S(2)}) %collective-permute-start.9) | collective-permute-done | bytes 1048608 | tf_op jit(solution)/shard_map/ppermute | solution.py:49
  32.7 12.3 %collective-permute-done.11 = f32[4,4,2,16,512]{4,3,2,1,0:T(8,128)S(1)} collective-permute-done((f32[4,4,2,16,512]{4,3,2,1,0:T(8,128)S(1)}, f32[4,4,2,16,512]{4,3,2,1,0:T(8,128)S(1)}, u32[]{:S(2)}, u32[]{:S(2)}) %collective-permute-start.11) | collective-permute-done | bytes 1048608 | tf_op jit(solution)/shard_map/ppermute | solution.py:48
  45.1 0.9 collective-permute-done.13
  46.0 0.6 add_add_fusion
  46.7 2.0 %collective-permute-start.14 = (f32[4,2,16,512]{3,2,1,0:T(8,128)S(1)}, f32[4,2,16,512]{3,2,1,0:T(8,128)S(1)}, u32[]{:S(2)}, u32[]{:S(2)}) collective-permute-start(f32[4,2,16,512]{3,2,1,0:T(8,128)S(1)} %get-tuple-element.29), channel_id=1, source_target_pairs={{0,8},{1,3},{2,10},{3,5},{4,12},{5,7},{6,14},{7,1},{8,16},{9,11},{... | collective-permute-start | bytes 786440 | tf_op jit(solution)/shard_map/ppermute | solution.py:42
  48.7 3.6 %collective-permute-start.15 = (f32[4,2,16,512]{3,2,1,0:T(8,128)S(1)}, f32[4,2,16,512]{3,2,1,0:T(8,128)S(1)}, u32[]{:S(2)}, u32[]{:S(2)}) collective-permute-start(f32[4,2,16,512]{3,2,1,0:T(8,128)S(1)} %get-tuple-element.31), channel_id=1, source_target_pairs={{0,16},{1,5},{2,18},{3,7},{4,20},{5,1},{6,22},{7,3},{8,24},{9,13},... | collective-permute-start | bytes 786440 | tf_op jit(solution)/shard_map/ppermute | solution.py:41
  52.3 1.0 collective-permute-start.16
  53.3 1.9 %collective-permute-done.14 = f32[4,2,16,512]{3,2,1,0:T(8,128)S(1)} collective-permute-done((f32[4,2,16,512]{3,2,1,0:T(8,128)S(1)}, f32[4,2,16,512]{3,2,1,0:T(8,128)S(1)}, u32[]{:S(2)}, u32[]{:S(2)}) %collective-permute-start.14) | collective-permute-done | bytes 262176 | tf_op jit(solution)/shard_map/ppermute | solution.py:42
  55.2 4.3 %collective-permute-done.15 = f32[4,2,16,512]{3,2,1,0:T(8,128)S(1)} collective-permute-done((f32[4,2,16,512]{3,2,1,0:T(8,128)S(1)}, f32[4,2,16,512]{3,2,1,0:T(8,128)S(1)}, u32[]{:S(2)}, u32[]{:S(2)}) %collective-permute-start.15) | collective-permute-done | bytes 262176 | tf_op jit(solution)/shard_map/ppermute | solution.py:41
  59.6 1.6 %collective-permute-start.17 = (f32[2,16,512]{2,1,0:T(8,128)S(1)}, f32[2,16,512]{2,1,0:T(8,128)S(1)}, u32[]{:S(2)}, u32[]{:S(2)}) collective-permute-start(f32[2,16,512]{2,1,0:T(8,128)S(1)} %get-tuple-element.32), channel_id=1, source_target_pairs={{0,32},{1,33},{2,34},{3,35},{4,36},{5,37},{6,38},{7,39},{8,40},{9,... | collective-permute-start | bytes 196616 | tf_op jit(solution)/shard_map/ppermute | solution.py:42
  61.2 2.9 %collective-permute-start.18 = (f32[2,16,512]{2,1,0:T(8,128)S(1)}, f32[2,16,512]{2,1,0:T(8,128)S(1)}, u32[]{:S(2)}, u32[]{:S(2)}) collective-permute-start(f32[2,16,512]{2,1,0:T(8,128)S(1)} %get-tuple-element.34), channel_id=1, source_target_pairs={{0,64},{1,65},{2,66},{3,67},{4,68},{5,69},{6,70},{7,71},{8,72},{9,... | collective-permute-start | bytes 196616 | tf_op jit(solution)/shard_map/ppermute | solution.py:41
  64.1 1.3 %collective-permute-start.19 = (f32[2,16,512]{2,1,0:T(8,128)S(1)}, f32[2,16,512]{2,1,0:T(8,128)S(1)}, u32[]{:S(2)}, u32[]{:S(2)}) collective-permute-start(f32[2,16,512]{2,1,0:T(8,128)S(1)} %get-tuple-element.33), channel_id=1, source_target_pairs={{0,96},{1,97},{2,98},{3,99},{4,100},{5,101},{6,102},{7,103},{8,104... | collective-permute-start | bytes 196616 | tf_op jit(solution)/shard_map/ppermute | solution.py:42
  65.5 1.3 %convolution_bitcast_fusion = f32[8,8,16]{0,1,2:T(8,128)S(1)} fusion(f32[8,2,16,512]{3,2,1,0:T(8,128)S(1)} %copy-done), kind=kOutput, calls=%fused_computation.4 | convolution fusion | flops 12582912 | bytes 528384 | tf_op jit(solution)/shard_map/knjc,mnjc->kmj/dot_general | solution.py:140
  67.0 1.3 %collective-permute-done.19 = f32[2,16,512]{2,1,0:T(8,128)S(1)} collective-permute-done((f32[2,16,512]{2,1,0:T(8,128)S(1)}, f32[2,16,512]{2,1,0:T(8,128)S(1)}, u32[]{:S(2)}, u32[]{:S(2)}) %collective-permute-start.19) | collective-permute-done | bytes 65568 | tf_op jit(solution)/shard_map/ppermute | solution.py:42
  68.5 1.5 %fusion.2 = f32[16,1,8,1]{2,1,3,0:T(1,128)S(1)} fusion(f32[8,2,16,512]{3,2,1,0:T(8,128)S(1)} %copy-done, f32[2,16,512,1]{2,1,0,3:T(8,128)S(1)} %bitcast.125), kind=kOutput, calls=%fused_computation.8 | convolution fusion | flops 1572864 | bytes 590336 | tf_op jit(solution)/shard_map/knjc,njc->kj/dot_general | solution.py:139
  70.0 0.2 collective-permute-start.20
  70.3 1.2 %collective-permute-done.20 = f32[73,16]{1,0:T(8,128)S(1)} collective-permute-done((f32[73,16]{1,0:T(8,128)S(1)}, f32[73,16]{1,0:T(8,128)S(1)}, u32[]{:S(2)}, u32[]{:S(2)}) %collective-permute-start.20) | collective-permute-done | bytes 4704 | tf_op jit(solution)/shard_map/ppermute | solution.py:33
  71.5 1.7 %collective-permute-start.21 = (f32[73,16]{1,0:T(8,128)S(1)}, f32[73,16]{1,0:T(8,128)S(1)}, u32[]{:S(2)}, u32[]{:S(2)}) collective-permute-start(f32[73,16]{1,0:T(8,128)S(1)} %fusion.32), channel_id=1, source_target_pairs={{0,2},{1,3},{2,0},{3,1},{4,6},{5,7},{6,4},{7,5},{8,10},{9,11},{10,... | collective-permute-start | bytes 14024 | tf_op jit(solution)/shard_map/ppermute | solution.py:36
  73.2 2.4 %collective-permute-done.21 = f32[73,16]{1,0:T(8,128)S(1)} collective-permute-done((f32[73,16]{1,0:T(8,128)S(1)}, f32[73,16]{1,0:T(8,128)S(1)}, u32[]{:S(2)}, u32[]{:S(2)}) %collective-permute-start.21) | collective-permute-done | bytes 4704 | tf_op jit(solution)/shard_map/ppermute | solution.py:36
  75.6 2.6 %collective-permute-start.22 = (f32[73,16]{1,0:T(8,128)S(1)}, f32[73,16]{1,0:T(8,128)S(1)}, u32[]{:S(2)}, u32[]{:S(2)}) collective-permute-start(f32[73,16]{1,0:T(8,128)S(1)} %add.214), channel_id=1, source_target_pairs={{0,6},{1,7},{2,4},{3,5},{4,2},{5,3},{6,0},{7,1},{8,14},{9,15},{10,... | collective-permute-start | bytes 14024 | tf_op jit(solution)/shard_map/ppermute | solution.py:36
  78.2 2.6 %collective-permute-done.22 = f32[73,16]{1,0:T(8,128)S(1)} collective-permute-done((f32[73,16]{1,0:T(8,128)S(1)}, f32[73,16]{1,0:T(8,128)S(1)}, u32[]{:S(2)}, u32[]{:S(2)}) %collective-permute-start.22) | collective-permute-done | bytes 4704 | tf_op jit(solution)/shard_map/ppermute | solution.py:36
  80.8 1.5 %collective-permute-start.23 = (f32[73,16]{1,0:T(8,128)S(1)}, f32[73,16]{1,0:T(8,128)S(1)}, u32[]{:S(2)}, u32[]{:S(2)}) collective-permute-start(f32[73,16]{1,0:T(8,128)S(1)} %add.215), channel_id=1, source_target_pairs={{0,8},{1,9},{2,10},{3,11},{4,12},{5,13},{6,14},{7,15},{8,0},{9,1},... | collective-permute-start | bytes 14024 | tf_op jit(solution)/shard_map/ppermute | solution.py:36
  82.3 2.5 %collective-permute-done.23 = f32[73,16]{1,0:T(8,128)S(1)} collective-permute-done((f32[73,16]{1,0:T(8,128)S(1)}, f32[73,16]{1,0:T(8,128)S(1)}, u32[]{:S(2)}, u32[]{:S(2)}) %collective-permute-start.23) | collective-permute-done | bytes 4704 | tf_op jit(solution)/shard_map/ppermute | solution.py:36
  84.8 2.2 %collective-permute-start.24 = (f32[73,16]{1,0:T(8,128)S(1)}, f32[73,16]{1,0:T(8,128)S(1)}, u32[]{:S(2)}, u32[]{:S(2)}) collective-permute-start(f32[73,16]{1,0:T(8,128)S(1)} %add.216), channel_id=1, source_target_pairs={{0,24},{1,25},{2,26},{3,27},{4,28},{5,29},{6,30},{7,31},{8,16},{9,... | collective-permute-start | bytes 14024 | tf_op jit(solution)/shard_map/ppermute | solution.py:36
  87.0 3.1 %collective-permute-done.24 = f32[73,16]{1,0:T(8,128)S(1)} collective-permute-done((f32[73,16]{1,0:T(8,128)S(1)}, f32[73,16]{1,0:T(8,128)S(1)}, u32[]{:S(2)}, u32[]{:S(2)}) %collective-permute-start.24) | collective-permute-done | bytes 4704 | tf_op jit(solution)/shard_map/ppermute | solution.py:36
  90.0 0.3 collective-permute-start.25
  90.4 3.7 %collective-permute-done.25 = f32[73,16]{1,0:T(8,128)S(1)} collective-permute-done((f32[73,16]{1,0:T(8,128)S(1)}, f32[73,16]{1,0:T(8,128)S(1)}, u32[]{:S(2)}, u32[]{:S(2)}) %collective-permute-start.25) | collective-permute-done | bytes 4704 | tf_op jit(solution)/shard_map/ppermute | solution.py:36
  94.0 2.6 %collective-permute-start.26 = (f32[73,16]{1,0:T(8,128)S(1)}, f32[73,16]{1,0:T(8,128)S(1)}, u32[]{:S(2)}, u32[]{:S(2)}) collective-permute-start(f32[73,16]{1,0:T(8,128)S(1)} %add.218), channel_id=1, source_target_pairs={{0,96},{1,97},{2,98},{3,99},{4,100},{5,101},{6,102},{7,103},{8,104... | collective-permute-start | bytes 14024 | tf_op jit(solution)/shard_map/ppermute | solution.py:36
  96.6 2.7 %collective-permute-done.26 = f32[73,16]{1,0:T(8,128)S(1)} collective-permute-done((f32[73,16]{1,0:T(8,128)S(1)}, f32[73,16]{1,0:T(8,128)S(1)}, u32[]{:S(2)}, u32[]{:S(2)}) %collective-permute-start.26) | collective-permute-done | bytes 4704 | tf_op jit(solution)/shard_map/ppermute | solution.py:36
  99.4 0.6 compare_reduce_fusion
  100.7 0.8 fusion
  101.6 0.6 pad_maximum_fusion.1
  102.2 0.7 broadcast_divide_fusion
  (45 shorter events, 1.5 us)
Async XLA Ops:
  2.9 4.5 %copy-start.4 = (bf16[16,512,512]{2,1,0:T(8,128)(2,1)S(1)}, bf16[16,512,512]{2,1,0:T(8,128)(2,1)}, u32[]{:S(2)}) copy-start(bf16[16,512,512]{2,1,0:T(8,128)(2,1)} %param.12) | copy-start | bytes 25165828
  8.6 2.7 %copy-start.2 = (s32[128]{0:T(128)S(1)}, s32[128]{0:T(128)}, u32[]{:S(2)}) copy-start(s32[128]{0:T(128)} %param.17) | copy-start | bytes 1540
  8.6 2.7 %copy-start.3 = (s32[128,1]{0,1:T(1,128)S(1)}, s32[128,1]{0,1:T(1,128)}, u32[]{:S(2)}) copy-start(s32[128,1]{0,1:T(1,128)} %param.16) | copy-start | bytes 1540
  13.7 2.7 %collective-permute-start.8 = (f32[4,4,2,16,512]{4,3,2,1,0:T(8,128)S(1)}, f32[4,4,2,16,512]{4,3,2,1,0:T(8,128)S(1)}, u32[]{:S(2)}, u32[]{:S(2)}) collective-permute-start(f32[4,4,2,16,512]{4,3,2,1,0:T(8,128)S(1)} %bitcast.124), channel_id=1, source_target_pairs={{0,1},{1,0},{2,3},{3,2},{4,5},{5,4},{6,7},{7,6},{8,9},{9,8},{10,11... | collective-permute-start | bytes 3145736 | tf_op jit(solution)/shard_map/ppermute | solution.py:47
  13.8 4.5 %collective-permute-start.10 = (f32[4,4,2,16,512]{4,3,2,1,0:T(8,128)S(1)}, f32[4,4,2,16,512]{4,3,2,1,0:T(8,128)S(1)}, u32[]{:S(2)}, u32[]{:S(2)}) collective-permute-start(f32[4,4,2,16,512]{4,3,2,1,0:T(8,128)S(1)} %bitcast.123), channel_id=1, source_target_pairs={{0,1},{1,0},{2,3},{3,2},{4,5},{5,4},{6,7},{7,6},{8,9},{9,8},{10,11... | collective-permute-start | bytes 3145736 | tf_op jit(solution)/shard_map/ppermute | solution.py:47
  14.3 7.1 %collective-permute-start.12 = (f32[4,4,2,16,512]{4,3,2,1,0:T(8,128)S(1)}, f32[4,4,2,16,512]{4,3,2,1,0:T(8,128)S(1)}, u32[]{:S(2)}, u32[]{:S(2)}) collective-permute-start(f32[4,4,2,16,512]{4,3,2,1,0:T(8,128)S(1)} %bitcast.122), channel_id=1, source_target_pairs={{0,1},{1,0},{2,3},{3,2},{4,5},{5,4},{6,7},{7,6},{8,9},{9,8},{10,11... | collective-permute-start | bytes 3145736 | tf_op jit(solution)/shard_map/ppermute | solution.py:47
  14.4 8.7 %collective-permute-start.7 = (f32[4,4,2,16,512]{4,3,2,1,0:T(8,128)S(1)}, f32[4,4,2,16,512]{4,3,2,1,0:T(8,128)S(1)}, u32[]{:S(2)}, u32[]{:S(2)}) collective-permute-start(f32[4,4,2,16,512]{4,3,2,1,0:T(8,128)S(1)} %bitcast.121), channel_id=1, source_target_pairs={{0,1},{1,0},{2,3},{3,2},{4,5},{5,4},{6,7},{7,6},{8,9},{9,8},{10,11... | collective-permute-start | bytes 3145736 | tf_op jit(solution)/shard_map/ppermute | solution.py:47
  16.7 16.1 %collective-permute-start.9 = (f32[4,4,2,16,512]{4,3,2,1,0:T(8,128)S(1)}, f32[4,4,2,16,512]{4,3,2,1,0:T(8,128)S(1)}, u32[]{:S(2)}, u32[]{:S(2)}) collective-permute-start(f32[4,4,2,16,512]{4,3,2,1,0:T(8,128)S(1)} %add.200), channel_id=1, source_target_pairs={{0,2},{1,9},{2,4},{3,11},{4,6},{5,13},{6,0},{7,15},{8,10},{9,17},{... | collective-permute-start | bytes 3145736 | tf_op jit(solution)/shard_map/ppermute | solution.py:49
  18.6 26.5 %collective-permute-start.11 = (f32[4,4,2,16,512]{4,3,2,1,0:T(8,128)S(1)}, f32[4,4,2,16,512]{4,3,2,1,0:T(8,128)S(1)}, u32[]{:S(2)}, u32[]{:S(2)}) collective-permute-start(f32[4,4,2,16,512]{4,3,2,1,0:T(8,128)S(1)} %add.202), channel_id=1, source_target_pairs={{0,4},{1,17},{2,6},{3,19},{4,0},{5,21},{6,2},{7,23},{8,12},{9,25},... | collective-permute-start | bytes 3145736 | tf_op jit(solution)/shard_map/ppermute | solution.py:48
  21.6 24.4 %collective-permute-start.13 = (f32[4,4,2,16,512]{4,3,2,1,0:T(8,128)S(1)}, f32[4,4,2,16,512]{4,3,2,1,0:T(8,128)S(1)}, u32[]{:S(2)}, u32[]{:S(2)}) collective-permute-start(f32[4,4,2,16,512]{4,3,2,1,0:T(8,128)S(1)} %add.204), channel_id=1, source_target_pairs={{0,6},{1,25},{2,0},{3,27},{4,2},{5,29},{6,4},{7,31},{8,14},{9,1},{... | collective-permute-start | bytes 3145736 | tf_op jit(solution)/shard_map/ppermute | solution.py:49
  46.0 19.4 %copy-start = (f32[8,2,16,512]{3,2,1,0:T(8,128)S(1)}, f32[8,2,16,512]{3,2,1,0:T(8,128)}, u32[]{:S(2)}) copy-start(f32[8,2,16,512]{3,2,1,0:T(8,128)} %param.10) | copy-start | bytes 1572868
  46.0 22.3 %copy-start.1 = (f32[2,512]{1,0:T(2,128)S(1)}, f32[2,512]{1,0:T(2,128)}, u32[]{:S(2)}) copy-start(f32[2,512]{1,0:T(2,128)} %param.11) | copy-start | bytes 12292
  46.7 8.5 %collective-permute-start.14 = (f32[4,2,16,512]{3,2,1,0:T(8,128)S(1)}, f32[4,2,16,512]{3,2,1,0:T(8,128)S(1)}, u32[]{:S(2)}, u32[]{:S(2)}) collective-permute-start(f32[4,2,16,512]{3,2,1,0:T(8,128)S(1)} %get-tuple-element.29), channel_id=1, source_target_pairs={{0,8},{1,3},{2,10},{3,5},{4,12},{5,7},{6,14},{7,1},{8,16},{9,11},{... | collective-permute-start | bytes 786440 | tf_op jit(solution)/shard_map/ppermute | solution.py:42
  48.7 10.7 %collective-permute-start.15 = (f32[4,2,16,512]{3,2,1,0:T(8,128)S(1)}, f32[4,2,16,512]{3,2,1,0:T(8,128)S(1)}, u32[]{:S(2)}, u32[]{:S(2)}) collective-permute-start(f32[4,2,16,512]{3,2,1,0:T(8,128)S(1)} %get-tuple-element.31), channel_id=1, source_target_pairs={{0,16},{1,5},{2,18},{3,7},{4,20},{5,1},{6,22},{7,3},{8,24},{9,13},... | collective-permute-start | bytes 786440 | tf_op jit(solution)/shard_map/ppermute | solution.py:41
  52.3 7.2 %collective-permute-start.16 = (f32[4,2,16,512]{3,2,1,0:T(8,128)S(1)}, f32[4,2,16,512]{3,2,1,0:T(8,128)S(1)}, u32[]{:S(2)}, u32[]{:S(2)}) collective-permute-start(f32[4,2,16,512]{3,2,1,0:T(8,128)S(1)} %get-tuple-element.30), channel_id=1, source_target_pairs={{0,24},{1,7},{2,26},{3,1},{4,28},{5,3},{6,30},{7,5},{8,0},{9,15},{... | collective-permute-start | bytes 786440 | tf_op jit(solution)/shard_map/ppermute | solution.py:42
  59.6 7.3 %collective-permute-start.17 = (f32[2,16,512]{2,1,0:T(8,128)S(1)}, f32[2,16,512]{2,1,0:T(8,128)S(1)}, u32[]{:S(2)}, u32[]{:S(2)}) collective-permute-start(f32[2,16,512]{2,1,0:T(8,128)S(1)} %get-tuple-element.32), channel_id=1, source_target_pairs={{0,32},{1,33},{2,34},{3,35},{4,36},{5,37},{6,38},{7,39},{8,40},{9,... | collective-permute-start | bytes 196616 | tf_op jit(solution)/shard_map/ppermute | solution.py:42
  61.2 5.8 %collective-permute-start.18 = (f32[2,16,512]{2,1,0:T(8,128)S(1)}, f32[2,16,512]{2,1,0:T(8,128)S(1)}, u32[]{:S(2)}, u32[]{:S(2)}) collective-permute-start(f32[2,16,512]{2,1,0:T(8,128)S(1)} %get-tuple-element.34), channel_id=1, source_target_pairs={{0,64},{1,65},{2,66},{3,67},{4,68},{5,69},{6,70},{7,71},{8,72},{9,... | collective-permute-start | bytes 196616 | tf_op jit(solution)/shard_map/ppermute | solution.py:41
  64.1 4.3 %collective-permute-start.19 = (f32[2,16,512]{2,1,0:T(8,128)S(1)}, f32[2,16,512]{2,1,0:T(8,128)S(1)}, u32[]{:S(2)}, u32[]{:S(2)}) collective-permute-start(f32[2,16,512]{2,1,0:T(8,128)S(1)} %get-tuple-element.33), channel_id=1, source_target_pairs={{0,96},{1,97},{2,98},{3,99},{4,100},{5,101},{6,102},{7,103},{8,104... | collective-permute-start | bytes 196616 | tf_op jit(solution)/shard_map/ppermute | solution.py:42
  70.0 1.4 %collective-permute-start.20 = (f32[73,16]{1,0:T(8,128)S(1)}, f32[73,16]{1,0:T(8,128)S(1)}, u32[]{:S(2)}, u32[]{:S(2)}) collective-permute-start(f32[73,16]{1,0:T(8,128)S(1)} %pad_maximum_fusion), channel_id=1, source_target_pairs={{0,1},{1,0},{2,3},{3,2},{4,5},{5,4},{6,7},{7,6},{8,9},{9,8},{10,11... | collective-permute-start | bytes 14024 | tf_op jit(solution)/shard_map/ppermute | solution.py:33
  71.5 4.1 %collective-permute-start.21 = (f32[73,16]{1,0:T(8,128)S(1)}, f32[73,16]{1,0:T(8,128)S(1)}, u32[]{:S(2)}, u32[]{:S(2)}) collective-permute-start(f32[73,16]{1,0:T(8,128)S(1)} %fusion.32), channel_id=1, source_target_pairs={{0,2},{1,3},{2,0},{3,1},{4,6},{5,7},{6,4},{7,5},{8,10},{9,11},{10,... | collective-permute-start | bytes 14024 | tf_op jit(solution)/shard_map/ppermute | solution.py:36
  75.6 5.2 %collective-permute-start.22 = (f32[73,16]{1,0:T(8,128)S(1)}, f32[73,16]{1,0:T(8,128)S(1)}, u32[]{:S(2)}, u32[]{:S(2)}) collective-permute-start(f32[73,16]{1,0:T(8,128)S(1)} %add.214), channel_id=1, source_target_pairs={{0,6},{1,7},{2,4},{3,5},{4,2},{5,3},{6,0},{7,1},{8,14},{9,15},{10,... | collective-permute-start | bytes 14024 | tf_op jit(solution)/shard_map/ppermute | solution.py:36
  80.8 4.0 %collective-permute-start.23 = (f32[73,16]{1,0:T(8,128)S(1)}, f32[73,16]{1,0:T(8,128)S(1)}, u32[]{:S(2)}, u32[]{:S(2)}) collective-permute-start(f32[73,16]{1,0:T(8,128)S(1)} %add.215), channel_id=1, source_target_pairs={{0,8},{1,9},{2,10},{3,11},{4,12},{5,13},{6,14},{7,15},{8,0},{9,1},... | collective-permute-start | bytes 14024 | tf_op jit(solution)/shard_map/ppermute | solution.py:36
  84.8 5.2 %collective-permute-start.24 = (f32[73,16]{1,0:T(8,128)S(1)}, f32[73,16]{1,0:T(8,128)S(1)}, u32[]{:S(2)}, u32[]{:S(2)}) collective-permute-start(f32[73,16]{1,0:T(8,128)S(1)} %add.216), channel_id=1, source_target_pairs={{0,24},{1,25},{2,26},{3,27},{4,28},{5,29},{6,30},{7,31},{8,16},{9,... | collective-permute-start | bytes 14024 | tf_op jit(solution)/shard_map/ppermute | solution.py:36
  90.0 4.0 %collective-permute-start.25 = (f32[73,16]{1,0:T(8,128)S(1)}, f32[73,16]{1,0:T(8,128)S(1)}, u32[]{:S(2)}, u32[]{:S(2)}) collective-permute-start(f32[73,16]{1,0:T(8,128)S(1)} %add.217), channel_id=1, source_target_pairs={{0,32},{1,33},{2,34},{3,35},{4,36},{5,37},{6,38},{7,39},{8,40},{9,... | collective-permute-start | bytes 14024 | tf_op jit(solution)/shard_map/ppermute | solution.py:36
  94.0 5.2 %collective-permute-start.26 = (f32[73,16]{1,0:T(8,128)S(1)}, f32[73,16]{1,0:T(8,128)S(1)}, u32[]{:S(2)}, u32[]{:S(2)}) collective-permute-start(f32[73,16]{1,0:T(8,128)S(1)} %add.218), channel_id=1, source_target_pairs={{0,96},{1,97},{2,98},{3,99},{4,100},{5,101},{6,102},{7,103},{8,104... | collective-permute-start | bytes 14024 | tf_op jit(solution)/shard_map/ppermute | solution.py:36

commit v14 on v13

--- a/solution.py
+++ b/solution.py
@@ -31,7 +31,7 @@
 
 def all_sum(v):
     v = v + lax.ppermute(v, AXES, flipped(1))
-    for axis in ("x", "z", "y"):
+    for axis in ("y", "z", "x"):
         for step in (1, 3):
             v = v + lax.ppermute(v, AXES, flipped(step * STRIDE[axis]))
     return v
@@ -105,6 +105,10 @@
     )(slot, near_part, far_part)
 
 
+def orthogonal(image, total, basis):
+    return image - jnp.einsum("kj,knjc->njc", total, basis, precision=lax.Precision.HIGHEST)
+
+
 def step(basis, diagonal, near_blocks, far_u, far_v, block_row, block_dest, block_col):
     highest = lax.Precision.HIGHEST
     basis_count = basis.shape[0]
@@ -147,7 +151,6 @@
     size = both[-1] / panels
     second = first - jnp.einsum("kmj,mj->kj", gram, first, precision=highest)
     total = first + second
-    twice = image - jnp.einsum("kj,knjc->njc", total, basis, precision=highest)
     cross = jnp.sum(total * first, axis=0)
     curve = jnp.sum(total * jnp.einsum("kmj,mj->kj", gram, total, precision=highest), axis=0)
     formula = size - 2.0 * cross + curve
@@ -155,8 +158,9 @@
     square = lax.cond(
         trusted,
         lambda: formula,
-        lambda: all_sum(jnp.sum(twice * twice, axis=(0, 2))) / panels,
+        lambda: all_sum(jnp.sum(orthogonal(image, total, basis) ** 2, axis=(0, 2))) / panels,
     )
+    twice = orthogonal(image, total, basis)
     beta = jnp.sqrt(square + 1e-06)
     next_vector = twice / beta[None, :, None]
     hess_column = jnp.concatenate([total, beta[None, :]], axis=0)

time: 103 us -> 103 us (level)
  no operation moved by 1% of the time
where the time goes in v14:
time: 103 us
  waiting for transfers between devices  50.2 us (49%)
  starting transfers between devices  30.7 us (30%)
  matrix products  10.7 us (10%)
  other arithmetic  4.26 us (4%)
  local copies, waits for them, and re-layouts  3.09 us (3%)
  Pallas kernels  2.36 us (2%)
  between operations  1.54 us (1%)
    ppermute x6, waiting for transfers between devices, all_sum(): v = v + lax.ppermute(v, AXES, flipped(step * STRIDE[axis]))  16.8 us
    ppermute x1, waiting for transfers between devices, reduce_to_owner(): far = lax.ppermute(pieces[2], AXES, moved('x', 2, 'z'))  12.3 us
    ppermute x6, starting transfers between devices, all_sum(): v = v + lax.ppermute(v, AXES, flipped(step * STRIDE[axis]))  10.9 us
    ppermute x2, waiting for transfers between devices, reduce_to_owner(): near = [lax.ppermute(pieces[k], AXES, moved('x', k, 'z')) for k in (1, 3)]  10.6 us
    ppermute x2, starting transfers between devices, spread(): far = lax.ppermute(pieces[2], AXES, moved(axis, 2, other))  6.48 us
    ppermute x4, starting transfers between devices, spread(): lax.ppermute(pieces[k], AXES, moved(axis, k, other))  5.99 us
    ppermute x2, waiting for transfers between devices, spread(): far = lax.ppermute(pieces[2], AXES, moved(axis, 2, other))  4.42 us
    dot_general x1, matrix products, step(): jnp.einsum('snc,skc->snk', picked[near_count:], far_u, preferred_element_...  3.24 us
  transfers between devices with their start and end apart: 20, of which 15 were waited for; matrix products, arithmetic and copies ran while one was open for 2% of the time, Pallas kernels for 0%

profile of v14, /device:TPU:0, one launch (start us, length us, event | category | flops | bytes accessed | tf_op | source)
XLA Modules:
  0.0 102.9 jit_solution(2556441606998552397)
XLA Ops:
  0.7 0.8 bitcast_convert_fusion
  1.6 0.7 compare_select_fusion
  2.2 0.7 gather_fusion
  2.9 3.2 %convolution_convert_fusion = bf16[112,16,32]{2,1,0:T(8,128)(2,1)S(1)} fusion(bf16[128,16,512]{2,1,0:T(8,128)(2,1)S(1)} %gather_fusion, bf16[112,32,512]{2,1,0:T(8,128)(2,1)} %param.13), kind=kOutput, calls=%fused_computation.7 | convolution fusion | flops 58777600 | bytes 5881856 | tf_op jit(solution)/shard_map/snc,skc->snk/dot_general | solution.py:127
  6.2 1.2 %copy-done.4 = bf16[16,512,512]{2,1,0:T(8,128)(2,1)S(1)} copy-done((bf16[16,512,512]{2,1,0:T(8,128)(2,1)S(1)}, bf16[16,512,512]{2,1,0:T(8,128)(2,1)}, u32[]{:S(2)}) %copy-start.4) | copy-done | bytes 8388632
  7.4 1.2 %fusion.40.near_ref = f32[16,16,512]{2,1,0:T(8,128)S(1)} fusion(bf16[128,16,512]{2,1,0:T(8,128)(2,1)S(1)} %gather_fusion, bf16[16,512,512]{2,1,0:T(8,128)(2,1)S(1)} %copy-done.4), kind=kOutput, calls=%fused_computation.108 | convolution fusion | flops 134217728 | bytes 11010048 | tf_op jit(solution)/shard_map/snc,scd->snd/dot_general | solution.py:124
  8.6 2.7 %fusion.39.far_ref = f32[112,16,512]{2,1,0:T(8,128)S(1)} fusion(bf16[112,16,32]{2,1,0:T(8,128)(2,1)S(1)} %convolution_convert_fusion, bf16[112,32,512]{2,1,0:T(8,128)(2,1)} %param.14), kind=kOutput, calls=%fused_computation.107 | convolution fusion | flops 58720256 | bytes 7454720 | tf_op jit(solution)/shard_map/snk,skc->snc/dot_general | solution.py:130
  11.3 2.4 %shard_map.95 = (f32[32,16,512]{2,1,0:T(8,128)S(1)}, f32[32,16,512]{2,1,0:T(8,128)S(1)}, f32[32,16,512]{2,1,0:T(8,128)S(1)}, f32[32,16,512]{2,1,0:T(8,128)S(1)},...) custom-call(s32[128]{0:T(128)S(1)} %multiply_add_fusion.slot_ref, ...), custom_call_target="tpu_custom_call" | custom-call | tf_op jit(solution)/shard_map/pallas_call | solution.py:98
  13.8 0.5 collective-permute-start.10
  14.4 0.4 collective-permute-start.7
  14.8 1.6 %collective-permute-done.8 = f32[4,4,2,16,512]{4,3,2,1,0:T(8,128)S(1)} collective-permute-done((f32[4,4,2,16,512]{4,3,2,1,0:T(8,128)S(1)}, f32[4,4,2,16,512]{4,3,2,1,0:T(8,128)S(1)}, u32[]{:S(2)}, u32[]{:S(2)}) %collective-permute-start.8) | collective-permute-done | bytes 1048608 | tf_op jit(solution)/shard_map/ppermute | solution.py:47
  16.5 0.2 add.200
  16.7 1.7 %collective-permute-start.9 = (f32[4,4,2,16,512]{4,3,2,1,0:T(8,128)S(1)}, f32[4,4,2,16,512]{4,3,2,1,0:T(8,128)S(1)}, u32[]{:S(2)}, u32[]{:S(2)}) collective-permute-start(f32[4,4,2,16,512]{4,3,2,1,0:T(8,128)S(1)} %add.200), channel_id=1, source_target_pairs={{0,2},{1,9},{2,4},{3,11},{4,6},{5,13},{6,0},{7,15},{8,10},{9,17},{... | collective-permute-start | bytes 3145736 | tf_op jit(solution)/shard_map/ppermute | solution.py:49
  18.6 2.8 %collective-permute-start.11 = (f32[4,4,2,16,512]{4,3,2,1,0:T(8,128)S(1)}, f32[4,4,2,16,512]{4,3,2,1,0:T(8,128)S(1)}, u32[]{:S(2)}, u32[]{:S(2)}) collective-permute-start(f32[4,4,2,16,512]{4,3,2,1,0:T(8,128)S(1)} %add.202), channel_id=1, source_target_pairs={{0,4},{1,17},{2,6},{3,19},{4,0},{5,21},{6,2},{7,23},{8,12},{9,25},... | collective-permute-start | bytes 3145736 | tf_op jit(solution)/shard_map/ppermute | solution.py:48
  21.6 1.5 %collective-permute-start.13 = (f32[4,4,2,16,512]{4,3,2,1,0:T(8,128)S(1)}, f32[4,4,2,16,512]{4,3,2,1,0:T(8,128)S(1)}, u32[]{:S(2)}, u32[]{:S(2)}) collective-permute-start(f32[4,4,2,16,512]{4,3,2,1,0:T(8,128)S(1)} %add.204), channel_id=1, source_target_pairs={{0,6},{1,25},{2,0},{3,27},{4,2},{5,29},{6,4},{7,31},{8,14},{9,1},{... | collective-permute-start | bytes 3145736 | tf_op jit(solution)/shard_map/ppermute | solution.py:49
  23.1 9.7 %collective-permute-done.9 = f32[4,4,2,16,512]{4,3,2,1,0:T(8,128)S(1)} collective-permute-done((f32[4,4,2,16,512]{4,3,2,1,0:T(8,128)S(1)}, f32[4,4,2,16,512]{4,3,2,1,0:T(8,128)S(1)}, u32[]{:S(2)}, u32[]{:S(2)}) %collective-permute-start.9) | collective-permute-done | bytes 1048608 | tf_op jit(solution)/shard_map/ppermute | solution.py:49
  32.7 12.3 %collective-permute-done.11 = f32[4,4,2,16,512]{4,3,2,1,0:T(8,128)S(1)} collective-permute-done((f32[4,4,2,16,512]{4,3,2,1,0:T(8,128)S(1)}, f32[4,4,2,16,512]{4,3,2,1,0:T(8,128)S(1)}, u32[]{:S(2)}, u32[]{:S(2)}) %collective-permute-start.11) | collective-permute-done | bytes 1048608 | tf_op jit(solution)/shard_map/ppermute | solution.py:48
  45.1 0.9 collective-permute-done.13
  46.0 0.6 add_add_fusion
  46.7 2.0 %collective-permute-start.14 = (f32[4,2,16,512]{3,2,1,0:T(8,128)S(1)}, f32[4,2,16,512]{3,2,1,0:T(8,128)S(1)}, u32[]{:S(2)}, u32[]{:S(2)}) collective-permute-start(f32[4,2,16,512]{3,2,1,0:T(8,128)S(1)} %get-tuple-element.40), channel_id=1, source_target_pairs={{0,8},{1,3},{2,10},{3,5},{4,12},{5,7},{6,14},{7,1},{8,16},{9,11},{... | collective-permute-start | bytes 786440 | tf_op jit(solution)/shard_map/ppermute | solution.py:42
  48.7 3.6 %collective-permute-start.15 = (f32[4,2,16,512]{3,2,1,0:T(8,128)S(1)}, f32[4,2,16,512]{3,2,1,0:T(8,128)S(1)}, u32[]{:S(2)}, u32[]{:S(2)}) collective-permute-start(f32[4,2,16,512]{3,2,1,0:T(8,128)S(1)} %get-tuple-element.42), channel_id=1, source_target_pairs={{0,16},{1,5},{2,18},{3,7},{4,20},{5,1},{6,22},{7,3},{8,24},{9,13},... | collective-permute-start | bytes 786440 | tf_op jit(solution)/shard_map/ppermute | solution.py:41
  52.3 1.0 collective-permute-start.16
  53.3 1.9 %collective-permute-done.14 = f32[4,2,16,512]{3,2,1,0:T(8,128)S(1)} collective-permute-done((f32[4,2,16,512]{3,2,1,0:T(8,128)S(1)}, f32[4,2,16,512]{3,2,1,0:T(8,128)S(1)}, u32[]{:S(2)}, u32[]{:S(2)}) %collective-permute-start.14) | collective-permute-done | bytes 262176 | tf_op jit(solution)/shard_map/ppermute | solution.py:42
  55.2 4.3 %collective-permute-done.15 = f32[4,2,16,512]{3,2,1,0:T(8,128)S(1)} collective-permute-done((f32[4,2,16,512]{3,2,1,0:T(8,128)S(1)}, f32[4,2,16,512]{3,2,1,0:T(8,128)S(1)}, u32[]{:S(2)}, u32[]{:S(2)}) %collective-permute-start.15) | collective-permute-done | bytes 262176 | tf_op jit(solution)/shard_map/ppermute | solution.py:41
  59.6 1.6 %collective-permute-start.17 = (f32[2,16,512]{2,1,0:T(8,128)S(1)}, f32[2,16,512]{2,1,0:T(8,128)S(1)}, u32[]{:S(2)}, u32[]{:S(2)}) collective-permute-start(f32[2,16,512]{2,1,0:T(8,128)S(1)} %get-tuple-element.43), channel_id=1, source_target_pairs={{0,32},{1,33},{2,34},{3,35},{4,36},{5,37},{6,38},{7,39},{8,40},{9,... | collective-permute-start | bytes 196616 | tf_op jit(solution)/shard_map/ppermute | solution.py:42
  61.2 2.9 %collective-permute-start.18 = (f32[2,16,512]{2,1,0:T(8,128)S(1)}, f32[2,16,512]{2,1,0:T(8,128)S(1)}, u32[]{:S(2)}, u32[]{:S(2)}) collective-permute-start(f32[2,16,512]{2,1,0:T(8,128)S(1)} %get-tuple-element.45), channel_id=1, source_target_pairs={{0,64},{1,65},{2,66},{3,67},{4,68},{5,69},{6,70},{7,71},{8,72},{9,... | collective-permute-start | bytes 196616 | tf_op jit(solution)/shard_map/ppermute | solution.py:41
  64.1 1.3 %collective-permute-start.19 = (f32[2,16,512]{2,1,0:T(8,128)S(1)}, f32[2,16,512]{2,1,0:T(8,128)S(1)}, u32[]{:S(2)}, u32[]{:S(2)}) collective-permute-start(f32[2,16,512]{2,1,0:T(8,128)S(1)} %get-tuple-element.44), channel_id=1, source_target_pairs={{0,96},{1,97},{2,98},{3,99},{4,100},{5,101},{6,102},{7,103},{8,104... | collective-permute-start | bytes 196616 | tf_op jit(solution)/shard_map/ppermute | solution.py:42
  65.5 1.3 %convolution_bitcast_fusion = f32[8,8,16]{0,1,2:T(8,128)S(1)} fusion(f32[8,2,16,512]{3,2,1,0:T(8,128)S(1)} %copy-done), kind=kOutput, calls=%fused_computation.8 | convolution fusion | flops 12582912 | bytes 528384 | tf_op jit(solution)/shard_map/knjc,mnjc->kmj/dot_general | solution.py:144
  67.0 1.3 %collective-permute-done.19 = f32[2,16,512]{2,1,0:T(8,128)S(1)} collective-permute-done((f32[2,16,512]{2,1,0:T(8,128)S(1)}, f32[2,16,512]{2,1,0:T(8,128)S(1)}, u32[]{:S(2)}, u32[]{:S(2)}) %collective-permute-start.19) | collective-permute-done | bytes 65568 | tf_op jit(solution)/shard_map/ppermute | solution.py:42
  68.5 1.5 %fusion.6 = f32[16,1,8,1]{2,1,3,0:T(1,128)S(1)} fusion(f32[8,2,16,512]{3,2,1,0:T(8,128)S(1)} %copy-done, f32[2,16,512,1]{2,1,0,3:T(8,128)S(1)} %bitcast.137), kind=kOutput, calls=%fused_computation.12 | convolution fusion | flops 1572864 | bytes 590336 | tf_op jit(solution)/shard_map/knjc,njc->kj/dot_general | solution.py:143
  70.0 0.2 collective-permute-start.20
  70.3 1.2 %collective-permute-done.20 = f32[73,16]{1,0:T(8,128)S(1)} collective-permute-done((f32[73,16]{1,0:T(8,128)S(1)}, f32[73,16]{1,0:T(8,128)S(1)}, u32[]{:S(2)}, u32[]{:S(2)}) %collective-permute-start.20) | collective-permute-done | bytes 4704 | tf_op jit(solution)/shard_map/ppermute | solution.py:33
  71.5 0.4 collective-permute-start.21
  71.9 3.7 %collective-permute-done.21 = f32[73,16]{1,0:T(8,128)S(1)} collective-permute-done((f32[73,16]{1,0:T(8,128)S(1)}, f32[73,16]{1,0:T(8,128)S(1)}, u32[]{:S(2)}, u32[]{:S(2)}) %collective-permute-start.21) | collective-permute-done | bytes 4704 | tf_op jit(solution)/shard_map/ppermute | solution.py:36
  75.6 2.6 %collective-permute-start.22 = (f32[73,16]{1,0:T(8,128)S(1)}, f32[73,16]{1,0:T(8,128)S(1)}, u32[]{:S(2)}, u32[]{:S(2)}) collective-permute-start(f32[73,16]{1,0:T(8,128)S(1)} %add.214), channel_id=1, source_target_pairs={{0,96},{1,97},{2,98},{3,99},{4,100},{5,101},{6,102},{7,103},{8,104... | collective-permute-start | bytes 14024 | tf_op jit(solution)/shard_map/ppermute | solution.py:36
  78.1 2.7 %collective-permute-done.22 = f32[73,16]{1,0:T(8,128)S(1)} collective-permute-done((f32[73,16]{1,0:T(8,128)S(1)}, f32[73,16]{1,0:T(8,128)S(1)}, u32[]{:S(2)}, u32[]{:S(2)}) %collective-permute-start.22) | collective-permute-done | bytes 4704 | tf_op jit(solution)/shard_map/ppermute | solution.py:36
  80.8 1.5 %collective-permute-start.23 = (f32[73,16]{1,0:T(8,128)S(1)}, f32[73,16]{1,0:T(8,128)S(1)}, u32[]{:S(2)}, u32[]{:S(2)}) collective-permute-start(f32[73,16]{1,0:T(8,128)S(1)} %add.215), channel_id=1, source_target_pairs={{0,8},{1,9},{2,10},{3,11},{4,12},{5,13},{6,14},{7,15},{8,0},{9,1},... | collective-permute-start | bytes 14024 | tf_op jit(solution)/shard_map/ppermute | solution.py:36
  82.3 2.5 %collective-permute-done.23 = f32[73,16]{1,0:T(8,128)S(1)} collective-permute-done((f32[73,16]{1,0:T(8,128)S(1)}, f32[73,16]{1,0:T(8,128)S(1)}, u32[]{:S(2)}, u32[]{:S(2)}) %collective-permute-start.23) | collective-permute-done | bytes 4704 | tf_op jit(solution)/shard_map/ppermute | solution.py:36
  84.8 2.2 %collective-permute-start.24 = (f32[73,16]{1,0:T(8,128)S(1)}, f32[73,16]{1,0:T(8,128)S(1)}, u32[]{:S(2)}, u32[]{:S(2)}) collective-permute-start(f32[73,16]{1,0:T(8,128)S(1)} %add.216), channel_id=1, source_target_pairs={{0,24},{1,25},{2,26},{3,27},{4,28},{5,29},{6,30},{7,31},{8,16},{9,... | collective-permute-start | bytes 14024 | tf_op jit(solution)/shard_map/ppermute | solution.py:36
  87.0 3.1 %collective-permute-done.24 = f32[73,16]{1,0:T(8,128)S(1)} collective-permute-done((f32[73,16]{1,0:T(8,128)S(1)}, f32[73,16]{1,0:T(8,128)S(1)}, u32[]{:S(2)}, u32[]{:S(2)}) %collective-permute-start.24) | collective-permute-done | bytes 4704 | tf_op jit(solution)/shard_map/ppermute | solution.py:36
  90.0 1.6 %collective-permute-start.25 = (f32[73,16]{1,0:T(8,128)S(1)}, f32[73,16]{1,0:T(8,128)S(1)}, u32[]{:S(2)}, u32[]{:S(2)}) collective-permute-start(f32[73,16]{1,0:T(8,128)S(1)} %add.217), channel_id=1, source_target_pairs={{0,2},{1,3},{2,0},{3,1},{4,6},{5,7},{6,4},{7,5},{8,10},{9,11},{10,... | collective-permute-start | bytes 14024 | tf_op jit(solution)/shard_map/ppermute | solution.py:36
  91.7 2.4 %collective-permute-done.25 = f32[73,16]{1,0:T(8,128)S(1)} collective-permute-done((f32[73,16]{1,0:T(8,128)S(1)}, f32[73,16]{1,0:T(8,128)S(1)}, u32[]{:S(2)}, u32[]{:S(2)}) %collective-permute-start.25) | collective-permute-done | bytes 4704 | tf_op jit(solution)/shard_map/ppermute | solution.py:36
  94.0 2.6 %collective-permute-start.26 = (f32[73,16]{1,0:T(8,128)S(1)}, f32[73,16]{1,0:T(8,128)S(1)}, u32[]{:S(2)}, u32[]{:S(2)}) collective-permute-start(f32[73,16]{1,0:T(8,128)S(1)} %add.218), channel_id=1, source_target_pairs={{0,6},{1,7},{2,4},{3,5},{4,2},{5,3},{6,0},{7,1},{8,14},{9,15},{10,... | collective-permute-start | bytes 14024 | tf_op jit(solution)/shard_map/ppermute | solution.py:36
  96.7 2.6 %collective-permute-done.26 = f32[73,16]{1,0:T(8,128)S(1)} collective-permute-done((f32[73,16]{1,0:T(8,128)S(1)}, f32[73,16]{1,0:T(8,128)S(1)}, u32[]{:S(2)}, u32[]{:S(2)}) %collective-permute-start.26) | collective-permute-done | bytes 4704 | tf_op jit(solution)/shard_map/ppermute | solution.py:36
  99.4 0.6 compare_reduce_fusion
  100.7 0.6 pad_maximum_fusion.1
  101.4 0.8 fusion.4
  102.2 0.7 fusion.16
  (44 shorter events, 1.5 us)
Async XLA Ops:
  2.9 4.5 %copy-start.4 = (bf16[16,512,512]{2,1,0:T(8,128)(2,1)S(1)}, bf16[16,512,512]{2,1,0:T(8,128)(2,1)}, u32[]{:S(2)}) copy-start(bf16[16,512,512]{2,1,0:T(8,128)(2,1)} %param.12) | copy-start | bytes 25165828
  8.6 2.7 %copy-start.2 = (s32[128]{0:T(128)S(1)}, s32[128]{0:T(128)}, u32[]{:S(2)}) copy-start(s32[128]{0:T(128)} %param.17) | copy-start | bytes 1540
  8.6 2.7 %copy-start.3 = (s32[128,1]{0,1:T(1,128)S(1)}, s32[128,1]{0,1:T(1,128)}, u32[]{:S(2)}) copy-start(s32[128,1]{0,1:T(1,128)} %param.16) | copy-start | bytes 1540
  13.7 2.7 %collective-permute-start.8 = (f32[4,4,2,16,512]{4,3,2,1,0:T(8,128)S(1)}, f32[4,4,2,16,512]{4,3,2,1,0:T(8,128)S(1)}, u32[]{:S(2)}, u32[]{:S(2)}) collective-permute-start(f32[4,4,2,16,512]{4,3,2,1,0:T(8,128)S(1)} %bitcast.136), channel_id=1, source_target_pairs={{0,1},{1,0},{2,3},{3,2},{4,5},{5,4},{6,7},{7,6},{8,9},{9,8},{10,11... | collective-permute-start | bytes 3145736 | tf_op jit(solution)/shard_map/ppermute | solution.py:47
  13.8 4.5 %collective-permute-start.10 = (f32[4,4,2,16,512]{4,3,2,1,0:T(8,128)S(1)}, f32[4,4,2,16,512]{4,3,2,1,0:T(8,128)S(1)}, u32[]{:S(2)}, u32[]{:S(2)}) collective-permute-start(f32[4,4,2,16,512]{4,3,2,1,0:T(8,128)S(1)} %bitcast.135), channel_id=1, source_target_pairs={{0,1},{1,0},{2,3},{3,2},{4,5},{5,4},{6,7},{7,6},{8,9},{9,8},{10,11... | collective-permute-start | bytes 3145736 | tf_op jit(solution)/shard_map/ppermute | solution.py:47
  14.3 7.1 %collective-permute-start.12 = (f32[4,4,2,16,512]{4,3,2,1,0:T(8,128)S(1)}, f32[4,4,2,16,512]{4,3,2,1,0:T(8,128)S(1)}, u32[]{:S(2)}, u32[]{:S(2)}) collective-permute-start(f32[4,4,2,16,512]{4,3,2,1,0:T(8,128)S(1)} %bitcast.134), channel_id=1, source_target_pairs={{0,1},{1,0},{2,3},{3,2},{4,5},{5,4},{6,7},{7,6},{8,9},{9,8},{10,11... | collective-permute-start | bytes 3145736 | tf_op jit(solution)/shard_map/ppermute | solution.py:47
  14.4 8.7 %collective-permute-start.7 = (f32[4,4,2,16,512]{4,3,2,1,0:T(8,128)S(1)}, f32[4,4,2,16,512]{4,3,2,1,0:T(8,128)S(1)}, u32[]{:S(2)}, u32[]{:S(2)}) collective-permute-start(f32[4,4,2,16,512]{4,3,2,1,0:T(8,128)S(1)} %bitcast.133), channel_id=1, source_target_pairs={{0,1},{1,0},{2,3},{3,2},{4,5},{5,4},{6,7},{7,6},{8,9},{9,8},{10,11... | collective-permute-start | bytes 3145736 | tf_op jit(solution)/shard_map/ppermute | solution.py:47
  16.7 16.1 %collective-permute-start.9 = (f32[4,4,2,16,512]{4,3,2,1,0:T(8,128)S(1)}, f32[4,4,2,16,512]{4,3,2,1,0:T(8,128)S(1)}, u32[]{:S(2)}, u32[]{:S(2)}) collective-permute-start(f32[4,4,2,16,512]{4,3,2,1,0:T(8,128)S(1)} %add.200), channel_id=1, source_target_pairs={{0,2},{1,9},{2,4},{3,11},{4,6},{5,13},{6,0},{7,15},{8,10},{9,17},{... | collective-permute-start | bytes 3145736 | tf_op jit(solution)/shard_map/ppermute | solution.py:49
  18.6 26.5 %collective-permute-start.11 = (f32[4,4,2,16,512]{4,3,2,1,0:T(8,128)S(1)}, f32[4,4,2,16,512]{4,3,2,1,0:T(8,128)S(1)}, u32[]{:S(2)}, u32[]{:S(2)}) collective-permute-start(f32[4,4,2,16,512]{4,3,2,1,0:T(8,128)S(1)} %add.202), channel_id=1, source_target_pairs={{0,4},{1,17},{2,6},{3,19},{4,0},{5,21},{6,2},{7,23},{8,12},{9,25},... | collective-permute-start | bytes 3145736 | tf_op jit(solution)/shard_map/ppermute | solution.py:48
  21.6 24.4 %collective-permute-start.13 = (f32[4,4,2,16,512]{4,3,2,1,0:T(8,128)S(1)}, f32[4,4,2,16,512]{4,3,2,1,0:T(8,128)S(1)}, u32[]{:S(2)}, u32[]{:S(2)}) collective-permute-start(f32[4,4,2,16,512]{4,3,2,1,0:T(8,128)S(1)} %add.204), channel_id=1, source_target_pairs={{0,6},{1,25},{2,0},{3,27},{4,2},{5,29},{6,4},{7,31},{8,14},{9,1},{... | collective-permute-start | bytes 3145736 | tf_op jit(solution)/shard_map/ppermute | solution.py:49
  46.0 19.4 %copy-start = (f32[8,2,16,512]{3,2,1,0:T(8,128)S(1)}, f32[8,2,16,512]{3,2,1,0:T(8,128)}, u32[]{:S(2)}) copy-start(f32[8,2,16,512]{3,2,1,0:T(8,128)} %param.10) | copy-start | bytes 1572868
  46.0 22.3 %copy-start.1 = (f32[2,512]{1,0:T(2,128)S(1)}, f32[2,512]{1,0:T(2,128)}, u32[]{:S(2)}) copy-start(f32[2,512]{1,0:T(2,128)} %param.11) | copy-start | bytes 12292
  46.7 8.5 %collective-permute-start.14 = (f32[4,2,16,512]{3,2,1,0:T(8,128)S(1)}, f32[4,2,16,512]{3,2,1,0:T(8,128)S(1)}, u32[]{:S(2)}, u32[]{:S(2)}) collective-permute-start(f32[4,2,16,512]{3,2,1,0:T(8,128)S(1)} %get-tuple-element.40), channel_id=1, source_target_pairs={{0,8},{1,3},{2,10},{3,5},{4,12},{5,7},{6,14},{7,1},{8,16},{9,11},{... | collective-permute-start | bytes 786440 | tf_op jit(solution)/shard_map/ppermute | solution.py:42
  48.7 10.7 %collective-permute-start.15 = (f32[4,2,16,512]{3,2,1,0:T(8,128)S(1)}, f32[4,2,16,512]{3,2,1,0:T(8,128)S(1)}, u32[]{:S(2)}, u32[]{:S(2)}) collective-permute-start(f32[4,2,16,512]{3,2,1,0:T(8,128)S(1)} %get-tuple-element.42), channel_id=1, source_target_pairs={{0,16},{1,5},{2,18},{3,7},{4,20},{5,1},{6,22},{7,3},{8,24},{9,13},... | collective-permute-start | bytes 786440 | tf_op jit(solution)/shard_map/ppermute | solution.py:41
  52.3 7.2 %collective-permute-start.16 = (f32[4,2,16,512]{3,2,1,0:T(8,128)S(1)}, f32[4,2,16,512]{3,2,1,0:T(8,128)S(1)}, u32[]{:S(2)}, u32[]{:S(2)}) collective-permute-start(f32[4,2,16,512]{3,2,1,0:T(8,128)S(1)} %get-tuple-element.41), channel_id=1, source_target_pairs={{0,24},{1,7},{2,26},{3,1},{4,28},{5,3},{6,30},{7,5},{8,0},{9,15},{... | collective-permute-start | bytes 786440 | tf_op jit(solution)/shard_map/ppermute | solution.py:42
  59.6 7.3 %collective-permute-start.17 = (f32[2,16,512]{2,1,0:T(8,128)S(1)}, f32[2,16,512]{2,1,0:T(8,128)S(1)}, u32[]{:S(2)}, u32[]{:S(2)}) collective-permute-start(f32[2,16,512]{2,1,0:T(8,128)S(1)} %get-tuple-element.43), channel_id=1, source_target_pairs={{0,32},{1,33},{2,34},{3,35},{4,36},{5,37},{6,38},{7,39},{8,40},{9,... | collective-permute-start | bytes 196616 | tf_op jit(solution)/shard_map/ppermute | solution.py:42
  61.2 5.8 %collective-permute-start.18 = (f32[2,16,512]{2,1,0:T(8,128)S(1)}, f32[2,16,512]{2,1,0:T(8,128)S(1)}, u32[]{:S(2)}, u32[]{:S(2)}) collective-permute-start(f32[2,16,512]{2,1,0:T(8,128)S(1)} %get-tuple-element.45), channel_id=1, source_target_pairs={{0,64},{1,65},{2,66},{3,67},{4,68},{5,69},{6,70},{7,71},{8,72},{9,... | collective-permute-start | bytes 196616 | tf_op jit(solution)/shard_map/ppermute | solution.py:41
  64.1 4.3 %collective-permute-start.19 = (f32[2,16,512]{2,1,0:T(8,128)S(1)}, f32[2,16,512]{2,1,0:T(8,128)S(1)}, u32[]{:S(2)}, u32[]{:S(2)}) collective-permute-start(f32[2,16,512]{2,1,0:T(8,128)S(1)} %get-tuple-element.44), channel_id=1, source_target_pairs={{0,96},{1,97},{2,98},{3,99},{4,100},{5,101},{6,102},{7,103},{8,104... | collective-permute-start | bytes 196616 | tf_op jit(solution)/shard_map/ppermute | solution.py:42
  70.0 1.4 %collective-permute-start.20 = (f32[73,16]{1,0:T(8,128)S(1)}, f32[73,16]{1,0:T(8,128)S(1)}, u32[]{:S(2)}, u32[]{:S(2)}) collective-permute-start(f32[73,16]{1,0:T(8,128)S(1)} %pad_maximum_fusion), channel_id=1, source_target_pairs={{0,1},{1,0},{2,3},{3,2},{4,5},{5,4},{6,7},{7,6},{8,9},{9,8},{10,11... | collective-permute-start | bytes 14024 | tf_op jit(solution)/shard_map/ppermute | solution.py:33
  71.5 4.1 %collective-permute-start.21 = (f32[73,16]{1,0:T(8,128)S(1)}, f32[73,16]{1,0:T(8,128)S(1)}, u32[]{:S(2)}, u32[]{:S(2)}) collective-permute-start(f32[73,16]{1,0:T(8,128)S(1)} %fusion.37), channel_id=1, source_target_pairs={{0,32},{1,33},{2,34},{3,35},{4,36},{5,37},{6,38},{7,39},{8,40},{9,... | collective-permute-start | bytes 14024 | tf_op jit(solution)/shard_map/ppermute | solution.py:36
  75.6 5.2 %collective-permute-start.22 = (f32[73,16]{1,0:T(8,128)S(1)}, f32[73,16]{1,0:T(8,128)S(1)}, u32[]{:S(2)}, u32[]{:S(2)}) collective-permute-start(f32[73,16]{1,0:T(8,128)S(1)} %add.214), channel_id=1, source_target_pairs={{0,96},{1,97},{2,98},{3,99},{4,100},{5,101},{6,102},{7,103},{8,104... | collective-permute-start | bytes 14024 | tf_op jit(solution)/shard_map/ppermute | solution.py:36
  80.8 4.0 %collective-permute-start.23 = (f32[73,16]{1,0:T(8,128)S(1)}, f32[73,16]{1,0:T(8,128)S(1)}, u32[]{:S(2)}, u32[]{:S(2)}) collective-permute-start(f32[73,16]{1,0:T(8,128)S(1)} %add.215), channel_id=1, source_target_pairs={{0,8},{1,9},{2,10},{3,11},{4,12},{5,13},{6,14},{7,15},{8,0},{9,1},... | collective-permute-start | bytes 14024 | tf_op jit(solution)/shard_map/ppermute | solution.py:36
  84.8 5.2 %collective-permute-start.24 = (f32[73,16]{1,0:T(8,128)S(1)}, f32[73,16]{1,0:T(8,128)S(1)}, u32[]{:S(2)}, u32[]{:S(2)}) collective-permute-start(f32[73,16]{1,0:T(8,128)S(1)} %add.216), channel_id=1, source_target_pairs={{0,24},{1,25},{2,26},{3,27},{4,28},{5,29},{6,30},{7,31},{8,16},{9,... | collective-permute-start | bytes 14024 | tf_op jit(solution)/shard_map/ppermute | solution.py:36
  90.0 4.0 %collective-permute-start.25 = (f32[73,16]{1,0:T(8,128)S(1)}, f32[73,16]{1,0:T(8,128)S(1)}, u32[]{:S(2)}, u32[]{:S(2)}) collective-permute-start(f32[73,16]{1,0:T(8,128)S(1)} %add.217), channel_id=1, source_target_pairs={{0,2},{1,3},{2,0},{3,1},{4,6},{5,7},{6,4},{7,5},{8,10},{9,11},{10,... | collective-permute-start | bytes 14024 | tf_op jit(solution)/shard_map/ppermute | solution.py:36
  94.0 5.2 %collective-permute-start.26 = (f32[73,16]{1,0:T(8,128)S(1)}, f32[73,16]{1,0:T(8,128)S(1)}, u32[]{:S(2)}, u32[]{:S(2)}) collective-permute-start(f32[73,16]{1,0:T(8,128)S(1)} %add.218), channel_id=1, source_target_pairs={{0,6},{1,7},{2,4},{3,5},{4,2},{5,3},{6,0},{7,1},{8,14},{9,15},{10,... | collective-permute-start | bytes 14024 | tf_op jit(solution)/shard_map/ppermute | solution.py:36
